TPU v7x, 32 devices: a whole 2x2x4 slice. The times are simulated.
32 devices in a mesh: group: 2 (over core), gx: 4 (over y, x), gy: 4 (over z).
Axes of the slice: x: 2, y: 2, z: 4, core: 2. Of those that a mesh axis runs over, the one named last changes fastest.
Arguments:
- gradient_windows: bfloat16 [2, 4, 4, 256, 4, 2, 128], P('group', 'gx', 'gy'), may hold values from -6 to 6
- illumination_windows: bfloat16 [2, 4, 4, 256, 4, 2, 128], P('group', 'gx', 'gy'), may hold values from 0.25 to 8
- window_owners: int32 [2, 4, 4, 256], P('group', 'gx', 'gy'), may hold values from 0 to 15, as said below
- window_patches: int32 [2, 4, 4, 256], P('group', 'gx', 'gy'), may hold values from 0 to 7
- velocity: float32 [4, 64, 512], P(None, 'gx', 'gy'), may hold values from 1.5 to 4.5
Outputs:
- updated_model: float32 [4, 64, 512], P(None, 'gx', 'gy')
- returned_windows: bfloat16 [2, 4, 4, 256, 4, 2, 128], P('group', 'gx', 'gy')
Inputs may be any that keep to these rules, and one draw needn't show every extreme that they name: `window_owners`: the window patches of one device name any tile at most 20 times; one tile is named exactly 20 times by the window patches of every device.
All inputs are finite; a program needn't handle non-finite values.
Results may differ from a plain program's by a relative error of at most 0.001.
Values may be sent and summed in bfloat16 or wider, within the bound.
No kernel may reach another device: no remote copies, remote signals or barrier semaphores. Data moves between devices by JAX's collectives and lax.ppermute only.
A program may use at most 64 MiB of HBM per device.

v0:
```python
import jax
import jax.numpy as jnp
from jax import lax
from jax.sharding import PartitionSpec as P

SWEEPS = 4


damping = 10.0
smooth_rate = 0.12
step_length = 24.0


def with_halo(cells, sides, width):
    for axis, dim in sides:
        count = lax.axis_size(axis)
        ends = count - 1
        head = lax.slice_in_dim(cells, 0, width, axis=dim)
        tail = lax.slice_in_dim(cells, cells.shape[dim] - width, cells.shape[dim], axis=dim)
        cells = jnp.concatenate(
            [
                lax.ppermute(tail, axis, [(i, (i + 1) % count) for i in range(ends)]),
                cells,
                lax.ppermute(head, axis, [((i + 1) % count, i) for i in range(ends)]),
            ],
            axis=dim,
        )
    return cells


def deliver(send_grad, send_illum, send_patch, size_x, size_y, capacity):
    sectioned_grad = send_grad.reshape((size_x, size_y, capacity) + send_grad.shape[1:])
    sectioned_illum = send_illum.reshape((size_x, size_y, capacity) + send_illum.shape[1:])
    sectioned_patch = send_patch.reshape(size_x, size_y, capacity)
    got_grad, got_illum, got_patch = (
        lax.all_to_all(
            lax.all_to_all(sectioned_grad, "gx", split_axis=0, concat_axis=0, tiled=True),
            "gy",
            split_axis=1,
            concat_axis=1,
            tiled=True,
        ),
        lax.all_to_all(
            lax.all_to_all(sectioned_illum, "gx", split_axis=0, concat_axis=0, tiled=True),
            "gy",
            split_axis=1,
            concat_axis=1,
            tiled=True,
        ),
        lax.all_to_all(
            lax.all_to_all(sectioned_patch, "gx", split_axis=0, concat_axis=0, tiled=True),
            "gy",
            split_axis=1,
            concat_axis=1,
            tiled=True,
        ),
    )
    return (
        got_grad.reshape(send_grad.shape),
        got_illum.reshape(send_illum.shape),
        got_patch.reshape(send_patch.shape),
    )


def send_back(back_rows, size_x, size_y, capacity):
    sectioned_back = back_rows.reshape((size_x, size_y, capacity) + back_rows.shape[1:])
    arrived = lax.all_to_all(
        lax.all_to_all(sectioned_back, "gx", split_axis=0, concat_axis=0, tiled=True),
        "gy",
        split_axis=1,
        concat_axis=1,
        tiled=True,
    )
    return arrived.reshape(back_rows.shape)


def smooth_whole(field_now):
    for sweep_index in range(SWEEPS):
        padded = with_halo(field_now, (("gx", 1), ("gy", 2)), 1)
        depth_pad = jnp.pad(field_now, ((1, 1), (0, 0), (0, 0)))
        beside = (
            padded[:, 2:, 1:-1]
            + padded[:, :-2, 1:-1]
            + (padded[:, 1:-1, 2:] + padded[:, 1:-1, :-2])
            + (depth_pad[2:] + depth_pad[:-2])
        )
        field_now = field_now + smooth_rate * (beside - 6.0 * field_now)
    return field_now


def local(gradient_windows, illumination_windows, window_owners, window_patches, velocity):
    size_x = lax.axis_size("gx")
    size_y = lax.axis_size("gy")
    holder_count = size_x * size_y
    slot_grad = gradient_windows[0, 0, 0]
    slot_illum = illumination_windows[0, 0, 0]
    owners = window_owners[0, 0, 0]
    patches = window_patches[0, 0, 0]
    slot_count, levels, patch_rows, patch_cols = slot_grad.shape
    patch_count = velocity.shape[1] // patch_rows
    mean_load = slot_count // holder_count
    capacity = mean_load + max(1, slot_count // (4 * holder_count))
    rows_total = holder_count * capacity
    cell_count = levels * patch_rows * patch_cols
    member = (owners[:, None] == jnp.arange(holder_count, dtype=jnp.int32)[None, :]).astype(
        jnp.int32
    )
    slot_rank = jnp.sum(jnp.cumsum(member, axis=0) * member, axis=1) - 1
    position = owners * capacity + slot_rank
    send_grad = (
        jnp.zeros((rows_total, levels, patch_rows, patch_cols), jnp.bfloat16)
        .at[position]
        .set(slot_grad)
    )
    send_illum = (
        jnp.zeros((rows_total, levels, patch_rows, patch_cols), jnp.bfloat16)
        .at[position]
        .set(slot_illum)
    )
    send_patch = jnp.full((rows_total,), -1, jnp.int32).at[position].set(patches)
    got_grad, got_illum, got_patch = deliver(
        send_grad, send_illum, send_patch, size_x, size_y, capacity
    )
    onehot = (got_patch[None, :] == jnp.arange(patch_count, dtype=jnp.int32)[:, None]).astype(
        jnp.bfloat16
    )
    grad_sum = jnp.dot(
        onehot, got_grad.reshape(rows_total, cell_count), preferred_element_type=jnp.float32
    )
    illum_sum = jnp.dot(
        onehot, got_illum.reshape(rows_total, cell_count), preferred_element_type=jnp.float32
    )

    def to_tile(patch_sums):
        return (
            patch_sums.reshape(patch_count, levels, patch_rows, patch_cols)
            .transpose(1, 0, 2, 3)
            .reshape(levels, patch_count * patch_rows, patch_cols)
        )

    grad_total, illum_total = lax.psum((to_tile(grad_sum), to_tile(illum_sum)), "group")
    smoothed = smooth_whole(grad_total / (illum_total + damping))
    updated_model = velocity - step_length * smoothed
    patch_table = (
        updated_model.reshape(levels, patch_count, patch_rows, patch_cols)
        .transpose(1, 0, 2, 3)
        .reshape(patch_count, cell_count)
        .astype(jnp.bfloat16)
    )
    back_rows = jnp.dot(onehot.T, patch_table, preferred_element_type=jnp.float32).astype(
        jnp.bfloat16
    )
    back_rows = back_rows.reshape(rows_total, levels, patch_rows, patch_cols)
    arrived = send_back(back_rows, size_x, size_y, capacity)
    returned = jnp.take(arrived, position, axis=0)
    returned_windows = returned.reshape((1, 1, 1) + returned.shape)
    return (updated_model, returned_windows)


def solution(mesh):
    return jax.shard_map(
        local,
        mesh=mesh,
        in_specs=(
            P("group", "gx", "gy", None, None, None, None),
            P("group", "gx", "gy", None, None, None, None),
            P("group", "gx", "gy", None),
            P("group", "gx", "gy", None),
            P(None, "gx", "gy"),
        ),
        out_specs=(P(None, "gx", "gy"), P("group", "gx", "gy", None, None, None, None)),
        check_vma=False,
    )
```

profile of v0, /device:TPU:0, one launch (start us, length us, event | category | flops | bytes accessed | tf_op | source)
XLA Modules:
  0.0 227.5 jit_solution(14534622303721739606)
XLA Ops:
  7.2 0.7 fusion.38
  7.8 0.6 reduce-window.6
  8.6 0.8 fusion.37
  9.4 0.7 compare_select_fusion
  10.1 1.6 scatter_custom_fusion
  11.8 9.7 %all_to_all.40 = s32[4,4,20]{2,1,0:T(4,128)S(1)} all-to-all(s32[4,4,20]{2,1,0:T(4,128)S(1)} %reshape.97), channel_id=1, replica_groups=mesh['group'=2,'gx'=4,'gy'=4] {'gx'}, dimensions={0} | all-to-all | bytes 2560 | tf_op jit(solution)/shard_map/all_to_all | solution.py:51
  21.4 0.6 copy.49
  22.0 4.9 %all-to-all-start.1 = ((s32[4,4,20]{2,0,1:T(4,128)}), s32[4,4,20]{2,0,1:T(4,128)S(1)}, u32[]{:S(2)}, u32[]{:S(2)}) async-start(s32[4,4,20]{2,0,1:T(4,128)} %copy.49), calls=%async_computation.1 | async-start | bytes 16384 | tf_op jit(solution)/shard_map/all_to_all | solution.py:50
  26.9 1.2 copy.57
  28.3 7.1 %scatter_fusion.1 = bf16[320,4,2,128]{3,1,2,0:T(4,128)(2,1)S(1)} fusion(bf16[320,4,2,128]{3,1,2,0:T(4,128)(2,1)S(1)} %broadcast.109.clone.1, s32[256]{0:T(256)S(1)} %bitcast.69, bf16[256,4,2,128]{3,1,2,0:T(4,128)(2,1)S(1)} %copy.57), kind=kCustom, calls=%fused_computation.3 | custom fusion | bytes 1573888 | tf_op jit(solution)/shard_map/scatter | solution.py:118
  35.4 1.5 copy.58
  36.9 3.6 %all-to-all-start.4 = ((bf16[4,4,20,4,2,128]{5,4,3,2,1,0:T(2,128)(2,1)}), bf16[4,4,20,4,2,128]{5,4,3,2,1,0:T(2,128)(2,1)S(1)}, u32[]{:S(2)}, u32[]{:S(2)}) async-start(bf16[4,4,20,4,2,128]{5,4,3,2,1,0:T(2,128)(2,1)} %copy.58), calls=%async_computation.4 | async-start | bytes 1310720 | tf_op jit(solution)/shard_map/all_to_all | solution.py:44
  40.9 7.1 %scatter_fusion = bf16[320,4,2,128]{3,1,2,0:T(4,128)(2,1)S(1)} fusion(bf16[320,4,2,128]{3,1,2,0:T(4,128)(2,1)S(1)} %broadcast.109.clone, s32[256]{0:T(256)S(1)} %bitcast.70, bf16[256,4,2,128]{3,1,2,0:T(4,128)(2,1)S(1)} %copy.51), kind=kCustom, calls=%fused_computation.2 | custom fusion | bytes 1573888 | tf_op jit(solution)/shard_map/scatter | solution.py:113
  48.0 1.5 copy.52
  49.5 4.1 %all-to-all-start.2 = ((bf16[4,4,20,4,2,128]{5,4,3,2,1,0:T(2,128)(2,1)}), bf16[4,4,20,4,2,128]{5,4,3,2,1,0:T(2,128)(2,1)S(1)}, u32[]{:S(2)}, u32[]{:S(2)}) async-start(bf16[4,4,20,4,2,128]{5,4,3,2,1,0:T(2,128)(2,1)} %copy.52), calls=%async_computation.2 | async-start | bytes 1310720 | tf_op jit(solution)/shard_map/all_to_all | solution.py:37
  53.7 1.3 copy.59
  55.0 6.1 %all-to-all-done.2 = bf16[4,4,20,4,2,128]{5,4,3,2,1,0:T(2,128)(2,1)S(1)} async-done(((bf16[4,4,20,4,2,128]{5,4,3,2,1,0:T(2,128)(2,1)}), bf16[4,4,20,4,2,128]{5,4,3,2,1,0:T(2,128)(2,1)S(1)}, u32[]{:S(2)}, u32[]{:S(2)}) %all-to-all-start.2) | async-done | bytes 655392 | tf_op jit(solution)/shard_map/all_to_all | solution.py:37
  61.1 4.9 %all-to-all-start.5 = ((bf16[4,4,20,4,2,128]{5,4,3,2,0,1:T(2,128)(2,1)}), bf16[4,4,20,4,2,128]{5,4,3,2,0,1:T(2,128)(2,1)S(1)}, u32[]{:S(2)}, u32[]{:S(2)}) async-start(bf16[4,4,20,4,2,128]{5,4,3,2,0,1:T(2,128)(2,1)} %copy.59), calls=%async_computation.5 | async-start | bytes 1310720 | tf_op jit(solution)/shard_map/all_to_all | solution.py:43
  66.1 1.3 copy.53
  67.4 12.3 %all-to-all-done.5 = bf16[4,4,20,4,2,128]{5,4,3,2,0,1:T(2,128)(2,1)S(1)} async-done(((bf16[4,4,20,4,2,128]{5,4,3,2,0,1:T(2,128)(2,1)}), bf16[4,4,20,4,2,128]{5,4,3,2,0,1:T(2,128)(2,1)S(1)}, u32[]{:S(2)}, u32[]{:S(2)}) %all-to-all-start.5) | async-done | bytes 655392 | tf_op jit(solution)/shard_map/all_to_all | solution.py:43
  79.7 3.5 %all-to-all-start.3 = ((bf16[4,4,20,4,2,128]{5,4,3,2,0,1:T(2,128)(2,1)}), bf16[4,4,20,4,2,128]{5,4,3,2,0,1:T(2,128)(2,1)S(1)}, u32[]{:S(2)}, u32[]{:S(2)}) async-start(bf16[4,4,20,4,2,128]{5,4,3,2,0,1:T(2,128)(2,1)} %copy.53), calls=%async_computation.3 | async-start | bytes 1310720 | tf_op jit(solution)/shard_map/all_to_all | solution.py:36
  83.3 0.5 copy.60
  83.8 0.5 reshape_reshape.10
  84.3 0.5 dot_general.21
  84.9 0.6 copy.62
  85.6 12.3 %all-to-all-done.3 = bf16[4,4,20,4,2,128]{5,4,3,2,0,1:T(2,128)(2,1)S(1)} async-done(((bf16[4,4,20,4,2,128]{5,4,3,2,0,1:T(2,128)(2,1)}), bf16[4,4,20,4,2,128]{5,4,3,2,0,1:T(2,128)(2,1)S(1)}, u32[]{:S(2)}, u32[]{:S(2)}) %all-to-all-start.3) | async-done | bytes 655392 | tf_op jit(solution)/shard_map/all_to_all | solution.py:36
  97.9 0.5 copy.54
  98.3 0.5 reshape_reshape.9
  98.8 0.5 dot_general.18
  99.5 0.6 copy.56
  100.1 16.3 %all-reduce.7.cloned.1.call-done = (f32[4,16,128]{2,1,0:T(8,128)}, f32[4,16,128]{2,1,0:T(8,128)}) async-done(((f32[4,16,128]{2,1,0:T(8,128)}, f32[4,16,128]{2,1,0:T(8,128)}), (f32[4,16,128]{2,1,0:T(8,128)}, f32[4,16,128]{2,1,0:T(8,128)})) %all-reduce.7.cloned.1.call-update) | async-done | bytes 65552 | tf_op jit(solution)/shard_map/psum | solution.py:141
  116.5 0.8 add_divide_fusion
  117.3 1.3 collective-permute-start
  118.6 4.5 %collective-permute-start.1 = (f32[4,1,128]{2,1,0:T(1,128)S(1)}, f32[4,1,128]{2,1,0:T(1,128)S(1)}, u32[]{:S(2)}, u32[]{:S(2)}) collective-permute-start(f32[4,1,128]{2,1,0:T(1,128)S(1)} %get-tuple-element.20), channel_id=1, source_target_pairs={{0,4},{4,8},{8,12},{1,5},{5,9},{9,13},{2,6},{6,10},{10,14},{3,7},{... | collective-permute-start | bytes 6152 | tf_op jit(solution)/shard_map/ppermute | solution.py:22
  123.1 1.3 collective-permute-done.1
  124.5 1.3 collective-permute-start.2
  125.8 4.5 %collective-permute-start.3 = (f32[4,18,1]{2,1,0:T(8,128)S(1)}, f32[4,18,1]{2,1,0:T(8,128)S(1)}, u32[]{:S(2)}, u32[]{:S(2)}) collective-permute-start(f32[4,18,1]{2,1,0:T(8,128)S(1)} %get-tuple-element.13), channel_id=1, source_target_pairs={{0,1},{1,2},{2,3},{4,5},{5,6},{6,7},{8,9},{9,10},{10,11},{12,13},{... | collective-permute-start | bytes 872 | tf_op jit(solution)/shard_map/ppermute | solution.py:22
  130.5 1.6 collective-permute-done.3
  132.2 1.3 collective-permute-start.4
  133.5 5.2 %collective-permute-start.5 = (f32[4,1,128]{2,1,0:T(1,128)S(1)}, f32[4,1,128]{2,1,0:T(1,128)S(1)}, u32[]{:S(2)}, u32[]{:S(2)}) collective-permute-start(f32[4,1,128]{2,1,0:T(1,128)S(1)} %get-tuple-element.18), channel_id=1, source_target_pairs={{0,4},{4,8},{8,12},{1,5},{5,9},{9,13},{2,6},{6,10},{10,14},{3,7},{... | collective-permute-start | bytes 6152 | tf_op jit(solution)/shard_map/ppermute | solution.py:22
  138.7 1.3 collective-permute-done.5
  140.1 1.3 collective-permute-start.6
  141.4 4.9 %collective-permute-start.7 = (f32[4,18,1]{2,1,0:T(8,128)S(1)}, f32[4,18,1]{2,1,0:T(8,128)S(1)}, u32[]{:S(2)}, u32[]{:S(2)}) collective-permute-start(f32[4,18,1]{2,1,0:T(8,128)S(1)} %get-tuple-element.11), channel_id=1, source_target_pairs={{0,1},{1,2},{2,3},{4,5},{5,6},{6,7},{8,9},{9,10},{10,11},{12,13},{... | collective-permute-start | bytes 872 | tf_op jit(solution)/shard_map/ppermute | solution.py:22
  146.4 1.6 collective-permute-done.7
  148.1 1.3 collective-permute-start.8
  149.4 5.7 %collective-permute-start.9 = (f32[4,1,128]{2,1,0:T(1,128)S(1)}, f32[4,1,128]{2,1,0:T(1,128)S(1)}, u32[]{:S(2)}, u32[]{:S(2)}) collective-permute-start(f32[4,1,128]{2,1,0:T(1,128)S(1)} %get-tuple-element.16), channel_id=1, source_target_pairs={{0,4},{4,8},{8,12},{1,5},{5,9},{9,13},{2,6},{6,10},{10,14},{3,7},{... | collective-permute-start | bytes 6152 | tf_op jit(solution)/shard_map/ppermute | solution.py:22
  155.1 1.3 collective-permute-done.9
  156.5 1.3 collective-permute-start.10
  157.8 4.9 %collective-permute-start.11 = (f32[4,18,1]{2,1,0:T(8,128)S(1)}, f32[4,18,1]{2,1,0:T(8,128)S(1)}, u32[]{:S(2)}, u32[]{:S(2)}) collective-permute-start(f32[4,18,1]{2,1,0:T(8,128)S(1)} %get-tuple-element.9), channel_id=1, source_target_pairs={{0,1},{1,2},{2,3},{4,5},{5,6},{6,7},{8,9},{9,10},{10,11},{12,13},{... | collective-permute-start | bytes 872 | tf_op jit(solution)/shard_map/ppermute | solution.py:22
  162.8 1.6 collective-permute-done.11
  164.6 1.3 collective-permute-start.12
  165.9 5.7 %collective-permute-start.13 = (f32[4,1,128]{2,1,0:T(1,128)S(1)}, f32[4,1,128]{2,1,0:T(1,128)S(1)}, u32[]{:S(2)}, u32[]{:S(2)}) collective-permute-start(f32[4,1,128]{2,1,0:T(1,128)S(1)} %get-tuple-element.14), channel_id=1, source_target_pairs={{0,4},{4,8},{8,12},{1,5},{5,9},{9,13},{2,6},{6,10},{10,14},{3,7},{... | collective-permute-start | bytes 6152 | tf_op jit(solution)/shard_map/ppermute | solution.py:22
  171.6 1.3 collective-permute-done.13
  172.9 1.3 collective-permute-start.14
  174.2 4.9 %collective-permute-start.15 = (f32[4,18,1]{2,1,0:T(8,128)S(1)}, f32[4,18,1]{2,1,0:T(8,128)S(1)}, u32[]{:S(2)}, u32[]{:S(2)}) collective-permute-start(f32[4,18,1]{2,1,0:T(8,128)S(1)} %get-tuple-element.7), channel_id=1, source_target_pairs={{0,1},{1,2},{2,3},{4,5},{5,6},{6,7},{8,9},{9,10},{10,11},{12,13},{... | collective-permute-start | bytes 872 | tf_op jit(solution)/shard_map/ppermute | solution.py:22
  179.3 1.6 collective-permute-done.15
  180.9 0.7 fusion.47
  182.0 0.5 reshape_reshape.11
  182.4 14.3 %all_to_all.41 = bf16[4,4,20,4,2,128]{5,4,3,2,1,0:T(2,128)(2,1)S(1)} all-to-all(bf16[4,4,20,4,2,128]{5,4,3,2,1,0:T(2,128)(2,1)S(1)} %reshape_reshape.11), channel_id=1, replica_groups=mesh['group'=2,'gx'=4,'gy'=4] {'gx'}, dimensions={0} | all-to-all | bytes 1310720 | tf_op jit(solution)/shard_map/all_to_all | solution.py:68
  196.8 1.3 copy.64
  198.1 6.8 %all-to-all-start.7 = ((bf16[4,4,20,4,2,128]{5,4,3,2,0,1:T(2,128)(2,1)}), bf16[4,4,20,4,2,128]{5,4,3,2,0,1:T(2,128)(2,1)S(1)}, u32[]{:S(2)}, u32[]{:S(2)}) async-start(bf16[4,4,20,4,2,128]{5,4,3,2,0,1:T(2,128)(2,1)} %copy.64), calls=%async_computation.7 | async-start | bytes 1310720 | tf_op jit(solution)/shard_map/all_to_all | solution.py:67
  205.0 11.7 %all-to-all-done.7 = bf16[4,4,20,4,2,128]{5,4,3,2,0,1:T(2,128)(2,1)S(1)} async-done(((bf16[4,4,20,4,2,128]{5,4,3,2,0,1:T(2,128)(2,1)}), bf16[4,4,20,4,2,128]{5,4,3,2,0,1:T(2,128)(2,1)S(1)}, u32[]{:S(2)}, u32[]{:S(2)}) %all-to-all-start.7) | async-done | bytes 655392 | tf_op jit(solution)/shard_map/all_to_all | solution.py:67
  217.1 1.7 gather_fusion
  218.9 1.7 broadcast_select_fusion
  (50 shorter events, 3.5 us)
Async XLA Ops:
  22.0 14.9 %all-to-all-start.1 = ((s32[4,4,20]{2,0,1:T(4,128)}), s32[4,4,20]{2,0,1:T(4,128)S(1)}, u32[]{:S(2)}, u32[]{:S(2)}) async-start(s32[4,4,20]{2,0,1:T(4,128)} %copy.49), calls=%async_computation.1 | async-start | bytes 16384 | tf_op jit(solution)/shard_map/all_to_all | solution.py:50
  36.9 3.6 %copy-start = (bf16[1,1,1,256,4,2,128]{6,5,4,3,2,1,0:T(2,128)(2,1)S(1)}, bf16[1,1,1,256,4,2,128]{6,5,4,3,2,1,0:T(2,128)(2,1)}, u32[]{:S(2)}) copy-start(bf16[1,1,1,256,4,2,128]{6,5,4,3,2,1,0:T(2,128)(2,1)} %param.5) | copy-start | bytes 1572868
  36.9 12.6 %all-to-all-start.4 = ((bf16[4,4,20,4,2,128]{5,4,3,2,1,0:T(2,128)(2,1)}), bf16[4,4,20,4,2,128]{5,4,3,2,1,0:T(2,128)(2,1)S(1)}, u32[]{:S(2)}, u32[]{:S(2)}) async-start(bf16[4,4,20,4,2,128]{5,4,3,2,1,0:T(2,128)(2,1)} %copy.58), calls=%async_computation.4 | async-start | bytes 1310720 | tf_op jit(solution)/shard_map/all_to_all | solution.py:44
  49.5 11.6 %all-to-all-start.2 = ((bf16[4,4,20,4,2,128]{5,4,3,2,1,0:T(2,128)(2,1)}), bf16[4,4,20,4,2,128]{5,4,3,2,1,0:T(2,128)(2,1)S(1)}, u32[]{:S(2)}, u32[]{:S(2)}) async-start(bf16[4,4,20,4,2,128]{5,4,3,2,1,0:T(2,128)(2,1)} %copy.52), calls=%async_computation.2 | async-start | bytes 1310720 | tf_op jit(solution)/shard_map/all_to_all | solution.py:37
  61.1 18.5 %all-to-all-start.5 = ((bf16[4,4,20,4,2,128]{5,4,3,2,0,1:T(2,128)(2,1)}), bf16[4,4,20,4,2,128]{5,4,3,2,0,1:T(2,128)(2,1)S(1)}, u32[]{:S(2)}, u32[]{:S(2)}) async-start(bf16[4,4,20,4,2,128]{5,4,3,2,0,1:T(2,128)(2,1)} %copy.59), calls=%async_computation.5 | async-start | bytes 1310720 | tf_op jit(solution)/shard_map/all_to_all | solution.py:43
  79.7 18.2 %all-to-all-start.3 = ((bf16[4,4,20,4,2,128]{5,4,3,2,0,1:T(2,128)(2,1)}), bf16[4,4,20,4,2,128]{5,4,3,2,0,1:T(2,128)(2,1)S(1)}, u32[]{:S(2)}, u32[]{:S(2)}) async-start(bf16[4,4,20,4,2,128]{5,4,3,2,0,1:T(2,128)(2,1)} %copy.53), calls=%async_computation.3 | async-start | bytes 1310720 | tf_op jit(solution)/shard_map/all_to_all | solution.py:36
  83.2 33.3 %all-reduce.7.cloned.1.call-start = ((), (), s32[]{:S(2)}) async-start(), calls=%async_computation.8 | async-start | bytes 131072 | tf_op jit(solution)/shard_map/psum | solution.py:141
  117.3 5.9 %collective-permute-start = (f32[4,1,128]{2,1,0:T(1,128)S(1)}, f32[4,1,128]{2,1,0:T(1,128)S(1)}, u32[]{:S(2)}, u32[]{:S(2)}) collective-permute-start(f32[4,1,128]{2,1,0:T(1,128)S(1)} %get-tuple-element.21), channel_id=1, source_target_pairs={{4,0},{8,4},{12,8},{5,1},{9,5},{13,9},{6,2},{10,6},{14,10},{7,3},{... | collective-permute-start | bytes 6152 | tf_op jit(solution)/shard_map/ppermute | solution.py:24
  118.6 5.8 %collective-permute-start.1 = (f32[4,1,128]{2,1,0:T(1,128)S(1)}, f32[4,1,128]{2,1,0:T(1,128)S(1)}, u32[]{:S(2)}, u32[]{:S(2)}) collective-permute-start(f32[4,1,128]{2,1,0:T(1,128)S(1)} %get-tuple-element.20), channel_id=1, source_target_pairs={{0,4},{4,8},{8,12},{1,5},{5,9},{9,13},{2,6},{6,10},{10,14},{3,7},{... | collective-permute-start | bytes 6152 | tf_op jit(solution)/shard_map/ppermute | solution.py:22
  124.5 6.0 %collective-permute-start.2 = (f32[4,18,1]{2,1,0:T(8,128)S(1)}, f32[4,18,1]{2,1,0:T(8,128)S(1)}, u32[]{:S(2)}, u32[]{:S(2)}) collective-permute-start(f32[4,18,1]{2,1,0:T(8,128)S(1)} %get-tuple-element.12), channel_id=1, source_target_pairs={{1,0},{2,1},{3,2},{5,4},{6,5},{7,6},{9,8},{10,9},{11,10},{13,12},{... | collective-permute-start | bytes 872 | tf_op jit(solution)/shard_map/ppermute | solution.py:24
  125.8 6.3 %collective-permute-start.3 = (f32[4,18,1]{2,1,0:T(8,128)S(1)}, f32[4,18,1]{2,1,0:T(8,128)S(1)}, u32[]{:S(2)}, u32[]{:S(2)}) collective-permute-start(f32[4,18,1]{2,1,0:T(8,128)S(1)} %get-tuple-element.13), channel_id=1, source_target_pairs={{0,1},{1,2},{2,3},{4,5},{5,6},{6,7},{8,9},{9,10},{10,11},{12,13},{... | collective-permute-start | bytes 872 | tf_op jit(solution)/shard_map/ppermute | solution.py:22
  132.2 48.7 %copy-start.1 = (f32[4,16,128]{2,1,0:T(8,128)S(1)}, f32[4,16,128]{2,1,0:T(8,128)}, u32[]{:S(2)}) copy-start(f32[4,16,128]{2,1,0:T(8,128)} %param.9) | copy-start | bytes 98308
  132.2 6.5 %collective-permute-start.4 = (f32[4,1,128]{2,1,0:T(1,128)S(1)}, f32[4,1,128]{2,1,0:T(1,128)S(1)}, u32[]{:S(2)}, u32[]{:S(2)}) collective-permute-start(f32[4,1,128]{2,1,0:T(1,128)S(1)} %get-tuple-element.19), channel_id=1, source_target_pairs={{4,0},{8,4},{12,8},{5,1},{9,5},{13,9},{6,2},{10,6},{14,10},{7,3},{... | collective-permute-start | bytes 6152 | tf_op jit(solution)/shard_map/ppermute | solution.py:24
  133.5 6.5 %collective-permute-start.5 = (f32[4,1,128]{2,1,0:T(1,128)S(1)}, f32[4,1,128]{2,1,0:T(1,128)S(1)}, u32[]{:S(2)}, u32[]{:S(2)}) collective-permute-start(f32[4,1,128]{2,1,0:T(1,128)S(1)} %get-tuple-element.18), channel_id=1, source_target_pairs={{0,4},{4,8},{8,12},{1,5},{5,9},{9,13},{2,6},{6,10},{10,14},{3,7},{... | collective-permute-start | bytes 6152 | tf_op jit(solution)/shard_map/ppermute | solution.py:22
  140.1 6.3 %collective-permute-start.6 = (f32[4,18,1]{2,1,0:T(8,128)S(1)}, f32[4,18,1]{2,1,0:T(8,128)S(1)}, u32[]{:S(2)}, u32[]{:S(2)}) collective-permute-start(f32[4,18,1]{2,1,0:T(8,128)S(1)} %get-tuple-element.10), channel_id=1, source_target_pairs={{1,0},{2,1},{3,2},{5,4},{6,5},{7,6},{9,8},{10,9},{11,10},{13,12},{... | collective-permute-start | bytes 872 | tf_op jit(solution)/shard_map/ppermute | solution.py:24
  141.4 6.6 %collective-permute-start.7 = (f32[4,18,1]{2,1,0:T(8,128)S(1)}, f32[4,18,1]{2,1,0:T(8,128)S(1)}, u32[]{:S(2)}, u32[]{:S(2)}) collective-permute-start(f32[4,18,1]{2,1,0:T(8,128)S(1)} %get-tuple-element.11), channel_id=1, source_target_pairs={{0,1},{1,2},{2,3},{4,5},{5,6},{6,7},{8,9},{9,10},{10,11},{12,13},{... | collective-permute-start | bytes 872 | tf_op jit(solution)/shard_map/ppermute | solution.py:22
  148.1 7.0 %collective-permute-start.8 = (f32[4,1,128]{2,1,0:T(1,128)S(1)}, f32[4,1,128]{2,1,0:T(1,128)S(1)}, u32[]{:S(2)}, u32[]{:S(2)}) collective-permute-start(f32[4,1,128]{2,1,0:T(1,128)S(1)} %get-tuple-element.17), channel_id=1, source_target_pairs={{4,0},{8,4},{12,8},{5,1},{9,5},{13,9},{6,2},{10,6},{14,10},{7,3},{... | collective-permute-start | bytes 6152 | tf_op jit(solution)/shard_map/ppermute | solution.py:24
  149.4 7.0 %collective-permute-start.9 = (f32[4,1,128]{2,1,0:T(1,128)S(1)}, f32[4,1,128]{2,1,0:T(1,128)S(1)}, u32[]{:S(2)}, u32[]{:S(2)}) collective-permute-start(f32[4,1,128]{2,1,0:T(1,128)S(1)} %get-tuple-element.16), channel_id=1, source_target_pairs={{0,4},{4,8},{8,12},{1,5},{5,9},{9,13},{2,6},{6,10},{10,14},{3,7},{... | collective-permute-start | bytes 6152 | tf_op jit(solution)/shard_map/ppermute | solution.py:22
  156.5 6.3 %collective-permute-start.10 = (f32[4,18,1]{2,1,0:T(8,128)S(1)}, f32[4,18,1]{2,1,0:T(8,128)S(1)}, u32[]{:S(2)}, u32[]{:S(2)}) collective-permute-start(f32[4,18,1]{2,1,0:T(8,128)S(1)} %get-tuple-element.8), channel_id=1, source_target_pairs={{1,0},{2,1},{3,2},{5,4},{6,5},{7,6},{9,8},{10,9},{11,10},{13,12},{... | collective-permute-start | bytes 872 | tf_op jit(solution)/shard_map/ppermute | solution.py:24
  157.8 6.6 %collective-permute-start.11 = (f32[4,18,1]{2,1,0:T(8,128)S(1)}, f32[4,18,1]{2,1,0:T(8,128)S(1)}, u32[]{:S(2)}, u32[]{:S(2)}) collective-permute-start(f32[4,18,1]{2,1,0:T(8,128)S(1)} %get-tuple-element.9), channel_id=1, source_target_pairs={{0,1},{1,2},{2,3},{4,5},{5,6},{6,7},{8,9},{9,10},{10,11},{12,13},{... | collective-permute-start | bytes 872 | tf_op jit(solution)/shard_map/ppermute | solution.py:22
  164.6 7.0 %collective-permute-start.12 = (f32[4,1,128]{2,1,0:T(1,128)S(1)}, f32[4,1,128]{2,1,0:T(1,128)S(1)}, u32[]{:S(2)}, u32[]{:S(2)}) collective-permute-start(f32[4,1,128]{2,1,0:T(1,128)S(1)} %get-tuple-element.15), channel_id=1, source_target_pairs={{4,0},{8,4},{12,8},{5,1},{9,5},{13,9},{6,2},{10,6},{14,10},{7,3},{... | collective-permute-start | bytes 6152 | tf_op jit(solution)/shard_map/ppermute | solution.py:24
  165.9 7.0 %collective-permute-start.13 = (f32[4,1,128]{2,1,0:T(1,128)S(1)}, f32[4,1,128]{2,1,0:T(1,128)S(1)}, u32[]{:S(2)}, u32[]{:S(2)}) collective-permute-start(f32[4,1,128]{2,1,0:T(1,128)S(1)} %get-tuple-element.14), channel_id=1, source_target_pairs={{0,4},{4,8},{8,12},{1,5},{5,9},{9,13},{2,6},{6,10},{10,14},{3,7},{... | collective-permute-start | bytes 6152 | tf_op jit(solution)/shard_map/ppermute | solution.py:22
  172.9 6.3 %collective-permute-start.14 = (f32[4,18,1]{2,1,0:T(8,128)S(1)}, f32[4,18,1]{2,1,0:T(8,128)S(1)}, u32[]{:S(2)}, u32[]{:S(2)}) collective-permute-start(f32[4,18,1]{2,1,0:T(8,128)S(1)} %get-tuple-element.6), channel_id=1, source_target_pairs={{1,0},{2,1},{3,2},{5,4},{6,5},{7,6},{9,8},{10,9},{11,10},{13,12},{... | collective-permute-start | bytes 872 | tf_op jit(solution)/shard_map/ppermute | solution.py:24
  174.2 6.6 %collective-permute-start.15 = (f32[4,18,1]{2,1,0:T(8,128)S(1)}, f32[4,18,1]{2,1,0:T(8,128)S(1)}, u32[]{:S(2)}, u32[]{:S(2)}) collective-permute-start(f32[4,18,1]{2,1,0:T(8,128)S(1)} %get-tuple-element.7), channel_id=1, source_target_pairs={{0,1},{1,2},{2,3},{4,5},{5,6},{6,7},{8,9},{9,10},{10,11},{12,13},{... | collective-permute-start | bytes 872 | tf_op jit(solution)/shard_map/ppermute | solution.py:22
  198.1 6.8 %copy-start.2 = (s32[1,1,1,256]{3,2,1,0:T(1,128)S(1)}, s32[1,1,1,256]{3,2,1,0:T(1,128)}, u32[]{:S(2)}) copy-start(s32[1,1,1,256]{3,2,1,0:T(1,128)} %param.7) | copy-start | bytes 3076
  198.1 18.5 %all-to-all-start.7 = ((bf16[4,4,20,4,2,128]{5,4,3,2,0,1:T(2,128)(2,1)}), bf16[4,4,20,4,2,128]{5,4,3,2,0,1:T(2,128)(2,1)S(1)}, u32[]{:S(2)}, u32[]{:S(2)}) async-start(bf16[4,4,20,4,2,128]{5,4,3,2,0,1:T(2,128)(2,1)} %copy.64), calls=%async_computation.7 | async-start | bytes 1310720 | tf_op jit(solution)/shard_map/all_to_all | solution.py:67
Sparse Core Ops, SparseCore 0:
  100.2 16.1 all-reduce.6
where the time goes:
time: 229 us; the launch traced here: 227 us
  starting transfers between devices  78.5 us (34%)
  waiting for transfers between devices  70.8 us (31%)
  local copies, waits for them, and re-layouts  32.6 us (14%)
  blocking collectives  24 us (10%)
  between operations  14.4 us (6%)
  other arithmetic  6.4 us (3%)
    ppermute x8, starting transfers between devices, with_halo(): lax.ppermute(tail, axis, [(i, (i + 1) % count) for i in range(ends)])  40.3 us
    psum x1, waiting for transfers between devices, local(): lax.psum((to_tile(grad_sum), to_tile(illum_sum)), 'group')  16.3 us
    all_to_all x1, blocking collectives, send_back(): lax.all_to_all(sectioned_back, 'gx', split_axis=0, concat_axis=0, tiled=T...  14.3 us
    all_to_all x1, waiting for transfers between devices, deliver(): lax.all_to_all(lax.all_to_all(sectioned_grad, 'gx', split_axis=0, concat_...  12.3 us
    all_to_all x1, waiting for transfers between devices, deliver(): lax.all_to_all(lax.all_to_all(sectioned_illum, 'gx', split_axis=0, concat...  12.3 us
    all_to_all x1, waiting for transfers between devices, send_back(): lax.all_to_all(lax.all_to_all(sectioned_back, 'gx', split_axis=0, concat_...  11.7 us
    ppermute x8, waiting for transfers between devices, with_halo(): lax.ppermute(tail, axis, [(i, (i + 1) % count) for i in range(ends)])  11.5 us
    ppermute x8, starting transfers between devices, with_halo(): lax.ppermute(head, axis, [((i + 1) % count, i) for i in range(ends)])  10.3 us
  transfers between devices with their start and end apart: 23, of which 17 were waited for; matrix products, arithmetic and copies ran while one was open for 11% of the time, Pallas kernels for 0%

commit v1 on v0

v1 whole, which is shorter than its diff:
```python
import jax
import jax.numpy as jnp
from jax import lax
from jax.sharding import PartitionSpec as P

SWEEPS = 4
HALO = SWEEPS


damping = 10.0
smooth_rate = 0.12
step_length = 24.0


def shifted(value, axis, count, step):
    return lax.ppermute(value, axis, [(s, (s + step) % count) for s in range(count)])


def local(gradient_windows, illumination_windows, window_owners, window_patches, velocity):
    size_x = lax.axis_size("gx")
    size_y = lax.axis_size("gy")
    size_g = lax.axis_size("group")
    me_x = lax.axis_index("gx")
    me_y = lax.axis_index("gy")
    slot_grad = gradient_windows[0, 0, 0]
    slot_illum = illumination_windows[0, 0, 0]
    owners = window_owners[0, 0, 0]
    patches = window_patches[0, 0, 0]
    slot_count, levels, patch_rows, patch_cols = slot_grad.shape
    tile_rows, tile_cols = velocity.shape[1], velocity.shape[2]
    per_tile = tile_rows // patch_rows
    tiles = size_x * size_y
    cell_count = levels * patch_rows * patch_cols
    h = HALO
    ext_rows = tile_rows + 2 * h
    ext_cols = tile_cols + 2 * h

    owner_x = owners // size_y
    owner_y = owners % size_y
    rel_row = (((owner_x - me_x) % size_x) * size_y + (owner_y - me_y) % size_y) * per_tile + patches
    onehot = (rel_row[None, :] == jnp.arange(tiles * per_tile, dtype=jnp.int32)[:, None]).astype(
        jnp.bfloat16
    )
    both = jnp.concatenate(
        [slot_grad.reshape(slot_count, cell_count), slot_illum.reshape(slot_count, cell_count)],
        axis=1,
    )
    table = jnp.dot(onehot, both, preferred_element_type=jnp.float32)
    model = table.reshape(size_x, size_y, per_tile, 2, levels, patch_rows, patch_cols)
    model = model.transpose(3, 4, 0, 2, 5, 1, 6).reshape(
        2, levels, size_x * tile_rows, size_y * tile_cols
    )
    model = jnp.concatenate([model[:, :, -h:], model, model[:, :, :h]], axis=2)
    model = jnp.concatenate([model[:, :, :, -h:], model, model[:, :, :, :h]], axis=3)
    ext = jnp.stack(
        [
            jnp.stack(
                [
                    model[
                        :,
                        :,
                        tx * tile_rows : tx * tile_rows + ext_rows,
                        ty * tile_cols : ty * tile_cols + ext_cols,
                    ]
                    for ty in range(size_y)
                ]
            )
            for tx in range(size_x)
        ]
    )
    flat = ext.reshape(size_x, size_y, -1, 128)

    part = flat[0]
    for step in range(1, size_x):
        part = part + shifted(flat[step], "gx", size_x, step)
    total = part[0]
    for step in range(1, size_y):
        total = total + shifted(part[step], "gy", size_y, step)
    mine = total
    for step in range(1, size_g):
        total = total + shifted(mine, "group", size_g, step)

    sums = total.reshape(2, levels, ext_rows, ext_cols)
    pos_x = me_x * tile_rows - h + jnp.arange(ext_rows)
    pos_y = me_y * tile_cols - h + jnp.arange(ext_cols)
    inside = ((pos_x >= 0) & (pos_x < size_x * tile_rows))[:, None] & (
        (pos_y >= 0) & (pos_y < size_y * tile_cols)
    )[None, :]
    field_now = jnp.where(inside, sums[0] / (sums[1] + damping), 0.0)
    for sweep_index in range(SWEEPS):
        padded = jnp.pad(field_now, 1)
        beside = (
            (padded[1:-1, 2:, 1:-1] + padded[1:-1, :-2, 1:-1])
            + (padded[1:-1, 1:-1, 2:] + padded[1:-1, 1:-1, :-2])
            + (padded[2:, 1:-1, 1:-1] + padded[:-2, 1:-1, 1:-1])
        )
        field_now = jnp.where(inside, field_now + smooth_rate * (beside - 6.0 * field_now), 0.0)
    updated_model = velocity - step_length * field_now[:, h : h + tile_rows, h : h + tile_cols]

    tile_table = (
        updated_model.reshape(levels, per_tile, patch_rows, tile_cols)
        .transpose(1, 0, 2, 3)
        .reshape(per_tile, cell_count)
        .astype(jnp.bfloat16)
    )
    along_y = jnp.stack(
        [tile_table] + [shifted(tile_table, "gy", size_y, step) for step in range(1, size_y)]
    )
    along_x = jnp.stack(
        [along_y] + [shifted(along_y, "gx", size_x, step) for step in range(1, size_x)]
    )
    whole = along_x.reshape(tiles * per_tile, cell_count)
    back_row = (
        ((me_x - owner_x) % size_x) * size_y + (me_y - owner_y) % size_y
    ) * per_tile + patches
    pick = (back_row[:, None] == jnp.arange(tiles * per_tile, dtype=jnp.int32)[None, :]).astype(
        jnp.bfloat16
    )
    returned = jnp.dot(pick, whole, preferred_element_type=jnp.float32).astype(jnp.bfloat16)
    returned_windows = returned.reshape((1, 1, 1, slot_count, levels, patch_rows, patch_cols))
    return (updated_model, returned_windows)


def solution(mesh):
    return jax.shard_map(
        local,
        mesh=mesh,
        in_specs=(
            P("group", "gx", "gy", None, None, None, None),
            P("group", "gx", "gy", None, None, None, None),
            P("group", "gx", "gy", None),
            P("group", "gx", "gy", None),
            P(None, "gx", "gy"),
        ),
        out_specs=(P(None, "gx", "gy"), P("group", "gx", "gy", None, None, None, None)),
        check_vma=False,
    )
```

time: 229 us -> 70 us (0.31)
  starting transfers between devices: 78.5 us -> 17.7 us
  waiting for transfers between devices: 70.8 us -> 33.3 us
  blocking collectives: 24 us -> 0 us
  local copies, waits for them, and re-layouts: 32.6 us -> 10 us
  between operations: 14.4 us -> 0.91 us
    all_to_all x6 -> x0, waiting for transfers between devices: 42.4 us -> none  [the longest x1 12.3 us: deliver(): lax.all_to_all(lax.all_to_all(sectioned_grad, 'gx', split_axis=0, concat_...]
    ppermute x16 -> x13, starting transfers between devices: 50.6 us -> 17.7 us  [shifted(): lax.ppermute(value, axis, [(s, (s + step) % count) for s in range(count)])]
    all_to_all x6 -> x0, starting transfers between devices: 27.9 us -> none  [the longest x1 6.82 us: send_back(): lax.all_to_all(lax.all_to_all(sectioned_back, 'gx', split_axis=0, concat_...]
    all_to_all x2 -> x0, blocking collectives: 24 us -> none  [the longest x1 14.3 us: send_back(): lax.all_to_all(sectioned_back, 'gx', split_axis=0, concat_axis=0, tiled=T...]
    ppermute x16 -> x13, waiting for transfers between devices: 12.1 us -> 33.3 us  [shifted(): lax.ppermute(value, axis, [(s, (s + step) % count) for s in range(count)])]
    psum x1 -> x0, waiting for transfers between devices: 16.3 us -> none  [local(): lax.psum((to_tile(grad_sum), to_tile(illum_sum)), 'group')]
    scatter x3 -> x0, local copies, waits for them, and re-layouts: 15.7 us -> none  [the longest x1 7.06 us: local(): send_illum = jnp.zeros((rows_total, levels, patch_rows, patch_cols), jnp....]
    all_to_all x8 -> x0, local copies, waits for them, and re-layouts: 6.01 us -> none  [the longest x1 1.34 us: send_back(): lax.all_to_all(sectioned_back, 'gx', split_axis=0, concat_axis=0, tiled=T...]
  transfers between devices with their start and end apart: 23 -> 13, of which waited for: 17 -> 13; matrix products, arithmetic and copies ran while one was open for 11% -> 3% of each run, Pallas kernels for 0% -> 0%
where the time goes in v1:
time: 70 us; the launch traced here: 69.7 us
  waiting for transfers between devices  33.3 us (48%)
  starting transfers between devices  17.7 us (25%)
  local copies, waits for them, and re-layouts  10 us (14%)
  other arithmetic  7.18 us (10%)
  between operations  0.91 us (1%)
    ppermute x13, waiting for transfers between devices, shifted(): lax.ppermute(value, axis, [(s, (s + step) % count) for s in range(count)])  33.3 us
    ppermute x13, starting transfers between devices, shifted(): lax.ppermute(value, axis, [(s, (s + step) % count) for s in range(count)])  17.7 us
    another operation x16, local copies, waits for them, and re-layouts, local(): jnp.stack([model[:, :, tx * tile_rows:tx * tile_rows + ext_rows, ty * til...  5.68 us
    slice x4, other arithmetic, local(): model[:, :, tx * tile_rows:tx * tile_rows + ext_rows, ty * tile_cols:ty *...  2.83 us
    another operation x3, other arithmetic, local(): jnp.stack([model[:, :, tx * tile_rows:tx * tile_rows + ext_rows, ty * til...  1.79 us
    another operation x1, local copies, waits for them, and re-layouts, local(): slot_grad.reshape(slot_count, cell_count)  1.46 us
  transfers between devices with their start and end apart: 13, of which 13 were waited for; matrix products, arithmetic and copies ran while one was open for 3% of the time, Pallas kernels for 0%

profile of v1, /device:TPU:0, one launch (start us, length us, event | category | flops | bytes accessed | tf_op | source)
XLA Modules:
  0.0 69.7 jit_solution(17276240166619312514)
XLA Ops:
  0.7 1.5 %reshape_squeeze.6 = bf16[256,1024]{1,0:T(8,128)(2,1)S(1)} reshape(bf16[1,1,1,256,4,2,128]{6,5,4,3,2,1,0:T(2,128)(2,1)} %param.5) | data formatting | bytes 1048576 | tf_op jit(solution)/shard_map/reshape;squeeze | solution.py:45
  2.1 0.4 reshape_squeeze.7
  2.6 0.3 fusion
  2.9 0.7 copy.12
  3.6 0.4 reshape.260
  4.0 0.4 maximum_maximum_fusion.4
  4.4 1.1 %maximum_maximum_fusion.5 = (f32[2,4,24,136]{3,2,1,0:T(8,128)S(1)}, f32[2,4,24,136]{3,2,1,0:T(8,128)S(1)}, f32[2,4,24,136]{3,2,1,0:T(8,128)}, f32[2,4,24,136]{3,2,1,0:T(8,128)S(1)}) fusion(f32[2,4,4,512]{3,2,1,0:T(4,128)S(1)} %get-tuple-element.23, f32[2,4,64,512]{3,2,1,0:T(8,128)S(1)} %reshape.260, f32[2,4,4,512]{3,2,1,0:T(4,128)S(1)} %get-tuple-element.22), kind=kLoop, calls=%fused_computation.56 | loop fusion | flops 391680 | bytes 1794048 | tf_op jit(solution)/shard_map/slice | solution.py:59
  5.5 1.2 %pad_maximum_fusion.15 = (f32[2,4,24,136]{3,2,1,0:T(8,128)S(1)}, f32[2,4,24,136]{3,2,1,0:T(8,128)S(1)}, f32[2,4,24,136]{3,2,1,0:T(8,128)S(1)}, f32[2,4,24,136]{3...) fusion(f32[2,4,64,512]{3,2,1,0:T(8,128)S(1)} %reshape.260, ...), kind=kLoop, calls=%fused_computation.55 | loop fusion | flops 339456 | bytes 2002944 | tf_op jit(solution)/shard_map/slice | solution.py:59
  6.7 0.8 %stack.106 = f32[1,204,128]{2,1,0:T(8,128)} reshape(f32[2,4,24,136]{3,2,1,0:T(8,128)S(1)} %get-tuple-element.9) | data formatting | bytes 208896 | tf_op jit(solution)/shard_map/stack | solution.py:57
  7.5 1.1 %stack.104 = f32[1,204,128]{2,1,0:T(8,128)S(1)} reshape(f32[2,4,24,136]{3,2,1,0:T(8,128)} %get-tuple-element.18) | data formatting | bytes 208896 | tf_op jit(solution)/shard_map/stack | solution.py:57
  8.6 1.1 %stack.103 = f32[1,204,128]{2,1,0:T(8,128)S(1)} reshape(f32[2,4,24,136]{3,2,1,0:T(8,128)} %get-tuple-element.6) | data formatting | bytes 208896 | tf_op jit(solution)/shard_map/stack | solution.py:57
  9.6 0.8 %stack.105 = f32[1,204,128]{2,1,0:T(8,128)} reshape(f32[2,4,24,136]{3,2,1,0:T(8,128)S(1)} %get-tuple-element.17) | data formatting | bytes 208896 | tf_op jit(solution)/shard_map/stack | solution.py:57
  10.4 1.7 %pad_maximum_fusion.1 = f32[4,204,128]{2,1,0:T(8,128)} fusion(f32[1,204,128]{2,1,0:T(8,128)} %stack.106, f32[1,204,128]{2,1,0:T(8,128)} %stack.105, f32[1,204,128]{2,1,0:T(8,128)S(1)} %stack.104, f32[1,204,128]{2,1,0:T(8,128)S(1)} %stack.103), kind=kLoop, calls=%fused_computation.10 | loop fusion | flops 313344 | bytes 835584 | tf_op jit(solution)/shard_map/stack | solution.py:57
  12.2 3.0 %collective-permute-start.1 = (f32[4,204,128]{2,1,0:T(8,128)}, f32[4,204,128]{2,1,0:T(8,128)}, u32[]{:S(2)}, u32[]{:S(2)}) collective-permute-start(f32[4,204,128]{2,1,0:T(8,128)} %pad_maximum_fusion.1), channel_id=1, source_target_pairs={{0,8},{4,12},{8,0},{12,4},{1,9},{5,13},{9,1},{13,5},{2,10},{6,14},... | collective-permute-start | bytes 1253384 | tf_op jit(solution)/shard_map/ppermute | solution.py:16
  15.1 0.2 fusion.62
  15.3 0.2 stack.109
  15.5 0.2 stack.108
  15.6 0.2 stack.110
  15.8 0.2 stack.111
  16.0 1.5 %collective-permute-start.2 = (f32[4,204,128]{2,1,0:T(8,128)S(1)}, f32[4,204,128]{2,1,0:T(8,128)S(1)}, u32[]{:S(2)}, u32[]{:S(2)}) collective-permute-start(f32[4,204,128]{2,1,0:T(8,128)S(1)} %pad_maximum_fusion.2), channel_id=1, source_target_pairs={{0,12},{4,0},{8,4},{12,8},{1,13},{5,1},{9,5},{13,9},{2,14},{6,2},{... | collective-permute-start | bytes 1253384 | tf_op jit(solution)/shard_map/ppermute | solution.py:16
  17.5 0.2 stack.99
  17.7 0.2 stack.98
  17.8 0.2 stack.100
  18.0 0.2 stack.101
  18.2 0.6 collective-permute-start
  18.8 0.2 stack.96
  19.0 0.2 stack.93
  19.2 0.2 stack.94
  19.3 0.2 stack.95
  19.5 5.8 %collective-permute-done.1 = f32[4,204,128]{2,1,0:T(8,128)} collective-permute-done((f32[4,204,128]{2,1,0:T(8,128)}, f32[4,204,128]{2,1,0:T(8,128)}, u32[]{:S(2)}, u32[]{:S(2)}) %collective-permute-start.1) | collective-permute-done | bytes 417824 | tf_op jit(solution)/shard_map/ppermute | solution.py:16
  25.3 3.5 %collective-permute-done.2 = f32[4,204,128]{2,1,0:T(8,128)S(1)} collective-permute-done((f32[4,204,128]{2,1,0:T(8,128)S(1)}, f32[4,204,128]{2,1,0:T(8,128)S(1)}, u32[]{:S(2)}, u32[]{:S(2)}) %collective-permute-start.2) | collective-permute-done | bytes 417824 | tf_op jit(solution)/shard_map/ppermute | solution.py:16
  28.8 7.4 %collective-permute-done = f32[4,204,128]{2,1,0:T(8,128)S(1)} collective-permute-done((f32[4,204,128]{2,1,0:T(8,128)S(1)}, f32[4,204,128]{2,1,0:T(8,128)S(1)}, u32[]{:S(2)}, u32[]{:S(2)}) %collective-permute-start) | collective-permute-done | bytes 417824 | tf_op jit(solution)/shard_map/ppermute | solution.py:16
  36.2 1.1 %fusion.5 = f32[4,204,128]{2,1,0:T(8,128)S(1)} fusion(f32[4,204,128]{2,1,0:T(8,128)S(1)} %collective-permute-done.2, f32[4,204,128]{2,1,0:T(8,128)} %collective-permute-done.1, f32[4,204,128]{2,1,0:T(8,128)S(1)} %collective-permute-done, f32[1,204,128]{2,1,0:T(8,128)S(1)} %stack.96, f32[1,204,128]{2,1,0:T(8,128)S(1)} %stack.95, f32[1,204,128]{2,1,0:T(8,128)S(1)} %stack.94, ...), kind=kLoop, calls=%fused_computation.8 | loop fusion | flops 626688 | bytes 2088960 | tf_op jit(solution)/shard_map/add | solution.py:75
  37.3 1.8 %collective-permute-start.3 = (f32[204,128]{1,0:T(8,128)S(1)}, f32[204,128]{1,0:T(8,128)S(1)}, u32[]{:S(2)}, u32[]{:S(2)}) collective-permute-start(f32[204,128]{1,0:T(8,128)S(1)} %get-tuple-element.24), channel_id=1, source_target_pairs={{0,1},{1,2},{2,3},{3,0},{4,5},{5,6},{6,7},{7,4},{8,9},{9,10},{10,1... | collective-permute-start | bytes 313352 | tf_op jit(solution)/shard_map/ppermute | solution.py:16
  39.2 2.1 %collective-permute-start.5 = (f32[204,128]{1,0:T(8,128)S(1)}, f32[204,128]{1,0:T(8,128)S(1)}, u32[]{:S(2)}, u32[]{:S(2)}) collective-permute-start(f32[204,128]{1,0:T(8,128)S(1)} %get-tuple-element.25), channel_id=1, source_target_pairs={{0,3},{1,0},{2,1},{3,2},{4,7},{5,4},{6,5},{7,6},{8,11},{9,8},{10,9... | collective-permute-start | bytes 313352 | tf_op jit(solution)/shard_map/ppermute | solution.py:16
  41.3 0.9 %collective-permute-start.4 = (f32[204,128]{1,0:T(8,128)S(1)}, f32[204,128]{1,0:T(8,128)S(1)}, u32[]{:S(2)}, u32[]{:S(2)}) collective-permute-start(f32[204,128]{1,0:T(8,128)S(1)} %get-tuple-element.26), channel_id=1, source_target_pairs={{0,2},{1,3},{2,0},{3,1},{4,6},{5,7},{6,4},{7,5},{8,10},{9,11},{10,... | collective-permute-start | bytes 313352 | tf_op jit(solution)/shard_map/ppermute | solution.py:16
  42.2 2.7 %collective-permute-done.3 = f32[204,128]{1,0:T(8,128)S(1)} collective-permute-done((f32[204,128]{1,0:T(8,128)S(1)}, f32[204,128]{1,0:T(8,128)S(1)}, u32[]{:S(2)}, u32[]{:S(2)}) %collective-permute-start.3) | collective-permute-done | bytes 104480 | tf_op jit(solution)/shard_map/ppermute | solution.py:16
  45.0 0.4 collective-permute-done.5
  45.4 4.5 %collective-permute-done.4 = f32[204,128]{1,0:T(8,128)S(1)} collective-permute-done((f32[204,128]{1,0:T(8,128)S(1)}, f32[204,128]{1,0:T(8,128)S(1)}, u32[]{:S(2)}, u32[]{:S(2)}) %collective-permute-start.4) | collective-permute-done | bytes 104480 | tf_op jit(solution)/shard_map/ppermute | solution.py:16
  49.9 0.0 copy-start.1
  49.9 0.1 collective-permute-start.6
  50.0 0.1 broadcast_and_fusion
  50.0 0.1 slice.243
  50.1 1.1 %collective-permute-done.6 = f32[204,128]{1,0:T(8,128)S(1)} collective-permute-done((f32[204,128]{1,0:T(8,128)S(1)}, f32[204,128]{1,0:T(8,128)S(1)}, u32[]{:S(2)}, u32[]{:S(2)}) %collective-permute-start.6) | collective-permute-done | bytes 104480 | tf_op jit(solution)/shard_map/ppermute | solution.py:16
  51.3 0.1 div.23
  51.5 0.1 fusion.17
  51.6 0.1 fusion.26
  51.7 0.1 fusion.35
  51.9 0.1 fusion.38
  52.0 0.7 %fusion.60 = (bf16[4,16,128]{2,1,0:T(8,128)(2,1)S(1)}, f32[4,16,128]{2,1,0:T(8,128)}) fusion(f32[4,16,128]{2,1,0:T(8,128)S(1)} %copy-done.1, f32[4,24,136]{2,1,0:T(8,128)S(1)} %get-tuple-element.30, f32[4,24,136]{2,1,0:T(8,128)S(1)} %get-tuple-element.29, f32[4,24,136]{2,1,0:T(8,128)S(1)} %get-tuple-element.28, f32[4,24,136]{2,1,0:T(8,128)S(1)} %get-tuple-element.27, ...), kind=kLoop, calls=%fused_computation.144 | loop fusion | flops 90112 | bytes 247808 | tf_op jit(solution)/shard_map/convert_element_type | solution.py:104
  52.7 2.5 %collective-permute-start.9 = (bf16[8,1024]{1,0:T(8,128)(2,1)S(1)}, bf16[8,1024]{1,0:T(8,128)(2,1)S(1)}, u32[]{:S(2)}, u32[]{:S(2)}) collective-permute-start(bf16[8,1024]{1,0:T(8,128)(2,1)S(1)} %bitcast.70), channel_id=1, source_target_pairs={{0,3},{1,0},{2,1},{3,2},{4,7},{5,4},{6,5},{7,6},{8,11},{9,8},{10,9... | collective-permute-start | bytes 49160 | tf_op jit(solution)/shard_map/ppermute | solution.py:16
  55.2 0.0 collective-permute-start.8
  55.2 0.6 collective-permute-start.7
  55.9 0.8 %collective-permute-done.9 = bf16[8,1024]{1,0:T(8,128)(2,1)S(1)} collective-permute-done((bf16[8,1024]{1,0:T(8,128)(2,1)S(1)}, bf16[8,1024]{1,0:T(8,128)(2,1)S(1)}, u32[]{:S(2)}, u32[]{:S(2)}) %collective-permute-start.9) | collective-permute-done | bytes 16416 | tf_op jit(solution)/shard_map/ppermute | solution.py:16
  56.7 3.2 %collective-permute-done.8 = bf16[8,1024]{1,0:T(8,128)(2,1)S(1)} collective-permute-done((bf16[8,1024]{1,0:T(8,128)(2,1)S(1)}, bf16[8,1024]{1,0:T(8,128)(2,1)S(1)}, u32[]{:S(2)}, u32[]{:S(2)}) %collective-permute-start.8) | collective-permute-done | bytes 16416 | tf_op jit(solution)/shard_map/ppermute | solution.py:16
  59.9 0.9 %collective-permute-done.7 = bf16[8,1024]{1,0:T(8,128)(2,1)S(1)} collective-permute-done((bf16[8,1024]{1,0:T(8,128)(2,1)S(1)}, bf16[8,1024]{1,0:T(8,128)(2,1)S(1)}, u32[]{:S(2)}, u32[]{:S(2)}) %collective-permute-start.7) | collective-permute-done | bytes 16416 | tf_op jit(solution)/shard_map/ppermute | solution.py:16
  60.8 1.6 %collective-permute-start.11 = (bf16[4,8,1024]{2,1,0:T(8,128)(2,1)S(1)}, bf16[4,8,1024]{2,1,0:T(8,128)(2,1)S(1)}, u32[]{:S(2)}, u32[]{:S(2)}) collective-permute-start(bf16[4,8,1024]{2,1,0:T(8,128)(2,1)S(1)} %get-tuple-element.32), channel_id=1, source_target_pairs={{0,8},{4,12},{8,0},{12,4},{1,9},{5,13},{9,1},{13,5},{2,10},{6,14},... | collective-permute-start | bytes 196616 | tf_op jit(solution)/shard_map/ppermute | solution.py:16
  62.4 1.6 %collective-permute-start.10 = (bf16[4,8,1024]{2,1,0:T(8,128)(2,1)S(1)}, bf16[4,8,1024]{2,1,0:T(8,128)(2,1)S(1)}, u32[]{:S(2)}, u32[]{:S(2)}) collective-permute-start(bf16[4,8,1024]{2,1,0:T(8,128)(2,1)S(1)} %get-tuple-element.32), channel_id=1, source_target_pairs={{0,4},{4,8},{8,12},{12,0},{1,5},{5,9},{9,13},{13,1},{2,6},{6,10},{... | collective-permute-start | bytes 196616 | tf_op jit(solution)/shard_map/ppermute | solution.py:16
  63.9 1.4 %collective-permute-start.12 = (bf16[4,8,1024]{2,1,0:T(8,128)(2,1)S(1)}, bf16[4,8,1024]{2,1,0:T(8,128)(2,1)S(1)}, u32[]{:S(2)}, u32[]{:S(2)}) collective-permute-start(bf16[4,8,1024]{2,1,0:T(8,128)(2,1)S(1)} %get-tuple-element.32), channel_id=1, source_target_pairs={{0,12},{4,0},{8,4},{12,8},{1,13},{5,1},{9,5},{13,9},{2,14},{6,2},{... | collective-permute-start | bytes 196616 | tf_op jit(solution)/shard_map/ppermute | solution.py:16
  65.3 0.4 collective-permute-done.11
  65.7 1.8 %collective-permute-done.10 = bf16[4,8,1024]{2,1,0:T(8,128)(2,1)S(1)} collective-permute-done((bf16[4,8,1024]{2,1,0:T(8,128)(2,1)S(1)}, bf16[4,8,1024]{2,1,0:T(8,128)(2,1)S(1)}, u32[]{:S(2)}, u32[]{:S(2)}) %collective-permute-start.10) | collective-permute-done | bytes 65568 | tf_op jit(solution)/shard_map/ppermute | solution.py:16
  67.5 0.7 collective-permute-done.12
  68.2 0.3 convolution_convert_fusion
  68.6 1.2 %reshape.262 = bf16[1,1,1,256,4,2,128]{6,5,4,3,2,1,0:T(2,128)(2,1)} reshape(bf16[256,1024]{1,0:T(8,128)(2,1)S(1)} %convolution_convert_fusion) | data formatting | bytes 1048576 | tf_op jit(solution)/shard_map/reshape | solution.py:120
  (21 shorter events, 0.3 us)
Async XLA Ops:
  0.6 1.5 %copy-start = (bf16[1,1,1,256,4,2,128]{6,5,4,3,2,1,0:T(2,128)(2,1)S(1)}, bf16[1,1,1,256,4,2,128]{6,5,4,3,2,1,0:T(2,128)(2,1)}, u32[]{:S(2)}) copy-start(bf16[1,1,1,256,4,2,128]{6,5,4,3,2,1,0:T(2,128)(2,1)} %param.6) | copy-start | bytes 1572868
  0.6 1.9 %copy-start.2 = (s32[1,1,1,256]{3,2,1,0:T(1,128)S(1)}, s32[1,1,1,256]{3,2,1,0:T(1,128)}, u32[]{:S(2)}) copy-start(s32[1,1,1,256]{3,2,1,0:T(1,128)} %param.8) | copy-start | bytes 3076
  0.7 1.9 %copy-start.3 = (s32[1,1,1,256]{3,2,1,0:T(1,128)S(1)}, s32[1,1,1,256]{3,2,1,0:T(1,128)}, u32[]{:S(2)}) copy-start(s32[1,1,1,256]{3,2,1,0:T(1,128)} %param.7) | copy-start | bytes 3076
  12.2 13.1 %collective-permute-start.1 = (f32[4,204,128]{2,1,0:T(8,128)}, f32[4,204,128]{2,1,0:T(8,128)}, u32[]{:S(2)}, u32[]{:S(2)}) collective-permute-start(f32[4,204,128]{2,1,0:T(8,128)} %pad_maximum_fusion.1), channel_id=1, source_target_pairs={{0,8},{4,12},{8,0},{12,4},{1,9},{5,13},{9,1},{13,5},{2,10},{6,14},... | collective-permute-start | bytes 1253384 | tf_op jit(solution)/shard_map/ppermute | solution.py:16
  16.0 12.8 %collective-permute-start.2 = (f32[4,204,128]{2,1,0:T(8,128)S(1)}, f32[4,204,128]{2,1,0:T(8,128)S(1)}, u32[]{:S(2)}, u32[]{:S(2)}) collective-permute-start(f32[4,204,128]{2,1,0:T(8,128)S(1)} %pad_maximum_fusion.2), channel_id=1, source_target_pairs={{0,12},{4,0},{8,4},{12,8},{1,13},{5,1},{9,5},{13,9},{2,14},{6,2},{... | collective-permute-start | bytes 1253384 | tf_op jit(solution)/shard_map/ppermute | solution.py:16
  18.2 18.0 %collective-permute-start = (f32[4,204,128]{2,1,0:T(8,128)S(1)}, f32[4,204,128]{2,1,0:T(8,128)S(1)}, u32[]{:S(2)}, u32[]{:S(2)}) collective-permute-start(f32[4,204,128]{2,1,0:T(8,128)S(1)} %pad_maximum_fusion), channel_id=1, source_target_pairs={{0,4},{4,8},{8,12},{12,0},{1,5},{5,9},{9,13},{13,1},{2,6},{6,10},{... | collective-permute-start | bytes 1253384 | tf_op jit(solution)/shard_map/ppermute | solution.py:16
  37.3 7.6 %collective-permute-start.3 = (f32[204,128]{1,0:T(8,128)S(1)}, f32[204,128]{1,0:T(8,128)S(1)}, u32[]{:S(2)}, u32[]{:S(2)}) collective-permute-start(f32[204,128]{1,0:T(8,128)S(1)} %get-tuple-element.24), channel_id=1, source_target_pairs={{0,1},{1,2},{2,3},{3,0},{4,5},{5,6},{6,7},{7,4},{8,9},{9,10},{10,1... | collective-permute-start | bytes 313352 | tf_op jit(solution)/shard_map/ppermute | solution.py:16
  39.2 6.2 %collective-permute-start.5 = (f32[204,128]{1,0:T(8,128)S(1)}, f32[204,128]{1,0:T(8,128)S(1)}, u32[]{:S(2)}, u32[]{:S(2)}) collective-permute-start(f32[204,128]{1,0:T(8,128)S(1)} %get-tuple-element.25), channel_id=1, source_target_pairs={{0,3},{1,0},{2,1},{3,2},{4,7},{5,4},{6,5},{7,6},{8,11},{9,8},{10,9... | collective-permute-start | bytes 313352 | tf_op jit(solution)/shard_map/ppermute | solution.py:16
  41.3 8.6 %collective-permute-start.4 = (f32[204,128]{1,0:T(8,128)S(1)}, f32[204,128]{1,0:T(8,128)S(1)}, u32[]{:S(2)}, u32[]{:S(2)}) collective-permute-start(f32[204,128]{1,0:T(8,128)S(1)} %get-tuple-element.26), channel_id=1, source_target_pairs={{0,2},{1,3},{2,0},{3,1},{4,6},{5,7},{6,4},{7,5},{8,10},{9,11},{10,... | collective-permute-start | bytes 313352 | tf_op jit(solution)/shard_map/ppermute | solution.py:16
  49.9 2.1 %copy-start.1 = (f32[4,16,128]{2,1,0:T(8,128)S(1)}, f32[4,16,128]{2,1,0:T(8,128)}, u32[]{:S(2)}) copy-start(f32[4,16,128]{2,1,0:T(8,128)} %param.9) | copy-start | bytes 98308
  49.9 1.4 %collective-permute-start.6 = (f32[204,128]{1,0:T(8,128)S(1)}, f32[204,128]{1,0:T(8,128)S(1)}, u32[]{:S(2)}, u32[]{:S(2)}) collective-permute-start(f32[204,128]{1,0:T(8,128)S(1)} %fusion.10), channel_id=1, source_target_pairs={{0,16},{16,0},{1,17},{17,1},{2,18},{18,2},{3,19},{19,3},{4,20},{20... | collective-permute-start | bytes 313352 | tf_op jit(solution)/shard_map/ppermute | solution.py:16
  52.7 3.9 %collective-permute-start.9 = (bf16[8,1024]{1,0:T(8,128)(2,1)S(1)}, bf16[8,1024]{1,0:T(8,128)(2,1)S(1)}, u32[]{:S(2)}, u32[]{:S(2)}) collective-permute-start(bf16[8,1024]{1,0:T(8,128)(2,1)S(1)} %bitcast.70), channel_id=1, source_target_pairs={{0,3},{1,0},{2,1},{3,2},{4,7},{5,4},{6,5},{7,6},{8,11},{9,8},{10,9... | collective-permute-start | bytes 49160 | tf_op jit(solution)/shard_map/ppermute | solution.py:16
  55.2 4.6 %collective-permute-start.8 = (bf16[8,1024]{1,0:T(8,128)(2,1)S(1)}, bf16[8,1024]{1,0:T(8,128)(2,1)S(1)}, u32[]{:S(2)}, u32[]{:S(2)}) collective-permute-start(bf16[8,1024]{1,0:T(8,128)(2,1)S(1)} %bitcast.71), channel_id=1, source_target_pairs={{0,2},{1,3},{2,0},{3,1},{4,6},{5,7},{6,4},{7,5},{8,10},{9,11},{10,... | collective-permute-start | bytes 49160 | tf_op jit(solution)/shard_map/ppermute | solution.py:16
  55.2 5.5 %collective-permute-start.7 = (bf16[8,1024]{1,0:T(8,128)(2,1)S(1)}, bf16[8,1024]{1,0:T(8,128)(2,1)S(1)}, u32[]{:S(2)}, u32[]{:S(2)}) collective-permute-start(bf16[8,1024]{1,0:T(8,128)(2,1)S(1)} %bitcast.72), channel_id=1, source_target_pairs={{0,1},{1,2},{2,3},{3,0},{4,5},{5,6},{6,7},{7,4},{8,9},{9,10},{10,1... | collective-permute-start | bytes 49160 | tf_op jit(solution)/shard_map/ppermute | solution.py:16
  60.8 4.9 %collective-permute-start.11 = (bf16[4,8,1024]{2,1,0:T(8,128)(2,1)S(1)}, bf16[4,8,1024]{2,1,0:T(8,128)(2,1)S(1)}, u32[]{:S(2)}, u32[]{:S(2)}) collective-permute-start(bf16[4,8,1024]{2,1,0:T(8,128)(2,1)S(1)} %get-tuple-element.32), channel_id=1, source_target_pairs={{0,8},{4,12},{8,0},{12,4},{1,9},{5,13},{9,1},{13,5},{2,10},{6,14},... | collective-permute-start | bytes 196616 | tf_op jit(solution)/shard_map/ppermute | solution.py:16
  62.4 5.2 %collective-permute-start.10 = (bf16[4,8,1024]{2,1,0:T(8,128)(2,1)S(1)}, bf16[4,8,1024]{2,1,0:T(8,128)(2,1)S(1)}, u32[]{:S(2)}, u32[]{:S(2)}) collective-permute-start(bf16[4,8,1024]{2,1,0:T(8,128)(2,1)S(1)} %get-tuple-element.32), channel_id=1, source_target_pairs={{0,4},{4,8},{8,12},{12,0},{1,5},{5,9},{9,13},{13,1},{2,6},{6,10},{... | collective-permute-start | bytes 196616 | tf_op jit(solution)/shard_map/ppermute | solution.py:16
  63.9 4.3 %collective-permute-start.12 = (bf16[4,8,1024]{2,1,0:T(8,128)(2,1)S(1)}, bf16[4,8,1024]{2,1,0:T(8,128)(2,1)S(1)}, u32[]{:S(2)}, u32[]{:S(2)}) collective-permute-start(bf16[4,8,1024]{2,1,0:T(8,128)(2,1)S(1)} %get-tuple-element.32), channel_id=1, source_target_pairs={{0,12},{4,0},{8,4},{12,8},{1,13},{5,1},{9,5},{13,9},{2,14},{6,2},{... | collective-permute-start | bytes 196616 | tf_op jit(solution)/shard_map/ppermute | solution.py:16

commit v2 on v1

--- a/solution.py
+++ b/solution.py
@@ -35,40 +35,51 @@
     ext_rows = tile_rows + 2 * h
     ext_cols = tile_cols + 2 * h
 
-    owner_x = owners // size_y
-    owner_y = owners % size_y
-    rel_row = (((owner_x - me_x) % size_x) * size_y + (owner_y - me_y) % size_y) * per_tile + patches
-    onehot = (rel_row[None, :] == jnp.arange(tiles * per_tile, dtype=jnp.int32)[:, None]).astype(
-        jnp.bfloat16
+    me_g = lax.axis_index("group")
+    quantities = jnp.stack(
+        [slot_grad.reshape(slot_count, cell_count), slot_illum.reshape(slot_count, cell_count)]
     )
-    both = jnp.concatenate(
-        [slot_grad.reshape(slot_count, cell_count), slot_illum.reshape(slot_count, cell_count)],
-        axis=1,
+    kept = lax.dynamic_index_in_dim(quantities, me_g, 0, keepdims=False)
+    given = lax.dynamic_index_in_dim(quantities, 1 - me_g, 0, keepdims=False)
+    places = jnp.stack([owners, patches])
+    taken = shifted(given, "group", size_g, 1)
+    taken_places = shifted(places, "group", size_g, 1)
+    rows_in = jnp.concatenate([kept, taken], axis=0)
+    all_owners = jnp.concatenate([owners, taken_places[0]])
+    all_patches = jnp.concatenate([patches, taken_places[1]])
+
+    halo_patches = h // patch_rows
+    ext_patches = per_tile + 2 * halo_patches
+    rel_x = (all_owners // size_y - me_x) % size_x
+    rel_y = (all_owners % size_y - me_y) % size_y
+    own_row = (rel_x * size_y + rel_y) * ext_patches + all_patches + halo_patches
+    next_row = jnp.where(
+        all_patches >= per_tile - halo_patches,
+        (((rel_x + 1) % size_x) * size_y + rel_y) * ext_patches
+        + all_patches
+        - (per_tile - halo_patches),
+        -1,
     )
-    table = jnp.dot(onehot, both, preferred_element_type=jnp.float32)
-    model = table.reshape(size_x, size_y, per_tile, 2, levels, patch_rows, patch_cols)
-    model = model.transpose(3, 4, 0, 2, 5, 1, 6).reshape(
-        2, levels, size_x * tile_rows, size_y * tile_cols
+    prev_row = jnp.where(
+        all_patches < halo_patches,
+        (((rel_x - 1) % size_x) * size_y + rel_y) * ext_patches
+        + all_patches
+        + per_tile
+        + halo_patches,
+        -1,
     )
-    model = jnp.concatenate([model[:, :, -h:], model, model[:, :, :h]], axis=2)
-    model = jnp.concatenate([model[:, :, :, -h:], model, model[:, :, :, :h]], axis=3)
-    ext = jnp.stack(
-        [
-            jnp.stack(
-                [
-                    model[
-                        :,
-                        :,
-                        tx * tile_rows : tx * tile_rows + ext_rows,
-                        ty * tile_cols : ty * tile_cols + ext_cols,
-                    ]
-                    for ty in range(size_y)
-                ]
-            )
-            for tx in range(size_x)
-        ]
-    )
-    flat = ext.reshape(size_x, size_y, -1, 128)
+    row_ids = jnp.arange(tiles * ext_patches, dtype=jnp.int32)[:, None]
+    onehot = (
+        (own_row[None, :] == row_ids) | (next_row[None, :] == row_ids) | (prev_row[None, :] == row_ids)
+    ).astype(jnp.bfloat16)
+    table = jnp.dot(onehot, rows_in, preferred_element_type=jnp.float32)
+    table = table.reshape(size_x, size_y, ext_patches, levels, patch_rows, patch_cols)
+    left = jnp.roll(table, 1, axis=1)[..., patch_cols - h :]
+    right = jnp.roll(table, -1, axis=1)[..., :h]
+    strips = jnp.concatenate([left, right], axis=-1)
+    flat = jnp.concatenate(
+        [table.reshape(size_x, size_y, -1), strips.reshape(size_x, size_y, -1)], axis=2
+    ).reshape(size_x, size_y, -1, 128)
 
     part = flat[0]
     for step in range(1, size_x):
@@ -76,17 +87,26 @@
     total = part[0]
     for step in range(1, size_y):
         total = total + shifted(part[step], "gy", size_y, step)
-    mine = total
-    for step in range(1, size_g):
-        total = total + shifted(mine, "group", size_g, step)
+    other = shifted(total, "group", size_g, 1)
+    is_grad = me_g == 0
+    grad_flat = jnp.where(is_grad, total, other).reshape(-1)
+    illum_flat = jnp.where(is_grad, other, total).reshape(-1)
 
-    sums = total.reshape(2, levels, ext_rows, ext_cols)
+    def unpack(values):
+        main_size = ext_patches * levels * patch_rows * patch_cols
+        main = values[:main_size].reshape(ext_patches, levels, patch_rows, patch_cols)
+        sides = values[main_size:].reshape(ext_patches, levels, patch_rows, 2 * h)
+        whole_rows = jnp.concatenate([sides[..., :h], main, sides[..., h:]], axis=-1)
+        return whole_rows.transpose(1, 0, 2, 3).reshape(levels, ext_rows, ext_cols)
+
+    grad_ext = unpack(grad_flat)
+    illum_ext = unpack(illum_flat)
     pos_x = me_x * tile_rows - h + jnp.arange(ext_rows)
     pos_y = me_y * tile_cols - h + jnp.arange(ext_cols)
     inside = ((pos_x >= 0) & (pos_x < size_x * tile_rows))[:, None] & (
         (pos_y >= 0) & (pos_y < size_y * tile_cols)
     )[None, :]
-    field_now = jnp.where(inside, sums[0] / (sums[1] + damping), 0.0)
+    field_now = jnp.where(inside, grad_ext / (illum_ext + damping), 0.0)
     for sweep_index in range(SWEEPS):
         padded = jnp.pad(field_now, 1)
         beside = (
@@ -110,6 +130,8 @@
         [along_y] + [shifted(along_y, "gx", size_x, step) for step in range(1, size_x)]
     )
     whole = along_x.reshape(tiles * per_tile, cell_count)
+    owner_x = owners // size_y
+    owner_y = owners % size_y
     back_row = (
         ((me_x - owner_x) % size_x) * size_y + (me_y - owner_y) % size_y
     ) * per_tile + patches

time: 70 us -> 53 us (0.76)
  waiting for transfers between devices: 33.3 us -> 18.6 us
  other arithmetic: 7.18 us -> 3.98 us
  starting transfers between devices: 17.7 us -> 20.4 us
  local copies, waits for them, and re-layouts: 10 us -> 8.17 us
    ppermute x13 -> x15, waiting for transfers between devices: 33.3 us -> 18.6 us  [shifted(): lax.ppermute(value, axis, [(s, (s + step) % count) for s in range(count)])]
    another operation x18 -> x4, local copies, waits for them, and re-layouts: 7.5 us -> 2.38 us  [the longest x3 1.86 us: local(): jnp.stack([slot_grad.reshape(slot_count, cell_count), slot_illum.reshape(...]
    slice x4 -> x0, other arithmetic: 2.83 us -> none  [local(): model[:, :, tx * tile_rows:tx * tile_rows + ext_rows, ty * tile_cols:ty *...]
    ppermute x13 -> x15, starting transfers between devices: 17.7 us -> 20.4 us  [shifted(): lax.ppermute(value, axis, [(s, (s + step) % count) for s in range(count)])]
    concatenate x0 -> x1, other arithmetic: none -> 1.69 us  [local(): strips = jnp.concatenate([left, right], axis=-1)]
    unnamed x8 -> x11, local copies, waits for them, and re-layouts: 0.02 us -> 1.18 us
    another operation x3 -> x1, other arithmetic: 1.79 us -> 0.71 us  [local(): places = jnp.stack([owners, patches])]
    add x1, other arithmetic: 1.09 us -> 0.06 us  [local(): part = part + shifted(flat[step], 'gx', size_x, step)]
  transfers between devices with their start and end apart: 13 -> 15, of which waited for: 13 -> 14; matrix products, arithmetic and copies ran while one was open for 3% -> 6% of each run, Pallas kernels for 0% -> 0%
where the time goes in v2:
time: 53 us; the launch traced here: 52.8 us
  starting transfers between devices  20.4 us (38%)
  waiting for transfers between devices  18.6 us (35%)
  local copies, waits for them, and re-layouts  8.17 us (15%)
  other arithmetic  3.98 us (8%)
  between operations  0.96 us (2%)
  matrix products  0.72 us (1%)
    ppermute x15, starting transfers between devices, shifted(): lax.ppermute(value, axis, [(s, (s + step) % count) for s in range(count)])  20.4 us
    ppermute x15, waiting for transfers between devices, shifted(): lax.ppermute(value, axis, [(s, (s + step) % count) for s in range(count)])  18.6 us
    another operation x3, local copies, waits for them, and re-layouts, local(): jnp.stack([slot_grad.reshape(slot_count, cell_count), slot_illum.reshape(...  1.86 us
    concatenate x1, other arithmetic, local(): strips = jnp.concatenate([left, right], axis=-1)  1.69 us
    unnamed x11, local copies, waits for them, and re-layouts  1.18 us
    reshape x1, local copies, waits for them, and re-layouts, local(): returned.reshape((1, 1, 1, slot_count, levels, patch_rows, patch_cols))  1.16 us
    reshape x1, local copies, waits for them, and re-layouts, local(): strips.reshape(size_x, size_y, -1)  1.11 us
  transfers between devices with their start and end apart: 15, of which 14 were waited for; matrix products, arithmetic and copies ran while one was open for 6% of the time, Pallas kernels for 0%

profile of v2, /device:TPU:0, one launch (start us, length us, event | category | flops | bytes accessed | tf_op | source)
XLA Modules:
  0.0 52.8 jit_solution(12417121185418250152)
XLA Ops:
  0.6 0.7 %pad_add_fusion = s32[2,256]{1,0:T(2,128)S(1)} fusion(s32[1,256]{1,0:T(1,128)} %bitcast.59, s32[1,256]{1,0:T(1,128)} %bitcast.65), kind=kLoop, calls=%fused_computation.142 | loop fusion | flops 512 | bytes 4096 | tf_op jit(solution)/shard_map/stack | solution.py:44
  1.3 0.5 collective-permute-start
  1.8 1.5 %stack_reshape_squeeze.6 = bf16[1,256,1024]{2,1,0:T(8,128)(2,1)S(1)} reshape(bf16[1,1,1,256,4,2,128]{6,5,4,3,2,1,0:T(2,128)(2,1)} %param.5) | data formatting | bytes 1048576 | tf_op jit(solution)/shard_map/stack;reshape;squeeze | solution.py:39
  3.3 0.4 stack_reshape_squeeze.7
  3.7 0.0 copy-start.2
  3.7 0.0 copy-start.3
  3.7 0.1 dynamic-slice_bitcast_fusion.1
  3.8 0.1 collective-permute-start.1
  4.0 0.4 copy-done.2
  4.4 0.0 copy-done.3
  4.5 1.3 %collective-permute-done.1 = bf16[256,1024]{1,0:T(8,128)(2,1)S(1)} collective-permute-done((bf16[256,1024]{1,0:T(8,128)(2,1)S(1)}, bf16[256,1024]{1,0:T(8,128)(2,1)S(1)}, u32[]{:S(2)}, u32[]{:S(2)}) %collective-permute-start.1) | collective-permute-done | bytes 524320 | tf_op jit(solution)/shard_map/ppermute | solution.py:16
  5.8 0.4 fusion
  6.2 0.7 %reshape.523 = f32[4,4,12,4,2,128]{5,4,3,2,1,0:T(2,128)S(1)} reshape(f32[192,1024]{1,0:T(8,128)S(1)} %fusion) | data formatting | bytes 1572864 | tf_op jit(solution)/shard_map/reshape | solution.py:76
  6.9 0.6 %fusion.82 = (f32[4,3,12,4,2,128]{5,4,3,2,1,0:T(2,128)S(1)}, f32[4,3,12,4,2,128]{5,4,3,2,1,0:T(2,128)S(1)}) fusion(f32[4,4,12,4,2,128]{5,4,3,2,1,0:T(2,128)S(1)} %reshape.523), kind=kLoop, calls=%fused_computation.169 | loop fusion | bytes 2359296 | tf_op jit(solution)/shard_map/jit(_roll_static)/slice | solution.py:77
  7.5 0.5 reshape_reshape.3
  8.0 1.7 %fusion.4 = f32[4,4,12,4,2,8]{5,4,3,2,1,0:T(2,128)S(1)} fusion(f32[4,1,12,4,2,128]{5,4,3,2,1,0:T(2,128)S(1)} %get-tuple-element.16, f32[4,3,12,4,2,128]{5,4,3,2,1,0:T(2,128)S(1)} %get-tuple-element.18, f32[4,3,12,4,2,128]{5,4,3,2,1,0:T(2,128)S(1)} %get-tuple-element.17, f32[4,1,12,4,2,128]{5,4,3,2,1,0:T(2,128)S(1)} %get-tuple-element.15), kind=kLoop, calls=%fused_computation.6 | loop fusion | flops 36864 | bytes 1622016 | tf_op jit(solution)/shard_map/concatenate | solution.py:79
  9.7 1.1 %reshape.524 = f32[4,4,768]{2,1,0:T(4,128)S(1)} reshape(f32[4,4,12,4,2,8]{5,4,3,2,1,0:T(2,128)S(1)} %fusion.4) | data formatting | bytes 98304 | tf_op jit(solution)/shard_map/reshape | solution.py:81
  10.8 0.1 constant_dynamic-update-slice_fusion.3
  10.9 0.1 fusion.80
  11.0 0.1 squeeze.38
  11.1 2.7 %collective-permute-start.2 = (f32[4,102,128]{2,1,0:T(8,128)S(1)}, f32[4,102,128]{2,1,0:T(8,128)S(1)}, u32[]{:S(2)}, u32[]{:S(2)}) collective-permute-start(f32[4,102,128]{2,1,0:T(8,128)S(1)} %squeeze.38), channel_id=1, source_target_pairs={{0,4},{4,8},{8,12},{12,0},{1,5},{5,9},{9,13},{13,1},{2,6},{6,10},{... | collective-permute-start | bytes 626696 | tf_op jit(solution)/shard_map/ppermute | solution.py:16
  13.8 0.1 squeeze.39
  13.8 1.6 %collective-permute-start.3 = (f32[4,102,128]{2,1,0:T(8,128)S(1)}, f32[4,102,128]{2,1,0:T(8,128)S(1)}, u32[]{:S(2)}, u32[]{:S(2)}) collective-permute-start(f32[4,102,128]{2,1,0:T(8,128)S(1)} %squeeze.39), channel_id=1, source_target_pairs={{0,8},{4,12},{8,0},{12,4},{1,9},{5,13},{9,1},{13,5},{2,10},{6,14},... | collective-permute-start | bytes 626696 | tf_op jit(solution)/shard_map/ppermute | solution.py:16
  15.4 0.1 squeeze.40
  15.5 1.5 %collective-permute-start.4 = (f32[4,102,128]{2,1,0:T(8,128)S(1)}, f32[4,102,128]{2,1,0:T(8,128)S(1)}, u32[]{:S(2)}, u32[]{:S(2)}) collective-permute-start(f32[4,102,128]{2,1,0:T(8,128)S(1)} %squeeze.40), channel_id=1, source_target_pairs={{0,12},{4,0},{8,4},{12,8},{1,13},{5,1},{9,5},{13,9},{2,14},{6,2},{... | collective-permute-start | bytes 626696 | tf_op jit(solution)/shard_map/ppermute | solution.py:16
  17.0 0.1 squeeze.37
  17.1 3.8 %collective-permute-done.2 = f32[4,102,128]{2,1,0:T(8,128)S(1)} collective-permute-done((f32[4,102,128]{2,1,0:T(8,128)S(1)}, f32[4,102,128]{2,1,0:T(8,128)S(1)}, u32[]{:S(2)}, u32[]{:S(2)}) %collective-permute-start.2) | collective-permute-done | bytes 208928 | tf_op jit(solution)/shard_map/ppermute | solution.py:16
  20.8 4.2 %collective-permute-done.3 = f32[4,102,128]{2,1,0:T(8,128)S(1)} collective-permute-done((f32[4,102,128]{2,1,0:T(8,128)S(1)}, f32[4,102,128]{2,1,0:T(8,128)S(1)}, u32[]{:S(2)}, u32[]{:S(2)}) %collective-permute-start.3) | collective-permute-done | bytes 208928 | tf_op jit(solution)/shard_map/ppermute | solution.py:16
  25.1 0.3 collective-permute-done.4
  25.3 0.1 add_add_fusion
  25.4 1.6 %collective-permute-start.5 = (f32[102,128]{1,0:T(8,128)S(1)}, f32[102,128]{1,0:T(8,128)S(1)}, u32[]{:S(2)}, u32[]{:S(2)}) collective-permute-start(f32[102,128]{1,0:T(8,128)S(1)} %get-tuple-element.19), channel_id=1, source_target_pairs={{0,1},{1,2},{2,3},{3,0},{4,5},{5,6},{6,7},{7,4},{8,9},{9,10},{10,1... | collective-permute-start | bytes 156680 | tf_op jit(solution)/shard_map/ppermute | solution.py:16
  27.1 2.6 %collective-permute-start.6 = (f32[102,128]{1,0:T(8,128)S(1)}, f32[102,128]{1,0:T(8,128)S(1)}, u32[]{:S(2)}, u32[]{:S(2)}) collective-permute-start(f32[102,128]{1,0:T(8,128)S(1)} %get-tuple-element.21), channel_id=1, source_target_pairs={{0,2},{1,3},{2,0},{3,1},{4,6},{5,7},{6,4},{7,5},{8,10},{9,11},{10,... | collective-permute-start | bytes 156680 | tf_op jit(solution)/shard_map/ppermute | solution.py:16
  29.6 1.3 %collective-permute-start.7 = (f32[102,128]{1,0:T(8,128)S(1)}, f32[102,128]{1,0:T(8,128)S(1)}, u32[]{:S(2)}, u32[]{:S(2)}) collective-permute-start(f32[102,128]{1,0:T(8,128)S(1)} %get-tuple-element.20), channel_id=1, source_target_pairs={{0,3},{1,0},{2,1},{3,2},{4,7},{5,4},{6,5},{7,6},{8,11},{9,8},{10,9... | collective-permute-start | bytes 156680 | tf_op jit(solution)/shard_map/ppermute | solution.py:16
  31.0 0.7 %collective-permute-done.5 = f32[102,128]{1,0:T(8,128)S(1)} collective-permute-done((f32[102,128]{1,0:T(8,128)S(1)}, f32[102,128]{1,0:T(8,128)S(1)}, u32[]{:S(2)}, u32[]{:S(2)}) %collective-permute-start.5) | collective-permute-done | bytes 52256 | tf_op jit(solution)/shard_map/ppermute | solution.py:16
  31.7 2.0 %collective-permute-done.6 = f32[102,128]{1,0:T(8,128)S(1)} collective-permute-done((f32[102,128]{1,0:T(8,128)S(1)}, f32[102,128]{1,0:T(8,128)S(1)}, u32[]{:S(2)}, u32[]{:S(2)}) %collective-permute-start.6) | collective-permute-done | bytes 52256 | tf_op jit(solution)/shard_map/ppermute | solution.py:16
  33.7 0.3 collective-permute-done.7
  34.1 0.1 collective-permute-start.8
  34.1 0.1 broadcast_and_fusion
  34.2 0.1 slice.235
  34.3 1.1 %collective-permute-done.8 = f32[102,128]{1,0:T(8,128)S(1)} collective-permute-done((f32[102,128]{1,0:T(8,128)S(1)}, f32[102,128]{1,0:T(8,128)S(1)}, u32[]{:S(2)}, u32[]{:S(2)}) %collective-permute-start.8) | collective-permute-done | bytes 52256 | tf_op jit(solution)/shard_map/ppermute | solution.py:16
  35.4 0.1 reshape.525
  35.5 0.1 reshape.527
  35.7 0.2 fusion.83
  35.9 0.4 fusion.40
  36.3 0.2 fusion.17
  36.5 0.2 fusion.26
  36.7 0.2 fusion.35
  36.9 0.2 fusion.38
  37.1 0.2 fusion.78
  37.3 1.0 %collective-permute-start.9 = (bf16[8,1024]{1,0:T(8,128)(2,1)S(1)}, bf16[8,1024]{1,0:T(8,128)(2,1)S(1)}, u32[]{:S(2)}, u32[]{:S(2)}) collective-permute-start(bf16[8,1024]{1,0:T(8,128)(2,1)S(1)} %bitcast.48), channel_id=1, source_target_pairs={{0,1},{1,2},{2,3},{3,0},{4,5},{5,6},{6,7},{7,4},{8,9},{9,10},{10,1... | collective-permute-start | bytes 49160 | tf_op jit(solution)/shard_map/ppermute | solution.py:16
  38.3 2.5 %collective-permute-start.10 = (bf16[8,1024]{1,0:T(8,128)(2,1)S(1)}, bf16[8,1024]{1,0:T(8,128)(2,1)S(1)}, u32[]{:S(2)}, u32[]{:S(2)}) collective-permute-start(bf16[8,1024]{1,0:T(8,128)(2,1)S(1)} %bitcast.49), channel_id=1, source_target_pairs={{0,2},{1,3},{2,0},{3,1},{4,6},{5,7},{6,4},{7,5},{8,10},{9,11},{10,... | collective-permute-start | bytes 49160 | tf_op jit(solution)/shard_map/ppermute | solution.py:16
  40.8 0.5 collective-permute-start.11
  41.3 1.6 %collective-permute-done.9 = bf16[8,1024]{1,0:T(8,128)(2,1)S(1)} collective-permute-done((bf16[8,1024]{1,0:T(8,128)(2,1)S(1)}, bf16[8,1024]{1,0:T(8,128)(2,1)S(1)}, u32[]{:S(2)}, u32[]{:S(2)}) %collective-permute-start.9) | collective-permute-done | bytes 16416 | tf_op jit(solution)/shard_map/ppermute | solution.py:16
  42.9 0.3 collective-permute-done.10
  43.2 1.3 %collective-permute-done.11 = bf16[8,1024]{1,0:T(8,128)(2,1)S(1)} collective-permute-done((bf16[8,1024]{1,0:T(8,128)(2,1)S(1)}, bf16[8,1024]{1,0:T(8,128)(2,1)S(1)}, u32[]{:S(2)}, u32[]{:S(2)}) %collective-permute-start.11) | collective-permute-done | bytes 16416 | tf_op jit(solution)/shard_map/ppermute | solution.py:16
  44.5 1.9 %collective-permute-start.12 = (bf16[4,8,1024]{2,1,0:T(8,128)(2,1)S(1)}, bf16[4,8,1024]{2,1,0:T(8,128)(2,1)S(1)}, u32[]{:S(2)}, u32[]{:S(2)}) collective-permute-start(bf16[4,8,1024]{2,1,0:T(8,128)(2,1)S(1)} %get-tuple-element.29), channel_id=1, source_target_pairs={{0,4},{4,8},{8,12},{12,0},{1,5},{5,9},{9,13},{13,1},{2,6},{6,10},{... | collective-permute-start | bytes 196616 | tf_op jit(solution)/shard_map/ppermute | solution.py:16
  46.5 0.5 collective-permute-start.13
  47.0 2.0 %collective-permute-start.14 = (bf16[4,8,1024]{2,1,0:T(8,128)(2,1)S(1)}, bf16[4,8,1024]{2,1,0:T(8,128)(2,1)S(1)}, u32[]{:S(2)}, u32[]{:S(2)}) collective-permute-start(bf16[4,8,1024]{2,1,0:T(8,128)(2,1)S(1)} %get-tuple-element.29), channel_id=1, source_target_pairs={{0,12},{4,0},{8,4},{12,8},{1,13},{5,1},{9,5},{13,9},{2,14},{6,2},{... | collective-permute-start | bytes 196616 | tf_op jit(solution)/shard_map/ppermute | solution.py:16
  49.0 0.6 %copy.12 = f32[4,16,128]{2,1,0:T(8,128)} copy(f32[4,16,128]{2,0,1:T(4,128)S(1)} %get-tuple-element.5) | data formatting | bytes 65536
  49.6 0.2 collective-permute-done.12
  49.8 0.9 %collective-permute-done.13 = bf16[4,8,1024]{2,1,0:T(8,128)(2,1)S(1)} collective-permute-done((bf16[4,8,1024]{2,1,0:T(8,128)(2,1)S(1)}, bf16[4,8,1024]{2,1,0:T(8,128)(2,1)S(1)}, u32[]{:S(2)}, u32[]{:S(2)}) %collective-permute-start.13) | collective-permute-done | bytes 65568 | tf_op jit(solution)/shard_map/ppermute | solution.py:16
  50.7 0.5 collective-permute-done.14
  51.3 0.3 convolution_convert_fusion
  51.6 1.2 %reshape.530 = bf16[1,1,1,256,4,2,128]{6,5,4,3,2,1,0:T(2,128)(2,1)} reshape(bf16[256,1024]{1,0:T(8,128)(2,1)S(1)} %convolution_convert_fusion) | data formatting | bytes 1048576 | tf_op jit(solution)/shard_map/reshape | solution.py:142
  (28 shorter events, 0.4 us)
Async XLA Ops:
  1.3 2.6 %collective-permute-start = (s32[2,256]{1,0:T(2,128)S(1)}, s32[2,256]{1,0:T(2,128)S(1)}, u32[]{:S(2)}, u32[]{:S(2)}) collective-permute-start(s32[2,256]{1,0:T(2,128)S(1)} %pad_add_fusion), channel_id=1, source_target_pairs={{0,16},{16,0},{1,17},{17,1},{2,18},{18,2},{3,19},{19,3},{4,20},{20... | collective-permute-start | bytes 6152 | tf_op jit(solution)/shard_map/ppermute | solution.py:16
  1.8 1.5 %copy-start = (bf16[1,1,1,256,4,2,128]{6,5,4,3,2,1,0:T(2,128)(2,1)S(1)}, bf16[1,1,1,256,4,2,128]{6,5,4,3,2,1,0:T(2,128)(2,1)}, u32[]{:S(2)}) copy-start(bf16[1,1,1,256,4,2,128]{6,5,4,3,2,1,0:T(2,128)(2,1)} %param.6) | copy-start | bytes 1572868
  3.7 0.7 %copy-start.2 = (s32[1,1,1,256]{3,2,1,0:T(1,128)S(1)}, s32[1,1,1,256]{3,2,1,0:T(1,128)}, u32[]{:S(2)}) copy-start(s32[1,1,1,256]{3,2,1,0:T(1,128)} %param.8) | copy-start | bytes 3076
  3.7 0.7 %copy-start.3 = (s32[1,1,1,256]{3,2,1,0:T(1,128)S(1)}, s32[1,1,1,256]{3,2,1,0:T(1,128)}, u32[]{:S(2)}) copy-start(s32[1,1,1,256]{3,2,1,0:T(1,128)} %param.7) | copy-start | bytes 3076
  3.8 2.0 %collective-permute-start.1 = (bf16[256,1024]{1,0:T(8,128)(2,1)S(1)}, bf16[256,1024]{1,0:T(8,128)(2,1)S(1)}, u32[]{:S(2)}, u32[]{:S(2)}) collective-permute-start(bf16[256,1024]{1,0:T(8,128)(2,1)S(1)} %get-tuple-element.10), channel_id=1, source_target_pairs={{0,16},{16,0},{1,17},{17,1},{2,18},{18,2},{3,19},{19,3},{4,20},{20... | collective-permute-start | bytes 1572872 | tf_op jit(solution)/shard_map/ppermute | solution.py:16
  11.1 9.8 %collective-permute-start.2 = (f32[4,102,128]{2,1,0:T(8,128)S(1)}, f32[4,102,128]{2,1,0:T(8,128)S(1)}, u32[]{:S(2)}, u32[]{:S(2)}) collective-permute-start(f32[4,102,128]{2,1,0:T(8,128)S(1)} %squeeze.38), channel_id=1, source_target_pairs={{0,4},{4,8},{8,12},{12,0},{1,5},{5,9},{9,13},{13,1},{2,6},{6,10},{... | collective-permute-start | bytes 626696 | tf_op jit(solution)/shard_map/ppermute | solution.py:16
  13.8 11.2 %collective-permute-start.3 = (f32[4,102,128]{2,1,0:T(8,128)S(1)}, f32[4,102,128]{2,1,0:T(8,128)S(1)}, u32[]{:S(2)}, u32[]{:S(2)}) collective-permute-start(f32[4,102,128]{2,1,0:T(8,128)S(1)} %squeeze.39), channel_id=1, source_target_pairs={{0,8},{4,12},{8,0},{12,4},{1,9},{5,13},{9,1},{13,5},{2,10},{6,14},... | collective-permute-start | bytes 626696 | tf_op jit(solution)/shard_map/ppermute | solution.py:16
  15.5 9.8 %collective-permute-start.4 = (f32[4,102,128]{2,1,0:T(8,128)S(1)}, f32[4,102,128]{2,1,0:T(8,128)S(1)}, u32[]{:S(2)}, u32[]{:S(2)}) collective-permute-start(f32[4,102,128]{2,1,0:T(8,128)S(1)} %squeeze.40), channel_id=1, source_target_pairs={{0,12},{4,0},{8,4},{12,8},{1,13},{5,1},{9,5},{13,9},{2,14},{6,2},{... | collective-permute-start | bytes 626696 | tf_op jit(solution)/shard_map/ppermute | solution.py:16
  25.4 6.3 %collective-permute-start.5 = (f32[102,128]{1,0:T(8,128)S(1)}, f32[102,128]{1,0:T(8,128)S(1)}, u32[]{:S(2)}, u32[]{:S(2)}) collective-permute-start(f32[102,128]{1,0:T(8,128)S(1)} %get-tuple-element.19), channel_id=1, source_target_pairs={{0,1},{1,2},{2,3},{3,0},{4,5},{5,6},{6,7},{7,4},{8,9},{9,10},{10,1... | collective-permute-start | bytes 156680 | tf_op jit(solution)/shard_map/ppermute | solution.py:16
  27.1 6.7 %collective-permute-start.6 = (f32[102,128]{1,0:T(8,128)S(1)}, f32[102,128]{1,0:T(8,128)S(1)}, u32[]{:S(2)}, u32[]{:S(2)}) collective-permute-start(f32[102,128]{1,0:T(8,128)S(1)} %get-tuple-element.21), channel_id=1, source_target_pairs={{0,2},{1,3},{2,0},{3,1},{4,6},{5,7},{6,4},{7,5},{8,10},{9,11},{10,... | collective-permute-start | bytes 156680 | tf_op jit(solution)/shard_map/ppermute | solution.py:16
  29.6 4.4 %collective-permute-start.7 = (f32[102,128]{1,0:T(8,128)S(1)}, f32[102,128]{1,0:T(8,128)S(1)}, u32[]{:S(2)}, u32[]{:S(2)}) collective-permute-start(f32[102,128]{1,0:T(8,128)S(1)} %get-tuple-element.20), channel_id=1, source_target_pairs={{0,3},{1,0},{2,1},{3,2},{4,7},{5,4},{6,5},{7,6},{8,11},{9,8},{10,9... | collective-permute-start | bytes 156680 | tf_op jit(solution)/shard_map/ppermute | solution.py:16
  34.1 1.3 %collective-permute-start.8 = (f32[102,128]{1,0:T(8,128)S(1)}, f32[102,128]{1,0:T(8,128)S(1)}, u32[]{:S(2)}, u32[]{:S(2)}) collective-permute-start(f32[102,128]{1,0:T(8,128)S(1)} %fusion.44), channel_id=1, source_target_pairs={{0,16},{16,0},{1,17},{17,1},{2,18},{18,2},{3,19},{19,3},{4,20},{20... | collective-permute-start | bytes 156680 | tf_op jit(solution)/shard_map/ppermute | solution.py:16
  35.9 1.2 %copy-start.1 = (f32[4,16,128]{2,1,0:T(8,128)S(1)}, f32[4,16,128]{2,1,0:T(8,128)}, u32[]{:S(2)}) copy-start(f32[4,16,128]{2,1,0:T(8,128)} %param.9) | copy-start | bytes 98308
  37.3 5.6 %collective-permute-start.9 = (bf16[8,1024]{1,0:T(8,128)(2,1)S(1)}, bf16[8,1024]{1,0:T(8,128)(2,1)S(1)}, u32[]{:S(2)}, u32[]{:S(2)}) collective-permute-start(bf16[8,1024]{1,0:T(8,128)(2,1)S(1)} %bitcast.48), channel_id=1, source_target_pairs={{0,1},{1,2},{2,3},{3,0},{4,5},{5,6},{6,7},{7,4},{8,9},{9,10},{10,1... | collective-permute-start | bytes 49160 | tf_op jit(solution)/shard_map/ppermute | solution.py:16
  38.3 4.9 %collective-permute-start.10 = (bf16[8,1024]{1,0:T(8,128)(2,1)S(1)}, bf16[8,1024]{1,0:T(8,128)(2,1)S(1)}, u32[]{:S(2)}, u32[]{:S(2)}) collective-permute-start(bf16[8,1024]{1,0:T(8,128)(2,1)S(1)} %bitcast.49), channel_id=1, source_target_pairs={{0,2},{1,3},{2,0},{3,1},{4,6},{5,7},{6,4},{7,5},{8,10},{9,11},{10,... | collective-permute-start | bytes 49160 | tf_op jit(solution)/shard_map/ppermute | solution.py:16
  40.8 3.7 %collective-permute-start.11 = (bf16[8,1024]{1,0:T(8,128)(2,1)S(1)}, bf16[8,1024]{1,0:T(8,128)(2,1)S(1)}, u32[]{:S(2)}, u32[]{:S(2)}) collective-permute-start(bf16[8,1024]{1,0:T(8,128)(2,1)S(1)} %bitcast.50), channel_id=1, source_target_pairs={{0,3},{1,0},{2,1},{3,2},{4,7},{5,4},{6,5},{7,6},{8,11},{9,8},{10,9... | collective-permute-start | bytes 49160 | tf_op jit(solution)/shard_map/ppermute | solution.py:16
  44.5 5.3 %collective-permute-start.12 = (bf16[4,8,1024]{2,1,0:T(8,128)(2,1)S(1)}, bf16[4,8,1024]{2,1,0:T(8,128)(2,1)S(1)}, u32[]{:S(2)}, u32[]{:S(2)}) collective-permute-start(bf16[4,8,1024]{2,1,0:T(8,128)(2,1)S(1)} %get-tuple-element.29), channel_id=1, source_target_pairs={{0,4},{4,8},{8,12},{12,0},{1,5},{5,9},{9,13},{13,1},{2,6},{6,10},{... | collective-permute-start | bytes 196616 | tf_op jit(solution)/shard_map/ppermute | solution.py:16
  46.5 4.3 %collective-permute-start.13 = (bf16[4,8,1024]{2,1,0:T(8,128)(2,1)S(1)}, bf16[4,8,1024]{2,1,0:T(8,128)(2,1)S(1)}, u32[]{:S(2)}, u32[]{:S(2)}) collective-permute-start(bf16[4,8,1024]{2,1,0:T(8,128)(2,1)S(1)} %get-tuple-element.29), channel_id=1, source_target_pairs={{0,8},{4,12},{8,0},{12,4},{1,9},{5,13},{9,1},{13,5},{2,10},{6,14},... | collective-permute-start | bytes 196616 | tf_op jit(solution)/shard_map/ppermute | solution.py:16
  47.0 4.3 %collective-permute-start.14 = (bf16[4,8,1024]{2,1,0:T(8,128)(2,1)S(1)}, bf16[4,8,1024]{2,1,0:T(8,128)(2,1)S(1)}, u32[]{:S(2)}, u32[]{:S(2)}) collective-permute-start(bf16[4,8,1024]{2,1,0:T(8,128)(2,1)S(1)} %get-tuple-element.29), channel_id=1, source_target_pairs={{0,12},{4,0},{8,4},{12,8},{1,13},{5,1},{9,5},{13,9},{2,14},{6,2},{... | collective-permute-start | bytes 196616 | tf_op jit(solution)/shard_map/ppermute | solution.py:16

commit v3 on v2

--- a/solution.py
+++ b/solution.py
@@ -73,20 +73,21 @@
         (own_row[None, :] == row_ids) | (next_row[None, :] == row_ids) | (prev_row[None, :] == row_ids)
     ).astype(jnp.bfloat16)
     table = jnp.dot(onehot, rows_in, preferred_element_type=jnp.float32)
-    table = table.reshape(size_x, size_y, ext_patches, levels, patch_rows, patch_cols)
-    left = jnp.roll(table, 1, axis=1)[..., patch_cols - h :]
-    right = jnp.roll(table, -1, axis=1)[..., :h]
-    strips = jnp.concatenate([left, right], axis=-1)
-    flat = jnp.concatenate(
-        [table.reshape(size_x, size_y, -1), strips.reshape(size_x, size_y, -1)], axis=2
-    ).reshape(size_x, size_y, -1, 128)
+    flat = table.reshape(size_x, size_y * ext_patches, cell_count)
 
     part = flat[0]
     for step in range(1, size_x):
         part = part + shifted(flat[step], "gx", size_x, step)
-    total = part[0]
+    part = part.reshape(size_y, ext_patches, levels, patch_rows, patch_cols)
+    left = jnp.roll(part, 1, axis=0)[..., patch_cols - h :]
+    right = jnp.roll(part, -1, axis=0)[..., :h]
+    strips = jnp.concatenate([left, right], axis=-1)
+    packed = jnp.concatenate(
+        [part.reshape(size_y, -1), strips.reshape(size_y, -1)], axis=1
+    ).reshape(size_y, -1, 128)
+    total = packed[0]
     for step in range(1, size_y):
-        total = total + shifted(part[step], "gy", size_y, step)
+        total = total + shifted(packed[step], "gy", size_y, step)
     other = shifted(total, "group", size_g, 1)
     is_grad = me_g == 0
     grad_flat = jnp.where(is_grad, total, other).reshape(-1)

time: 53 us -> 51.3 us (0.968)
  waiting for transfers between devices: 18.6 us -> 24.7 us
  starting transfers between devices: 20.4 us -> 15.8 us
  local copies, waits for them, and re-layouts: 8.17 us -> 6.23 us
  other arithmetic: 3.98 us -> 2.75 us
    ppermute x15, waiting for transfers between devices: 18.6 us -> 24.7 us  [shifted(): lax.ppermute(value, axis, [(s, (s + step) % count) for s in range(count)])]
    ppermute x15, starting transfers between devices: 20.4 us -> 15.8 us  [shifted(): lax.ppermute(value, axis, [(s, (s + step) % count) for s in range(count)])]
    reshape x2 -> x1, local copies, waits for them, and re-layouts: 1.77 us -> 0.28 us  [local(): strips.reshape(size_y, -1)]
    concatenate x1, other arithmetic: 1.69 us -> 0.47 us  [local(): strips = jnp.concatenate([left, right], axis=-1)]
  transfers between devices with their start and end apart: 15 -> 15, of which waited for: 14 -> 13; matrix products, arithmetic and copies ran while one was open for 6% -> 6% of each run, Pallas kernels for 0% -> 0%
where the time goes in v3:
time: 51.3 us; the launch traced here: 51.2 us
  waiting for transfers between devices  24.7 us (48%)
  starting transfers between devices  15.8 us (31%)
  local copies, waits for them, and re-layouts  6.23 us (12%)
  other arithmetic  2.75 us (5%)
  between operations  0.95 us (2%)
  matrix products  0.72 us (1%)
    ppermute x15, waiting for transfers between devices, shifted(): lax.ppermute(value, axis, [(s, (s + step) % count) for s in range(count)])  24.7 us
    ppermute x15, starting transfers between devices, shifted(): lax.ppermute(value, axis, [(s, (s + step) % count) for s in range(count)])  15.8 us
    another operation x3, local copies, waits for them, and re-layouts, local(): jnp.stack([slot_grad.reshape(slot_count, cell_count), slot_illum.reshape(...  1.86 us
    reshape x1, local copies, waits for them, and re-layouts, local(): returned.reshape((1, 1, 1, slot_count, levels, patch_rows, patch_cols))  1.16 us
    unnamed x11, local copies, waits for them, and re-layouts  1.14 us
  transfers between devices with their start and end apart: 15, of which 13 were waited for; matrix products, arithmetic and copies ran while one was open for 6% of the time, Pallas kernels for 0%

profile of v3, /device:TPU:0, one launch (start us, length us, event | category | flops | bytes accessed | tf_op | source)
XLA Modules:
  0.0 51.2 jit_solution(9506549064540626397)
XLA Ops:
  0.6 0.7 %pad_add_fusion = s32[2,256]{1,0:T(2,128)S(1)} fusion(s32[1,256]{1,0:T(1,128)} %bitcast.57, s32[1,256]{1,0:T(1,128)} %bitcast.63), kind=kLoop, calls=%fused_computation.144 | loop fusion | flops 512 | bytes 4096 | tf_op jit(solution)/shard_map/stack | solution.py:44
  1.3 0.5 collective-permute-start
  1.8 0.0 copy-start
  1.8 1.5 %stack_reshape_squeeze.6 = bf16[1,256,1024]{2,1,0:T(8,128)(2,1)S(1)} reshape(bf16[1,1,1,256,4,2,128]{6,5,4,3,2,1,0:T(2,128)(2,1)} %param.5) | data formatting | bytes 1048576 | tf_op jit(solution)/shard_map/stack;reshape;squeeze | solution.py:39
  3.3 0.0 copy-done
  3.3 0.4 stack_reshape_squeeze.7
  3.7 0.0 copy-start.2
  3.7 0.0 copy-start.3
  3.8 0.1 dynamic-slice_bitcast_fusion.1
  3.8 0.1 collective-permute-start.1
  4.0 0.0 collective-permute-done
  4.0 0.4 copy-done.2
  4.4 0.0 copy-done.3
  4.5 1.3 %collective-permute-done.1 = bf16[256,1024]{1,0:T(8,128)(2,1)S(1)} collective-permute-done((bf16[256,1024]{1,0:T(8,128)(2,1)S(1)}, bf16[256,1024]{1,0:T(8,128)(2,1)S(1)}, u32[]{:S(2)}, u32[]{:S(2)}) %collective-permute-start.1) | collective-permute-done | bytes 524320 | tf_op jit(solution)/shard_map/ppermute | solution.py:16
  5.8 0.4 fusion
  6.3 3.6 %collective-permute-start.4 = (f32[48,1024]{1,0:T(8,128)S(1)}, f32[48,1024]{1,0:T(8,128)S(1)}, u32[]{:S(2)}, u32[]{:S(2)}) collective-permute-start(f32[48,1024]{1,0:T(8,128)S(1)} %get-tuple-element.16), channel_id=1, source_target_pairs={{0,12},{4,0},{8,4},{12,8},{1,13},{5,1},{9,5},{13,9},{2,14},{6,2},{... | collective-permute-start | bytes 589832 | tf_op jit(solution)/shard_map/ppermute | solution.py:16
  9.9 0.5 collective-permute-start.3
  10.4 0.6 %collective-permute-start.2 = (f32[48,1024]{1,0:T(8,128)S(1)}, f32[48,1024]{1,0:T(8,128)S(1)}, u32[]{:S(2)}, u32[]{:S(2)}) collective-permute-start(f32[48,1024]{1,0:T(8,128)S(1)} %get-tuple-element.15), channel_id=1, source_target_pairs={{0,4},{4,8},{8,12},{12,0},{1,5},{5,9},{9,13},{13,1},{2,6},{6,10},{... | collective-permute-start | bytes 589832 | tf_op jit(solution)/shard_map/ppermute | solution.py:16
  11.0 4.2 %collective-permute-done.4 = f32[48,1024]{1,0:T(8,128)S(1)} collective-permute-done((f32[48,1024]{1,0:T(8,128)S(1)}, f32[48,1024]{1,0:T(8,128)S(1)}, u32[]{:S(2)}, u32[]{:S(2)}) %collective-permute-start.4) | collective-permute-done | bytes 196640 | tf_op jit(solution)/shard_map/ppermute | solution.py:16
  15.2 5.8 %collective-permute-done.3 = f32[48,1024]{1,0:T(8,128)S(1)} collective-permute-done((f32[48,1024]{1,0:T(8,128)S(1)}, f32[48,1024]{1,0:T(8,128)S(1)}, u32[]{:S(2)}, u32[]{:S(2)}) %collective-permute-start.3) | collective-permute-done | bytes 196640 | tf_op jit(solution)/shard_map/ppermute | solution.py:16
  21.0 0.0 collective-permute-done.2
  21.1 0.1 reshape_reshape.3
  21.3 0.1 slice.187
  21.5 0.1 slice.184
  21.6 0.5 fusion.7
  22.1 0.3 reshape.534
  22.4 0.6 %slice_reduce_fusion.3 = (f32[13056]{0:T(1024)S(1)}, f32[13056]{0:T(1024)S(1)}, f32[13056]{0:T(1024)S(1)}, f32[13056]{0:T(1024)S(1)}) fusion(f32[4,13056]{1,0:T(4,128)S(1)} %constant_dynamic-update-slice_fusion.2), kind=kLoop, calls=%fused_computation.88 | loop fusion | bytes 417792 | tf_op jit(solution)/shard_map/slice | solution.py:88
  23.0 3.7 %collective-permute-start.7 = (f32[102,128]{1,0:T(8,128)S(1)}, f32[102,128]{1,0:T(8,128)S(1)}, u32[]{:S(2)}, u32[]{:S(2)}) collective-permute-start(f32[102,128]{1,0:T(8,128)S(1)} %bitcast.53), channel_id=1, source_target_pairs={{0,3},{1,0},{2,1},{3,2},{4,7},{5,4},{6,5},{7,6},{8,11},{9,8},{10,9... | collective-permute-start | bytes 156680 | tf_op jit(solution)/shard_map/ppermute | solution.py:16
  26.6 0.0 collective-permute-start.6
  26.6 1.0 %collective-permute-start.5 = (f32[102,128]{1,0:T(8,128)S(1)}, f32[102,128]{1,0:T(8,128)S(1)}, u32[]{:S(2)}, u32[]{:S(2)}) collective-permute-start(f32[102,128]{1,0:T(8,128)S(1)} %bitcast.51), channel_id=1, source_target_pairs={{0,1},{1,2},{2,3},{3,0},{4,5},{5,6},{6,7},{7,4},{8,9},{9,10},{10,1... | collective-permute-start | bytes 156680 | tf_op jit(solution)/shard_map/ppermute | solution.py:16
  27.7 0.8 %collective-permute-done.7 = f32[102,128]{1,0:T(8,128)S(1)} collective-permute-done((f32[102,128]{1,0:T(8,128)S(1)}, f32[102,128]{1,0:T(8,128)S(1)}, u32[]{:S(2)}, u32[]{:S(2)}) %collective-permute-start.7) | collective-permute-done | bytes 52256 | tf_op jit(solution)/shard_map/ppermute | solution.py:16
  28.4 3.2 %collective-permute-done.6 = f32[102,128]{1,0:T(8,128)S(1)} collective-permute-done((f32[102,128]{1,0:T(8,128)S(1)}, f32[102,128]{1,0:T(8,128)S(1)}, u32[]{:S(2)}, u32[]{:S(2)}) %collective-permute-start.6) | collective-permute-done | bytes 52256 | tf_op jit(solution)/shard_map/ppermute | solution.py:16
  31.7 0.9 %collective-permute-done.5 = f32[102,128]{1,0:T(8,128)S(1)} collective-permute-done((f32[102,128]{1,0:T(8,128)S(1)}, f32[102,128]{1,0:T(8,128)S(1)}, u32[]{:S(2)}, u32[]{:S(2)}) %collective-permute-start.5) | collective-permute-done | bytes 52256 | tf_op jit(solution)/shard_map/ppermute | solution.py:16
  32.6 0.1 collective-permute-start.8
  32.7 0.1 broadcast_and_fusion
  32.7 0.1 slice.255
  32.8 1.1 %collective-permute-done.8 = f32[102,128]{1,0:T(8,128)S(1)} collective-permute-done((f32[102,128]{1,0:T(8,128)S(1)}, f32[102,128]{1,0:T(8,128)S(1)}, u32[]{:S(2)}, u32[]{:S(2)}) %collective-permute-start.8) | collective-permute-done | bytes 52256 | tf_op jit(solution)/shard_map/ppermute | solution.py:16
  33.9 0.1 reshape.535
  34.1 0.1 reshape.537
  34.2 0.2 fusion.84
  34.4 0.0 copy-start.1
  34.4 0.4 fusion.42
  34.9 0.2 fusion.19
  35.1 0.2 fusion.28
  35.2 0.2 fusion.37
  35.4 0.2 fusion.40
  35.6 0.0 copy-done.1
  35.6 0.2 fusion.79
  35.8 1.1 %collective-permute-start.11 = (bf16[8,1024]{1,0:T(8,128)(2,1)S(1)}, bf16[8,1024]{1,0:T(8,128)(2,1)S(1)}, u32[]{:S(2)}, u32[]{:S(2)}) collective-permute-start(bf16[8,1024]{1,0:T(8,128)(2,1)S(1)} %bitcast.43), channel_id=1, source_target_pairs={{0,3},{1,0},{2,1},{3,2},{4,7},{5,4},{6,5},{7,6},{8,11},{9,8},{10,9... | collective-permute-start | bytes 49160 | tf_op jit(solution)/shard_map/ppermute | solution.py:16
  36.9 0.1 collective-permute-start.10
  37.1 1.9 %collective-permute-start.9 = (bf16[8,1024]{1,0:T(8,128)(2,1)S(1)}, bf16[8,1024]{1,0:T(8,128)(2,1)S(1)}, u32[]{:S(2)}, u32[]{:S(2)}) collective-permute-start(bf16[8,1024]{1,0:T(8,128)(2,1)S(1)} %bitcast.45), channel_id=1, source_target_pairs={{0,1},{1,2},{2,3},{3,0},{4,5},{5,6},{6,7},{7,4},{8,9},{9,10},{10,1... | collective-permute-start | bytes 49160 | tf_op jit(solution)/shard_map/ppermute | solution.py:16
  39.0 0.6 %collective-permute-done.11 = bf16[8,1024]{1,0:T(8,128)(2,1)S(1)} collective-permute-done((bf16[8,1024]{1,0:T(8,128)(2,1)S(1)}, bf16[8,1024]{1,0:T(8,128)(2,1)S(1)}, u32[]{:S(2)}, u32[]{:S(2)}) %collective-permute-start.11) | collective-permute-done | bytes 16416 | tf_op jit(solution)/shard_map/ppermute | solution.py:16
  39.6 2.1 %collective-permute-done.10 = bf16[8,1024]{1,0:T(8,128)(2,1)S(1)} collective-permute-done((bf16[8,1024]{1,0:T(8,128)(2,1)S(1)}, bf16[8,1024]{1,0:T(8,128)(2,1)S(1)}, u32[]{:S(2)}, u32[]{:S(2)}) %collective-permute-start.10) | collective-permute-done | bytes 16416 | tf_op jit(solution)/shard_map/ppermute | solution.py:16
  41.7 0.9 %collective-permute-done.9 = bf16[8,1024]{1,0:T(8,128)(2,1)S(1)} collective-permute-done((bf16[8,1024]{1,0:T(8,128)(2,1)S(1)}, bf16[8,1024]{1,0:T(8,128)(2,1)S(1)}, u32[]{:S(2)}, u32[]{:S(2)}) %collective-permute-start.9) | collective-permute-done | bytes 16416 | tf_op jit(solution)/shard_map/ppermute | solution.py:16
  42.6 0.6 %collective-permute-start.14 = (bf16[4,8,1024]{2,1,0:T(8,128)(2,1)S(1)}, bf16[4,8,1024]{2,1,0:T(8,128)(2,1)S(1)}, u32[]{:S(2)}, u32[]{:S(2)}) collective-permute-start(bf16[4,8,1024]{2,1,0:T(8,128)(2,1)S(1)} %get-tuple-element.29), channel_id=1, source_target_pairs={{0,12},{4,0},{8,4},{12,8},{1,13},{5,1},{9,5},{13,9},{2,14},{6,2},{... | collective-permute-start | bytes 196616 | tf_op jit(solution)/shard_map/ppermute | solution.py:16
  43.2 1.2 %collective-permute-start.13 = (bf16[4,8,1024]{2,1,0:T(8,128)(2,1)S(1)}, bf16[4,8,1024]{2,1,0:T(8,128)(2,1)S(1)}, u32[]{:S(2)}, u32[]{:S(2)}) collective-permute-start(bf16[4,8,1024]{2,1,0:T(8,128)(2,1)S(1)} %get-tuple-element.29), channel_id=1, source_target_pairs={{0,8},{4,12},{8,0},{12,4},{1,9},{5,13},{9,1},{13,5},{2,10},{6,14},... | collective-permute-start | bytes 196616 | tf_op jit(solution)/shard_map/ppermute | solution.py:16
  44.5 0.7 %collective-permute-start.12 = (bf16[4,8,1024]{2,1,0:T(8,128)(2,1)S(1)}, bf16[4,8,1024]{2,1,0:T(8,128)(2,1)S(1)}, u32[]{:S(2)}, u32[]{:S(2)}) collective-permute-start(bf16[4,8,1024]{2,1,0:T(8,128)(2,1)S(1)} %get-tuple-element.29), channel_id=1, source_target_pairs={{0,4},{4,8},{8,12},{12,0},{1,5},{5,9},{9,13},{13,1},{2,6},{6,10},{... | collective-permute-start | bytes 196616 | tf_op jit(solution)/shard_map/ppermute | solution.py:16
  45.2 0.6 %copy.12 = f32[4,16,128]{2,1,0:T(8,128)} copy(f32[4,16,128]{2,0,1:T(4,128)S(1)} %get-tuple-element.9) | data formatting | bytes 65536
  45.9 1.1 %collective-permute-done.14 = bf16[4,8,1024]{2,1,0:T(8,128)(2,1)S(1)} collective-permute-done((bf16[4,8,1024]{2,1,0:T(8,128)(2,1)S(1)}, bf16[4,8,1024]{2,1,0:T(8,128)(2,1)S(1)}, u32[]{:S(2)}, u32[]{:S(2)}) %collective-permute-start.14) | collective-permute-done | bytes 65568 | tf_op jit(solution)/shard_map/ppermute | solution.py:16
  46.9 0.9 %collective-permute-done.13 = bf16[4,8,1024]{2,1,0:T(8,128)(2,1)S(1)} collective-permute-done((bf16[4,8,1024]{2,1,0:T(8,128)(2,1)S(1)}, bf16[4,8,1024]{2,1,0:T(8,128)(2,1)S(1)}, u32[]{:S(2)}, u32[]{:S(2)}) %collective-permute-start.13) | collective-permute-done | bytes 65568 | tf_op jit(solution)/shard_map/ppermute | solution.py:16
  47.8 1.8 %collective-permute-done.12 = bf16[4,8,1024]{2,1,0:T(8,128)(2,1)S(1)} collective-permute-done((bf16[4,8,1024]{2,1,0:T(8,128)(2,1)S(1)}, bf16[4,8,1024]{2,1,0:T(8,128)(2,1)S(1)}, u32[]{:S(2)}, u32[]{:S(2)}) %collective-permute-start.12) | collective-permute-done | bytes 65568 | tf_op jit(solution)/shard_map/ppermute | solution.py:16
  49.7 0.3 convolution_convert_fusion
  50.0 1.2 %reshape.540 = bf16[1,1,1,256,4,2,128]{6,5,4,3,2,1,0:T(2,128)(2,1)} reshape(bf16[256,1024]{1,0:T(8,128)(2,1)S(1)} %convolution_convert_fusion) | data formatting | bytes 1048576 | tf_op jit(solution)/shard_map/reshape | solution.py:143
  (28 shorter events, 0.6 us)
Async XLA Ops:
  1.3 2.6 %collective-permute-start = (s32[2,256]{1,0:T(2,128)S(1)}, s32[2,256]{1,0:T(2,128)S(1)}, u32[]{:S(2)}, u32[]{:S(2)}) collective-permute-start(s32[2,256]{1,0:T(2,128)S(1)} %pad_add_fusion), channel_id=1, source_target_pairs={{0,16},{16,0},{1,17},{17,1},{2,18},{18,2},{3,19},{19,3},{4,20},{20... | collective-permute-start | bytes 6152 | tf_op jit(solution)/shard_map/ppermute | solution.py:16
  1.8 1.5 %copy-start = (bf16[1,1,1,256,4,2,128]{6,5,4,3,2,1,0:T(2,128)(2,1)S(1)}, bf16[1,1,1,256,4,2,128]{6,5,4,3,2,1,0:T(2,128)(2,1)}, u32[]{:S(2)}) copy-start(bf16[1,1,1,256,4,2,128]{6,5,4,3,2,1,0:T(2,128)(2,1)} %param.6) | copy-start | bytes 1572868
  3.7 0.7 %copy-start.2 = (s32[1,1,1,256]{3,2,1,0:T(1,128)S(1)}, s32[1,1,1,256]{3,2,1,0:T(1,128)}, u32[]{:S(2)}) copy-start(s32[1,1,1,256]{3,2,1,0:T(1,128)} %param.8) | copy-start | bytes 3076
  3.7 0.7 %copy-start.3 = (s32[1,1,1,256]{3,2,1,0:T(1,128)S(1)}, s32[1,1,1,256]{3,2,1,0:T(1,128)}, u32[]{:S(2)}) copy-start(s32[1,1,1,256]{3,2,1,0:T(1,128)} %param.7) | copy-start | bytes 3076
  3.8 2.0 %collective-permute-start.1 = (bf16[256,1024]{1,0:T(8,128)(2,1)S(1)}, bf16[256,1024]{1,0:T(8,128)(2,1)S(1)}, u32[]{:S(2)}, u32[]{:S(2)}) collective-permute-start(bf16[256,1024]{1,0:T(8,128)(2,1)S(1)} %get-tuple-element.14), channel_id=1, source_target_pairs={{0,16},{16,0},{1,17},{17,1},{2,18},{18,2},{3,19},{19,3},{4,20},{20... | collective-permute-start | bytes 1572872 | tf_op jit(solution)/shard_map/ppermute | solution.py:16
  6.3 8.9 %collective-permute-start.4 = (f32[48,1024]{1,0:T(8,128)S(1)}, f32[48,1024]{1,0:T(8,128)S(1)}, u32[]{:S(2)}, u32[]{:S(2)}) collective-permute-start(f32[48,1024]{1,0:T(8,128)S(1)} %get-tuple-element.16), channel_id=1, source_target_pairs={{0,12},{4,0},{8,4},{12,8},{1,13},{5,1},{9,5},{13,9},{2,14},{6,2},{... | collective-permute-start | bytes 589832 | tf_op jit(solution)/shard_map/ppermute | solution.py:16
  9.9 11.1 %collective-permute-start.3 = (f32[48,1024]{1,0:T(8,128)S(1)}, f32[48,1024]{1,0:T(8,128)S(1)}, u32[]{:S(2)}, u32[]{:S(2)}) collective-permute-start(f32[48,1024]{1,0:T(8,128)S(1)} %get-tuple-element.17), channel_id=1, source_target_pairs={{0,8},{4,12},{8,0},{12,4},{1,9},{5,13},{9,1},{13,5},{2,10},{6,14},... | collective-permute-start | bytes 589832 | tf_op jit(solution)/shard_map/ppermute | solution.py:16
  10.4 10.6 %collective-permute-start.2 = (f32[48,1024]{1,0:T(8,128)S(1)}, f32[48,1024]{1,0:T(8,128)S(1)}, u32[]{:S(2)}, u32[]{:S(2)}) collective-permute-start(f32[48,1024]{1,0:T(8,128)S(1)} %get-tuple-element.15), channel_id=1, source_target_pairs={{0,4},{4,8},{8,12},{12,0},{1,5},{5,9},{9,13},{13,1},{2,6},{6,10},{... | collective-permute-start | bytes 589832 | tf_op jit(solution)/shard_map/ppermute | solution.py:16
  23.0 5.4 %collective-permute-start.7 = (f32[102,128]{1,0:T(8,128)S(1)}, f32[102,128]{1,0:T(8,128)S(1)}, u32[]{:S(2)}, u32[]{:S(2)}) collective-permute-start(f32[102,128]{1,0:T(8,128)S(1)} %bitcast.53), channel_id=1, source_target_pairs={{0,3},{1,0},{2,1},{3,2},{4,7},{5,4},{6,5},{7,6},{8,11},{9,8},{10,9... | collective-permute-start | bytes 156680 | tf_op jit(solution)/shard_map/ppermute | solution.py:16
  26.6 5.0 %collective-permute-start.6 = (f32[102,128]{1,0:T(8,128)S(1)}, f32[102,128]{1,0:T(8,128)S(1)}, u32[]{:S(2)}, u32[]{:S(2)}) collective-permute-start(f32[102,128]{1,0:T(8,128)S(1)} %bitcast.52), channel_id=1, source_target_pairs={{0,2},{1,3},{2,0},{3,1},{4,6},{5,7},{6,4},{7,5},{8,10},{9,11},{10,... | collective-permute-start | bytes 156680 | tf_op jit(solution)/shard_map/ppermute | solution.py:16
  26.6 5.9 %collective-permute-start.5 = (f32[102,128]{1,0:T(8,128)S(1)}, f32[102,128]{1,0:T(8,128)S(1)}, u32[]{:S(2)}, u32[]{:S(2)}) collective-permute-start(f32[102,128]{1,0:T(8,128)S(1)} %bitcast.51), channel_id=1, source_target_pairs={{0,1},{1,2},{2,3},{3,0},{4,5},{5,6},{6,7},{7,4},{8,9},{9,10},{10,1... | collective-permute-start | bytes 156680 | tf_op jit(solution)/shard_map/ppermute | solution.py:16
  32.6 1.3 %collective-permute-start.8 = (f32[102,128]{1,0:T(8,128)S(1)}, f32[102,128]{1,0:T(8,128)S(1)}, u32[]{:S(2)}, u32[]{:S(2)}) collective-permute-start(f32[102,128]{1,0:T(8,128)S(1)} %fusion.45), channel_id=1, source_target_pairs={{0,16},{16,0},{1,17},{17,1},{2,18},{18,2},{3,19},{19,3},{4,20},{20... | collective-permute-start | bytes 156680 | tf_op jit(solution)/shard_map/ppermute | solution.py:16
  34.4 1.2 %copy-start.1 = (f32[4,16,128]{2,1,0:T(8,128)S(1)}, f32[4,16,128]{2,1,0:T(8,128)}, u32[]{:S(2)}) copy-start(f32[4,16,128]{2,1,0:T(8,128)} %param.9) | copy-start | bytes 98308
  35.8 3.8 %collective-permute-start.11 = (bf16[8,1024]{1,0:T(8,128)(2,1)S(1)}, bf16[8,1024]{1,0:T(8,128)(2,1)S(1)}, u32[]{:S(2)}, u32[]{:S(2)}) collective-permute-start(bf16[8,1024]{1,0:T(8,128)(2,1)S(1)} %bitcast.43), channel_id=1, source_target_pairs={{0,3},{1,0},{2,1},{3,2},{4,7},{5,4},{6,5},{7,6},{8,11},{9,8},{10,9... | collective-permute-start | bytes 49160 | tf_op jit(solution)/shard_map/ppermute | solution.py:16
  36.9 4.7 %collective-permute-start.10 = (bf16[8,1024]{1,0:T(8,128)(2,1)S(1)}, bf16[8,1024]{1,0:T(8,128)(2,1)S(1)}, u32[]{:S(2)}, u32[]{:S(2)}) collective-permute-start(bf16[8,1024]{1,0:T(8,128)(2,1)S(1)} %bitcast.44), channel_id=1, source_target_pairs={{0,2},{1,3},{2,0},{3,1},{4,6},{5,7},{6,4},{7,5},{8,10},{9,11},{10,... | collective-permute-start | bytes 49160 | tf_op jit(solution)/shard_map/ppermute | solution.py:16
  37.1 5.5 %collective-permute-start.9 = (bf16[8,1024]{1,0:T(8,128)(2,1)S(1)}, bf16[8,1024]{1,0:T(8,128)(2,1)S(1)}, u32[]{:S(2)}, u32[]{:S(2)}) collective-permute-start(bf16[8,1024]{1,0:T(8,128)(2,1)S(1)} %bitcast.45), channel_id=1, source_target_pairs={{0,1},{1,2},{2,3},{3,0},{4,5},{5,6},{6,7},{7,4},{8,9},{9,10},{10,1... | collective-permute-start | bytes 49160 | tf_op jit(solution)/shard_map/ppermute | solution.py:16
  42.6 4.3 %collective-permute-start.14 = (bf16[4,8,1024]{2,1,0:T(8,128)(2,1)S(1)}, bf16[4,8,1024]{2,1,0:T(8,128)(2,1)S(1)}, u32[]{:S(2)}, u32[]{:S(2)}) collective-permute-start(bf16[4,8,1024]{2,1,0:T(8,128)(2,1)S(1)} %get-tuple-element.29), channel_id=1, source_target_pairs={{0,12},{4,0},{8,4},{12,8},{1,13},{5,1},{9,5},{13,9},{2,14},{6,2},{... | collective-permute-start | bytes 196616 | tf_op jit(solution)/shard_map/ppermute | solution.py:16
  43.2 4.6 %collective-permute-start.13 = (bf16[4,8,1024]{2,1,0:T(8,128)(2,1)S(1)}, bf16[4,8,1024]{2,1,0:T(8,128)(2,1)S(1)}, u32[]{:S(2)}, u32[]{:S(2)}) collective-permute-start(bf16[4,8,1024]{2,1,0:T(8,128)(2,1)S(1)} %get-tuple-element.29), channel_id=1, source_target_pairs={{0,8},{4,12},{8,0},{12,4},{1,9},{5,13},{9,1},{13,5},{2,10},{6,14},... | collective-permute-start | bytes 196616 | tf_op jit(solution)/shard_map/ppermute | solution.py:16
  44.5 5.2 %collective-permute-start.12 = (bf16[4,8,1024]{2,1,0:T(8,128)(2,1)S(1)}, bf16[4,8,1024]{2,1,0:T(8,128)(2,1)S(1)}, u32[]{:S(2)}, u32[]{:S(2)}) collective-permute-start(bf16[4,8,1024]{2,1,0:T(8,128)(2,1)S(1)} %get-tuple-element.29), channel_id=1, source_target_pairs={{0,4},{4,8},{8,12},{12,0},{1,5},{5,9},{9,13},{13,1},{2,6},{6,10},{... | collective-permute-start | bytes 196616 | tf_op jit(solution)/shard_map/ppermute | solution.py:16

commit v4 on v3

--- a/solution.py
+++ b/solution.py
@@ -36,11 +36,9 @@
     ext_cols = tile_cols + 2 * h
 
     me_g = lax.axis_index("group")
-    quantities = jnp.stack(
-        [slot_grad.reshape(slot_count, cell_count), slot_illum.reshape(slot_count, cell_count)]
-    )
-    kept = lax.dynamic_index_in_dim(quantities, me_g, 0, keepdims=False)
-    given = lax.dynamic_index_in_dim(quantities, 1 - me_g, 0, keepdims=False)
+    is_grad = me_g == 0
+    kept = jnp.where(is_grad, slot_grad, slot_illum)
+    given = jnp.where(is_grad, slot_illum, slot_grad)
     places = jnp.stack([owners, patches])
     taken = shifted(given, "group", size_g, 1)
     taken_places = shifted(places, "group", size_g, 1)
@@ -72,8 +70,8 @@
     onehot = (
         (own_row[None, :] == row_ids) | (next_row[None, :] == row_ids) | (prev_row[None, :] == row_ids)
     ).astype(jnp.bfloat16)
-    table = jnp.dot(onehot, rows_in, preferred_element_type=jnp.float32)
-    flat = table.reshape(size_x, size_y * ext_patches, cell_count)
+    table = jnp.einsum("rw,wlpc->rlpc", onehot, rows_in, preferred_element_type=jnp.float32)
+    flat = table.reshape(size_x, size_y * ext_patches, levels, patch_rows, patch_cols)
 
     part = flat[0]
     for step in range(1, size_x):
@@ -89,7 +87,6 @@
     for step in range(1, size_y):
         total = total + shifted(packed[step], "gy", size_y, step)
     other = shifted(total, "group", size_g, 1)
-    is_grad = me_g == 0
     grad_flat = jnp.where(is_grad, total, other).reshape(-1)
     illum_flat = jnp.where(is_grad, other, total).reshape(-1)
 
@@ -121,7 +118,6 @@
     tile_table = (
         updated_model.reshape(levels, per_tile, patch_rows, tile_cols)
         .transpose(1, 0, 2, 3)
-        .reshape(per_tile, cell_count)
         .astype(jnp.bfloat16)
     )
     along_y = jnp.stack(
@@ -130,7 +126,7 @@
     along_x = jnp.stack(
         [along_y] + [shifted(along_y, "gx", size_x, step) for step in range(1, size_x)]
     )
-    whole = along_x.reshape(tiles * per_tile, cell_count)
+    whole = along_x.reshape(tiles * per_tile, levels, patch_rows, patch_cols)
     owner_x = owners // size_y
     owner_y = owners % size_y
     back_row = (
@@ -139,7 +135,9 @@
     pick = (back_row[:, None] == jnp.arange(tiles * per_tile, dtype=jnp.int32)[None, :]).astype(
         jnp.bfloat16
     )
-    returned = jnp.dot(pick, whole, preferred_element_type=jnp.float32).astype(jnp.bfloat16)
+    returned = jnp.einsum("wr,rlpc->wlpc", pick, whole, preferred_element_type=jnp.float32).astype(
+        jnp.bfloat16
+    )
     returned_windows = returned.reshape((1, 1, 1, slot_count, levels, patch_rows, patch_cols))
     return (updated_model, returned_windows)
 

time: 51.3 us -> 48.7 us (0.949)
  waiting for transfers between devices: 24.7 us -> 18.5 us
  starting transfers between devices: 15.8 us -> 20.3 us
  local copies, waits for them, and re-layouts: 6.23 us -> 3.97 us
  other arithmetic: 2.75 us -> 4.15 us
    ppermute x15, waiting for transfers between devices: 24.7 us -> 18.5 us  [shifted(): lax.ppermute(value, axis, [(s, (s + step) % count) for s in range(count)])]
    ppermute x15, starting transfers between devices: 15.8 us -> 20.3 us  [shifted(): lax.ppermute(value, axis, [(s, (s + step) % count) for s in range(count)])]
    another operation x3 -> x0, local copies, waits for them, and re-layouts: 1.86 us -> none  [local(): jnp.stack([slot_grad.reshape(slot_count, cell_count), slot_illum.reshape(...]
    select_n x0 -> x1, other arithmetic: none -> 1.39 us  [local(): kept = jnp.where(is_grad, slot_grad, slot_illum)]
    reshape x1 -> x0, local copies, waits for them, and re-layouts: 1.16 us -> none  [local(): returned.reshape((1, 1, 1, slot_count, levels, patch_rows, patch_cols))]
    unnamed x11 -> x9, local copies, waits for them, and re-layouts: 1.14 us -> 1.98 us
  transfers between devices with their start and end apart: 15 -> 15, of which waited for: 13 -> 14; matrix products, arithmetic and copies ran while one was open for 6% -> 5% of each run, Pallas kernels for 0% -> 0%
where the time goes in v4:
time: 48.7 us; the launch traced here: 48.6 us
  starting transfers between devices  20.3 us (42%)
  waiting for transfers between devices  18.5 us (38%)
  other arithmetic  4.15 us (9%)
  local copies, waits for them, and re-layouts  3.97 us (8%)
  between operations  0.92 us (2%)
  matrix products  0.71 us (1%)
    ppermute x15, starting transfers between devices, shifted(): lax.ppermute(value, axis, [(s, (s + step) % count) for s in range(count)])  20.3 us
    ppermute x15, waiting for transfers between devices, shifted(): lax.ppermute(value, axis, [(s, (s + step) % count) for s in range(count)])  18.5 us
    unnamed x9, local copies, waits for them, and re-layouts  1.98 us
    select_n x1, other arithmetic, local(): kept = jnp.where(is_grad, slot_grad, slot_illum)  1.39 us
  transfers between devices with their start and end apart: 15, of which 14 were waited for; matrix products, arithmetic and copies ran while one was open for 5% of the time, Pallas kernels for 0%

profile of v4, /device:TPU:0, one launch (start us, length us, event | category | flops | bytes accessed | tf_op | source)
XLA Modules:
  0.0 48.6 jit_solution(638913459612322076)
XLA Ops:
  0.6 0.7 %pad_add_fusion = s32[2,256]{1,0:T(2,128)S(1)} fusion(s32[1,256]{1,0:T(1,128)} %bitcast.91, s32[1,256]{1,0:T(1,128)} %bitcast.97), kind=kLoop, calls=%fused_computation.149 | loop fusion | flops 512 | bytes 4096 | tf_op jit(solution)/shard_map/stack | solution.py:42
  1.3 0.5 collective-permute-start
  1.8 0.0 copy-start.1
  1.8 0.0 copy-start.2
  1.8 1.4 %select_bitcast_fusion.1 = (bf16[256,4,2,128]{3,0,2,1:T(8,128)(2,1)S(1)}, bf16[256,4,2,128]{3,0,2,1:T(8,128)(2,1)S(1)}) fusion(pred[]{:T(512)S(6)} %eq.65, bf16[1,1,1,256,4,2,128]{6,5,4,3,2,1,0:T(2,128)(2,1)} %param.6, bf16[1,1,1,256,4,2,128]{6,5,4,3,2,1,0:T(2,128)(2,1)} %param.5), kind=kLoop, calls=%fused_computation.7 | loop fusion | flops 524288 | bytes 2097153 | tf_op jit(solution)/shard_map/jit(_where)/select_n | solution.py:40
  3.2 0.1 collective-permute-start.1
  3.3 0.0 collective-permute-done
  3.3 0.0 copy-done.1
  3.3 0.0 copy-done.2
  3.4 1.8 %collective-permute-done.1 = bf16[256,4,2,128]{3,0,2,1:T(8,128)(2,1)S(1)} collective-permute-done((bf16[256,4,2,128]{3,0,2,1:T(8,128)(2,1)S(1)}, bf16[256,4,2,128]{3,0,2,1:T(8,128)(2,1)S(1)}, u32[]{:S(2)}, u32[]{:S(2)}) %collective-permute-start.1) | collective-permute-done | bytes 524320 | tf_op jit(solution)/shard_map/ppermute | solution.py:16
  5.2 0.4 fusion.1
  5.6 2.7 %collective-permute-start.2 = (f32[48,4,2,128]{3,0,2,1:T(8,128)S(1)}, f32[48,4,2,128]{3,0,2,1:T(8,128)S(1)}, u32[]{:S(2)}, u32[]{:S(2)}) collective-permute-start(f32[48,4,2,128]{3,0,2,1:T(8,128)S(1)} %get-tuple-element.19), channel_id=1, source_target_pairs={{0,4},{4,8},{8,12},{12,0},{1,5},{5,9},{9,13},{13,1},{2,6},{6,10},{... | collective-permute-start | bytes 589832 | tf_op jit(solution)/shard_map/ppermute | solution.py:16
  8.3 1.5 %collective-permute-start.3 = (f32[48,4,2,128]{3,0,2,1:T(8,128)S(1)}, f32[48,4,2,128]{3,0,2,1:T(8,128)S(1)}, u32[]{:S(2)}, u32[]{:S(2)}) collective-permute-start(f32[48,4,2,128]{3,0,2,1:T(8,128)S(1)} %get-tuple-element.21), channel_id=1, source_target_pairs={{0,8},{4,12},{8,0},{12,4},{1,9},{5,13},{9,1},{13,5},{2,10},{6,14},... | collective-permute-start | bytes 589832 | tf_op jit(solution)/shard_map/ppermute | solution.py:16
  9.8 1.4 %collective-permute-start.4 = (f32[48,4,2,128]{3,0,2,1:T(8,128)S(1)}, f32[48,4,2,128]{3,0,2,1:T(8,128)S(1)}, u32[]{:S(2)}, u32[]{:S(2)}) collective-permute-start(f32[48,4,2,128]{3,0,2,1:T(8,128)S(1)} %get-tuple-element.20), channel_id=1, source_target_pairs={{0,12},{4,0},{8,4},{12,8},{1,13},{5,1},{9,5},{13,9},{2,14},{6,2},{... | collective-permute-start | bytes 589832 | tf_op jit(solution)/shard_map/ppermute | solution.py:16
  11.2 3.8 %collective-permute-done.2 = f32[48,4,2,128]{3,0,2,1:T(8,128)S(1)} collective-permute-done((f32[48,4,2,128]{3,0,2,1:T(8,128)S(1)}, f32[48,4,2,128]{3,0,2,1:T(8,128)S(1)}, u32[]{:S(2)}, u32[]{:S(2)}) %collective-permute-start.2) | collective-permute-done | bytes 196640 | tf_op jit(solution)/shard_map/ppermute | solution.py:16
  15.0 3.9 %collective-permute-done.3 = f32[48,4,2,128]{3,0,2,1:T(8,128)S(1)} collective-permute-done((f32[48,4,2,128]{3,0,2,1:T(8,128)S(1)}, f32[48,4,2,128]{3,0,2,1:T(8,128)S(1)}, u32[]{:S(2)}, u32[]{:S(2)}) %collective-permute-start.3) | collective-permute-done | bytes 196640 | tf_op jit(solution)/shard_map/ppermute | solution.py:16
  18.9 0.3 collective-permute-done.4
  19.3 0.1 copy.42
  19.4 0.1 copy.43
  19.5 0.1 copy.45
  19.6 0.5 fusion.9
  20.1 0.3 reshape.524
  20.4 0.2 reshape_reshape.3
  20.6 0.6 %slice_reduce_fusion.3 = (f32[13056]{0:T(1024)S(1)}, f32[13056]{0:T(1024)S(1)}, f32[13056]{0:T(1024)S(1)}, f32[13056]{0:T(1024)S(1)}) fusion(f32[4,13056]{1,0:T(4,128)S(1)} %constant_dynamic-update-slice_fusion), kind=kLoop, calls=%fused_computation.93 | loop fusion | bytes 417792 | tf_op jit(solution)/shard_map/slice | solution.py:86
  21.2 1.6 %collective-permute-start.5 = (f32[102,128]{1,0:T(8,128)S(1)}, f32[102,128]{1,0:T(8,128)S(1)}, u32[]{:S(2)}, u32[]{:S(2)}) collective-permute-start(f32[102,128]{1,0:T(8,128)S(1)} %bitcast.87), channel_id=1, source_target_pairs={{0,1},{1,2},{2,3},{3,0},{4,5},{5,6},{6,7},{7,4},{8,9},{9,10},{10,1... | collective-permute-start | bytes 156680 | tf_op jit(solution)/shard_map/ppermute | solution.py:16
  22.8 2.6 %collective-permute-start.6 = (f32[102,128]{1,0:T(8,128)S(1)}, f32[102,128]{1,0:T(8,128)S(1)}, u32[]{:S(2)}, u32[]{:S(2)}) collective-permute-start(f32[102,128]{1,0:T(8,128)S(1)} %bitcast.86), channel_id=1, source_target_pairs={{0,2},{1,3},{2,0},{3,1},{4,6},{5,7},{6,4},{7,5},{8,10},{9,11},{10,... | collective-permute-start | bytes 156680 | tf_op jit(solution)/shard_map/ppermute | solution.py:16
  25.4 1.3 %collective-permute-start.7 = (f32[102,128]{1,0:T(8,128)S(1)}, f32[102,128]{1,0:T(8,128)S(1)}, u32[]{:S(2)}, u32[]{:S(2)}) collective-permute-start(f32[102,128]{1,0:T(8,128)S(1)} %bitcast.85), channel_id=1, source_target_pairs={{0,3},{1,0},{2,1},{3,2},{4,7},{5,4},{6,5},{7,6},{8,11},{9,8},{10,9... | collective-permute-start | bytes 156680 | tf_op jit(solution)/shard_map/ppermute | solution.py:16
  26.8 0.7 %collective-permute-done.5 = f32[102,128]{1,0:T(8,128)S(1)} collective-permute-done((f32[102,128]{1,0:T(8,128)S(1)}, f32[102,128]{1,0:T(8,128)S(1)}, u32[]{:S(2)}, u32[]{:S(2)}) %collective-permute-start.5) | collective-permute-done | bytes 52256 | tf_op jit(solution)/shard_map/ppermute | solution.py:16
  27.4 2.1 %collective-permute-done.6 = f32[102,128]{1,0:T(8,128)S(1)} collective-permute-done((f32[102,128]{1,0:T(8,128)S(1)}, f32[102,128]{1,0:T(8,128)S(1)}, u32[]{:S(2)}, u32[]{:S(2)}) %collective-permute-start.6) | collective-permute-done | bytes 52256 | tf_op jit(solution)/shard_map/ppermute | solution.py:16
  29.5 0.3 collective-permute-done.7
  29.8 0.1 collective-permute-start.8
  29.9 0.1 broadcast_and_fusion
  30.0 0.1 slice.255
  30.0 1.1 %collective-permute-done.8 = f32[102,128]{1,0:T(8,128)S(1)} collective-permute-done((f32[102,128]{1,0:T(8,128)S(1)}, f32[102,128]{1,0:T(8,128)S(1)}, u32[]{:S(2)}, u32[]{:S(2)}) %collective-permute-start.8) | collective-permute-done | bytes 52256 | tf_op jit(solution)/shard_map/ppermute | solution.py:16
  31.2 0.1 reshape.525
  31.3 0.1 reshape.527
  31.4 0.2 fusion.87
  31.6 0.4 fusion.46
  32.0 0.0 copy-start
  32.1 0.2 fusion.23
  32.3 0.2 fusion.32
  32.5 0.2 fusion.41
  32.7 0.2 fusion.44
  32.8 0.0 copy-done
  32.9 0.2 fusion.83
  33.0 1.0 %collective-permute-start.9 = (bf16[8,4,2,128]{3,0,2,1:T(8,128)(2,1)S(1)}, bf16[8,4,2,128]{3,0,2,1:T(8,128)(2,1)S(1)}, u32[]{:S(2)}, u32[]{:S(2)}) collective-permute-start(bf16[8,4,2,128]{3,0,2,1:T(8,128)(2,1)S(1)} %bitcast.77), channel_id=1, source_target_pairs={{0,1},{1,2},{2,3},{3,0},{4,5},{5,6},{6,7},{7,4},{8,9},{9,10},{10,1... | collective-permute-start | bytes 49160 | tf_op jit(solution)/shard_map/ppermute | solution.py:16
  34.0 2.5 %collective-permute-start.10 = (bf16[8,4,2,128]{3,0,2,1:T(8,128)(2,1)S(1)}, bf16[8,4,2,128]{3,0,2,1:T(8,128)(2,1)S(1)}, u32[]{:S(2)}, u32[]{:S(2)}) collective-permute-start(bf16[8,4,2,128]{3,0,2,1:T(8,128)(2,1)S(1)} %bitcast.78), channel_id=1, source_target_pairs={{0,2},{1,3},{2,0},{3,1},{4,6},{5,7},{6,4},{7,5},{8,10},{9,11},{10,... | collective-permute-start | bytes 49160 | tf_op jit(solution)/shard_map/ppermute | solution.py:16
  36.5 0.5 %collective-permute-start.11 = (bf16[8,4,2,128]{3,0,2,1:T(8,128)(2,1)S(1)}, bf16[8,4,2,128]{3,0,2,1:T(8,128)(2,1)S(1)}, u32[]{:S(2)}, u32[]{:S(2)}) collective-permute-start(bf16[8,4,2,128]{3,0,2,1:T(8,128)(2,1)S(1)} %bitcast.79), channel_id=1, source_target_pairs={{0,3},{1,0},{2,1},{3,2},{4,7},{5,4},{6,5},{7,6},{8,11},{9,8},{10,9... | collective-permute-start | bytes 49160 | tf_op jit(solution)/shard_map/ppermute | solution.py:16
  37.0 1.6 %collective-permute-done.9 = bf16[8,4,2,128]{3,0,2,1:T(8,128)(2,1)S(1)} collective-permute-done((bf16[8,4,2,128]{3,0,2,1:T(8,128)(2,1)S(1)}, bf16[8,4,2,128]{3,0,2,1:T(8,128)(2,1)S(1)}, u32[]{:S(2)}, u32[]{:S(2)}) %collective-permute-start.9) | collective-permute-done | bytes 16416 | tf_op jit(solution)/shard_map/ppermute | solution.py:16
  38.7 0.3 collective-permute-done.10
  38.9 1.3 %collective-permute-done.11 = bf16[8,4,2,128]{3,0,2,1:T(8,128)(2,1)S(1)} collective-permute-done((bf16[8,4,2,128]{3,0,2,1:T(8,128)(2,1)S(1)}, bf16[8,4,2,128]{3,0,2,1:T(8,128)(2,1)S(1)}, u32[]{:S(2)}, u32[]{:S(2)}) %collective-permute-start.11) | collective-permute-done | bytes 16416 | tf_op jit(solution)/shard_map/ppermute | solution.py:16
  40.3 1.8 %collective-permute-start.12 = (bf16[4,8,4,2,128]{4,1,0,3,2:T(8,128)(2,1)S(1)}, bf16[4,8,4,2,128]{4,1,0,3,2:T(8,128)(2,1)S(1)}, u32[]{:S(2)}, u32[]{:S(2)}) collective-permute-start(bf16[4,8,4,2,128]{4,1,0,3,2:T(8,128)(2,1)S(1)} %get-tuple-element.33), channel_id=1, source_target_pairs={{0,4},{4,8},{8,12},{12,0},{1,5},{5,9},{9,13},{13,1},{2,6},{6,10},{... | collective-permute-start | bytes 196616 | tf_op jit(solution)/shard_map/ppermute | solution.py:16
  42.1 0.5 %collective-permute-start.13 = (bf16[4,8,4,2,128]{4,1,0,3,2:T(8,128)(2,1)S(1)}, bf16[4,8,4,2,128]{4,1,0,3,2:T(8,128)(2,1)S(1)}, u32[]{:S(2)}, u32[]{:S(2)}) collective-permute-start(bf16[4,8,4,2,128]{4,1,0,3,2:T(8,128)(2,1)S(1)} %get-tuple-element.33), channel_id=1, source_target_pairs={{0,8},{4,12},{8,0},{12,4},{1,9},{5,13},{9,1},{13,5},{2,10},{6,14},... | collective-permute-start | bytes 196616 | tf_op jit(solution)/shard_map/ppermute | solution.py:16
  42.6 2.1 %collective-permute-start.14 = (bf16[4,8,4,2,128]{4,1,0,3,2:T(8,128)(2,1)S(1)}, bf16[4,8,4,2,128]{4,1,0,3,2:T(8,128)(2,1)S(1)}, u32[]{:S(2)}, u32[]{:S(2)}) collective-permute-start(bf16[4,8,4,2,128]{4,1,0,3,2:T(8,128)(2,1)S(1)} %get-tuple-element.33), channel_id=1, source_target_pairs={{0,12},{4,0},{8,4},{12,8},{1,13},{5,1},{9,5},{13,9},{2,14},{6,2},{... | collective-permute-start | bytes 196616 | tf_op jit(solution)/shard_map/ppermute | solution.py:16
  44.7 0.6 %copy.56 = f32[4,16,128]{2,1,0:T(8,128)} copy(f32[4,16,128]{2,0,1:T(4,128)S(1)} %get-tuple-element.13) | data formatting | bytes 65536
  45.3 0.2 collective-permute-done.12
  45.5 0.8 %collective-permute-done.13 = bf16[4,8,4,2,128]{4,1,0,3,2:T(8,128)(2,1)S(1)} collective-permute-done((bf16[4,8,4,2,128]{4,1,0,3,2:T(8,128)(2,1)S(1)}, bf16[4,8,4,2,128]{4,1,0,3,2:T(8,128)(2,1)S(1)}, u32[]{:S(2)}, u32[]{:S(2)}) %collective-permute-start.13) | collective-permute-done | bytes 65568 | tf_op jit(solution)/shard_map/ppermute | solution.py:16
  46.3 0.5 %collective-permute-done.14 = bf16[4,8,4,2,128]{4,1,0,3,2:T(8,128)(2,1)S(1)} collective-permute-done((bf16[4,8,4,2,128]{4,1,0,3,2:T(8,128)(2,1)S(1)}, bf16[4,8,4,2,128]{4,1,0,3,2:T(8,128)(2,1)S(1)}, u32[]{:S(2)}, u32[]{:S(2)}) %collective-permute-start.14) | collective-permute-done | bytes 65568 | tf_op jit(solution)/shard_map/ppermute | solution.py:16
  46.9 0.3 fusion
  47.2 1.3 %copy.57 = bf16[1,1,1,256,4,2,128]{6,5,4,3,2,1,0:T(2,128)(2,1)} copy(bf16[1,1,1,256,4,2,128]{6,3,5,4,2,1,0:T(8,128)(2,1)S(1)} %fusion) | data formatting | bytes 1048576
  (25 shorter events, 0.5 us)
Async XLA Ops:
  1.3 2.0 %collective-permute-start = (s32[2,256]{1,0:T(2,128)S(1)}, s32[2,256]{1,0:T(2,128)S(1)}, u32[]{:S(2)}, u32[]{:S(2)}) collective-permute-start(s32[2,256]{1,0:T(2,128)S(1)} %pad_add_fusion), channel_id=1, source_target_pairs={{0,16},{16,0},{1,17},{17,1},{2,18},{18,2},{3,19},{19,3},{4,20},{20... | collective-permute-start | bytes 6152 | tf_op jit(solution)/shard_map/ppermute | solution.py:16
  1.8 1.5 %copy-start.1 = (s32[1,1,1,256]{3,2,1,0:T(1,128)S(1)}, s32[1,1,1,256]{3,2,1,0:T(1,128)}, u32[]{:S(2)}) copy-start(s32[1,1,1,256]{3,2,1,0:T(1,128)} %param.8) | copy-start | bytes 3076
  1.8 1.5 %copy-start.2 = (s32[1,1,1,256]{3,2,1,0:T(1,128)S(1)}, s32[1,1,1,256]{3,2,1,0:T(1,128)}, u32[]{:S(2)}) copy-start(s32[1,1,1,256]{3,2,1,0:T(1,128)} %param.7) | copy-start | bytes 3076
  3.2 2.0 %collective-permute-start.1 = (bf16[256,4,2,128]{3,0,2,1:T(8,128)(2,1)S(1)}, bf16[256,4,2,128]{3,0,2,1:T(8,128)(2,1)S(1)}, u32[]{:S(2)}, u32[]{:S(2)}) collective-permute-start(bf16[256,4,2,128]{3,0,2,1:T(8,128)(2,1)S(1)} %get-tuple-element.18), channel_id=1, source_target_pairs={{0,16},{16,0},{1,17},{17,1},{2,18},{18,2},{3,19},{19,3},{4,20},{20... | collective-permute-start | bytes 1572872 | tf_op jit(solution)/shard_map/ppermute | solution.py:16
  5.6 9.4 %collective-permute-start.2 = (f32[48,4,2,128]{3,0,2,1:T(8,128)S(1)}, f32[48,4,2,128]{3,0,2,1:T(8,128)S(1)}, u32[]{:S(2)}, u32[]{:S(2)}) collective-permute-start(f32[48,4,2,128]{3,0,2,1:T(8,128)S(1)} %get-tuple-element.19), channel_id=1, source_target_pairs={{0,4},{4,8},{8,12},{12,0},{1,5},{5,9},{9,13},{13,1},{2,6},{6,10},{... | collective-permute-start | bytes 589832 | tf_op jit(solution)/shard_map/ppermute | solution.py:16
  8.3 10.6 %collective-permute-start.3 = (f32[48,4,2,128]{3,0,2,1:T(8,128)S(1)}, f32[48,4,2,128]{3,0,2,1:T(8,128)S(1)}, u32[]{:S(2)}, u32[]{:S(2)}) collective-permute-start(f32[48,4,2,128]{3,0,2,1:T(8,128)S(1)} %get-tuple-element.21), channel_id=1, source_target_pairs={{0,8},{4,12},{8,0},{12,4},{1,9},{5,13},{9,1},{13,5},{2,10},{6,14},... | collective-permute-start | bytes 589832 | tf_op jit(solution)/shard_map/ppermute | solution.py:16
  9.8 9.4 %collective-permute-start.4 = (f32[48,4,2,128]{3,0,2,1:T(8,128)S(1)}, f32[48,4,2,128]{3,0,2,1:T(8,128)S(1)}, u32[]{:S(2)}, u32[]{:S(2)}) collective-permute-start(f32[48,4,2,128]{3,0,2,1:T(8,128)S(1)} %get-tuple-element.20), channel_id=1, source_target_pairs={{0,12},{4,0},{8,4},{12,8},{1,13},{5,1},{9,5},{13,9},{2,14},{6,2},{... | collective-permute-start | bytes 589832 | tf_op jit(solution)/shard_map/ppermute | solution.py:16
  21.2 6.3 %collective-permute-start.5 = (f32[102,128]{1,0:T(8,128)S(1)}, f32[102,128]{1,0:T(8,128)S(1)}, u32[]{:S(2)}, u32[]{:S(2)}) collective-permute-start(f32[102,128]{1,0:T(8,128)S(1)} %bitcast.87), channel_id=1, source_target_pairs={{0,1},{1,2},{2,3},{3,0},{4,5},{5,6},{6,7},{7,4},{8,9},{9,10},{10,1... | collective-permute-start | bytes 156680 | tf_op jit(solution)/shard_map/ppermute | solution.py:16
  22.8 6.7 %collective-permute-start.6 = (f32[102,128]{1,0:T(8,128)S(1)}, f32[102,128]{1,0:T(8,128)S(1)}, u32[]{:S(2)}, u32[]{:S(2)}) collective-permute-start(f32[102,128]{1,0:T(8,128)S(1)} %bitcast.86), channel_id=1, source_target_pairs={{0,2},{1,3},{2,0},{3,1},{4,6},{5,7},{6,4},{7,5},{8,10},{9,11},{10,... | collective-permute-start | bytes 156680 | tf_op jit(solution)/shard_map/ppermute | solution.py:16
  25.4 4.4 %collective-permute-start.7 = (f32[102,128]{1,0:T(8,128)S(1)}, f32[102,128]{1,0:T(8,128)S(1)}, u32[]{:S(2)}, u32[]{:S(2)}) collective-permute-start(f32[102,128]{1,0:T(8,128)S(1)} %bitcast.85), channel_id=1, source_target_pairs={{0,3},{1,0},{2,1},{3,2},{4,7},{5,4},{6,5},{7,6},{8,11},{9,8},{10,9... | collective-permute-start | bytes 156680 | tf_op jit(solution)/shard_map/ppermute | solution.py:16
  29.8 1.3 %collective-permute-start.8 = (f32[102,128]{1,0:T(8,128)S(1)}, f32[102,128]{1,0:T(8,128)S(1)}, u32[]{:S(2)}, u32[]{:S(2)}) collective-permute-start(f32[102,128]{1,0:T(8,128)S(1)} %fusion.49), channel_id=1, source_target_pairs={{0,16},{16,0},{1,17},{17,1},{2,18},{18,2},{3,19},{19,3},{4,20},{20... | collective-permute-start | bytes 156680 | tf_op jit(solution)/shard_map/ppermute | solution.py:16
  32.0 0.8 %copy-start = (f32[4,16,128]{2,1,0:T(8,128)S(1)}, f32[4,16,128]{2,1,0:T(8,128)}, u32[]{:S(2)}) copy-start(f32[4,16,128]{2,1,0:T(8,128)} %param.9) | copy-start | bytes 98308
  33.0 5.6 %collective-permute-start.9 = (bf16[8,4,2,128]{3,0,2,1:T(8,128)(2,1)S(1)}, bf16[8,4,2,128]{3,0,2,1:T(8,128)(2,1)S(1)}, u32[]{:S(2)}, u32[]{:S(2)}) collective-permute-start(bf16[8,4,2,128]{3,0,2,1:T(8,128)(2,1)S(1)} %bitcast.77), channel_id=1, source_target_pairs={{0,1},{1,2},{2,3},{3,0},{4,5},{5,6},{6,7},{7,4},{8,9},{9,10},{10,1... | collective-permute-start | bytes 49160 | tf_op jit(solution)/shard_map/ppermute | solution.py:16
  34.0 4.9 %collective-permute-start.10 = (bf16[8,4,2,128]{3,0,2,1:T(8,128)(2,1)S(1)}, bf16[8,4,2,128]{3,0,2,1:T(8,128)(2,1)S(1)}, u32[]{:S(2)}, u32[]{:S(2)}) collective-permute-start(bf16[8,4,2,128]{3,0,2,1:T(8,128)(2,1)S(1)} %bitcast.78), channel_id=1, source_target_pairs={{0,2},{1,3},{2,0},{3,1},{4,6},{5,7},{6,4},{7,5},{8,10},{9,11},{10,... | collective-permute-start | bytes 49160 | tf_op jit(solution)/shard_map/ppermute | solution.py:16
  36.5 3.7 %collective-permute-start.11 = (bf16[8,4,2,128]{3,0,2,1:T(8,128)(2,1)S(1)}, bf16[8,4,2,128]{3,0,2,1:T(8,128)(2,1)S(1)}, u32[]{:S(2)}, u32[]{:S(2)}) collective-permute-start(bf16[8,4,2,128]{3,0,2,1:T(8,128)(2,1)S(1)} %bitcast.79), channel_id=1, source_target_pairs={{0,3},{1,0},{2,1},{3,2},{4,7},{5,4},{6,5},{7,6},{8,11},{9,8},{10,9... | collective-permute-start | bytes 49160 | tf_op jit(solution)/shard_map/ppermute | solution.py:16
  40.3 5.2 %collective-permute-start.12 = (bf16[4,8,4,2,128]{4,1,0,3,2:T(8,128)(2,1)S(1)}, bf16[4,8,4,2,128]{4,1,0,3,2:T(8,128)(2,1)S(1)}, u32[]{:S(2)}, u32[]{:S(2)}) collective-permute-start(bf16[4,8,4,2,128]{4,1,0,3,2:T(8,128)(2,1)S(1)} %get-tuple-element.33), channel_id=1, source_target_pairs={{0,4},{4,8},{8,12},{12,0},{1,5},{5,9},{9,13},{13,1},{2,6},{6,10},{... | collective-permute-start | bytes 196616 | tf_op jit(solution)/shard_map/ppermute | solution.py:16
  42.1 4.3 %collective-permute-start.13 = (bf16[4,8,4,2,128]{4,1,0,3,2:T(8,128)(2,1)S(1)}, bf16[4,8,4,2,128]{4,1,0,3,2:T(8,128)(2,1)S(1)}, u32[]{:S(2)}, u32[]{:S(2)}) collective-permute-start(bf16[4,8,4,2,128]{4,1,0,3,2:T(8,128)(2,1)S(1)} %get-tuple-element.33), channel_id=1, source_target_pairs={{0,8},{4,12},{8,0},{12,4},{1,9},{5,13},{9,1},{13,5},{2,10},{6,14},... | collective-permute-start | bytes 196616 | tf_op jit(solution)/shard_map/ppermute | solution.py:16
  42.6 4.3 %collective-permute-start.14 = (bf16[4,8,4,2,128]{4,1,0,3,2:T(8,128)(2,1)S(1)}, bf16[4,8,4,2,128]{4,1,0,3,2:T(8,128)(2,1)S(1)}, u32[]{:S(2)}, u32[]{:S(2)}) collective-permute-start(bf16[4,8,4,2,128]{4,1,0,3,2:T(8,128)(2,1)S(1)} %get-tuple-element.33), channel_id=1, source_target_pairs={{0,12},{4,0},{8,4},{12,8},{1,13},{5,1},{9,5},{13,9},{2,14},{6,2},{... | collective-permute-start | bytes 196616 | tf_op jit(solution)/shard_map/ppermute | solution.py:16

commit v5 on v4

--- a/solution.py
+++ b/solution.py
@@ -38,9 +38,8 @@
     me_g = lax.axis_index("group")
     is_grad = me_g == 0
     kept = jnp.where(is_grad, slot_grad, slot_illum)
-    given = jnp.where(is_grad, slot_illum, slot_grad)
+    taken = lax.ppermute(slot_illum, "group", [(0, 1)]) + lax.ppermute(slot_grad, "group", [(1, 0)])
     places = jnp.stack([owners, patches])
-    taken = shifted(given, "group", size_g, 1)
     taken_places = shifted(places, "group", size_g, 1)
     rows_in = jnp.concatenate([kept, taken], axis=0)
     all_owners = jnp.concatenate([owners, taken_places[0]])

time: 48.7 us -> 54.6 us (1.12)
  waiting for transfers between devices: 18.5 us -> 23.4 us
  local copies, waits for them, and re-layouts: 3.97 us -> 6.1 us
  other arithmetic: 4.15 us -> 3.16 us
    ppermute x15 -> x14, waiting for transfers between devices: 18.5 us -> 23.4 us  [shifted(): lax.ppermute(value, axis, [(s, (s + step) % count) for s in range(count)])]
    ppermute x15 -> x14, starting transfers between devices: 20.3 us -> 16.2 us  [shifted(): lax.ppermute(value, axis, [(s, (s + step) % count) for s in range(count)])]
    ppermute x0 -> x2, starting transfers between devices: none -> 3.81 us  [the longest x1 2.52 us: local(): lax.ppermute(slot_illum, 'group', [(0, 1)])]
    unnamed x9 -> x17, local copies, waits for them, and re-layouts: 1.98 us -> 4.1 us
    another operation x1, other arithmetic: 0.71 us -> 0.01 us  [local(): places = jnp.stack([owners, patches])]
  transfers between devices with their start and end apart: 15 -> 16, of which waited for: 14 -> 13; matrix products, arithmetic and copies ran while one was open for 5% -> 3% of each run, Pallas kernels for 0% -> 0%
where the time goes in v5:
time: 54.6 us; the launch traced here: 54.4 us
  waiting for transfers between devices  23.4 us (43%)
  starting transfers between devices  20 us (37%)
  local copies, waits for them, and re-layouts  6.1 us (11%)
  other arithmetic  3.16 us (6%)
  between operations  1.03 us (2%)
  matrix products  0.71 us (1%)
    ppermute x14, waiting for transfers between devices, shifted(): lax.ppermute(value, axis, [(s, (s + step) % count) for s in range(count)])  23.4 us
    ppermute x14, starting transfers between devices, shifted(): lax.ppermute(value, axis, [(s, (s + step) % count) for s in range(count)])  16.2 us
    unnamed x17, local copies, waits for them, and re-layouts  4.1 us
    ppermute x1, starting transfers between devices, local(): lax.ppermute(slot_illum, 'group', [(0, 1)])  2.52 us
    ppermute x1, starting transfers between devices, local(): lax.ppermute(slot_grad, 'group', [(1, 0)])  1.29 us
  transfers between devices with their start and end apart: 16, of which 13 were waited for; matrix products, arithmetic and copies ran while one was open for 3% of the time, Pallas kernels for 0%

profile of v5, /device:TPU:0, one launch (start us, length us, event | category | flops | bytes accessed | tf_op | source)
XLA Modules:
  0.0 54.4 jit_solution(15726176170678193280)
XLA Ops:
  0.6 1.2 %copy.64 = bf16[1,1,1,256,4,2,128]{6,3,5,4,2,1,0:T(8,128)(2,1)S(1)} copy(bf16[1,1,1,256,4,2,128]{6,5,4,3,2,1,0:T(2,128)(2,1)} %param.6) | data formatting | bytes 1048576 | tf_op args[1]
  1.8 0.0 copy-start.4
  1.8 0.0 copy-start.5
  1.8 0.0 copy-start
  1.8 2.5 %collective-permute-start.1 = (bf16[256,4,2,128]{3,0,2,1:T(8,128)(2,1)S(1)}, bf16[256,4,2,128]{3,0,2,1:T(8,128)(2,1)S(1)}, u32[]{:S(2)}, u32[]{:S(2)}) collective-permute-start(bf16[256,4,2,128]{3,0,2,1:T(8,128)(2,1)S(1)} %bitcast.81), channel_id=1, source_target_pairs={{0,16},{1,17},{2,18},{3,19},{4,20},{5,21},{6,22},{7,23},{8,24},{9,... | collective-permute-start | bytes 1572872 | tf_op jit(solution)/shard_map/ppermute | solution.py:41
  4.4 0.1 copy.65
  4.5 1.3 %collective-permute-start.2 = (bf16[256,4,2,128]{3,0,2,1:T(8,128)(2,1)S(1)}, bf16[256,4,2,128]{3,0,2,1:T(8,128)(2,1)S(1)}, u32[]{:S(2)}, u32[]{:S(2)}) collective-permute-start(bf16[256,4,2,128]{3,0,2,1:T(8,128)(2,1)S(1)} %bitcast.82), channel_id=1, source_target_pairs={{16,0},{17,1},{18,2},{19,3},{20,4},{21,5},{22,6},{23,7},{24,8},{25... | collective-permute-start | bytes 1572872 | tf_op jit(solution)/shard_map/ppermute | solution.py:41
  5.8 1.2 %collective-permute-start = (s32[2,256]{1,0:T(2,128)S(1)}, s32[2,256]{1,0:T(2,128)S(1)}, u32[]{:S(2)}, u32[]{:S(2)}) collective-permute-start(s32[2,256]{1,0:T(2,128)S(1)} %pad_add_fusion), channel_id=1, source_target_pairs={{0,16},{16,0},{1,17},{17,1},{2,18},{18,2},{3,19},{19,3},{4,20},{20... | collective-permute-start | bytes 6152 | tf_op jit(solution)/shard_map/ppermute | solution.py:16
  7.0 1.0 %broadcast_select_fusion = bf16[256,4,2,128]{3,0,2,1:T(8,128)(2,1)} fusion(pred[]{:T(512)S(6)} %eq.65, bf16[1,1,1,256,4,2,128]{6,5,4,3,2,1,0:T(2,128)(2,1)S(1)} %copy-done.1, bf16[1,1,1,256,4,2,128]{6,5,4,3,2,1,0:T(2,128)(2,1)S(1)} %copy-done), kind=kLoop, calls=%fused_computation.8 | loop fusion | flops 262144 | bytes 1572865 | tf_op jit(solution)/shard_map/jit(_where)/select_n | solution.py:40
  8.0 0.3 collective-permute-done
  8.3 0.0 copy-start.2
  8.3 0.0 collective-permute-done.1
  8.4 0.0 collective-permute-done.2
  8.4 0.1 add.345
  8.5 0.9 %copy-done.2 = bf16[256,4,2,128]{3,0,2,1:T(8,128)(2,1)S(1)} copy-done((bf16[256,4,2,128]{3,0,2,1:T(8,128)(2,1)S(1)}, bf16[256,4,2,128]{3,0,2,1:T(8,128)(2,1)}, u32[]{:S(2)}) %copy-start.2) | copy-done | bytes 524312
  9.4 0.4 fusion.1
  9.8 3.3 %collective-permute-start.5 = (f32[48,4,2,128]{3,0,2,1:T(8,128)S(1)}, f32[48,4,2,128]{3,0,2,1:T(8,128)S(1)}, u32[]{:S(2)}, u32[]{:S(2)}) collective-permute-start(f32[48,4,2,128]{3,0,2,1:T(8,128)S(1)} %get-tuple-element.18), channel_id=1, source_target_pairs={{0,12},{4,0},{8,4},{12,8},{1,13},{5,1},{9,5},{13,9},{2,14},{6,2},{... | collective-permute-start | bytes 589832 | tf_op jit(solution)/shard_map/ppermute | solution.py:16
  13.1 0.5 collective-permute-start.4
  13.6 0.6 %collective-permute-start.3 = (f32[48,4,2,128]{3,0,2,1:T(8,128)S(1)}, f32[48,4,2,128]{3,0,2,1:T(8,128)S(1)}, u32[]{:S(2)}, u32[]{:S(2)}) collective-permute-start(f32[48,4,2,128]{3,0,2,1:T(8,128)S(1)} %get-tuple-element.17), channel_id=1, source_target_pairs={{0,4},{4,8},{8,12},{12,0},{1,5},{5,9},{9,13},{13,1},{2,6},{6,10},{... | collective-permute-start | bytes 589832 | tf_op jit(solution)/shard_map/ppermute | solution.py:16
  14.2 4.2 %collective-permute-done.5 = f32[48,4,2,128]{3,0,2,1:T(8,128)S(1)} collective-permute-done((f32[48,4,2,128]{3,0,2,1:T(8,128)S(1)}, f32[48,4,2,128]{3,0,2,1:T(8,128)S(1)}, u32[]{:S(2)}, u32[]{:S(2)}) %collective-permute-start.5) | collective-permute-done | bytes 196640 | tf_op jit(solution)/shard_map/ppermute | solution.py:16
  18.4 5.6 %collective-permute-done.4 = f32[48,4,2,128]{3,0,2,1:T(8,128)S(1)} collective-permute-done((f32[48,4,2,128]{3,0,2,1:T(8,128)S(1)}, f32[48,4,2,128]{3,0,2,1:T(8,128)S(1)}, u32[]{:S(2)}, u32[]{:S(2)}) %collective-permute-start.4) | collective-permute-done | bytes 196640 | tf_op jit(solution)/shard_map/ppermute | solution.py:16
  24.0 0.0 collective-permute-done.3
  24.1 0.1 copy.36
  24.2 0.2 reshape_reshape.3
  24.5 0.1 copy.39
  24.6 0.1 copy.37
  24.7 0.5 fusion.9
  25.2 0.3 reshape.520
  25.5 0.6 %slice_reduce_fusion.3 = (f32[13056]{0:T(1024)S(1)}, f32[13056]{0:T(1024)S(1)}, f32[13056]{0:T(1024)S(1)}, f32[13056]{0:T(1024)S(1)}) fusion(f32[4,13056]{1,0:T(4,128)S(1)} %constant_dynamic-update-slice_fusion), kind=kLoop, calls=%fused_computation.94 | loop fusion | bytes 417792 | tf_op jit(solution)/shard_map/slice | solution.py:85
  26.0 3.7 %collective-permute-start.8 = (f32[102,128]{1,0:T(8,128)S(1)}, f32[102,128]{1,0:T(8,128)S(1)}, u32[]{:S(2)}, u32[]{:S(2)}) collective-permute-start(f32[102,128]{1,0:T(8,128)S(1)} %bitcast.95), channel_id=1, source_target_pairs={{0,3},{1,0},{2,1},{3,2},{4,7},{5,4},{6,5},{7,6},{8,11},{9,8},{10,9... | collective-permute-start | bytes 156680 | tf_op jit(solution)/shard_map/ppermute | solution.py:16
  29.7 0.0 collective-permute-start.7
  29.7 1.0 %collective-permute-start.6 = (f32[102,128]{1,0:T(8,128)S(1)}, f32[102,128]{1,0:T(8,128)S(1)}, u32[]{:S(2)}, u32[]{:S(2)}) collective-permute-start(f32[102,128]{1,0:T(8,128)S(1)} %bitcast.93), channel_id=1, source_target_pairs={{0,1},{1,2},{2,3},{3,0},{4,5},{5,6},{6,7},{7,4},{8,9},{9,10},{10,1... | collective-permute-start | bytes 156680 | tf_op jit(solution)/shard_map/ppermute | solution.py:16
  30.7 0.8 %collective-permute-done.8 = f32[102,128]{1,0:T(8,128)S(1)} collective-permute-done((f32[102,128]{1,0:T(8,128)S(1)}, f32[102,128]{1,0:T(8,128)S(1)}, u32[]{:S(2)}, u32[]{:S(2)}) %collective-permute-start.8) | collective-permute-done | bytes 52256 | tf_op jit(solution)/shard_map/ppermute | solution.py:16
  31.5 3.2 %collective-permute-done.7 = f32[102,128]{1,0:T(8,128)S(1)} collective-permute-done((f32[102,128]{1,0:T(8,128)S(1)}, f32[102,128]{1,0:T(8,128)S(1)}, u32[]{:S(2)}, u32[]{:S(2)}) %collective-permute-start.7) | collective-permute-done | bytes 52256 | tf_op jit(solution)/shard_map/ppermute | solution.py:16
  34.7 0.9 %collective-permute-done.6 = f32[102,128]{1,0:T(8,128)S(1)} collective-permute-done((f32[102,128]{1,0:T(8,128)S(1)}, f32[102,128]{1,0:T(8,128)S(1)}, u32[]{:S(2)}, u32[]{:S(2)}) %collective-permute-start.6) | collective-permute-done | bytes 52256 | tf_op jit(solution)/shard_map/ppermute | solution.py:16
  35.7 0.1 collective-permute-start.9
  35.7 0.1 broadcast_and_fusion
  35.8 0.1 slice.255
  35.9 1.1 %collective-permute-done.9 = f32[102,128]{1,0:T(8,128)S(1)} collective-permute-done((f32[102,128]{1,0:T(8,128)S(1)}, f32[102,128]{1,0:T(8,128)S(1)}, u32[]{:S(2)}, u32[]{:S(2)}) %collective-permute-start.9) | collective-permute-done | bytes 52256 | tf_op jit(solution)/shard_map/ppermute | solution.py:16
  37.0 0.1 reshape.521
  37.1 0.1 reshape.523
  37.3 0.2 fusion.87
  37.5 0.4 fusion.46
  37.8 0.0 copy-start.3
  37.9 0.2 fusion.23
  38.1 0.2 fusion.32
  38.3 0.2 fusion.41
  38.5 0.2 fusion.44
  38.7 0.2 fusion.83
  38.9 0.7 %collective-permute-start.12 = (bf16[8,4,2,128]{3,0,2,1:T(8,128)(2,1)S(1)}, bf16[8,4,2,128]{3,0,2,1:T(8,128)(2,1)S(1)}, u32[]{:S(2)}, u32[]{:S(2)}) collective-permute-start(bf16[8,4,2,128]{3,0,2,1:T(8,128)(2,1)S(1)} %bitcast.85), channel_id=1, source_target_pairs={{0,3},{1,0},{2,1},{3,2},{4,7},{5,4},{6,5},{7,6},{8,11},{9,8},{10,9... | collective-permute-start | bytes 49160 | tf_op jit(solution)/shard_map/ppermute | solution.py:16
  39.6 0.5 collective-permute-start.11
  40.1 1.9 %collective-permute-start.10 = (bf16[8,4,2,128]{3,0,2,1:T(8,128)(2,1)S(1)}, bf16[8,4,2,128]{3,0,2,1:T(8,128)(2,1)S(1)}, u32[]{:S(2)}, u32[]{:S(2)}) collective-permute-start(bf16[8,4,2,128]{3,0,2,1:T(8,128)(2,1)S(1)} %bitcast.87), channel_id=1, source_target_pairs={{0,1},{1,2},{2,3},{3,0},{4,5},{5,6},{6,7},{7,4},{8,9},{9,10},{10,1... | collective-permute-start | bytes 49160 | tf_op jit(solution)/shard_map/ppermute | solution.py:16
  42.1 0.6 %collective-permute-done.12 = bf16[8,4,2,128]{3,0,2,1:T(8,128)(2,1)S(1)} collective-permute-done((bf16[8,4,2,128]{3,0,2,1:T(8,128)(2,1)S(1)}, bf16[8,4,2,128]{3,0,2,1:T(8,128)(2,1)S(1)}, u32[]{:S(2)}, u32[]{:S(2)}) %collective-permute-start.12) | collective-permute-done | bytes 16416 | tf_op jit(solution)/shard_map/ppermute | solution.py:16
  42.7 1.6 %collective-permute-done.11 = bf16[8,4,2,128]{3,0,2,1:T(8,128)(2,1)S(1)} collective-permute-done((bf16[8,4,2,128]{3,0,2,1:T(8,128)(2,1)S(1)}, bf16[8,4,2,128]{3,0,2,1:T(8,128)(2,1)S(1)}, u32[]{:S(2)}, u32[]{:S(2)}) %collective-permute-start.11) | collective-permute-done | bytes 16416 | tf_op jit(solution)/shard_map/ppermute | solution.py:16
  44.3 1.4 %collective-permute-done.10 = bf16[8,4,2,128]{3,0,2,1:T(8,128)(2,1)S(1)} collective-permute-done((bf16[8,4,2,128]{3,0,2,1:T(8,128)(2,1)S(1)}, bf16[8,4,2,128]{3,0,2,1:T(8,128)(2,1)S(1)}, u32[]{:S(2)}, u32[]{:S(2)}) %collective-permute-start.10) | collective-permute-done | bytes 16416 | tf_op jit(solution)/shard_map/ppermute | solution.py:16
  45.7 0.6 %collective-permute-start.15 = (bf16[4,8,4,2,128]{4,1,0,3,2:T(8,128)(2,1)S(1)}, bf16[4,8,4,2,128]{4,1,0,3,2:T(8,128)(2,1)S(1)}, u32[]{:S(2)}, u32[]{:S(2)}) collective-permute-start(bf16[4,8,4,2,128]{4,1,0,3,2:T(8,128)(2,1)S(1)} %get-tuple-element.31), channel_id=1, source_target_pairs={{0,12},{4,0},{8,4},{12,8},{1,13},{5,1},{9,5},{13,9},{2,14},{6,2},{... | collective-permute-start | bytes 196616 | tf_op jit(solution)/shard_map/ppermute | solution.py:16
  46.3 1.2 %collective-permute-start.14 = (bf16[4,8,4,2,128]{4,1,0,3,2:T(8,128)(2,1)S(1)}, bf16[4,8,4,2,128]{4,1,0,3,2:T(8,128)(2,1)S(1)}, u32[]{:S(2)}, u32[]{:S(2)}) collective-permute-start(bf16[4,8,4,2,128]{4,1,0,3,2:T(8,128)(2,1)S(1)} %get-tuple-element.31), channel_id=1, source_target_pairs={{0,8},{4,12},{8,0},{12,4},{1,9},{5,13},{9,1},{13,5},{2,10},{6,14},... | collective-permute-start | bytes 196616 | tf_op jit(solution)/shard_map/ppermute | solution.py:16
  47.5 0.7 %collective-permute-start.13 = (bf16[4,8,4,2,128]{4,1,0,3,2:T(8,128)(2,1)S(1)}, bf16[4,8,4,2,128]{4,1,0,3,2:T(8,128)(2,1)S(1)}, u32[]{:S(2)}, u32[]{:S(2)}) collective-permute-start(bf16[4,8,4,2,128]{4,1,0,3,2:T(8,128)(2,1)S(1)} %get-tuple-element.31), channel_id=1, source_target_pairs={{0,4},{4,8},{8,12},{12,0},{1,5},{5,9},{9,13},{13,1},{2,6},{6,10},{... | collective-permute-start | bytes 196616 | tf_op jit(solution)/shard_map/ppermute | solution.py:16
  48.3 0.6 %copy.50 = f32[4,16,128]{2,1,0:T(8,128)} copy(f32[4,16,128]{2,0,1:T(4,128)S(1)} %get-tuple-element.13) | data formatting | bytes 65536
  48.9 1.1 %collective-permute-done.15 = bf16[4,8,4,2,128]{4,1,0,3,2:T(8,128)(2,1)S(1)} collective-permute-done((bf16[4,8,4,2,128]{4,1,0,3,2:T(8,128)(2,1)S(1)}, bf16[4,8,4,2,128]{4,1,0,3,2:T(8,128)(2,1)S(1)}, u32[]{:S(2)}, u32[]{:S(2)}) %collective-permute-start.15) | collective-permute-done | bytes 65568 | tf_op jit(solution)/shard_map/ppermute | solution.py:16
  50.0 1.0 %collective-permute-done.14 = bf16[4,8,4,2,128]{4,1,0,3,2:T(8,128)(2,1)S(1)} collective-permute-done((bf16[4,8,4,2,128]{4,1,0,3,2:T(8,128)(2,1)S(1)}, bf16[4,8,4,2,128]{4,1,0,3,2:T(8,128)(2,1)S(1)}, u32[]{:S(2)}, u32[]{:S(2)}) %collective-permute-start.14) | collective-permute-done | bytes 65568 | tf_op jit(solution)/shard_map/ppermute | solution.py:16
  51.0 1.7 %collective-permute-done.13 = bf16[4,8,4,2,128]{4,1,0,3,2:T(8,128)(2,1)S(1)} collective-permute-done((bf16[4,8,4,2,128]{4,1,0,3,2:T(8,128)(2,1)S(1)}, bf16[4,8,4,2,128]{4,1,0,3,2:T(8,128)(2,1)S(1)}, u32[]{:S(2)}, u32[]{:S(2)}) %collective-permute-start.13) | collective-permute-done | bytes 65568 | tf_op jit(solution)/shard_map/ppermute | solution.py:16
  52.7 0.3 fusion
  53.1 1.3 %copy.51 = bf16[1,1,1,256,4,2,128]{6,5,4,3,2,1,0:T(2,128)(2,1)} copy(bf16[1,1,1,256,4,2,128]{6,3,5,4,2,1,0:T(8,128)(2,1)S(1)} %fusion) | data formatting | bytes 1048576
  (32 shorter events, 0.5 us)
Async XLA Ops:
  0.6 3.8 %copy-start.1 = (bf16[1,1,1,256,4,2,128]{6,5,4,3,2,1,0:T(2,128)(2,1)S(1)}, bf16[1,1,1,256,4,2,128]{6,5,4,3,2,1,0:T(2,128)(2,1)}, u32[]{:S(2)}) copy-start(bf16[1,1,1,256,4,2,128]{6,5,4,3,2,1,0:T(2,128)(2,1)} %param.5) | copy-start | bytes 1572868
  1.8 4.0 %copy-start.4 = (s32[1,1,1,256]{3,2,1,0:T(1,128)S(1)}, s32[1,1,1,256]{3,2,1,0:T(1,128)}, u32[]{:S(2)}) copy-start(s32[1,1,1,256]{3,2,1,0:T(1,128)} %param.8) | copy-start | bytes 3076
  1.8 4.0 %copy-start.5 = (s32[1,1,1,256]{3,2,1,0:T(1,128)S(1)}, s32[1,1,1,256]{3,2,1,0:T(1,128)}, u32[]{:S(2)}) copy-start(s32[1,1,1,256]{3,2,1,0:T(1,128)} %param.7) | copy-start | bytes 3076
  1.8 5.2 %copy-start = (bf16[1,1,1,256,4,2,128]{6,5,4,3,2,1,0:T(2,128)(2,1)S(1)}, bf16[1,1,1,256,4,2,128]{6,5,4,3,2,1,0:T(2,128)(2,1)}, u32[]{:S(2)}) copy-start(bf16[1,1,1,256,4,2,128]{6,5,4,3,2,1,0:T(2,128)(2,1)} %param.6) | copy-start | bytes 1572868
  1.8 6.5 %collective-permute-start.1 = (bf16[256,4,2,128]{3,0,2,1:T(8,128)(2,1)S(1)}, bf16[256,4,2,128]{3,0,2,1:T(8,128)(2,1)S(1)}, u32[]{:S(2)}, u32[]{:S(2)}) collective-permute-start(bf16[256,4,2,128]{3,0,2,1:T(8,128)(2,1)S(1)} %bitcast.81), channel_id=1, source_target_pairs={{0,16},{1,17},{2,18},{3,19},{4,20},{5,21},{6,22},{7,23},{8,24},{9,... | collective-permute-start | bytes 1572872 | tf_op jit(solution)/shard_map/ppermute | solution.py:41
  4.5 3.9 %collective-permute-start.2 = (bf16[256,4,2,128]{3,0,2,1:T(8,128)(2,1)S(1)}, bf16[256,4,2,128]{3,0,2,1:T(8,128)(2,1)S(1)}, u32[]{:S(2)}, u32[]{:S(2)}) collective-permute-start(bf16[256,4,2,128]{3,0,2,1:T(8,128)(2,1)S(1)} %bitcast.82), channel_id=1, source_target_pairs={{16,0},{17,1},{18,2},{19,3},{20,4},{21,5},{22,6},{23,7},{24,8},{25... | collective-permute-start | bytes 1572872 | tf_op jit(solution)/shard_map/ppermute | solution.py:41
  5.8 2.5 %collective-permute-start = (s32[2,256]{1,0:T(2,128)S(1)}, s32[2,256]{1,0:T(2,128)S(1)}, u32[]{:S(2)}, u32[]{:S(2)}) collective-permute-start(s32[2,256]{1,0:T(2,128)S(1)} %pad_add_fusion), channel_id=1, source_target_pairs={{0,16},{16,0},{1,17},{17,1},{2,18},{18,2},{3,19},{19,3},{4,20},{20... | collective-permute-start | bytes 6152 | tf_op jit(solution)/shard_map/ppermute | solution.py:16
  8.3 1.0 %copy-start.2 = (bf16[256,4,2,128]{3,0,2,1:T(8,128)(2,1)S(1)}, bf16[256,4,2,128]{3,0,2,1:T(8,128)(2,1)}, u32[]{:S(2)}) copy-start(bf16[256,4,2,128]{3,0,2,1:T(8,128)(2,1)} %broadcast_select_fusion) | copy-start | bytes 1572868
  9.8 8.6 %collective-permute-start.5 = (f32[48,4,2,128]{3,0,2,1:T(8,128)S(1)}, f32[48,4,2,128]{3,0,2,1:T(8,128)S(1)}, u32[]{:S(2)}, u32[]{:S(2)}) collective-permute-start(f32[48,4,2,128]{3,0,2,1:T(8,128)S(1)} %get-tuple-element.18), channel_id=1, source_target_pairs={{0,12},{4,0},{8,4},{12,8},{1,13},{5,1},{9,5},{13,9},{2,14},{6,2},{... | collective-permute-start | bytes 589832 | tf_op jit(solution)/shard_map/ppermute | solution.py:16
  13.1 10.9 %collective-permute-start.4 = (f32[48,4,2,128]{3,0,2,1:T(8,128)S(1)}, f32[48,4,2,128]{3,0,2,1:T(8,128)S(1)}, u32[]{:S(2)}, u32[]{:S(2)}) collective-permute-start(f32[48,4,2,128]{3,0,2,1:T(8,128)S(1)} %get-tuple-element.19), channel_id=1, source_target_pairs={{0,8},{4,12},{8,0},{12,4},{1,9},{5,13},{9,1},{13,5},{2,10},{6,14},... | collective-permute-start | bytes 589832 | tf_op jit(solution)/shard_map/ppermute | solution.py:16
  13.6 10.4 %collective-permute-start.3 = (f32[48,4,2,128]{3,0,2,1:T(8,128)S(1)}, f32[48,4,2,128]{3,0,2,1:T(8,128)S(1)}, u32[]{:S(2)}, u32[]{:S(2)}) collective-permute-start(f32[48,4,2,128]{3,0,2,1:T(8,128)S(1)} %get-tuple-element.17), channel_id=1, source_target_pairs={{0,4},{4,8},{8,12},{12,0},{1,5},{5,9},{9,13},{13,1},{2,6},{6,10},{... | collective-permute-start | bytes 589832 | tf_op jit(solution)/shard_map/ppermute | solution.py:16
  26.0 5.5 %collective-permute-start.8 = (f32[102,128]{1,0:T(8,128)S(1)}, f32[102,128]{1,0:T(8,128)S(1)}, u32[]{:S(2)}, u32[]{:S(2)}) collective-permute-start(f32[102,128]{1,0:T(8,128)S(1)} %bitcast.95), channel_id=1, source_target_pairs={{0,3},{1,0},{2,1},{3,2},{4,7},{5,4},{6,5},{7,6},{8,11},{9,8},{10,9... | collective-permute-start | bytes 156680 | tf_op jit(solution)/shard_map/ppermute | solution.py:16
  29.7 5.0 %collective-permute-start.7 = (f32[102,128]{1,0:T(8,128)S(1)}, f32[102,128]{1,0:T(8,128)S(1)}, u32[]{:S(2)}, u32[]{:S(2)}) collective-permute-start(f32[102,128]{1,0:T(8,128)S(1)} %bitcast.94), channel_id=1, source_target_pairs={{0,2},{1,3},{2,0},{3,1},{4,6},{5,7},{6,4},{7,5},{8,10},{9,11},{10,... | collective-permute-start | bytes 156680 | tf_op jit(solution)/shard_map/ppermute | solution.py:16
  29.7 5.9 %collective-permute-start.6 = (f32[102,128]{1,0:T(8,128)S(1)}, f32[102,128]{1,0:T(8,128)S(1)}, u32[]{:S(2)}, u32[]{:S(2)}) collective-permute-start(f32[102,128]{1,0:T(8,128)S(1)} %bitcast.93), channel_id=1, source_target_pairs={{0,1},{1,2},{2,3},{3,0},{4,5},{5,6},{6,7},{7,4},{8,9},{9,10},{10,1... | collective-permute-start | bytes 156680 | tf_op jit(solution)/shard_map/ppermute | solution.py:16
  35.7 1.3 %collective-permute-start.9 = (f32[102,128]{1,0:T(8,128)S(1)}, f32[102,128]{1,0:T(8,128)S(1)}, u32[]{:S(2)}, u32[]{:S(2)}) collective-permute-start(f32[102,128]{1,0:T(8,128)S(1)} %fusion.49), channel_id=1, source_target_pairs={{0,16},{16,0},{1,17},{17,1},{2,18},{18,2},{3,19},{19,3},{4,20},{20... | collective-permute-start | bytes 156680 | tf_op jit(solution)/shard_map/ppermute | solution.py:16
  37.8 0.8 %copy-start.3 = (f32[4,16,128]{2,1,0:T(8,128)S(1)}, f32[4,16,128]{2,1,0:T(8,128)}, u32[]{:S(2)}) copy-start(f32[4,16,128]{2,1,0:T(8,128)} %param.9) | copy-start | bytes 98308
  38.9 3.8 %collective-permute-start.12 = (bf16[8,4,2,128]{3,0,2,1:T(8,128)(2,1)S(1)}, bf16[8,4,2,128]{3,0,2,1:T(8,128)(2,1)S(1)}, u32[]{:S(2)}, u32[]{:S(2)}) collective-permute-start(bf16[8,4,2,128]{3,0,2,1:T(8,128)(2,1)S(1)} %bitcast.85), channel_id=1, source_target_pairs={{0,3},{1,0},{2,1},{3,2},{4,7},{5,4},{6,5},{7,6},{8,11},{9,8},{10,9... | collective-permute-start | bytes 49160 | tf_op jit(solution)/shard_map/ppermute | solution.py:16
  39.6 4.6 %collective-permute-start.11 = (bf16[8,4,2,128]{3,0,2,1:T(8,128)(2,1)S(1)}, bf16[8,4,2,128]{3,0,2,1:T(8,128)(2,1)S(1)}, u32[]{:S(2)}, u32[]{:S(2)}) collective-permute-start(bf16[8,4,2,128]{3,0,2,1:T(8,128)(2,1)S(1)} %bitcast.86), channel_id=1, source_target_pairs={{0,2},{1,3},{2,0},{3,1},{4,6},{5,7},{6,4},{7,5},{8,10},{9,11},{10,... | collective-permute-start | bytes 49160 | tf_op jit(solution)/shard_map/ppermute | solution.py:16
  40.1 5.5 %collective-permute-start.10 = (bf16[8,4,2,128]{3,0,2,1:T(8,128)(2,1)S(1)}, bf16[8,4,2,128]{3,0,2,1:T(8,128)(2,1)S(1)}, u32[]{:S(2)}, u32[]{:S(2)}) collective-permute-start(bf16[8,4,2,128]{3,0,2,1:T(8,128)(2,1)S(1)} %bitcast.87), channel_id=1, source_target_pairs={{0,1},{1,2},{2,3},{3,0},{4,5},{5,6},{6,7},{7,4},{8,9},{9,10},{10,1... | collective-permute-start | bytes 49160 | tf_op jit(solution)/shard_map/ppermute | solution.py:16
  45.7 4.3 %collective-permute-start.15 = (bf16[4,8,4,2,128]{4,1,0,3,2:T(8,128)(2,1)S(1)}, bf16[4,8,4,2,128]{4,1,0,3,2:T(8,128)(2,1)S(1)}, u32[]{:S(2)}, u32[]{:S(2)}) collective-permute-start(bf16[4,8,4,2,128]{4,1,0,3,2:T(8,128)(2,1)S(1)} %get-tuple-element.31), channel_id=1, source_target_pairs={{0,12},{4,0},{8,4},{12,8},{1,13},{5,1},{9,5},{13,9},{2,14},{6,2},{... | collective-permute-start | bytes 196616 | tf_op jit(solution)/shard_map/ppermute | solution.py:16
  46.3 4.7 %collective-permute-start.14 = (bf16[4,8,4,2,128]{4,1,0,3,2:T(8,128)(2,1)S(1)}, bf16[4,8,4,2,128]{4,1,0,3,2:T(8,128)(2,1)S(1)}, u32[]{:S(2)}, u32[]{:S(2)}) collective-permute-start(bf16[4,8,4,2,128]{4,1,0,3,2:T(8,128)(2,1)S(1)} %get-tuple-element.31), channel_id=1, source_target_pairs={{0,8},{4,12},{8,0},{12,4},{1,9},{5,13},{9,1},{13,5},{2,10},{6,14},... | collective-permute-start | bytes 196616 | tf_op jit(solution)/shard_map/ppermute | solution.py:16
  47.5 5.2 %collective-permute-start.13 = (bf16[4,8,4,2,128]{4,1,0,3,2:T(8,128)(2,1)S(1)}, bf16[4,8,4,2,128]{4,1,0,3,2:T(8,128)(2,1)S(1)}, u32[]{:S(2)}, u32[]{:S(2)}) collective-permute-start(bf16[4,8,4,2,128]{4,1,0,3,2:T(8,128)(2,1)S(1)} %get-tuple-element.31), channel_id=1, source_target_pairs={{0,4},{4,8},{8,12},{12,0},{1,5},{5,9},{9,13},{13,1},{2,6},{6,10},{... | collective-permute-start | bytes 196616 | tf_op jit(solution)/shard_map/ppermute | solution.py:16

commit v6 on v4

--- a/solution.py
+++ b/solution.py
@@ -33,7 +33,6 @@
     cell_count = levels * patch_rows * patch_cols
     h = HALO
     ext_rows = tile_rows + 2 * h
-    ext_cols = tile_cols + 2 * h
 
     me_g = lax.axis_index("group")
     is_grad = me_g == 0
@@ -49,18 +48,18 @@
     halo_patches = h // patch_rows
     ext_patches = per_tile + 2 * halo_patches
     rel_x = (all_owners // size_y - me_x) % size_x
-    rel_y = (all_owners % size_y - me_y) % size_y
-    own_row = (rel_x * size_y + rel_y) * ext_patches + all_patches + halo_patches
+    abs_y = all_owners % size_y
+    own_row = (rel_x * size_y + abs_y) * ext_patches + all_patches + halo_patches
     next_row = jnp.where(
         all_patches >= per_tile - halo_patches,
-        (((rel_x + 1) % size_x) * size_y + rel_y) * ext_patches
+        (((rel_x + 1) % size_x) * size_y + abs_y) * ext_patches
         + all_patches
         - (per_tile - halo_patches),
         -1,
     )
     prev_row = jnp.where(
         all_patches < halo_patches,
-        (((rel_x - 1) % size_x) * size_y + rel_y) * ext_patches
+        (((rel_x - 1) % size_x) * size_y + abs_y) * ext_patches
         + all_patches
         + per_tile
         + halo_patches,
@@ -73,37 +72,29 @@
     table = jnp.einsum("rw,wlpc->rlpc", onehot, rows_in, preferred_element_type=jnp.float32)
     flat = table.reshape(size_x, size_y * ext_patches, levels, patch_rows, patch_cols)
 
+    velocity_seen = jnp.stack(
+        [velocity] + [shifted(velocity, "gy", size_y, step) for step in range(1, size_y)]
+    )
+    velocity_row = jnp.take(velocity_seen, (me_y - jnp.arange(size_y)) % size_y, axis=0)
+    velocity_row = velocity_row.transpose(1, 2, 0, 3).reshape(levels, tile_rows, size_y * tile_cols)
+
     part = flat[0]
     for step in range(1, size_x):
         part = part + shifted(flat[step], "gx", size_x, step)
-    part = part.reshape(size_y, ext_patches, levels, patch_rows, patch_cols)
-    left = jnp.roll(part, 1, axis=0)[..., patch_cols - h :]
-    right = jnp.roll(part, -1, axis=0)[..., :h]
-    strips = jnp.concatenate([left, right], axis=-1)
-    packed = jnp.concatenate(
-        [part.reshape(size_y, -1), strips.reshape(size_y, -1)], axis=1
-    ).reshape(size_y, -1, 128)
-    total = packed[0]
+    row_sums = part
     for step in range(1, size_y):
-        total = total + shifted(packed[step], "gy", size_y, step)
-    other = shifted(total, "group", size_g, 1)
-    grad_flat = jnp.where(is_grad, total, other).reshape(-1)
-    illum_flat = jnp.where(is_grad, other, total).reshape(-1)
+        row_sums = row_sums + shifted(part, "gy", size_y, step)
+    other = shifted(row_sums, "group", size_g, 1)
 
     def unpack(values):
-        main_size = ext_patches * levels * patch_rows * patch_cols
-        main = values[:main_size].reshape(ext_patches, levels, patch_rows, patch_cols)
-        sides = values[main_size:].reshape(ext_patches, levels, patch_rows, 2 * h)
-        whole_rows = jnp.concatenate([sides[..., :h], main, sides[..., h:]], axis=-1)
-        return whole_rows.transpose(1, 0, 2, 3).reshape(levels, ext_rows, ext_cols)
+        return values.reshape(size_y, ext_patches, levels, patch_rows, patch_cols).transpose(
+            2, 1, 3, 0, 4
+        ).reshape(levels, ext_rows, size_y * tile_cols)
 
-    grad_ext = unpack(grad_flat)
-    illum_ext = unpack(illum_flat)
+    grad_ext = unpack(jnp.where(is_grad, row_sums, other))
+    illum_ext = unpack(jnp.where(is_grad, other, row_sums))
     pos_x = me_x * tile_rows - h + jnp.arange(ext_rows)
-    pos_y = me_y * tile_cols - h + jnp.arange(ext_cols)
-    inside = ((pos_x >= 0) & (pos_x < size_x * tile_rows))[:, None] & (
-        (pos_y >= 0) & (pos_y < size_y * tile_cols)
-    )[None, :]
+    inside = ((pos_x >= 0) & (pos_x < size_x * tile_rows))[:, None]
     field_now = jnp.where(inside, grad_ext / (illum_ext + damping), 0.0)
     for sweep_index in range(SWEEPS):
         padded = jnp.pad(field_now, 1)
@@ -113,25 +104,21 @@
             + (padded[2:, 1:-1, 1:-1] + padded[:-2, 1:-1, 1:-1])
         )
         field_now = jnp.where(inside, field_now + smooth_rate * (beside - 6.0 * field_now), 0.0)
-    updated_model = velocity - step_length * field_now[:, h : h + tile_rows, h : h + tile_cols]
+    updated_row = velocity_row - step_length * field_now[:, h : h + tile_rows, :]
+    updated_model = lax.dynamic_slice_in_dim(updated_row, me_y * tile_cols, tile_cols, axis=2)
 
-    tile_table = (
-        updated_model.reshape(levels, per_tile, patch_rows, tile_cols)
-        .transpose(1, 0, 2, 3)
+    row_table = (
+        updated_row.reshape(levels, per_tile, patch_rows, size_y, tile_cols)
+        .transpose(3, 1, 0, 2, 4)
         .astype(jnp.bfloat16)
     )
-    along_y = jnp.stack(
-        [tile_table] + [shifted(tile_table, "gy", size_y, step) for step in range(1, size_y)]
-    )
     along_x = jnp.stack(
-        [along_y] + [shifted(along_y, "gx", size_x, step) for step in range(1, size_x)]
+        [row_table] + [shifted(row_table, "gx", size_x, step) for step in range(1, size_x)]
     )
     whole = along_x.reshape(tiles * per_tile, levels, patch_rows, patch_cols)
     owner_x = owners // size_y
     owner_y = owners % size_y
-    back_row = (
-        ((me_x - owner_x) % size_x) * size_y + (me_y - owner_y) % size_y
-    ) * per_tile + patches
+    back_row = (((me_x - owner_x) % size_x) * size_y + owner_y) * per_tile + patches
     pick = (back_row[:, None] == jnp.arange(tiles * per_tile, dtype=jnp.int32)[None, :]).astype(
         jnp.bfloat16
     )

time: 48.7 us -> 54.3 us (1.11)
  waiting for transfers between devices: 18.5 us -> 28.5 us
  starting transfers between devices: 20.3 us -> 17.8 us
  local copies, waits for them, and re-layouts: 3.97 us -> 3 us
  other arithmetic: 4.15 us -> 3.3 us
    ppermute x15, waiting for transfers between devices: 18.5 us -> 28.5 us  [shifted(): lax.ppermute(value, axis, [(s, (s + step) % count) for s in range(count)])]
    ppermute x15, starting transfers between devices: 20.3 us -> 17.8 us  [shifted(): lax.ppermute(value, axis, [(s, (s + step) % count) for s in range(count)])]
    slice x13 -> x1, local copies, waits for them, and re-layouts: 1.08 us -> 0.08 us  [local(): updated_row = velocity_row - step_length * field_now[:, h:h + tile_rows, :]]
    unnamed x9 -> x7, local copies, waits for them, and re-layouts: 1.98 us -> 1.35 us
    dynamic_slice x0 -> x1, local copies, waits for them, and re-layouts: none -> 0.62 us  [local(): lax.dynamic_slice_in_dim(updated_row, me_y * tile_cols, tile_cols, axis=2)]
    gather x0 -> x1, local copies, waits for them, and re-layouts: none -> 0.56 us  [local(): jnp.take(velocity_seen, (me_y - jnp.arange(size_y)) % size_y, axis=0)]
  transfers between devices with their start and end apart: 15 -> 15, of which waited for: 14 -> 10; matrix products, arithmetic and copies ran while one was open for 5% -> 7% of each run, Pallas kernels for 0% -> 0%
where the time goes in v6:
time: 54.3 us; the launch traced here: 54.1 us
  waiting for transfers between devices  28.5 us (52%)
  starting transfers between devices  17.8 us (33%)
  other arithmetic  3.3 us (6%)
  local copies, waits for them, and re-layouts  3 us (6%)
  between operations  0.87 us (2%)
  matrix products  0.72 us (1%)
    ppermute x15, waiting for transfers between devices, shifted(): lax.ppermute(value, axis, [(s, (s + step) % count) for s in range(count)])  28.5 us
    ppermute x15, starting transfers between devices, shifted(): lax.ppermute(value, axis, [(s, (s + step) % count) for s in range(count)])  17.8 us
    select_n x1, other arithmetic, local(): kept = jnp.where(is_grad, slot_grad, slot_illum)  1.38 us
    unnamed x7, local copies, waits for them, and re-layouts  1.35 us
  transfers between devices with their start and end apart: 15, of which 10 were waited for; matrix products, arithmetic and copies ran while one was open for 7% of the time, Pallas kernels for 0%

profile of v6, /device:TPU:0, one launch (start us, length us, event | category | flops | bytes accessed | tf_op | source)
XLA Modules:
  0.0 54.1 jit_solution(4823049558342591172)
XLA Ops:
  0.6 3.1 %collective-permute-start = (f32[4,16,128]{2,1,0:T(8,128)}, f32[4,16,128]{2,1,0:T(8,128)S(1)}, u32[]{:S(2)}, u32[]{:S(2)}) collective-permute-start(f32[4,16,128]{2,1,0:T(8,128)} %param.9), channel_id=1, source_target_pairs={{0,1},{1,2},{2,3},{3,0},{4,5},{5,6},{6,7},{7,4},{8,9},{9,10},{10,1... | collective-permute-start | bytes 98312 | tf_op jit(solution)/shard_map/ppermute | solution.py:16
  3.7 2.6 %collective-permute-start.1 = (f32[4,16,128]{2,1,0:T(8,128)}, f32[4,16,128]{2,1,0:T(8,128)S(1)}, u32[]{:S(2)}, u32[]{:S(2)}) collective-permute-start(f32[4,16,128]{2,1,0:T(8,128)} %param.9), channel_id=1, source_target_pairs={{0,2},{1,3},{2,0},{3,1},{4,6},{5,7},{6,4},{7,5},{8,10},{9,11},{10,... | collective-permute-start | bytes 98312 | tf_op jit(solution)/shard_map/ppermute | solution.py:16
  6.3 0.7 %pad_add_fusion = s32[2,256]{1,0:T(2,128)S(1)} fusion(s32[1,256]{1,0:T(1,128)} %bitcast.68, s32[1,256]{1,0:T(1,128)} %bitcast.72), kind=kLoop, calls=%fused_computation.133 | loop fusion | flops 512 | bytes 4096 | tf_op jit(solution)/shard_map/stack | solution.py:41
  7.0 0.0 collective-permute-start.3
  7.0 0.0 copy-start.1
  7.0 0.0 copy-start.2
  7.0 1.4 %select_bitcast_fusion.1 = (bf16[256,4,2,128]{3,0,2,1:T(8,128)(2,1)S(1)}, bf16[256,4,2,128]{3,0,2,1:T(8,128)(2,1)S(1)}) fusion(pred[]{:T(512)S(6)} %eq.65, bf16[1,1,1,256,4,2,128]{6,5,4,3,2,1,0:T(2,128)(2,1)} %param.6, bf16[1,1,1,256,4,2,128]{6,5,4,3,2,1,0:T(2,128)(2,1)} %param.5), kind=kLoop, calls=%fused_computation.32 | loop fusion | flops 524288 | bytes 2097153 | tf_op jit(solution)/shard_map/jit(_where)/select_n | solution.py:39
  8.4 0.6 %collective-permute-start.4 = (bf16[256,4,2,128]{3,0,2,1:T(8,128)(2,1)S(1)}, bf16[256,4,2,128]{3,0,2,1:T(8,128)(2,1)S(1)}, u32[]{:S(2)}, u32[]{:S(2)}) collective-permute-start(bf16[256,4,2,128]{3,0,2,1:T(8,128)(2,1)S(1)} %get-tuple-element.13), channel_id=1, source_target_pairs={{0,16},{16,0},{1,17},{17,1},{2,18},{18,2},{3,19},{19,3},{4,20},{20... | collective-permute-start | bytes 1572872 | tf_op jit(solution)/shard_map/ppermute | solution.py:16
  9.0 0.0 collective-permute-done.3
  9.0 0.0 copy-done.1
  9.0 0.0 copy-done.2
  9.1 1.4 %collective-permute-done.4 = bf16[256,4,2,128]{3,0,2,1:T(8,128)(2,1)S(1)} collective-permute-done((bf16[256,4,2,128]{3,0,2,1:T(8,128)(2,1)S(1)}, bf16[256,4,2,128]{3,0,2,1:T(8,128)(2,1)S(1)}, u32[]{:S(2)}, u32[]{:S(2)}) %collective-permute-start.4) | collective-permute-done | bytes 524320 | tf_op jit(solution)/shard_map/ppermute | solution.py:16
  10.5 0.4 fusion.1
  10.9 0.0 copy-start
  11.0 1.6 %collective-permute-start.5 = (f32[48,4,2,128]{3,0,2,1:T(8,128)S(1)}, f32[48,4,2,128]{3,0,2,1:T(8,128)S(1)}, u32[]{:S(2)}, u32[]{:S(2)}) collective-permute-start(f32[48,4,2,128]{3,0,2,1:T(8,128)S(1)} %get-tuple-element.14), channel_id=1, source_target_pairs={{0,4},{4,8},{8,12},{12,0},{1,5},{5,9},{9,13},{13,1},{2,6},{6,10},{... | collective-permute-start | bytes 589832 | tf_op jit(solution)/shard_map/ppermute | solution.py:16
  12.5 1.5 %collective-permute-start.6 = (f32[48,4,2,128]{3,0,2,1:T(8,128)S(1)}, f32[48,4,2,128]{3,0,2,1:T(8,128)S(1)}, u32[]{:S(2)}, u32[]{:S(2)}) collective-permute-start(f32[48,4,2,128]{3,0,2,1:T(8,128)S(1)} %get-tuple-element.16), channel_id=1, source_target_pairs={{0,8},{4,12},{8,0},{12,4},{1,9},{5,13},{9,1},{13,5},{2,10},{6,14},... | collective-permute-start | bytes 589832 | tf_op jit(solution)/shard_map/ppermute | solution.py:16
  14.0 1.4 %collective-permute-start.7 = (f32[48,4,2,128]{3,0,2,1:T(8,128)S(1)}, f32[48,4,2,128]{3,0,2,1:T(8,128)S(1)}, u32[]{:S(2)}, u32[]{:S(2)}) collective-permute-start(f32[48,4,2,128]{3,0,2,1:T(8,128)S(1)} %get-tuple-element.15), channel_id=1, source_target_pairs={{0,12},{4,0},{8,4},{12,8},{1,13},{5,1},{9,5},{13,9},{2,14},{6,2},{... | collective-permute-start | bytes 589832 | tf_op jit(solution)/shard_map/ppermute | solution.py:16
  15.5 4.2 %collective-permute-done.5 = f32[48,4,2,128]{3,0,2,1:T(8,128)S(1)} collective-permute-done((f32[48,4,2,128]{3,0,2,1:T(8,128)S(1)}, f32[48,4,2,128]{3,0,2,1:T(8,128)S(1)}, u32[]{:S(2)}, u32[]{:S(2)}) %collective-permute-start.5) | collective-permute-done | bytes 196640 | tf_op jit(solution)/shard_map/ppermute | solution.py:16
  19.7 3.6 %collective-permute-done.6 = f32[48,4,2,128]{3,0,2,1:T(8,128)S(1)} collective-permute-done((f32[48,4,2,128]{3,0,2,1:T(8,128)S(1)}, f32[48,4,2,128]{3,0,2,1:T(8,128)S(1)}, u32[]{:S(2)}, u32[]{:S(2)}) %collective-permute-start.6) | collective-permute-done | bytes 196640 | tf_op jit(solution)/shard_map/ppermute | solution.py:16
  23.3 0.1 collective-permute-done.7
  23.5 1.4 %collective-permute-start.10 = (f32[48,4,2,128]{3,0,2,1:T(8,128)S(1)}, f32[48,4,2,128]{3,0,2,1:T(8,128)S(1)}, u32[]{:S(2)}, u32[]{:S(2)}) collective-permute-start(f32[48,4,2,128]{3,0,2,1:T(8,128)S(1)} %fusion.39), channel_id=1, source_target_pairs={{0,3},{1,0},{2,1},{3,2},{4,7},{5,4},{6,5},{7,6},{8,11},{9,8},{10,9... | collective-permute-start | bytes 589832 | tf_op jit(solution)/shard_map/ppermute | solution.py:16
  24.9 0.7 %collective-permute-start.8 = (f32[48,4,2,128]{3,0,2,1:T(8,128)S(1)}, f32[48,4,2,128]{3,0,2,1:T(8,128)S(1)}, u32[]{:S(2)}, u32[]{:S(2)}) collective-permute-start(f32[48,4,2,128]{3,0,2,1:T(8,128)S(1)} %fusion.39), channel_id=1, source_target_pairs={{0,1},{1,2},{2,3},{3,0},{4,5},{5,6},{6,7},{7,4},{8,9},{9,10},{10,1... | collective-permute-start | bytes 589832 | tf_op jit(solution)/shard_map/ppermute | solution.py:16
  25.5 0.3 collective-permute-start.9
  25.9 9.7 %collective-permute-done.10 = f32[48,4,2,128]{3,0,2,1:T(8,128)S(1)} collective-permute-done((f32[48,4,2,128]{3,0,2,1:T(8,128)S(1)}, f32[48,4,2,128]{3,0,2,1:T(8,128)S(1)}, u32[]{:S(2)}, u32[]{:S(2)}) %collective-permute-start.10) | collective-permute-done | bytes 196640 | tf_op jit(solution)/shard_map/ppermute | solution.py:16
  35.6 0.0 copy-done
  35.6 0.0 collective-permute-start.2
  35.6 0.0 collective-permute-done.8
  35.6 7.3 %collective-permute-done.9 = f32[48,4,2,128]{3,0,2,1:T(8,128)S(1)} collective-permute-done((f32[48,4,2,128]{3,0,2,1:T(8,128)S(1)}, f32[48,4,2,128]{3,0,2,1:T(8,128)S(1)}, u32[]{:S(2)}, u32[]{:S(2)}) %collective-permute-start.9) | collective-permute-done | bytes 196640 | tf_op jit(solution)/shard_map/ppermute | solution.py:16
  42.9 0.1 collective-permute-start.11
  43.0 0.1 slice.141
  43.1 0.0 collective-permute-done
  43.1 0.0 collective-permute-done.1
  43.1 0.0 collective-permute-done.2
  43.1 0.6 %gather_fusion = f32[4,4,16,128]{3,2,1,0:T(8,128)S(1)} fusion(f32[4,4,16,128]{3,2,1,0:T(8,128)S(1)} %pad_maximum_fusion.1, s32[1024]{0:T(1024)S(1)} %pad_clamp_fusion), kind=kCustom, calls=%fused_computation | custom fusion | bytes 262160 | tf_op jit(solution)/shard_map/jit(_take)/gather | solution.py:78
  43.7 0.7 %collective-permute-done.11 = f32[48,4,2,128]{3,0,2,1:T(8,128)S(1)} collective-permute-done((f32[48,4,2,128]{3,0,2,1:T(8,128)S(1)}, f32[48,4,2,128]{3,0,2,1:T(8,128)S(1)}, u32[]{:S(2)}, u32[]{:S(2)}) %collective-permute-start.11) | collective-permute-done | bytes 196640 | tf_op jit(solution)/shard_map/ppermute | solution.py:16
  44.5 0.1 copy.34
  44.6 0.1 copy.35
  44.7 0.1 div.43
  44.8 0.1 broadcast_select_fusion
  44.9 0.2 fusion.15
  45.1 0.2 fusion.24
  45.2 0.2 fusion.33
  45.4 0.2 fusion.36
  45.6 0.1 fusion.76
  45.8 1.3 %collective-permute-start.12 = (bf16[4,8,4,2,128]{4,1,0,3,2:T(8,128)(2,1)S(1)}, bf16[4,8,4,2,128]{4,1,0,3,2:T(8,128)(2,1)S(1)}, u32[]{:S(2)}, u32[]{:S(2)}) collective-permute-start(bf16[4,8,4,2,128]{4,1,0,3,2:T(8,128)(2,1)S(1)} %bitcast.57), channel_id=1, source_target_pairs={{0,4},{4,8},{8,12},{12,0},{1,5},{5,9},{9,13},{13,1},{2,6},{6,10},{... | collective-permute-start | bytes 196616 | tf_op jit(solution)/shard_map/ppermute | solution.py:16
  47.1 0.5 collective-permute-start.13
  47.6 2.7 %collective-permute-start.14 = (bf16[4,8,4,2,128]{4,1,0,3,2:T(8,128)(2,1)S(1)}, bf16[4,8,4,2,128]{4,1,0,3,2:T(8,128)(2,1)S(1)}, u32[]{:S(2)}, u32[]{:S(2)}) collective-permute-start(bf16[4,8,4,2,128]{4,1,0,3,2:T(8,128)(2,1)S(1)} %bitcast.59), channel_id=1, source_target_pairs={{0,12},{4,0},{8,4},{12,8},{1,13},{5,1},{9,5},{13,9},{2,14},{6,2},{... | collective-permute-start | bytes 196616 | tf_op jit(solution)/shard_map/ppermute | solution.py:16
  50.3 0.6 %constant_dynamic-slice_fusion = f32[4,16,128]{2,1,0:T(8,128)} fusion(f32[4,16,512]{2,1,0:T(8,128)S(1)} %get-tuple-element.9, s32[]{:T(128)S(6)} %select_n.220), kind=kLoop, calls=%fused_computation.157 | loop fusion | bytes 65540 | tf_op jit(solution)/shard_map/dynamic_slice | solution.py:108
  51.0 0.4 collective-permute-done.12
  51.4 0.9 %collective-permute-done.13 = bf16[4,8,4,2,128]{4,1,0,3,2:T(8,128)(2,1)S(1)} collective-permute-done((bf16[4,8,4,2,128]{4,1,0,3,2:T(8,128)(2,1)S(1)}, bf16[4,8,4,2,128]{4,1,0,3,2:T(8,128)(2,1)S(1)}, u32[]{:S(2)}, u32[]{:S(2)}) %collective-permute-start.13) | collective-permute-done | bytes 65568 | tf_op jit(solution)/shard_map/ppermute | solution.py:16
  52.3 0.1 collective-permute-done.14
  52.4 0.3 fusion
  52.8 1.3 %copy.40 = bf16[1,1,1,256,4,2,128]{6,5,4,3,2,1,0:T(2,128)(2,1)} copy(bf16[1,1,1,256,4,2,128]{6,3,5,4,2,1,0:T(8,128)(2,1)S(1)} %fusion) | data formatting | bytes 1048576
  (16 shorter events, 0.4 us)
Async XLA Ops:
  0.6 42.4 %collective-permute-start = (f32[4,16,128]{2,1,0:T(8,128)}, f32[4,16,128]{2,1,0:T(8,128)S(1)}, u32[]{:S(2)}, u32[]{:S(2)}) collective-permute-start(f32[4,16,128]{2,1,0:T(8,128)} %param.9), channel_id=1, source_target_pairs={{0,1},{1,2},{2,3},{3,0},{4,5},{5,6},{6,7},{7,4},{8,9},{9,10},{10,1... | collective-permute-start | bytes 98312 | tf_op jit(solution)/shard_map/ppermute | solution.py:16
  3.7 39.4 %collective-permute-start.1 = (f32[4,16,128]{2,1,0:T(8,128)}, f32[4,16,128]{2,1,0:T(8,128)S(1)}, u32[]{:S(2)}, u32[]{:S(2)}) collective-permute-start(f32[4,16,128]{2,1,0:T(8,128)} %param.9), channel_id=1, source_target_pairs={{0,2},{1,3},{2,0},{3,1},{4,6},{5,7},{6,4},{7,5},{8,10},{9,11},{10,... | collective-permute-start | bytes 98312 | tf_op jit(solution)/shard_map/ppermute | solution.py:16
  7.0 2.0 %collective-permute-start.3 = (s32[2,256]{1,0:T(2,128)S(1)}, s32[2,256]{1,0:T(2,128)S(1)}, u32[]{:S(2)}, u32[]{:S(2)}) collective-permute-start(s32[2,256]{1,0:T(2,128)S(1)} %pad_add_fusion), channel_id=1, source_target_pairs={{0,16},{16,0},{1,17},{17,1},{2,18},{18,2},{3,19},{19,3},{4,20},{20... | collective-permute-start | bytes 6152 | tf_op jit(solution)/shard_map/ppermute | solution.py:16
  7.0 2.0 %copy-start.1 = (s32[1,1,1,256]{3,2,1,0:T(1,128)S(1)}, s32[1,1,1,256]{3,2,1,0:T(1,128)}, u32[]{:S(2)}) copy-start(s32[1,1,1,256]{3,2,1,0:T(1,128)} %param.8) | copy-start | bytes 3076
  7.0 2.0 %copy-start.2 = (s32[1,1,1,256]{3,2,1,0:T(1,128)S(1)}, s32[1,1,1,256]{3,2,1,0:T(1,128)}, u32[]{:S(2)}) copy-start(s32[1,1,1,256]{3,2,1,0:T(1,128)} %param.7) | copy-start | bytes 3076
  8.4 2.1 %collective-permute-start.4 = (bf16[256,4,2,128]{3,0,2,1:T(8,128)(2,1)S(1)}, bf16[256,4,2,128]{3,0,2,1:T(8,128)(2,1)S(1)}, u32[]{:S(2)}, u32[]{:S(2)}) collective-permute-start(bf16[256,4,2,128]{3,0,2,1:T(8,128)(2,1)S(1)} %get-tuple-element.13), channel_id=1, source_target_pairs={{0,16},{16,0},{1,17},{17,1},{2,18},{18,2},{3,19},{19,3},{4,20},{20... | collective-permute-start | bytes 1572872 | tf_op jit(solution)/shard_map/ppermute | solution.py:16
  10.9 24.6 %copy-start = (f32[4,16,128]{2,1,0:T(8,128)S(1)}, f32[4,16,128]{2,1,0:T(8,128)}, u32[]{:S(2)}) copy-start(f32[4,16,128]{2,1,0:T(8,128)} %param.9) | copy-start | bytes 98308
  11.0 8.7 %collective-permute-start.5 = (f32[48,4,2,128]{3,0,2,1:T(8,128)S(1)}, f32[48,4,2,128]{3,0,2,1:T(8,128)S(1)}, u32[]{:S(2)}, u32[]{:S(2)}) collective-permute-start(f32[48,4,2,128]{3,0,2,1:T(8,128)S(1)} %get-tuple-element.14), channel_id=1, source_target_pairs={{0,4},{4,8},{8,12},{12,0},{1,5},{5,9},{9,13},{13,1},{2,6},{6,10},{... | collective-permute-start | bytes 589832 | tf_op jit(solution)/shard_map/ppermute | solution.py:16
  12.5 10.8 %collective-permute-start.6 = (f32[48,4,2,128]{3,0,2,1:T(8,128)S(1)}, f32[48,4,2,128]{3,0,2,1:T(8,128)S(1)}, u32[]{:S(2)}, u32[]{:S(2)}) collective-permute-start(f32[48,4,2,128]{3,0,2,1:T(8,128)S(1)} %get-tuple-element.16), channel_id=1, source_target_pairs={{0,8},{4,12},{8,0},{12,4},{1,9},{5,13},{9,1},{13,5},{2,10},{6,14},... | collective-permute-start | bytes 589832 | tf_op jit(solution)/shard_map/ppermute | solution.py:16
  14.0 9.4 %collective-permute-start.7 = (f32[48,4,2,128]{3,0,2,1:T(8,128)S(1)}, f32[48,4,2,128]{3,0,2,1:T(8,128)S(1)}, u32[]{:S(2)}, u32[]{:S(2)}) collective-permute-start(f32[48,4,2,128]{3,0,2,1:T(8,128)S(1)} %get-tuple-element.15), channel_id=1, source_target_pairs={{0,12},{4,0},{8,4},{12,8},{1,13},{5,1},{9,5},{13,9},{2,14},{6,2},{... | collective-permute-start | bytes 589832 | tf_op jit(solution)/shard_map/ppermute | solution.py:16
  23.5 12.1 %collective-permute-start.10 = (f32[48,4,2,128]{3,0,2,1:T(8,128)S(1)}, f32[48,4,2,128]{3,0,2,1:T(8,128)S(1)}, u32[]{:S(2)}, u32[]{:S(2)}) collective-permute-start(f32[48,4,2,128]{3,0,2,1:T(8,128)S(1)} %fusion.39), channel_id=1, source_target_pairs={{0,3},{1,0},{2,1},{3,2},{4,7},{5,4},{6,5},{7,6},{8,11},{9,8},{10,9... | collective-permute-start | bytes 589832 | tf_op jit(solution)/shard_map/ppermute | solution.py:16
  24.9 10.7 %collective-permute-start.8 = (f32[48,4,2,128]{3,0,2,1:T(8,128)S(1)}, f32[48,4,2,128]{3,0,2,1:T(8,128)S(1)}, u32[]{:S(2)}, u32[]{:S(2)}) collective-permute-start(f32[48,4,2,128]{3,0,2,1:T(8,128)S(1)} %fusion.39), channel_id=1, source_target_pairs={{0,1},{1,2},{2,3},{3,0},{4,5},{5,6},{6,7},{7,4},{8,9},{9,10},{10,1... | collective-permute-start | bytes 589832 | tf_op jit(solution)/shard_map/ppermute | solution.py:16
  25.5 17.3 %collective-permute-start.9 = (f32[48,4,2,128]{3,0,2,1:T(8,128)S(1)}, f32[48,4,2,128]{3,0,2,1:T(8,128)S(1)}, u32[]{:S(2)}, u32[]{:S(2)}) collective-permute-start(f32[48,4,2,128]{3,0,2,1:T(8,128)S(1)} %fusion.39), channel_id=1, source_target_pairs={{0,2},{1,3},{2,0},{3,1},{4,6},{5,7},{6,4},{7,5},{8,10},{9,11},{10,... | collective-permute-start | bytes 589832 | tf_op jit(solution)/shard_map/ppermute | solution.py:16
  35.6 7.5 %collective-permute-start.2 = (f32[4,16,128]{2,1,0:T(8,128)S(1)}, f32[4,16,128]{2,1,0:T(8,128)S(1)}, u32[]{:S(2)}, u32[]{:S(2)}) collective-permute-start(f32[4,16,128]{2,1,0:T(8,128)S(1)} %copy-done), channel_id=1, source_target_pairs={{0,3},{1,0},{2,1},{3,2},{4,7},{5,4},{6,5},{7,6},{8,11},{9,8},{10,9... | collective-permute-start | bytes 98312 | tf_op jit(solution)/shard_map/ppermute | solution.py:16
  42.9 1.5 %collective-permute-start.11 = (f32[48,4,2,128]{3,0,2,1:T(8,128)S(1)}, f32[48,4,2,128]{3,0,2,1:T(8,128)S(1)}, u32[]{:S(2)}, u32[]{:S(2)}) collective-permute-start(f32[48,4,2,128]{3,0,2,1:T(8,128)S(1)} %add_add_fusion), channel_id=1, source_target_pairs={{0,16},{16,0},{1,17},{17,1},{2,18},{18,2},{3,19},{19,3},{4,20},{20... | collective-permute-start | bytes 589832 | tf_op jit(solution)/shard_map/ppermute | solution.py:16
  45.8 5.6 %collective-permute-start.12 = (bf16[4,8,4,2,128]{4,1,0,3,2:T(8,128)(2,1)S(1)}, bf16[4,8,4,2,128]{4,1,0,3,2:T(8,128)(2,1)S(1)}, u32[]{:S(2)}, u32[]{:S(2)}) collective-permute-start(bf16[4,8,4,2,128]{4,1,0,3,2:T(8,128)(2,1)S(1)} %bitcast.57), channel_id=1, source_target_pairs={{0,4},{4,8},{8,12},{12,0},{1,5},{5,9},{9,13},{13,1},{2,6},{6,10},{... | collective-permute-start | bytes 196616 | tf_op jit(solution)/shard_map/ppermute | solution.py:16
  47.1 5.2 %collective-permute-start.13 = (bf16[4,8,4,2,128]{4,1,0,3,2:T(8,128)(2,1)S(1)}, bf16[4,8,4,2,128]{4,1,0,3,2:T(8,128)(2,1)S(1)}, u32[]{:S(2)}, u32[]{:S(2)}) collective-permute-start(bf16[4,8,4,2,128]{4,1,0,3,2:T(8,128)(2,1)S(1)} %bitcast.58), channel_id=1, source_target_pairs={{0,8},{4,12},{8,0},{12,4},{1,9},{5,13},{9,1},{13,5},{2,10},{6,14},... | collective-permute-start | bytes 196616 | tf_op jit(solution)/shard_map/ppermute | solution.py:16
  47.6 4.8 %collective-permute-start.14 = (bf16[4,8,4,2,128]{4,1,0,3,2:T(8,128)(2,1)S(1)}, bf16[4,8,4,2,128]{4,1,0,3,2:T(8,128)(2,1)S(1)}, u32[]{:S(2)}, u32[]{:S(2)}) collective-permute-start(bf16[4,8,4,2,128]{4,1,0,3,2:T(8,128)(2,1)S(1)} %bitcast.59), channel_id=1, source_target_pairs={{0,12},{4,0},{8,4},{12,8},{1,13},{5,1},{9,5},{13,9},{2,14},{6,2},{... | collective-permute-start | bytes 196616 | tf_op jit(solution)/shard_map/ppermute | solution.py:16

commit v7 on v4

--- a/solution.py
+++ b/solution.py
@@ -132,12 +132,16 @@
     back_row = (
         ((me_x - owner_x) % size_x) * size_y + (me_y - owner_y) % size_y
     ) * per_tile + patches
-    pick = (back_row[:, None] == jnp.arange(tiles * per_tile, dtype=jnp.int32)[None, :]).astype(
-        jnp.bfloat16
-    )
-    returned = jnp.einsum("wr,rlpc->wlpc", pick, whole, preferred_element_type=jnp.float32).astype(
-        jnp.bfloat16
-    )
+    rows_per_window = levels * patch_rows
+    target = (
+        back_row[:, None] * rows_per_window + jnp.arange(rows_per_window, dtype=jnp.int32)[None, :]
+    ).reshape(-1)
+    pick = (
+        target[:, None] == jnp.arange(tiles * per_tile * rows_per_window, dtype=jnp.int32)[None, :]
+    ).astype(jnp.bfloat16)
+    returned = jnp.dot(
+        pick, whole.reshape(-1, patch_cols), preferred_element_type=jnp.float32
+    ).astype(jnp.bfloat16)
     returned_windows = returned.reshape((1, 1, 1, slot_count, levels, patch_rows, patch_cols))
     return (updated_model, returned_windows)
 

time: 48.7 us -> 50 us (1.027)
  matrix products: 0.71 us -> 2.76 us
  local copies, waits for them, and re-layouts: 3.97 us -> 2.75 us
  other arithmetic: 4.15 us -> 4.9 us
    dot_general x1, matrix products: 0.34 us -> 2.39 us  [local(): jnp.dot(pick, whole.reshape(-1, patch_cols), preferred_element_type=jnp.f...]
    unnamed x9 -> x8, local copies, waits for them, and re-layouts: 1.98 us -> 0.65 us
    another operation x2, other arithmetic: 0.05 us -> 0.58 us  [local(): jnp.stack([along_y] + [shifted(along_y, 'gx', size_x, step) for step in r...]
where the time goes in v7:
time: 50 us; the launch traced here: 49.8 us
  starting transfers between devices  20.3 us (41%)
  waiting for transfers between devices  18.2 us (36%)
  other arithmetic  4.9 us (10%)
  matrix products  2.76 us (6%)
  local copies, waits for them, and re-layouts  2.75 us (6%)
  between operations  0.93 us (2%)
    ppermute x15, starting transfers between devices, shifted(): lax.ppermute(value, axis, [(s, (s + step) % count) for s in range(count)])  20.3 us
    ppermute x15, waiting for transfers between devices, shifted(): lax.ppermute(value, axis, [(s, (s + step) % count) for s in range(count)])  18.2 us
    dot_general x1, matrix products, local(): jnp.dot(pick, whole.reshape(-1, patch_cols), preferred_element_type=jnp.f...  2.39 us
    select_n x1, other arithmetic, local(): kept = jnp.where(is_grad, slot_grad, slot_illum)  1.39 us
  transfers between devices with their start and end apart: 15, of which 14 were waited for; matrix products, arithmetic and copies ran while one was open for 5% of the time, Pallas kernels for 0%

profile of v7, /device:TPU:0, one launch (start us, length us, event | category | flops | bytes accessed | tf_op | source)
XLA Modules:
  0.0 49.8 jit_solution(8013409409493619828)
XLA Ops:
  0.6 0.7 %pad_add_fusion = s32[2,256]{1,0:T(2,128)S(1)} fusion(s32[1,256]{1,0:T(1,128)} %bitcast.77, s32[1,256]{1,0:T(1,128)} %bitcast.83), kind=kLoop, calls=%fused_computation.149 | loop fusion | flops 512 | bytes 4096 | tf_op jit(solution)/shard_map/stack | solution.py:42
  1.3 0.5 collective-permute-start
  1.8 0.0 copy-start.1
  1.8 0.0 copy-start.2
  1.8 1.4 %select_bitcast_fusion.1 = (bf16[256,4,2,128]{3,0,2,1:T(8,128)(2,1)S(1)}, bf16[256,4,2,128]{3,0,2,1:T(8,128)(2,1)S(1)}) fusion(pred[]{:T(512)S(6)} %eq.65, bf16[1,1,1,256,4,2,128]{6,5,4,3,2,1,0:T(2,128)(2,1)} %param.6, bf16[1,1,1,256,4,2,128]{6,5,4,3,2,1,0:T(2,128)(2,1)} %param.5), kind=kLoop, calls=%fused_computation.9 | loop fusion | flops 524288 | bytes 2097153 | tf_op jit(solution)/shard_map/jit(_where)/select_n | solution.py:40
  3.2 0.1 collective-permute-start.1
  3.3 0.0 collective-permute-done
  3.3 0.0 copy-done.1
  3.3 0.0 copy-done.2
  3.4 1.8 %collective-permute-done.1 = bf16[256,4,2,128]{3,0,2,1:T(8,128)(2,1)S(1)} collective-permute-done((bf16[256,4,2,128]{3,0,2,1:T(8,128)(2,1)S(1)}, bf16[256,4,2,128]{3,0,2,1:T(8,128)(2,1)S(1)}, u32[]{:S(2)}, u32[]{:S(2)}) %collective-permute-start.1) | collective-permute-done | bytes 524320 | tf_op jit(solution)/shard_map/ppermute | solution.py:16
  5.2 0.4 fusion.3
  5.6 2.7 %collective-permute-start.2 = (f32[48,4,2,128]{3,0,2,1:T(8,128)S(1)}, f32[48,4,2,128]{3,0,2,1:T(8,128)S(1)}, u32[]{:S(2)}, u32[]{:S(2)}) collective-permute-start(f32[48,4,2,128]{3,0,2,1:T(8,128)S(1)} %get-tuple-element.15), channel_id=1, source_target_pairs={{0,4},{4,8},{8,12},{12,0},{1,5},{5,9},{9,13},{13,1},{2,6},{6,10},{... | collective-permute-start | bytes 589832 | tf_op jit(solution)/shard_map/ppermute | solution.py:16
  8.3 1.5 %collective-permute-start.3 = (f32[48,4,2,128]{3,0,2,1:T(8,128)S(1)}, f32[48,4,2,128]{3,0,2,1:T(8,128)S(1)}, u32[]{:S(2)}, u32[]{:S(2)}) collective-permute-start(f32[48,4,2,128]{3,0,2,1:T(8,128)S(1)} %get-tuple-element.17), channel_id=1, source_target_pairs={{0,8},{4,12},{8,0},{12,4},{1,9},{5,13},{9,1},{13,5},{2,10},{6,14},... | collective-permute-start | bytes 589832 | tf_op jit(solution)/shard_map/ppermute | solution.py:16
  9.8 1.4 %collective-permute-start.4 = (f32[48,4,2,128]{3,0,2,1:T(8,128)S(1)}, f32[48,4,2,128]{3,0,2,1:T(8,128)S(1)}, u32[]{:S(2)}, u32[]{:S(2)}) collective-permute-start(f32[48,4,2,128]{3,0,2,1:T(8,128)S(1)} %get-tuple-element.16), channel_id=1, source_target_pairs={{0,12},{4,0},{8,4},{12,8},{1,13},{5,1},{9,5},{13,9},{2,14},{6,2},{... | collective-permute-start | bytes 589832 | tf_op jit(solution)/shard_map/ppermute | solution.py:16
  11.3 3.8 %collective-permute-done.2 = f32[48,4,2,128]{3,0,2,1:T(8,128)S(1)} collective-permute-done((f32[48,4,2,128]{3,0,2,1:T(8,128)S(1)}, f32[48,4,2,128]{3,0,2,1:T(8,128)S(1)}, u32[]{:S(2)}, u32[]{:S(2)}) %collective-permute-start.2) | collective-permute-done | bytes 196640 | tf_op jit(solution)/shard_map/ppermute | solution.py:16
  15.0 3.9 %collective-permute-done.3 = f32[48,4,2,128]{3,0,2,1:T(8,128)S(1)} collective-permute-done((f32[48,4,2,128]{3,0,2,1:T(8,128)S(1)}, f32[48,4,2,128]{3,0,2,1:T(8,128)S(1)}, u32[]{:S(2)}, u32[]{:S(2)}) %collective-permute-start.3) | collective-permute-done | bytes 196640 | tf_op jit(solution)/shard_map/ppermute | solution.py:16
  18.9 0.3 collective-permute-done.4
  19.3 0.1 copy.27
  19.4 0.1 copy.28
  19.5 0.1 copy.30
  19.6 0.5 fusion.11
  20.1 0.3 reshape.537
  20.4 0.2 reshape_reshape.6
  20.6 0.6 %slice_reduce_fusion.3 = (f32[13056]{0:T(1024)S(1)}, f32[13056]{0:T(1024)S(1)}, f32[13056]{0:T(1024)S(1)}, f32[13056]{0:T(1024)S(1)}) fusion(f32[4,13056]{1,0:T(4,128)S(1)} %constant_dynamic-update-slice_fusion), kind=kLoop, calls=%fused_computation.93 | loop fusion | bytes 417792 | tf_op jit(solution)/shard_map/slice | solution.py:86
  21.2 1.6 %collective-permute-start.5 = (f32[102,128]{1,0:T(8,128)S(1)}, f32[102,128]{1,0:T(8,128)S(1)}, u32[]{:S(2)}, u32[]{:S(2)}) collective-permute-start(f32[102,128]{1,0:T(8,128)S(1)} %bitcast.76), channel_id=1, source_target_pairs={{0,1},{1,2},{2,3},{3,0},{4,5},{5,6},{6,7},{7,4},{8,9},{9,10},{10,1... | collective-permute-start | bytes 156680 | tf_op jit(solution)/shard_map/ppermute | solution.py:16
  22.8 2.6 %collective-permute-start.6 = (f32[102,128]{1,0:T(8,128)S(1)}, f32[102,128]{1,0:T(8,128)S(1)}, u32[]{:S(2)}, u32[]{:S(2)}) collective-permute-start(f32[102,128]{1,0:T(8,128)S(1)} %bitcast.75), channel_id=1, source_target_pairs={{0,2},{1,3},{2,0},{3,1},{4,6},{5,7},{6,4},{7,5},{8,10},{9,11},{10,... | collective-permute-start | bytes 156680 | tf_op jit(solution)/shard_map/ppermute | solution.py:16
  25.4 1.3 %collective-permute-start.7 = (f32[102,128]{1,0:T(8,128)S(1)}, f32[102,128]{1,0:T(8,128)S(1)}, u32[]{:S(2)}, u32[]{:S(2)}) collective-permute-start(f32[102,128]{1,0:T(8,128)S(1)} %bitcast.74), channel_id=1, source_target_pairs={{0,3},{1,0},{2,1},{3,2},{4,7},{5,4},{6,5},{7,6},{8,11},{9,8},{10,9... | collective-permute-start | bytes 156680 | tf_op jit(solution)/shard_map/ppermute | solution.py:16
  26.8 0.1 broadcast_and_fusion
  26.8 0.6 %collective-permute-done.5 = f32[102,128]{1,0:T(8,128)S(1)} collective-permute-done((f32[102,128]{1,0:T(8,128)S(1)}, f32[102,128]{1,0:T(8,128)S(1)}, u32[]{:S(2)}, u32[]{:S(2)}) %collective-permute-start.5) | collective-permute-done | bytes 52256 | tf_op jit(solution)/shard_map/ppermute | solution.py:16
  27.5 2.0 %collective-permute-done.6 = f32[102,128]{1,0:T(8,128)S(1)} collective-permute-done((f32[102,128]{1,0:T(8,128)S(1)}, f32[102,128]{1,0:T(8,128)S(1)}, u32[]{:S(2)}, u32[]{:S(2)}) %collective-permute-start.6) | collective-permute-done | bytes 52256 | tf_op jit(solution)/shard_map/ppermute | solution.py:16
  29.5 0.3 collective-permute-done.7
  29.8 0.1 collective-permute-start.8
  29.9 0.1 slice.255
  30.0 1.1 %collective-permute-done.8 = f32[102,128]{1,0:T(8,128)S(1)} collective-permute-done((f32[102,128]{1,0:T(8,128)S(1)}, f32[102,128]{1,0:T(8,128)S(1)}, u32[]{:S(2)}, u32[]{:S(2)}) %collective-permute-start.8) | collective-permute-done | bytes 52256 | tf_op jit(solution)/shard_map/ppermute | solution.py:16
  31.2 0.1 reshape.538
  31.3 0.1 reshape.540
  31.4 0.2 fusion.85
  31.6 0.4 fusion.46
  32.0 0.0 copy-start
  32.1 0.2 fusion.23
  32.3 0.2 fusion.32
  32.5 0.2 fusion.41
  32.7 0.2 fusion.44
  32.8 0.0 copy-done
  32.9 0.2 fusion.81
  33.0 1.0 %collective-permute-start.9 = (bf16[8,4,2,128]{3,2,1,0:T(2,128)(2,1)S(1)}, bf16[8,4,2,128]{3,2,1,0:T(2,128)(2,1)S(1)}, u32[]{:S(2)}, u32[]{:S(2)}) collective-permute-start(bf16[8,4,2,128]{3,2,1,0:T(2,128)(2,1)S(1)} %bitcast.59), channel_id=1, source_target_pairs={{0,1},{1,2},{2,3},{3,0},{4,5},{5,6},{6,7},{7,4},{8,9},{9,10},{10,1... | collective-permute-start | bytes 49160 | tf_op jit(solution)/shard_map/ppermute | solution.py:16
  34.1 2.5 %collective-permute-start.10 = (bf16[8,4,2,128]{3,2,1,0:T(2,128)(2,1)S(1)}, bf16[8,4,2,128]{3,2,1,0:T(2,128)(2,1)S(1)}, u32[]{:S(2)}, u32[]{:S(2)}) collective-permute-start(bf16[8,4,2,128]{3,2,1,0:T(2,128)(2,1)S(1)} %bitcast.60), channel_id=1, source_target_pairs={{0,2},{1,3},{2,0},{3,1},{4,6},{5,7},{6,4},{7,5},{8,10},{9,11},{10,... | collective-permute-start | bytes 49160 | tf_op jit(solution)/shard_map/ppermute | solution.py:16
  36.6 0.5 %collective-permute-start.11 = (bf16[8,4,2,128]{3,2,1,0:T(2,128)(2,1)S(1)}, bf16[8,4,2,128]{3,2,1,0:T(2,128)(2,1)S(1)}, u32[]{:S(2)}, u32[]{:S(2)}) collective-permute-start(bf16[8,4,2,128]{3,2,1,0:T(2,128)(2,1)S(1)} %bitcast.61), channel_id=1, source_target_pairs={{0,3},{1,0},{2,1},{3,2},{4,7},{5,4},{6,5},{7,6},{8,11},{9,8},{10,9... | collective-permute-start | bytes 49160 | tf_op jit(solution)/shard_map/ppermute | solution.py:16
  37.1 0.1 iota_add_fusion
  37.2 0.1 add.402
  37.3 0.6 %copy.35 = f32[4,16,128]{2,1,0:T(8,128)} copy(f32[4,16,128]{2,0,1:T(4,128)S(1)} %get-tuple-element.9) | data formatting | bytes 65536
  37.9 0.8 %collective-permute-done.9 = bf16[8,4,2,128]{3,2,1,0:T(2,128)(2,1)S(1)} collective-permute-done((bf16[8,4,2,128]{3,2,1,0:T(2,128)(2,1)S(1)}, bf16[8,4,2,128]{3,2,1,0:T(2,128)(2,1)S(1)}, u32[]{:S(2)}, u32[]{:S(2)}) %collective-permute-start.9) | collective-permute-done | bytes 16416 | tf_op jit(solution)/shard_map/ppermute | solution.py:16
  38.7 0.3 collective-permute-done.10
  39.0 1.3 %collective-permute-done.11 = bf16[8,4,2,128]{3,2,1,0:T(2,128)(2,1)S(1)} collective-permute-done((bf16[8,4,2,128]{3,2,1,0:T(2,128)(2,1)S(1)}, bf16[8,4,2,128]{3,2,1,0:T(2,128)(2,1)S(1)}, u32[]{:S(2)}, u32[]{:S(2)}) %collective-permute-start.11) | collective-permute-done | bytes 16416 | tf_op jit(solution)/shard_map/ppermute | solution.py:16
  40.3 0.1 pad_maximum_fusion.3
  40.4 1.8 %collective-permute-start.12 = (bf16[4,8,4,2,128]{4,3,2,1,0:T(2,128)(2,1)S(1)}, bf16[4,8,4,2,128]{4,3,2,1,0:T(2,128)(2,1)S(1)}, u32[]{:S(2)}, u32[]{:S(2)}) collective-permute-start(bf16[4,8,4,2,128]{4,3,2,1,0:T(2,128)(2,1)S(1)} %pad_maximum_fusion.3), channel_id=1, source_target_pairs={{0,4},{4,8},{8,12},{12,0},{1,5},{5,9},{9,13},{13,1},{2,6},{6,10},{... | collective-permute-start | bytes 196616 | tf_op jit(solution)/shard_map/ppermute | solution.py:16
  42.2 0.5 %collective-permute-start.13 = (bf16[4,8,4,2,128]{4,3,2,1,0:T(2,128)(2,1)S(1)}, bf16[4,8,4,2,128]{4,3,2,1,0:T(2,128)(2,1)S(1)}, u32[]{:S(2)}, u32[]{:S(2)}) collective-permute-start(bf16[4,8,4,2,128]{4,3,2,1,0:T(2,128)(2,1)S(1)} %pad_maximum_fusion.3), channel_id=1, source_target_pairs={{0,8},{4,12},{8,0},{12,4},{1,9},{5,13},{9,1},{13,5},{2,10},{6,14},... | collective-permute-start | bytes 196616 | tf_op jit(solution)/shard_map/ppermute | solution.py:16
  42.7 2.1 %collective-permute-start.14 = (bf16[4,8,4,2,128]{4,3,2,1,0:T(2,128)(2,1)S(1)}, bf16[4,8,4,2,128]{4,3,2,1,0:T(2,128)(2,1)S(1)}, u32[]{:S(2)}, u32[]{:S(2)}) collective-permute-start(bf16[4,8,4,2,128]{4,3,2,1,0:T(2,128)(2,1)S(1)} %pad_maximum_fusion.3), channel_id=1, source_target_pairs={{0,12},{4,0},{8,4},{12,8},{1,13},{5,1},{9,5},{13,9},{2,14},{6,2},{... | collective-permute-start | bytes 196616 | tf_op jit(solution)/shard_map/ppermute | solution.py:16
  44.8 0.1 fusion.89
  44.9 0.7 %collective-permute-done.12 = bf16[4,8,4,2,128]{4,3,2,1,0:T(2,128)(2,1)S(1)} collective-permute-done((bf16[4,8,4,2,128]{4,3,2,1,0:T(2,128)(2,1)S(1)}, bf16[4,8,4,2,128]{4,3,2,1,0:T(2,128)(2,1)S(1)}, u32[]{:S(2)}, u32[]{:S(2)}) %collective-permute-start.12) | collective-permute-done | bytes 65568 | tf_op jit(solution)/shard_map/ppermute | solution.py:16
  45.6 0.8 %collective-permute-done.13 = bf16[4,8,4,2,128]{4,3,2,1,0:T(2,128)(2,1)S(1)} collective-permute-done((bf16[4,8,4,2,128]{4,3,2,1,0:T(2,128)(2,1)S(1)}, bf16[4,8,4,2,128]{4,3,2,1,0:T(2,128)(2,1)S(1)}, u32[]{:S(2)}, u32[]{:S(2)}) %collective-permute-start.13) | collective-permute-done | bytes 65568 | tf_op jit(solution)/shard_map/ppermute | solution.py:16
  46.4 0.5 %collective-permute-done.14 = bf16[4,8,4,2,128]{4,3,2,1,0:T(2,128)(2,1)S(1)} collective-permute-done((bf16[4,8,4,2,128]{4,3,2,1,0:T(2,128)(2,1)S(1)}, bf16[4,8,4,2,128]{4,3,2,1,0:T(2,128)(2,1)S(1)}, u32[]{:S(2)}, u32[]{:S(2)}) %collective-permute-start.14) | collective-permute-done | bytes 65568 | tf_op jit(solution)/shard_map/ppermute | solution.py:16
  46.9 0.5 pad_maximum_fusion
  47.4 2.4 %fusion.2 = bf16[2048,128]{1,0:T(8,128)(2,1)} fusion(bf16[1024,128]{1,0:T(8,128)(2,1)S(1)} %bitcast.56, s32[2048]{0:T(1024)S(1)} %add.402), kind=kOutput, calls=%fused_computation.3 | convolution fusion | flops 539230208 | bytes 794624 | tf_op jit(solution)/shard_map/dot_general | solution.py:142
  (23 shorter events, 0.4 us)
Async XLA Ops:
  1.3 2.0 %collective-permute-start = (s32[2,256]{1,0:T(2,128)S(1)}, s32[2,256]{1,0:T(2,128)S(1)}, u32[]{:S(2)}, u32[]{:S(2)}) collective-permute-start(s32[2,256]{1,0:T(2,128)S(1)} %pad_add_fusion), channel_id=1, source_target_pairs={{0,16},{16,0},{1,17},{17,1},{2,18},{18,2},{3,19},{19,3},{4,20},{20... | collective-permute-start | bytes 6152 | tf_op jit(solution)/shard_map/ppermute | solution.py:16
  1.8 1.5 %copy-start.1 = (s32[1,1,1,256]{3,2,1,0:T(1,128)S(1)}, s32[1,1,1,256]{3,2,1,0:T(1,128)}, u32[]{:S(2)}) copy-start(s32[1,1,1,256]{3,2,1,0:T(1,128)} %param.8) | copy-start | bytes 3076
  1.8 1.5 %copy-start.2 = (s32[1,1,1,256]{3,2,1,0:T(1,128)S(1)}, s32[1,1,1,256]{3,2,1,0:T(1,128)}, u32[]{:S(2)}) copy-start(s32[1,1,1,256]{3,2,1,0:T(1,128)} %param.7) | copy-start | bytes 3076
  3.2 2.0 %collective-permute-start.1 = (bf16[256,4,2,128]{3,0,2,1:T(8,128)(2,1)S(1)}, bf16[256,4,2,128]{3,0,2,1:T(8,128)(2,1)S(1)}, u32[]{:S(2)}, u32[]{:S(2)}) collective-permute-start(bf16[256,4,2,128]{3,0,2,1:T(8,128)(2,1)S(1)} %get-tuple-element.14), channel_id=1, source_target_pairs={{0,16},{16,0},{1,17},{17,1},{2,18},{18,2},{3,19},{19,3},{4,20},{20... | collective-permute-start | bytes 1572872 | tf_op jit(solution)/shard_map/ppermute | solution.py:16
  5.6 9.4 %collective-permute-start.2 = (f32[48,4,2,128]{3,0,2,1:T(8,128)S(1)}, f32[48,4,2,128]{3,0,2,1:T(8,128)S(1)}, u32[]{:S(2)}, u32[]{:S(2)}) collective-permute-start(f32[48,4,2,128]{3,0,2,1:T(8,128)S(1)} %get-tuple-element.15), channel_id=1, source_target_pairs={{0,4},{4,8},{8,12},{12,0},{1,5},{5,9},{9,13},{13,1},{2,6},{6,10},{... | collective-permute-start | bytes 589832 | tf_op jit(solution)/shard_map/ppermute | solution.py:16
  8.3 10.6 %collective-permute-start.3 = (f32[48,4,2,128]{3,0,2,1:T(8,128)S(1)}, f32[48,4,2,128]{3,0,2,1:T(8,128)S(1)}, u32[]{:S(2)}, u32[]{:S(2)}) collective-permute-start(f32[48,4,2,128]{3,0,2,1:T(8,128)S(1)} %get-tuple-element.17), channel_id=1, source_target_pairs={{0,8},{4,12},{8,0},{12,4},{1,9},{5,13},{9,1},{13,5},{2,10},{6,14},... | collective-permute-start | bytes 589832 | tf_op jit(solution)/shard_map/ppermute | solution.py:16
  9.8 9.4 %collective-permute-start.4 = (f32[48,4,2,128]{3,0,2,1:T(8,128)S(1)}, f32[48,4,2,128]{3,0,2,1:T(8,128)S(1)}, u32[]{:S(2)}, u32[]{:S(2)}) collective-permute-start(f32[48,4,2,128]{3,0,2,1:T(8,128)S(1)} %get-tuple-element.16), channel_id=1, source_target_pairs={{0,12},{4,0},{8,4},{12,8},{1,13},{5,1},{9,5},{13,9},{2,14},{6,2},{... | collective-permute-start | bytes 589832 | tf_op jit(solution)/shard_map/ppermute | solution.py:16
  21.2 6.3 %collective-permute-start.5 = (f32[102,128]{1,0:T(8,128)S(1)}, f32[102,128]{1,0:T(8,128)S(1)}, u32[]{:S(2)}, u32[]{:S(2)}) collective-permute-start(f32[102,128]{1,0:T(8,128)S(1)} %bitcast.76), channel_id=1, source_target_pairs={{0,1},{1,2},{2,3},{3,0},{4,5},{5,6},{6,7},{7,4},{8,9},{9,10},{10,1... | collective-permute-start | bytes 156680 | tf_op jit(solution)/shard_map/ppermute | solution.py:16
  22.8 6.7 %collective-permute-start.6 = (f32[102,128]{1,0:T(8,128)S(1)}, f32[102,128]{1,0:T(8,128)S(1)}, u32[]{:S(2)}, u32[]{:S(2)}) collective-permute-start(f32[102,128]{1,0:T(8,128)S(1)} %bitcast.75), channel_id=1, source_target_pairs={{0,2},{1,3},{2,0},{3,1},{4,6},{5,7},{6,4},{7,5},{8,10},{9,11},{10,... | collective-permute-start | bytes 156680 | tf_op jit(solution)/shard_map/ppermute | solution.py:16
  25.4 4.4 %collective-permute-start.7 = (f32[102,128]{1,0:T(8,128)S(1)}, f32[102,128]{1,0:T(8,128)S(1)}, u32[]{:S(2)}, u32[]{:S(2)}) collective-permute-start(f32[102,128]{1,0:T(8,128)S(1)} %bitcast.74), channel_id=1, source_target_pairs={{0,3},{1,0},{2,1},{3,2},{4,7},{5,4},{6,5},{7,6},{8,11},{9,8},{10,9... | collective-permute-start | bytes 156680 | tf_op jit(solution)/shard_map/ppermute | solution.py:16
  29.8 1.3 %collective-permute-start.8 = (f32[102,128]{1,0:T(8,128)S(1)}, f32[102,128]{1,0:T(8,128)S(1)}, u32[]{:S(2)}, u32[]{:S(2)}) collective-permute-start(f32[102,128]{1,0:T(8,128)S(1)} %fusion.48), channel_id=1, source_target_pairs={{0,16},{16,0},{1,17},{17,1},{2,18},{18,2},{3,19},{19,3},{4,20},{20... | collective-permute-start | bytes 156680 | tf_op jit(solution)/shard_map/ppermute | solution.py:16
  32.0 0.8 %copy-start = (f32[4,16,128]{2,1,0:T(8,128)S(1)}, f32[4,16,128]{2,1,0:T(8,128)}, u32[]{:S(2)}) copy-start(f32[4,16,128]{2,1,0:T(8,128)} %param.9) | copy-start | bytes 98308
  33.0 5.6 %collective-permute-start.9 = (bf16[8,4,2,128]{3,2,1,0:T(2,128)(2,1)S(1)}, bf16[8,4,2,128]{3,2,1,0:T(2,128)(2,1)S(1)}, u32[]{:S(2)}, u32[]{:S(2)}) collective-permute-start(bf16[8,4,2,128]{3,2,1,0:T(2,128)(2,1)S(1)} %bitcast.59), channel_id=1, source_target_pairs={{0,1},{1,2},{2,3},{3,0},{4,5},{5,6},{6,7},{7,4},{8,9},{9,10},{10,1... | collective-permute-start | bytes 49160 | tf_op jit(solution)/shard_map/ppermute | solution.py:16
  34.1 4.9 %collective-permute-start.10 = (bf16[8,4,2,128]{3,2,1,0:T(2,128)(2,1)S(1)}, bf16[8,4,2,128]{3,2,1,0:T(2,128)(2,1)S(1)}, u32[]{:S(2)}, u32[]{:S(2)}) collective-permute-start(bf16[8,4,2,128]{3,2,1,0:T(2,128)(2,1)S(1)} %bitcast.60), channel_id=1, source_target_pairs={{0,2},{1,3},{2,0},{3,1},{4,6},{5,7},{6,4},{7,5},{8,10},{9,11},{10,... | collective-permute-start | bytes 49160 | tf_op jit(solution)/shard_map/ppermute | solution.py:16
  36.6 3.7 %collective-permute-start.11 = (bf16[8,4,2,128]{3,2,1,0:T(2,128)(2,1)S(1)}, bf16[8,4,2,128]{3,2,1,0:T(2,128)(2,1)S(1)}, u32[]{:S(2)}, u32[]{:S(2)}) collective-permute-start(bf16[8,4,2,128]{3,2,1,0:T(2,128)(2,1)S(1)} %bitcast.61), channel_id=1, source_target_pairs={{0,3},{1,0},{2,1},{3,2},{4,7},{5,4},{6,5},{7,6},{8,11},{9,8},{10,9... | collective-permute-start | bytes 49160 | tf_op jit(solution)/shard_map/ppermute | solution.py:16
  40.4 5.2 %collective-permute-start.12 = (bf16[4,8,4,2,128]{4,3,2,1,0:T(2,128)(2,1)S(1)}, bf16[4,8,4,2,128]{4,3,2,1,0:T(2,128)(2,1)S(1)}, u32[]{:S(2)}, u32[]{:S(2)}) collective-permute-start(bf16[4,8,4,2,128]{4,3,2,1,0:T(2,128)(2,1)S(1)} %pad_maximum_fusion.3), channel_id=1, source_target_pairs={{0,4},{4,8},{8,12},{12,0},{1,5},{5,9},{9,13},{13,1},{2,6},{6,10},{... | collective-permute-start | bytes 196616 | tf_op jit(solution)/shard_map/ppermute | solution.py:16
  42.2 4.3 %collective-permute-start.13 = (bf16[4,8,4,2,128]{4,3,2,1,0:T(2,128)(2,1)S(1)}, bf16[4,8,4,2,128]{4,3,2,1,0:T(2,128)(2,1)S(1)}, u32[]{:S(2)}, u32[]{:S(2)}) collective-permute-start(bf16[4,8,4,2,128]{4,3,2,1,0:T(2,128)(2,1)S(1)} %pad_maximum_fusion.3), channel_id=1, source_target_pairs={{0,8},{4,12},{8,0},{12,4},{1,9},{5,13},{9,1},{13,5},{2,10},{6,14},... | collective-permute-start | bytes 196616 | tf_op jit(solution)/shard_map/ppermute | solution.py:16
  42.7 4.3 %collective-permute-start.14 = (bf16[4,8,4,2,128]{4,3,2,1,0:T(2,128)(2,1)S(1)}, bf16[4,8,4,2,128]{4,3,2,1,0:T(2,128)(2,1)S(1)}, u32[]{:S(2)}, u32[]{:S(2)}) collective-permute-start(bf16[4,8,4,2,128]{4,3,2,1,0:T(2,128)(2,1)S(1)} %pad_maximum_fusion.3), channel_id=1, source_target_pairs={{0,12},{4,0},{8,4},{12,8},{1,13},{5,1},{9,5},{13,9},{2,14},{6,2},{... | collective-permute-start | bytes 196616 | tf_op jit(solution)/shard_map/ppermute | solution.py:16

commit v8 on v4

--- a/solution.py
+++ b/solution.py
@@ -39,12 +39,17 @@
     is_grad = me_g == 0
     kept = jnp.where(is_grad, slot_grad, slot_illum)
     given = jnp.where(is_grad, slot_illum, slot_grad)
-    places = jnp.stack([owners, patches])
-    taken = shifted(given, "group", size_g, 1)
-    taken_places = shifted(places, "group", size_g, 1)
+    block_size = levels * patch_rows * patch_cols
+    places = jnp.concatenate(
+        [owners, patches, jnp.zeros((block_size - 2 * slot_count,), jnp.int32)]
+    ).astype(jnp.bfloat16)
+    sent = jnp.concatenate([given, places.reshape(1, levels, patch_rows, patch_cols)], axis=0)
+    arrived = shifted(sent, "group", size_g, 1)
+    taken = arrived[:slot_count]
+    taken_places = arrived[slot_count].reshape(-1).astype(jnp.int32)
     rows_in = jnp.concatenate([kept, taken], axis=0)
-    all_owners = jnp.concatenate([owners, taken_places[0]])
-    all_patches = jnp.concatenate([patches, taken_places[1]])
+    all_owners = jnp.concatenate([owners, taken_places[:slot_count]])
+    all_patches = jnp.concatenate([patches, taken_places[slot_count : 2 * slot_count]])
 
     halo_patches = h // patch_rows
     ext_patches = per_tile + 2 * halo_patches

time: 48.7 us -> 50.3 us (1.033)
  local copies, waits for them, and re-layouts: 3.97 us -> 5.04 us
  other arithmetic: 4.15 us -> 4.84 us
    unnamed x9 -> x10, local copies, waits for them, and re-layouts: 1.98 us -> 2.64 us
    another operation x1 -> x2, other arithmetic: 0.71 us -> 1.37 us  [local(): places = jnp.stack([owners, patches])]
    ppermute x15 -> x14, waiting for transfers between devices: 18.5 us -> 18.1 us  [shifted(): lax.ppermute(value, axis, [(s, (s + step) % count) for s in range(count)])]
    ppermute x15 -> x14, starting transfers between devices: 20.3 us -> 20.4 us  [shifted(): lax.ppermute(value, axis, [(s, (s + step) % count) for s in range(count)])]
  transfers between devices with their start and end apart: 15 -> 14, of which waited for: 14 -> 14; matrix products, arithmetic and copies ran while one was open for 5% -> 2% of each run, Pallas kernels for 0% -> 0%
where the time goes in v8:
time: 50.3 us; the launch traced here: 50.1 us
  starting transfers between devices  20.4 us (41%)
  waiting for transfers between devices  18.1 us (36%)
  local copies, waits for them, and re-layouts  5.04 us (10%)
  other arithmetic  4.84 us (10%)
  between operations  0.97 us (2%)
  matrix products  0.71 us (1%)
    ppermute x14, starting transfers between devices, shifted(): lax.ppermute(value, axis, [(s, (s + step) % count) for s in range(count)])  20.4 us
    ppermute x14, waiting for transfers between devices, shifted(): lax.ppermute(value, axis, [(s, (s + step) % count) for s in range(count)])  18.1 us
    unnamed x10, local copies, waits for them, and re-layouts  2.64 us
    select_n x1, other arithmetic, local(): kept = jnp.where(is_grad, slot_grad, slot_illum)  1.37 us
    another operation x2, other arithmetic  1.37 us
  transfers between devices with their start and end apart: 14, of which 14 were waited for; matrix products, arithmetic and copies ran while one was open for 2% of the time, Pallas kernels for 0%

profile of v8, /device:TPU:0, one launch (start us, length us, event | category | flops | bytes accessed | tf_op | source)
XLA Modules:
  0.0 50.1 jit_solution(6231633866169401706)
XLA Ops:
  0.6 0.7 %convert.9 = bf16[256]{0:T(256)(128)(2,1)S(1)} convert(s32[256]{0:T(256)} %bitcast.90) | non-fusion elementwise | flops 256 | bytes 1536 | tf_op jit(solution)/shard_map/convert.1
  1.3 0.7 %convert.8 = bf16[256]{0:T(256)(128)(2,1)S(1)} convert(s32[256]{0:T(256)} %bitcast.97) | non-fusion elementwise | flops 256 | bytes 1536 | tf_op jit(solution)/shard_map/convert
  2.0 1.4 %select_bitcast_fusion = (bf16[256,4,2,128]{3,0,2,1:T(8,128)(2,1)S(1)}, bf16[256,4,2,128]{3,0,2,1:T(8,128)(2,1)S(1)}) fusion(pred[]{:T(512)S(6)} %eq.65, bf16[1,1,1,256,4,2,128]{6,5,4,3,2,1,0:T(2,128)(2,1)} %param.5, bf16[1,1,1,256,4,2,128]{6,5,4,3,2,1,0:T(2,128)(2,1)} %param.6), kind=kLoop, calls=%fused_computation.7 | loop fusion | flops 524288 | bytes 2097153 | tf_op jit(solution)/shard_map/jit(_where)/select_n | solution.py:40
  3.5 0.2 copy.63
  3.7 0.5 %collective-permute-start = (bf16[257,4,2,128]{3,1,2,0:T(4,128)(2,1)S(1)}, bf16[257,4,2,128]{3,1,2,0:T(4,128)(2,1)S(1)}, u32[]{:S(2)}, u32[]{:S(2)}) collective-permute-start(bf16[257,4,2,128]{3,1,2,0:T(4,128)(2,1)S(1)} %copy.63), channel_id=1, source_target_pairs={{0,16},{16,0},{1,17},{17,1},{2,18},{18,2},{3,19},{19,3},{4,20},{20... | collective-permute-start | bytes 1579016 | tf_op jit(solution)/shard_map/ppermute | solution.py:16
  4.2 1.5 %collective-permute-done = bf16[257,4,2,128]{3,1,2,0:T(4,128)(2,1)S(1)} collective-permute-done((bf16[257,4,2,128]{3,1,2,0:T(4,128)(2,1)S(1)}, bf16[257,4,2,128]{3,1,2,0:T(4,128)(2,1)S(1)}, u32[]{:S(2)}, u32[]{:S(2)}) %collective-permute-start) | collective-permute-done | bytes 526368 | tf_op jit(solution)/shard_map/ppermute | solution.py:16
  5.7 0.2 slice.247
  5.9 0.0 copy-start.1
  5.9 0.0 copy-start.2
  5.9 0.1 copy.85
  6.0 0.6 %copy-done.1 = s32[1,1,1,256]{3,2,1,0:T(1,128)S(1)} copy-done((s32[1,1,1,256]{3,2,1,0:T(1,128)S(1)}, s32[1,1,1,256]{3,2,1,0:T(1,128)}, u32[]{:S(2)}) %copy-start.1) | copy-done | bytes 1048
  6.6 0.0 copy-done.2
  6.7 0.4 fusion.1
  7.1 2.9 %collective-permute-start.1 = (f32[48,4,2,128]{3,0,2,1:T(8,128)S(1)}, f32[48,4,2,128]{3,0,2,1:T(8,128)S(1)}, u32[]{:S(2)}, u32[]{:S(2)}) collective-permute-start(f32[48,4,2,128]{3,0,2,1:T(8,128)S(1)} %get-tuple-element.21), channel_id=1, source_target_pairs={{0,4},{4,8},{8,12},{12,0},{1,5},{5,9},{9,13},{13,1},{2,6},{6,10},{... | collective-permute-start | bytes 589832 | tf_op jit(solution)/shard_map/ppermute | solution.py:16
  10.0 1.5 %collective-permute-start.2 = (f32[48,4,2,128]{3,0,2,1:T(8,128)S(1)}, f32[48,4,2,128]{3,0,2,1:T(8,128)S(1)}, u32[]{:S(2)}, u32[]{:S(2)}) collective-permute-start(f32[48,4,2,128]{3,0,2,1:T(8,128)S(1)} %get-tuple-element.23), channel_id=1, source_target_pairs={{0,8},{4,12},{8,0},{12,4},{1,9},{5,13},{9,1},{13,5},{2,10},{6,14},... | collective-permute-start | bytes 589832 | tf_op jit(solution)/shard_map/ppermute | solution.py:16
  11.5 1.4 %collective-permute-start.3 = (f32[48,4,2,128]{3,0,2,1:T(8,128)S(1)}, f32[48,4,2,128]{3,0,2,1:T(8,128)S(1)}, u32[]{:S(2)}, u32[]{:S(2)}) collective-permute-start(f32[48,4,2,128]{3,0,2,1:T(8,128)S(1)} %get-tuple-element.22), channel_id=1, source_target_pairs={{0,12},{4,0},{8,4},{12,8},{1,13},{5,1},{9,5},{13,9},{2,14},{6,2},{... | collective-permute-start | bytes 589832 | tf_op jit(solution)/shard_map/ppermute | solution.py:16
  13.0 3.7 %collective-permute-done.1 = f32[48,4,2,128]{3,0,2,1:T(8,128)S(1)} collective-permute-done((f32[48,4,2,128]{3,0,2,1:T(8,128)S(1)}, f32[48,4,2,128]{3,0,2,1:T(8,128)S(1)}, u32[]{:S(2)}, u32[]{:S(2)}) %collective-permute-start.1) | collective-permute-done | bytes 196640 | tf_op jit(solution)/shard_map/ppermute | solution.py:16
  16.7 3.7 %collective-permute-done.2 = f32[48,4,2,128]{3,0,2,1:T(8,128)S(1)} collective-permute-done((f32[48,4,2,128]{3,0,2,1:T(8,128)S(1)}, f32[48,4,2,128]{3,0,2,1:T(8,128)S(1)}, u32[]{:S(2)}, u32[]{:S(2)}) %collective-permute-start.2) | collective-permute-done | bytes 196640 | tf_op jit(solution)/shard_map/ppermute | solution.py:16
  20.4 0.3 collective-permute-done.3
  20.8 0.1 copy.67
  20.9 0.1 copy.68
  21.0 0.1 copy.70
  21.1 0.5 fusion.9
  21.6 0.3 reshape.531
  21.9 0.2 reshape_reshape.3
  22.1 0.6 %slice_reduce_fusion.3 = (f32[13056]{0:T(1024)S(1)}, f32[13056]{0:T(1024)S(1)}, f32[13056]{0:T(1024)S(1)}, f32[13056]{0:T(1024)S(1)}) fusion(f32[4,13056]{1,0:T(4,128)S(1)} %constant_dynamic-update-slice_fusion), kind=kLoop, calls=%fused_computation.94 | loop fusion | bytes 417792 | tf_op jit(solution)/shard_map/slice | solution.py:91
  22.7 1.6 %collective-permute-start.4 = (f32[102,128]{1,0:T(8,128)S(1)}, f32[102,128]{1,0:T(8,128)S(1)}, u32[]{:S(2)}, u32[]{:S(2)}) collective-permute-start(f32[102,128]{1,0:T(8,128)S(1)} %bitcast.86), channel_id=1, source_target_pairs={{0,1},{1,2},{2,3},{3,0},{4,5},{5,6},{6,7},{7,4},{8,9},{9,10},{10,1... | collective-permute-start | bytes 156680 | tf_op jit(solution)/shard_map/ppermute | solution.py:16
  24.3 2.6 %collective-permute-start.5 = (f32[102,128]{1,0:T(8,128)S(1)}, f32[102,128]{1,0:T(8,128)S(1)}, u32[]{:S(2)}, u32[]{:S(2)}) collective-permute-start(f32[102,128]{1,0:T(8,128)S(1)} %bitcast.85), channel_id=1, source_target_pairs={{0,2},{1,3},{2,0},{3,1},{4,6},{5,7},{6,4},{7,5},{8,10},{9,11},{10,... | collective-permute-start | bytes 156680 | tf_op jit(solution)/shard_map/ppermute | solution.py:16
  26.9 1.3 %collective-permute-start.6 = (f32[102,128]{1,0:T(8,128)S(1)}, f32[102,128]{1,0:T(8,128)S(1)}, u32[]{:S(2)}, u32[]{:S(2)}) collective-permute-start(f32[102,128]{1,0:T(8,128)S(1)} %bitcast.84), channel_id=1, source_target_pairs={{0,3},{1,0},{2,1},{3,2},{4,7},{5,4},{6,5},{7,6},{8,11},{9,8},{10,9... | collective-permute-start | bytes 156680 | tf_op jit(solution)/shard_map/ppermute | solution.py:16
  28.3 0.7 %collective-permute-done.4 = f32[102,128]{1,0:T(8,128)S(1)} collective-permute-done((f32[102,128]{1,0:T(8,128)S(1)}, f32[102,128]{1,0:T(8,128)S(1)}, u32[]{:S(2)}, u32[]{:S(2)}) %collective-permute-start.4) | collective-permute-done | bytes 52256 | tf_op jit(solution)/shard_map/ppermute | solution.py:16
  29.0 2.0 %collective-permute-done.5 = f32[102,128]{1,0:T(8,128)S(1)} collective-permute-done((f32[102,128]{1,0:T(8,128)S(1)}, f32[102,128]{1,0:T(8,128)S(1)}, u32[]{:S(2)}, u32[]{:S(2)}) %collective-permute-start.5) | collective-permute-done | bytes 52256 | tf_op jit(solution)/shard_map/ppermute | solution.py:16
  31.0 0.3 collective-permute-done.6
  31.3 0.1 collective-permute-start.7
  31.4 0.1 broadcast_and_fusion
  31.5 0.1 slice.273
  31.6 1.1 %collective-permute-done.7 = f32[102,128]{1,0:T(8,128)S(1)} collective-permute-done((f32[102,128]{1,0:T(8,128)S(1)}, f32[102,128]{1,0:T(8,128)S(1)}, u32[]{:S(2)}, u32[]{:S(2)}) %collective-permute-start.7) | collective-permute-done | bytes 52256 | tf_op jit(solution)/shard_map/ppermute | solution.py:16
  32.7 0.1 reshape.532
  32.8 0.1 reshape.534
  32.9 0.2 fusion.87
  33.1 0.4 fusion.46
  33.5 0.0 copy-start
  33.6 0.2 fusion.23
  33.8 0.2 fusion.32
  34.0 0.2 fusion.41
  34.2 0.2 fusion.44
  34.4 0.0 copy-done
  34.4 0.2 fusion.83
  34.5 1.0 %collective-permute-start.8 = (bf16[8,4,2,128]{3,0,2,1:T(8,128)(2,1)S(1)}, bf16[8,4,2,128]{3,0,2,1:T(8,128)(2,1)S(1)}, u32[]{:S(2)}, u32[]{:S(2)}) collective-permute-start(bf16[8,4,2,128]{3,0,2,1:T(8,128)(2,1)S(1)} %bitcast.76), channel_id=1, source_target_pairs={{0,1},{1,2},{2,3},{3,0},{4,5},{5,6},{6,7},{7,4},{8,9},{9,10},{10,1... | collective-permute-start | bytes 49160 | tf_op jit(solution)/shard_map/ppermute | solution.py:16
  35.5 2.5 %collective-permute-start.9 = (bf16[8,4,2,128]{3,0,2,1:T(8,128)(2,1)S(1)}, bf16[8,4,2,128]{3,0,2,1:T(8,128)(2,1)S(1)}, u32[]{:S(2)}, u32[]{:S(2)}) collective-permute-start(bf16[8,4,2,128]{3,0,2,1:T(8,128)(2,1)S(1)} %bitcast.77), channel_id=1, source_target_pairs={{0,2},{1,3},{2,0},{3,1},{4,6},{5,7},{6,4},{7,5},{8,10},{9,11},{10,... | collective-permute-start | bytes 49160 | tf_op jit(solution)/shard_map/ppermute | solution.py:16
  38.0 0.5 %collective-permute-start.10 = (bf16[8,4,2,128]{3,0,2,1:T(8,128)(2,1)S(1)}, bf16[8,4,2,128]{3,0,2,1:T(8,128)(2,1)S(1)}, u32[]{:S(2)}, u32[]{:S(2)}) collective-permute-start(bf16[8,4,2,128]{3,0,2,1:T(8,128)(2,1)S(1)} %bitcast.78), channel_id=1, source_target_pairs={{0,3},{1,0},{2,1},{3,2},{4,7},{5,4},{6,5},{7,6},{8,11},{9,8},{10,9... | collective-permute-start | bytes 49160 | tf_op jit(solution)/shard_map/ppermute | solution.py:16
  38.6 1.6 %collective-permute-done.8 = bf16[8,4,2,128]{3,0,2,1:T(8,128)(2,1)S(1)} collective-permute-done((bf16[8,4,2,128]{3,0,2,1:T(8,128)(2,1)S(1)}, bf16[8,4,2,128]{3,0,2,1:T(8,128)(2,1)S(1)}, u32[]{:S(2)}, u32[]{:S(2)}) %collective-permute-start.8) | collective-permute-done | bytes 16416 | tf_op jit(solution)/shard_map/ppermute | solution.py:16
  40.2 0.3 collective-permute-done.9
  40.5 1.3 %collective-permute-done.10 = bf16[8,4,2,128]{3,0,2,1:T(8,128)(2,1)S(1)} collective-permute-done((bf16[8,4,2,128]{3,0,2,1:T(8,128)(2,1)S(1)}, bf16[8,4,2,128]{3,0,2,1:T(8,128)(2,1)S(1)}, u32[]{:S(2)}, u32[]{:S(2)}) %collective-permute-start.10) | collective-permute-done | bytes 16416 | tf_op jit(solution)/shard_map/ppermute | solution.py:16
  41.8 1.8 %collective-permute-start.11 = (bf16[4,8,4,2,128]{4,1,0,3,2:T(8,128)(2,1)S(1)}, bf16[4,8,4,2,128]{4,1,0,3,2:T(8,128)(2,1)S(1)}, u32[]{:S(2)}, u32[]{:S(2)}) collective-permute-start(bf16[4,8,4,2,128]{4,1,0,3,2:T(8,128)(2,1)S(1)} %get-tuple-element.35), channel_id=1, source_target_pairs={{0,4},{4,8},{8,12},{12,0},{1,5},{5,9},{9,13},{13,1},{2,6},{6,10},{... | collective-permute-start | bytes 196616 | tf_op jit(solution)/shard_map/ppermute | solution.py:16
  43.6 0.5 %collective-permute-start.12 = (bf16[4,8,4,2,128]{4,1,0,3,2:T(8,128)(2,1)S(1)}, bf16[4,8,4,2,128]{4,1,0,3,2:T(8,128)(2,1)S(1)}, u32[]{:S(2)}, u32[]{:S(2)}) collective-permute-start(bf16[4,8,4,2,128]{4,1,0,3,2:T(8,128)(2,1)S(1)} %get-tuple-element.35), channel_id=1, source_target_pairs={{0,8},{4,12},{8,0},{12,4},{1,9},{5,13},{9,1},{13,5},{2,10},{6,14},... | collective-permute-start | bytes 196616 | tf_op jit(solution)/shard_map/ppermute | solution.py:16
  44.1 2.1 %collective-permute-start.13 = (bf16[4,8,4,2,128]{4,1,0,3,2:T(8,128)(2,1)S(1)}, bf16[4,8,4,2,128]{4,1,0,3,2:T(8,128)(2,1)S(1)}, u32[]{:S(2)}, u32[]{:S(2)}) collective-permute-start(bf16[4,8,4,2,128]{4,1,0,3,2:T(8,128)(2,1)S(1)} %get-tuple-element.35), channel_id=1, source_target_pairs={{0,12},{4,0},{8,4},{12,8},{1,13},{5,1},{9,5},{13,9},{2,14},{6,2},{... | collective-permute-start | bytes 196616 | tf_op jit(solution)/shard_map/ppermute | solution.py:16
  46.2 0.6 %copy.81 = f32[4,16,128]{2,1,0:T(8,128)} copy(f32[4,16,128]{2,0,1:T(4,128)S(1)} %get-tuple-element.15) | data formatting | bytes 65536
  46.9 0.2 collective-permute-done.11
  47.0 0.8 %collective-permute-done.12 = bf16[4,8,4,2,128]{4,1,0,3,2:T(8,128)(2,1)S(1)} collective-permute-done((bf16[4,8,4,2,128]{4,1,0,3,2:T(8,128)(2,1)S(1)}, bf16[4,8,4,2,128]{4,1,0,3,2:T(8,128)(2,1)S(1)}, u32[]{:S(2)}, u32[]{:S(2)}) %collective-permute-start.12) | collective-permute-done | bytes 65568 | tf_op jit(solution)/shard_map/ppermute | solution.py:16
  47.8 0.5 %collective-permute-done.13 = bf16[4,8,4,2,128]{4,1,0,3,2:T(8,128)(2,1)S(1)} collective-permute-done((bf16[4,8,4,2,128]{4,1,0,3,2:T(8,128)(2,1)S(1)}, bf16[4,8,4,2,128]{4,1,0,3,2:T(8,128)(2,1)S(1)}, u32[]{:S(2)}, u32[]{:S(2)}) %collective-permute-start.13) | collective-permute-done | bytes 65568 | tf_op jit(solution)/shard_map/ppermute | solution.py:16
  48.4 0.3 fusion
  48.7 1.3 %copy.82 = bf16[1,1,1,256,4,2,128]{6,5,4,3,2,1,0:T(2,128)(2,1)} copy(bf16[1,1,1,256,4,2,128]{6,3,5,4,2,1,0:T(8,128)(2,1)S(1)} %fusion) | data formatting | bytes 1048576
  (30 shorter events, 0.5 us)
Async XLA Ops:
  3.7 2.1 %collective-permute-start = (bf16[257,4,2,128]{3,1,2,0:T(4,128)(2,1)S(1)}, bf16[257,4,2,128]{3,1,2,0:T(4,128)(2,1)S(1)}, u32[]{:S(2)}, u32[]{:S(2)}) collective-permute-start(bf16[257,4,2,128]{3,1,2,0:T(4,128)(2,1)S(1)} %copy.63), channel_id=1, source_target_pairs={{0,16},{16,0},{1,17},{17,1},{2,18},{18,2},{3,19},{19,3},{4,20},{20... | collective-permute-start | bytes 1579016 | tf_op jit(solution)/shard_map/ppermute | solution.py:16
  5.9 0.7 %copy-start.1 = (s32[1,1,1,256]{3,2,1,0:T(1,128)S(1)}, s32[1,1,1,256]{3,2,1,0:T(1,128)}, u32[]{:S(2)}) copy-start(s32[1,1,1,256]{3,2,1,0:T(1,128)} %param.8) | copy-start | bytes 3076
  5.9 0.7 %copy-start.2 = (s32[1,1,1,256]{3,2,1,0:T(1,128)S(1)}, s32[1,1,1,256]{3,2,1,0:T(1,128)}, u32[]{:S(2)}) copy-start(s32[1,1,1,256]{3,2,1,0:T(1,128)} %param.7) | copy-start | bytes 3076
  7.1 9.6 %collective-permute-start.1 = (f32[48,4,2,128]{3,0,2,1:T(8,128)S(1)}, f32[48,4,2,128]{3,0,2,1:T(8,128)S(1)}, u32[]{:S(2)}, u32[]{:S(2)}) collective-permute-start(f32[48,4,2,128]{3,0,2,1:T(8,128)S(1)} %get-tuple-element.21), channel_id=1, source_target_pairs={{0,4},{4,8},{8,12},{12,0},{1,5},{5,9},{9,13},{13,1},{2,6},{6,10},{... | collective-permute-start | bytes 589832 | tf_op jit(solution)/shard_map/ppermute | solution.py:16
  10.0 10.4 %collective-permute-start.2 = (f32[48,4,2,128]{3,0,2,1:T(8,128)S(1)}, f32[48,4,2,128]{3,0,2,1:T(8,128)S(1)}, u32[]{:S(2)}, u32[]{:S(2)}) collective-permute-start(f32[48,4,2,128]{3,0,2,1:T(8,128)S(1)} %get-tuple-element.23), channel_id=1, source_target_pairs={{0,8},{4,12},{8,0},{12,4},{1,9},{5,13},{9,1},{13,5},{2,10},{6,14},... | collective-permute-start | bytes 589832 | tf_op jit(solution)/shard_map/ppermute | solution.py:16
  11.5 9.1 %collective-permute-start.3 = (f32[48,4,2,128]{3,0,2,1:T(8,128)S(1)}, f32[48,4,2,128]{3,0,2,1:T(8,128)S(1)}, u32[]{:S(2)}, u32[]{:S(2)}) collective-permute-start(f32[48,4,2,128]{3,0,2,1:T(8,128)S(1)} %get-tuple-element.22), channel_id=1, source_target_pairs={{0,12},{4,0},{8,4},{12,8},{1,13},{5,1},{9,5},{13,9},{2,14},{6,2},{... | collective-permute-start | bytes 589832 | tf_op jit(solution)/shard_map/ppermute | solution.py:16
  22.7 6.3 %collective-permute-start.4 = (f32[102,128]{1,0:T(8,128)S(1)}, f32[102,128]{1,0:T(8,128)S(1)}, u32[]{:S(2)}, u32[]{:S(2)}) collective-permute-start(f32[102,128]{1,0:T(8,128)S(1)} %bitcast.86), channel_id=1, source_target_pairs={{0,1},{1,2},{2,3},{3,0},{4,5},{5,6},{6,7},{7,4},{8,9},{9,10},{10,1... | collective-permute-start | bytes 156680 | tf_op jit(solution)/shard_map/ppermute | solution.py:16
  24.3 6.7 %collective-permute-start.5 = (f32[102,128]{1,0:T(8,128)S(1)}, f32[102,128]{1,0:T(8,128)S(1)}, u32[]{:S(2)}, u32[]{:S(2)}) collective-permute-start(f32[102,128]{1,0:T(8,128)S(1)} %bitcast.85), channel_id=1, source_target_pairs={{0,2},{1,3},{2,0},{3,1},{4,6},{5,7},{6,4},{7,5},{8,10},{9,11},{10,... | collective-permute-start | bytes 156680 | tf_op jit(solution)/shard_map/ppermute | solution.py:16
  26.9 4.4 %collective-permute-start.6 = (f32[102,128]{1,0:T(8,128)S(1)}, f32[102,128]{1,0:T(8,128)S(1)}, u32[]{:S(2)}, u32[]{:S(2)}) collective-permute-start(f32[102,128]{1,0:T(8,128)S(1)} %bitcast.84), channel_id=1, source_target_pairs={{0,3},{1,0},{2,1},{3,2},{4,7},{5,4},{6,5},{7,6},{8,11},{9,8},{10,9... | collective-permute-start | bytes 156680 | tf_op jit(solution)/shard_map/ppermute | solution.py:16
  31.3 1.3 %collective-permute-start.7 = (f32[102,128]{1,0:T(8,128)S(1)}, f32[102,128]{1,0:T(8,128)S(1)}, u32[]{:S(2)}, u32[]{:S(2)}) collective-permute-start(f32[102,128]{1,0:T(8,128)S(1)} %fusion.49), channel_id=1, source_target_pairs={{0,16},{16,0},{1,17},{17,1},{2,18},{18,2},{3,19},{19,3},{4,20},{20... | collective-permute-start | bytes 156680 | tf_op jit(solution)/shard_map/ppermute | solution.py:16
  33.5 0.8 %copy-start = (f32[4,16,128]{2,1,0:T(8,128)S(1)}, f32[4,16,128]{2,1,0:T(8,128)}, u32[]{:S(2)}) copy-start(f32[4,16,128]{2,1,0:T(8,128)} %param.9) | copy-start | bytes 98308
  34.5 5.6 %collective-permute-start.8 = (bf16[8,4,2,128]{3,0,2,1:T(8,128)(2,1)S(1)}, bf16[8,4,2,128]{3,0,2,1:T(8,128)(2,1)S(1)}, u32[]{:S(2)}, u32[]{:S(2)}) collective-permute-start(bf16[8,4,2,128]{3,0,2,1:T(8,128)(2,1)S(1)} %bitcast.76), channel_id=1, source_target_pairs={{0,1},{1,2},{2,3},{3,0},{4,5},{5,6},{6,7},{7,4},{8,9},{9,10},{10,1... | collective-permute-start | bytes 49160 | tf_op jit(solution)/shard_map/ppermute | solution.py:16
  35.5 4.9 %collective-permute-start.9 = (bf16[8,4,2,128]{3,0,2,1:T(8,128)(2,1)S(1)}, bf16[8,4,2,128]{3,0,2,1:T(8,128)(2,1)S(1)}, u32[]{:S(2)}, u32[]{:S(2)}) collective-permute-start(bf16[8,4,2,128]{3,0,2,1:T(8,128)(2,1)S(1)} %bitcast.77), channel_id=1, source_target_pairs={{0,2},{1,3},{2,0},{3,1},{4,6},{5,7},{6,4},{7,5},{8,10},{9,11},{10,... | collective-permute-start | bytes 49160 | tf_op jit(solution)/shard_map/ppermute | solution.py:16
  38.0 3.7 %collective-permute-start.10 = (bf16[8,4,2,128]{3,0,2,1:T(8,128)(2,1)S(1)}, bf16[8,4,2,128]{3,0,2,1:T(8,128)(2,1)S(1)}, u32[]{:S(2)}, u32[]{:S(2)}) collective-permute-start(bf16[8,4,2,128]{3,0,2,1:T(8,128)(2,1)S(1)} %bitcast.78), channel_id=1, source_target_pairs={{0,3},{1,0},{2,1},{3,2},{4,7},{5,4},{6,5},{7,6},{8,11},{9,8},{10,9... | collective-permute-start | bytes 49160 | tf_op jit(solution)/shard_map/ppermute | solution.py:16
  41.8 5.2 %collective-permute-start.11 = (bf16[4,8,4,2,128]{4,1,0,3,2:T(8,128)(2,1)S(1)}, bf16[4,8,4,2,128]{4,1,0,3,2:T(8,128)(2,1)S(1)}, u32[]{:S(2)}, u32[]{:S(2)}) collective-permute-start(bf16[4,8,4,2,128]{4,1,0,3,2:T(8,128)(2,1)S(1)} %get-tuple-element.35), channel_id=1, source_target_pairs={{0,4},{4,8},{8,12},{12,0},{1,5},{5,9},{9,13},{13,1},{2,6},{6,10},{... | collective-permute-start | bytes 196616 | tf_op jit(solution)/shard_map/ppermute | solution.py:16
  43.6 4.3 %collective-permute-start.12 = (bf16[4,8,4,2,128]{4,1,0,3,2:T(8,128)(2,1)S(1)}, bf16[4,8,4,2,128]{4,1,0,3,2:T(8,128)(2,1)S(1)}, u32[]{:S(2)}, u32[]{:S(2)}) collective-permute-start(bf16[4,8,4,2,128]{4,1,0,3,2:T(8,128)(2,1)S(1)} %get-tuple-element.35), channel_id=1, source_target_pairs={{0,8},{4,12},{8,0},{12,4},{1,9},{5,13},{9,1},{13,5},{2,10},{6,14},... | collective-permute-start | bytes 196616 | tf_op jit(solution)/shard_map/ppermute | solution.py:16
  44.1 4.3 %collective-permute-start.13 = (bf16[4,8,4,2,128]{4,1,0,3,2:T(8,128)(2,1)S(1)}, bf16[4,8,4,2,128]{4,1,0,3,2:T(8,128)(2,1)S(1)}, u32[]{:S(2)}, u32[]{:S(2)}) collective-permute-start(bf16[4,8,4,2,128]{4,1,0,3,2:T(8,128)(2,1)S(1)} %get-tuple-element.35), channel_id=1, source_target_pairs={{0,12},{4,0},{8,4},{12,8},{1,13},{5,1},{9,5},{13,9},{2,14},{6,2},{... | collective-permute-start | bytes 196616 | tf_op jit(solution)/shard_map/ppermute | solution.py:16

commit v9 on v4

--- a/solution.py
+++ b/solution.py
@@ -14,6 +14,14 @@
 
 def shifted(value, axis, count, step):
     return lax.ppermute(value, axis, [(s, (s + step) % count) for s in range(count)])
+
+
+def far_first(count):
+    steps = list(range(1, count))
+    if count % 2 == 0:
+        steps.remove(count // 2)
+        steps.append(count // 2)
+    return steps
 
 
 def local(gradient_windows, illumination_windows, window_owners, window_patches, velocity):
@@ -74,7 +82,7 @@
     flat = table.reshape(size_x, size_y * ext_patches, levels, patch_rows, patch_cols)
 
     part = flat[0]
-    for step in range(1, size_x):
+    for step in far_first(size_x):
         part = part + shifted(flat[step], "gx", size_x, step)
     part = part.reshape(size_y, ext_patches, levels, patch_rows, patch_cols)
     left = jnp.roll(part, 1, axis=0)[..., patch_cols - h :]
@@ -123,9 +131,8 @@
     along_y = jnp.stack(
         [tile_table] + [shifted(tile_table, "gy", size_y, step) for step in range(1, size_y)]
     )
-    along_x = jnp.stack(
-        [along_y] + [shifted(along_y, "gx", size_x, step) for step in range(1, size_x)]
-    )
+    arrived_x = {step: shifted(along_y, "gx", size_x, step) for step in far_first(size_x)}
+    along_x = jnp.stack([along_y] + [arrived_x[step] for step in range(1, size_x)])
     whole = along_x.reshape(tiles * per_tile, levels, patch_rows, patch_cols)
     owner_x = owners // size_y
     owner_y = owners % size_y

time: 48.7 us -> 50 us (1.027)
  waiting for transfers between devices: 18.5 us -> 19.8 us
    ppermute x15, waiting for transfers between devices: 18.5 us -> 19.8 us  [shifted(): lax.ppermute(value, axis, [(s, (s + step) % count) for s in range(count)])]
  transfers between devices with their start and end apart: 15 -> 15, of which waited for: 14 -> 13; matrix products, arithmetic and copies ran while one was open for 5% -> 5% of each run, Pallas kernels for 0% -> 0%
where the time goes in v9:
time: 50 us; the launch traced here: 49.8 us
  starting transfers between devices  20.2 us (40%)
  waiting for transfers between devices  19.8 us (40%)
  other arithmetic  4.15 us (8%)
  local copies, waits for them, and re-layouts  3.97 us (8%)
  between operations  0.93 us (2%)
  matrix products  0.71 us (1%)
    ppermute x15, starting transfers between devices, shifted(): lax.ppermute(value, axis, [(s, (s + step) % count) for s in range(count)])  20.2 us
    ppermute x15, waiting for transfers between devices, shifted(): lax.ppermute(value, axis, [(s, (s + step) % count) for s in range(count)])  19.8 us
    unnamed x9, local copies, waits for them, and re-layouts  1.98 us
    select_n x1, other arithmetic, local(): kept = jnp.where(is_grad, slot_grad, slot_illum)  1.39 us
  transfers between devices with their start and end apart: 15, of which 13 were waited for; matrix products, arithmetic and copies ran while one was open for 5% of the time, Pallas kernels for 0%

profile of v9, /device:TPU:0, one launch (start us, length us, event | category | flops | bytes accessed | tf_op | source)
XLA Modules:
  0.0 49.8 jit_solution(12164235111433644295)
XLA Ops:
  0.6 0.7 %pad_add_fusion = s32[2,256]{1,0:T(2,128)S(1)} fusion(s32[1,256]{1,0:T(1,128)} %bitcast.91, s32[1,256]{1,0:T(1,128)} %bitcast.97), kind=kLoop, calls=%fused_computation.149 | loop fusion | flops 512 | bytes 4096 | tf_op jit(solution)/shard_map/stack | solution.py:50
  1.3 0.5 collective-permute-start
  1.8 0.0 copy-start.1
  1.8 0.0 copy-start.2
  1.8 1.4 %select_bitcast_fusion.1 = (bf16[256,4,2,128]{3,0,2,1:T(8,128)(2,1)S(1)}, bf16[256,4,2,128]{3,0,2,1:T(8,128)(2,1)S(1)}) fusion(pred[]{:T(512)S(6)} %eq.65, bf16[1,1,1,256,4,2,128]{6,5,4,3,2,1,0:T(2,128)(2,1)} %param.6, bf16[1,1,1,256,4,2,128]{6,5,4,3,2,1,0:T(2,128)(2,1)} %param.5), kind=kLoop, calls=%fused_computation.7 | loop fusion | flops 524288 | bytes 2097153 | tf_op jit(solution)/shard_map/jit(_where)/select_n | solution.py:48
  3.2 0.1 collective-permute-start.1
  3.3 0.0 collective-permute-done
  3.3 0.0 copy-done.1
  3.3 0.0 copy-done.2
  3.4 1.8 %collective-permute-done.1 = bf16[256,4,2,128]{3,0,2,1:T(8,128)(2,1)S(1)} collective-permute-done((bf16[256,4,2,128]{3,0,2,1:T(8,128)(2,1)S(1)}, bf16[256,4,2,128]{3,0,2,1:T(8,128)(2,1)S(1)}, u32[]{:S(2)}, u32[]{:S(2)}) %collective-permute-start.1) | collective-permute-done | bytes 524320 | tf_op jit(solution)/shard_map/ppermute | solution.py:16
  5.2 0.4 fusion.1
  5.6 2.7 %collective-permute-start.2 = (f32[48,4,2,128]{3,0,2,1:T(8,128)S(1)}, f32[48,4,2,128]{3,0,2,1:T(8,128)S(1)}, u32[]{:S(2)}, u32[]{:S(2)}) collective-permute-start(f32[48,4,2,128]{3,0,2,1:T(8,128)S(1)} %get-tuple-element.19), channel_id=1, source_target_pairs={{0,4},{4,8},{8,12},{12,0},{1,5},{5,9},{9,13},{13,1},{2,6},{6,10},{... | collective-permute-start | bytes 589832 | tf_op jit(solution)/shard_map/ppermute | solution.py:16
  8.3 1.0 %collective-permute-start.3 = (f32[48,4,2,128]{3,0,2,1:T(8,128)S(1)}, f32[48,4,2,128]{3,0,2,1:T(8,128)S(1)}, u32[]{:S(2)}, u32[]{:S(2)}) collective-permute-start(f32[48,4,2,128]{3,0,2,1:T(8,128)S(1)} %get-tuple-element.21), channel_id=1, source_target_pairs={{0,12},{4,0},{8,4},{12,8},{1,13},{5,1},{9,5},{13,9},{2,14},{6,2},{... | collective-permute-start | bytes 589832 | tf_op jit(solution)/shard_map/ppermute | solution.py:16
  9.3 1.9 %collective-permute-start.4 = (f32[48,4,2,128]{3,0,2,1:T(8,128)S(1)}, f32[48,4,2,128]{3,0,2,1:T(8,128)S(1)}, u32[]{:S(2)}, u32[]{:S(2)}) collective-permute-start(f32[48,4,2,128]{3,0,2,1:T(8,128)S(1)} %get-tuple-element.20), channel_id=1, source_target_pairs={{0,8},{4,12},{8,0},{12,4},{1,9},{5,13},{9,1},{13,5},{2,10},{6,14},... | collective-permute-start | bytes 589832 | tf_op jit(solution)/shard_map/ppermute | solution.py:16
  11.2 3.8 %collective-permute-done.2 = f32[48,4,2,128]{3,0,2,1:T(8,128)S(1)} collective-permute-done((f32[48,4,2,128]{3,0,2,1:T(8,128)S(1)}, f32[48,4,2,128]{3,0,2,1:T(8,128)S(1)}, u32[]{:S(2)}, u32[]{:S(2)}) %collective-permute-start.2) | collective-permute-done | bytes 196640 | tf_op jit(solution)/shard_map/ppermute | solution.py:16
  15.0 4.1 %collective-permute-done.3 = f32[48,4,2,128]{3,0,2,1:T(8,128)S(1)} collective-permute-done((f32[48,4,2,128]{3,0,2,1:T(8,128)S(1)}, f32[48,4,2,128]{3,0,2,1:T(8,128)S(1)}, u32[]{:S(2)}, u32[]{:S(2)}) %collective-permute-start.3) | collective-permute-done | bytes 196640 | tf_op jit(solution)/shard_map/ppermute | solution.py:16
  19.2 0.0 collective-permute-done.4
  19.3 0.1 copy.42
  19.4 0.1 copy.43
  19.5 0.1 copy.45
  19.6 0.5 fusion.9
  20.1 0.3 reshape.524
  20.4 0.2 reshape_reshape.3
  20.6 0.6 %slice_reduce_fusion.3 = (f32[13056]{0:T(1024)S(1)}, f32[13056]{0:T(1024)S(1)}, f32[13056]{0:T(1024)S(1)}, f32[13056]{0:T(1024)S(1)}) fusion(f32[4,13056]{1,0:T(4,128)S(1)} %constant_dynamic-update-slice_fusion), kind=kLoop, calls=%fused_computation.93 | loop fusion | bytes 417792 | tf_op jit(solution)/shard_map/slice | solution.py:94
  21.2 1.6 %collective-permute-start.5 = (f32[102,128]{1,0:T(8,128)S(1)}, f32[102,128]{1,0:T(8,128)S(1)}, u32[]{:S(2)}, u32[]{:S(2)}) collective-permute-start(f32[102,128]{1,0:T(8,128)S(1)} %bitcast.87), channel_id=1, source_target_pairs={{0,1},{1,2},{2,3},{3,0},{4,5},{5,6},{6,7},{7,4},{8,9},{9,10},{10,1... | collective-permute-start | bytes 156680 | tf_op jit(solution)/shard_map/ppermute | solution.py:16
  22.8 2.6 %collective-permute-start.6 = (f32[102,128]{1,0:T(8,128)S(1)}, f32[102,128]{1,0:T(8,128)S(1)}, u32[]{:S(2)}, u32[]{:S(2)}) collective-permute-start(f32[102,128]{1,0:T(8,128)S(1)} %bitcast.86), channel_id=1, source_target_pairs={{0,2},{1,3},{2,0},{3,1},{4,6},{5,7},{6,4},{7,5},{8,10},{9,11},{10,... | collective-permute-start | bytes 156680 | tf_op jit(solution)/shard_map/ppermute | solution.py:16
  25.4 1.3 %collective-permute-start.7 = (f32[102,128]{1,0:T(8,128)S(1)}, f32[102,128]{1,0:T(8,128)S(1)}, u32[]{:S(2)}, u32[]{:S(2)}) collective-permute-start(f32[102,128]{1,0:T(8,128)S(1)} %bitcast.85), channel_id=1, source_target_pairs={{0,3},{1,0},{2,1},{3,2},{4,7},{5,4},{6,5},{7,6},{8,11},{9,8},{10,9... | collective-permute-start | bytes 156680 | tf_op jit(solution)/shard_map/ppermute | solution.py:16
  26.8 0.7 %collective-permute-done.5 = f32[102,128]{1,0:T(8,128)S(1)} collective-permute-done((f32[102,128]{1,0:T(8,128)S(1)}, f32[102,128]{1,0:T(8,128)S(1)}, u32[]{:S(2)}, u32[]{:S(2)}) %collective-permute-start.5) | collective-permute-done | bytes 52256 | tf_op jit(solution)/shard_map/ppermute | solution.py:16
  27.5 2.0 %collective-permute-done.6 = f32[102,128]{1,0:T(8,128)S(1)} collective-permute-done((f32[102,128]{1,0:T(8,128)S(1)}, f32[102,128]{1,0:T(8,128)S(1)}, u32[]{:S(2)}, u32[]{:S(2)}) %collective-permute-start.6) | collective-permute-done | bytes 52256 | tf_op jit(solution)/shard_map/ppermute | solution.py:16
  29.5 0.3 collective-permute-done.7
  29.8 0.1 collective-permute-start.8
  29.9 0.1 broadcast_and_fusion
  30.0 0.1 slice.255
  30.1 1.1 %collective-permute-done.8 = f32[102,128]{1,0:T(8,128)S(1)} collective-permute-done((f32[102,128]{1,0:T(8,128)S(1)}, f32[102,128]{1,0:T(8,128)S(1)}, u32[]{:S(2)}, u32[]{:S(2)}) %collective-permute-start.8) | collective-permute-done | bytes 52256 | tf_op jit(solution)/shard_map/ppermute | solution.py:16
  31.2 0.1 reshape.525
  31.3 0.1 reshape.527
  31.4 0.2 fusion.87
  31.6 0.4 fusion.46
  32.0 0.0 copy-start
  32.1 0.2 fusion.23
  32.3 0.2 fusion.32
  32.5 0.2 fusion.41
  32.7 0.2 fusion.44
  32.8 0.0 copy-done
  32.9 0.2 fusion.83
  33.0 1.0 %collective-permute-start.9 = (bf16[8,4,2,128]{3,0,2,1:T(8,128)(2,1)S(1)}, bf16[8,4,2,128]{3,0,2,1:T(8,128)(2,1)S(1)}, u32[]{:S(2)}, u32[]{:S(2)}) collective-permute-start(bf16[8,4,2,128]{3,0,2,1:T(8,128)(2,1)S(1)} %bitcast.77), channel_id=1, source_target_pairs={{0,1},{1,2},{2,3},{3,0},{4,5},{5,6},{6,7},{7,4},{8,9},{9,10},{10,1... | collective-permute-start | bytes 49160 | tf_op jit(solution)/shard_map/ppermute | solution.py:16
  34.0 2.5 %collective-permute-start.10 = (bf16[8,4,2,128]{3,0,2,1:T(8,128)(2,1)S(1)}, bf16[8,4,2,128]{3,0,2,1:T(8,128)(2,1)S(1)}, u32[]{:S(2)}, u32[]{:S(2)}) collective-permute-start(bf16[8,4,2,128]{3,0,2,1:T(8,128)(2,1)S(1)} %bitcast.78), channel_id=1, source_target_pairs={{0,2},{1,3},{2,0},{3,1},{4,6},{5,7},{6,4},{7,5},{8,10},{9,11},{10,... | collective-permute-start | bytes 49160 | tf_op jit(solution)/shard_map/ppermute | solution.py:16
  36.5 0.5 collective-permute-start.11
  37.0 1.6 %collective-permute-done.9 = bf16[8,4,2,128]{3,0,2,1:T(8,128)(2,1)S(1)} collective-permute-done((bf16[8,4,2,128]{3,0,2,1:T(8,128)(2,1)S(1)}, bf16[8,4,2,128]{3,0,2,1:T(8,128)(2,1)S(1)}, u32[]{:S(2)}, u32[]{:S(2)}) %collective-permute-start.9) | collective-permute-done | bytes 16416 | tf_op jit(solution)/shard_map/ppermute | solution.py:16
  38.7 0.2 collective-permute-done.10
  38.9 1.3 %collective-permute-done.11 = bf16[8,4,2,128]{3,0,2,1:T(8,128)(2,1)S(1)} collective-permute-done((bf16[8,4,2,128]{3,0,2,1:T(8,128)(2,1)S(1)}, bf16[8,4,2,128]{3,0,2,1:T(8,128)(2,1)S(1)}, u32[]{:S(2)}, u32[]{:S(2)}) %collective-permute-start.11) | collective-permute-done | bytes 16416 | tf_op jit(solution)/shard_map/ppermute | solution.py:16
  40.3 2.0 %collective-permute-start.12 = (bf16[4,8,4,2,128]{4,1,0,3,2:T(8,128)(2,1)S(1)}, bf16[4,8,4,2,128]{4,1,0,3,2:T(8,128)(2,1)S(1)}, u32[]{:S(2)}, u32[]{:S(2)}) collective-permute-start(bf16[4,8,4,2,128]{4,1,0,3,2:T(8,128)(2,1)S(1)} %get-tuple-element.33), channel_id=1, source_target_pairs={{0,4},{4,8},{8,12},{12,0},{1,5},{5,9},{9,13},{13,1},{2,6},{6,10},{... | collective-permute-start | bytes 196616 | tf_op jit(solution)/shard_map/ppermute | solution.py:16
  42.3 1.5 %collective-permute-start.13 = (bf16[4,8,4,2,128]{4,1,0,3,2:T(8,128)(2,1)S(1)}, bf16[4,8,4,2,128]{4,1,0,3,2:T(8,128)(2,1)S(1)}, u32[]{:S(2)}, u32[]{:S(2)}) collective-permute-start(bf16[4,8,4,2,128]{4,1,0,3,2:T(8,128)(2,1)S(1)} %get-tuple-element.33), channel_id=1, source_target_pairs={{0,8},{4,12},{8,0},{12,4},{1,9},{5,13},{9,1},{13,5},{2,10},{6,14},... | collective-permute-start | bytes 196616 | tf_op jit(solution)/shard_map/ppermute | solution.py:16
  43.8 0.9 %collective-permute-start.14 = (bf16[4,8,4,2,128]{4,1,0,3,2:T(8,128)(2,1)S(1)}, bf16[4,8,4,2,128]{4,1,0,3,2:T(8,128)(2,1)S(1)}, u32[]{:S(2)}, u32[]{:S(2)}) collective-permute-start(bf16[4,8,4,2,128]{4,1,0,3,2:T(8,128)(2,1)S(1)} %get-tuple-element.33), channel_id=1, source_target_pairs={{0,12},{4,0},{8,4},{12,8},{1,13},{5,1},{9,5},{13,9},{2,14},{6,2},{... | collective-permute-start | bytes 196616 | tf_op jit(solution)/shard_map/ppermute | solution.py:16
  44.7 0.6 %copy.56 = f32[4,16,128]{2,1,0:T(8,128)} copy(f32[4,16,128]{2,0,1:T(4,128)S(1)} %get-tuple-element.13) | data formatting | bytes 65536
  45.3 0.3 collective-permute-done.12
  45.7 0.9 %collective-permute-done.13 = bf16[4,8,4,2,128]{4,1,0,3,2:T(8,128)(2,1)S(1)} collective-permute-done((bf16[4,8,4,2,128]{4,1,0,3,2:T(8,128)(2,1)S(1)}, bf16[4,8,4,2,128]{4,1,0,3,2:T(8,128)(2,1)S(1)}, u32[]{:S(2)}, u32[]{:S(2)}) %collective-permute-start.13) | collective-permute-done | bytes 65568 | tf_op jit(solution)/shard_map/ppermute | solution.py:16
  46.6 1.5 %collective-permute-done.14 = bf16[4,8,4,2,128]{4,1,0,3,2:T(8,128)(2,1)S(1)} collective-permute-done((bf16[4,8,4,2,128]{4,1,0,3,2:T(8,128)(2,1)S(1)}, bf16[4,8,4,2,128]{4,1,0,3,2:T(8,128)(2,1)S(1)}, u32[]{:S(2)}, u32[]{:S(2)}) %collective-permute-start.14) | collective-permute-done | bytes 65568 | tf_op jit(solution)/shard_map/ppermute | solution.py:16
  48.1 0.3 fusion
  48.5 1.3 %copy.57 = bf16[1,1,1,256,4,2,128]{6,5,4,3,2,1,0:T(2,128)(2,1)} copy(bf16[1,1,1,256,4,2,128]{6,3,5,4,2,1,0:T(8,128)(2,1)S(1)} %fusion) | data formatting | bytes 1048576
  (25 shorter events, 0.5 us)
Async XLA Ops:
  1.3 2.0 %collective-permute-start = (s32[2,256]{1,0:T(2,128)S(1)}, s32[2,256]{1,0:T(2,128)S(1)}, u32[]{:S(2)}, u32[]{:S(2)}) collective-permute-start(s32[2,256]{1,0:T(2,128)S(1)} %pad_add_fusion), channel_id=1, source_target_pairs={{0,16},{16,0},{1,17},{17,1},{2,18},{18,2},{3,19},{19,3},{4,20},{20... | collective-permute-start | bytes 6152 | tf_op jit(solution)/shard_map/ppermute | solution.py:16
  1.8 1.5 %copy-start.1 = (s32[1,1,1,256]{3,2,1,0:T(1,128)S(1)}, s32[1,1,1,256]{3,2,1,0:T(1,128)}, u32[]{:S(2)}) copy-start(s32[1,1,1,256]{3,2,1,0:T(1,128)} %param.8) | copy-start | bytes 3076
  1.8 1.5 %copy-start.2 = (s32[1,1,1,256]{3,2,1,0:T(1,128)S(1)}, s32[1,1,1,256]{3,2,1,0:T(1,128)}, u32[]{:S(2)}) copy-start(s32[1,1,1,256]{3,2,1,0:T(1,128)} %param.7) | copy-start | bytes 3076
  3.2 2.0 %collective-permute-start.1 = (bf16[256,4,2,128]{3,0,2,1:T(8,128)(2,1)S(1)}, bf16[256,4,2,128]{3,0,2,1:T(8,128)(2,1)S(1)}, u32[]{:S(2)}, u32[]{:S(2)}) collective-permute-start(bf16[256,4,2,128]{3,0,2,1:T(8,128)(2,1)S(1)} %get-tuple-element.18), channel_id=1, source_target_pairs={{0,16},{16,0},{1,17},{17,1},{2,18},{18,2},{3,19},{19,3},{4,20},{20... | collective-permute-start | bytes 1572872 | tf_op jit(solution)/shard_map/ppermute | solution.py:16
  5.6 9.4 %collective-permute-start.2 = (f32[48,4,2,128]{3,0,2,1:T(8,128)S(1)}, f32[48,4,2,128]{3,0,2,1:T(8,128)S(1)}, u32[]{:S(2)}, u32[]{:S(2)}) collective-permute-start(f32[48,4,2,128]{3,0,2,1:T(8,128)S(1)} %get-tuple-element.19), channel_id=1, source_target_pairs={{0,4},{4,8},{8,12},{12,0},{1,5},{5,9},{9,13},{13,1},{2,6},{6,10},{... | collective-permute-start | bytes 589832 | tf_op jit(solution)/shard_map/ppermute | solution.py:16
  8.3 10.9 %collective-permute-start.3 = (f32[48,4,2,128]{3,0,2,1:T(8,128)S(1)}, f32[48,4,2,128]{3,0,2,1:T(8,128)S(1)}, u32[]{:S(2)}, u32[]{:S(2)}) collective-permute-start(f32[48,4,2,128]{3,0,2,1:T(8,128)S(1)} %get-tuple-element.21), channel_id=1, source_target_pairs={{0,12},{4,0},{8,4},{12,8},{1,13},{5,1},{9,5},{13,9},{2,14},{6,2},{... | collective-permute-start | bytes 589832 | tf_op jit(solution)/shard_map/ppermute | solution.py:16
  9.3 9.9 %collective-permute-start.4 = (f32[48,4,2,128]{3,0,2,1:T(8,128)S(1)}, f32[48,4,2,128]{3,0,2,1:T(8,128)S(1)}, u32[]{:S(2)}, u32[]{:S(2)}) collective-permute-start(f32[48,4,2,128]{3,0,2,1:T(8,128)S(1)} %get-tuple-element.20), channel_id=1, source_target_pairs={{0,8},{4,12},{8,0},{12,4},{1,9},{5,13},{9,1},{13,5},{2,10},{6,14},... | collective-permute-start | bytes 589832 | tf_op jit(solution)/shard_map/ppermute | solution.py:16
  21.2 6.3 %collective-permute-start.5 = (f32[102,128]{1,0:T(8,128)S(1)}, f32[102,128]{1,0:T(8,128)S(1)}, u32[]{:S(2)}, u32[]{:S(2)}) collective-permute-start(f32[102,128]{1,0:T(8,128)S(1)} %bitcast.87), channel_id=1, source_target_pairs={{0,1},{1,2},{2,3},{3,0},{4,5},{5,6},{6,7},{7,4},{8,9},{9,10},{10,1... | collective-permute-start | bytes 156680 | tf_op jit(solution)/shard_map/ppermute | solution.py:16
  22.8 6.7 %collective-permute-start.6 = (f32[102,128]{1,0:T(8,128)S(1)}, f32[102,128]{1,0:T(8,128)S(1)}, u32[]{:S(2)}, u32[]{:S(2)}) collective-permute-start(f32[102,128]{1,0:T(8,128)S(1)} %bitcast.86), channel_id=1, source_target_pairs={{0,2},{1,3},{2,0},{3,1},{4,6},{5,7},{6,4},{7,5},{8,10},{9,11},{10,... | collective-permute-start | bytes 156680 | tf_op jit(solution)/shard_map/ppermute | solution.py:16
  25.4 4.4 %collective-permute-start.7 = (f32[102,128]{1,0:T(8,128)S(1)}, f32[102,128]{1,0:T(8,128)S(1)}, u32[]{:S(2)}, u32[]{:S(2)}) collective-permute-start(f32[102,128]{1,0:T(8,128)S(1)} %bitcast.85), channel_id=1, source_target_pairs={{0,3},{1,0},{2,1},{3,2},{4,7},{5,4},{6,5},{7,6},{8,11},{9,8},{10,9... | collective-permute-start | bytes 156680 | tf_op jit(solution)/shard_map/ppermute | solution.py:16
  29.8 1.3 %collective-permute-start.8 = (f32[102,128]{1,0:T(8,128)S(1)}, f32[102,128]{1,0:T(8,128)S(1)}, u32[]{:S(2)}, u32[]{:S(2)}) collective-permute-start(f32[102,128]{1,0:T(8,128)S(1)} %fusion.49), channel_id=1, source_target_pairs={{0,16},{16,0},{1,17},{17,1},{2,18},{18,2},{3,19},{19,3},{4,20},{20... | collective-permute-start | bytes 156680 | tf_op jit(solution)/shard_map/ppermute | solution.py:16
  32.0 0.8 %copy-start = (f32[4,16,128]{2,1,0:T(8,128)S(1)}, f32[4,16,128]{2,1,0:T(8,128)}, u32[]{:S(2)}) copy-start(f32[4,16,128]{2,1,0:T(8,128)} %param.9) | copy-start | bytes 98308
  33.0 5.6 %collective-permute-start.9 = (bf16[8,4,2,128]{3,0,2,1:T(8,128)(2,1)S(1)}, bf16[8,4,2,128]{3,0,2,1:T(8,128)(2,1)S(1)}, u32[]{:S(2)}, u32[]{:S(2)}) collective-permute-start(bf16[8,4,2,128]{3,0,2,1:T(8,128)(2,1)S(1)} %bitcast.77), channel_id=1, source_target_pairs={{0,1},{1,2},{2,3},{3,0},{4,5},{5,6},{6,7},{7,4},{8,9},{9,10},{10,1... | collective-permute-start | bytes 49160 | tf_op jit(solution)/shard_map/ppermute | solution.py:16
  34.0 4.9 %collective-permute-start.10 = (bf16[8,4,2,128]{3,0,2,1:T(8,128)(2,1)S(1)}, bf16[8,4,2,128]{3,0,2,1:T(8,128)(2,1)S(1)}, u32[]{:S(2)}, u32[]{:S(2)}) collective-permute-start(bf16[8,4,2,128]{3,0,2,1:T(8,128)(2,1)S(1)} %bitcast.78), channel_id=1, source_target_pairs={{0,2},{1,3},{2,0},{3,1},{4,6},{5,7},{6,4},{7,5},{8,10},{9,11},{10,... | collective-permute-start | bytes 49160 | tf_op jit(solution)/shard_map/ppermute | solution.py:16
  36.5 3.7 %collective-permute-start.11 = (bf16[8,4,2,128]{3,0,2,1:T(8,128)(2,1)S(1)}, bf16[8,4,2,128]{3,0,2,1:T(8,128)(2,1)S(1)}, u32[]{:S(2)}, u32[]{:S(2)}) collective-permute-start(bf16[8,4,2,128]{3,0,2,1:T(8,128)(2,1)S(1)} %bitcast.79), channel_id=1, source_target_pairs={{0,3},{1,0},{2,1},{3,2},{4,7},{5,4},{6,5},{7,6},{8,11},{9,8},{10,9... | collective-permute-start | bytes 49160 | tf_op jit(solution)/shard_map/ppermute | solution.py:16
  40.3 5.4 %collective-permute-start.12 = (bf16[4,8,4,2,128]{4,1,0,3,2:T(8,128)(2,1)S(1)}, bf16[4,8,4,2,128]{4,1,0,3,2:T(8,128)(2,1)S(1)}, u32[]{:S(2)}, u32[]{:S(2)}) collective-permute-start(bf16[4,8,4,2,128]{4,1,0,3,2:T(8,128)(2,1)S(1)} %get-tuple-element.33), channel_id=1, source_target_pairs={{0,4},{4,8},{8,12},{12,0},{1,5},{5,9},{9,13},{13,1},{2,6},{6,10},{... | collective-permute-start | bytes 196616 | tf_op jit(solution)/shard_map/ppermute | solution.py:16
  42.3 4.3 %collective-permute-start.13 = (bf16[4,8,4,2,128]{4,1,0,3,2:T(8,128)(2,1)S(1)}, bf16[4,8,4,2,128]{4,1,0,3,2:T(8,128)(2,1)S(1)}, u32[]{:S(2)}, u32[]{:S(2)}) collective-permute-start(bf16[4,8,4,2,128]{4,1,0,3,2:T(8,128)(2,1)S(1)} %get-tuple-element.33), channel_id=1, source_target_pairs={{0,8},{4,12},{8,0},{12,4},{1,9},{5,13},{9,1},{13,5},{2,10},{6,14},... | collective-permute-start | bytes 196616 | tf_op jit(solution)/shard_map/ppermute | solution.py:16
  43.8 4.3 %collective-permute-start.14 = (bf16[4,8,4,2,128]{4,1,0,3,2:T(8,128)(2,1)S(1)}, bf16[4,8,4,2,128]{4,1,0,3,2:T(8,128)(2,1)S(1)}, u32[]{:S(2)}, u32[]{:S(2)}) collective-permute-start(bf16[4,8,4,2,128]{4,1,0,3,2:T(8,128)(2,1)S(1)} %get-tuple-element.33), channel_id=1, source_target_pairs={{0,12},{4,0},{8,4},{12,8},{1,13},{5,1},{9,5},{13,9},{2,14},{6,2},{... | collective-permute-start | bytes 196616 | tf_op jit(solution)/shard_map/ppermute | solution.py:16

commit v10 on v4

--- a/solution.py
+++ b/solution.py
@@ -39,12 +39,8 @@
     is_grad = me_g == 0
     kept = jnp.where(is_grad, slot_grad, slot_illum)
     given = jnp.where(is_grad, slot_illum, slot_grad)
-    places = jnp.stack([owners, patches])
-    taken = shifted(given, "group", size_g, 1)
-    taken_places = shifted(places, "group", size_g, 1)
-    rows_in = jnp.concatenate([kept, taken], axis=0)
-    all_owners = jnp.concatenate([owners, taken_places[0]])
-    all_patches = jnp.concatenate([patches, taken_places[1]])
+    all_owners = owners
+    all_patches = patches
 
     halo_patches = h // patch_rows
     ext_patches = per_tile + 2 * halo_patches
@@ -70,7 +66,10 @@
     onehot = (
         (own_row[None, :] == row_ids) | (next_row[None, :] == row_ids) | (prev_row[None, :] == row_ids)
     ).astype(jnp.bfloat16)
-    table = jnp.einsum("rw,wlpc->rlpc", onehot, rows_in, preferred_element_type=jnp.float32)
+    for_partner = jnp.einsum("rw,wlpc->rlpc", onehot, given, preferred_element_type=jnp.float32)
+    table = jnp.einsum(
+        "rw,wlpc->rlpc", onehot, kept, preferred_element_type=jnp.float32
+    ) + shifted(for_partner, "group", size_g, 1)
     flat = table.reshape(size_x, size_y * ext_patches, levels, patch_rows, patch_cols)
 
     part = flat[0]

time: 48.7 us -> 50.3 us (1.033)
  local copies, waits for them, and re-layouts: 3.97 us -> 5.2 us
    unnamed x9, local copies, waits for them, and re-layouts: 1.98 us -> 3.22 us
    another operation x1 -> x0, other arithmetic: 0.71 us -> none  [local(): places = jnp.stack([owners, patches])]
    select_n x1, other arithmetic: 1.39 us -> 2.08 us  [local(): kept = jnp.where(is_grad, slot_grad, slot_illum)]
    ppermute x15 -> x14, starting transfers between devices: 20.3 us -> 20.4 us  [shifted(): lax.ppermute(value, axis, [(s, (s + step) % count) for s in range(count)])]
    ppermute x15 -> x14, waiting for transfers between devices: 18.5 us -> 18.5 us  [shifted(): lax.ppermute(value, axis, [(s, (s + step) % count) for s in range(count)])]
  transfers between devices with their start and end apart: 15 -> 14, of which waited for: 14 -> 14; matrix products, arithmetic and copies ran while one was open for 5% -> 2% of each run, Pallas kernels for 0% -> 0%
where the time goes in v10:
time: 50.3 us; the launch traced here: 50 us
  starting transfers between devices  20.4 us (41%)
  waiting for transfers between devices  18.5 us (37%)
  local copies, waits for them, and re-layouts  5.2 us (10%)
  other arithmetic  4.12 us (8%)
  between operations  0.95 us (2%)
  matrix products  0.88 us (2%)
    ppermute x14, starting transfers between devices, shifted(): lax.ppermute(value, axis, [(s, (s + step) % count) for s in range(count)])  20.4 us
    ppermute x14, waiting for transfers between devices, shifted(): lax.ppermute(value, axis, [(s, (s + step) % count) for s in range(count)])  18.5 us
    unnamed x9, local copies, waits for them, and re-layouts  3.22 us
    select_n x1, other arithmetic, local(): kept = jnp.where(is_grad, slot_grad, slot_illum)  2.08 us
  transfers between devices with their start and end apart: 14, of which 14 were waited for; matrix products, arithmetic and copies ran while one was open for 2% of the time, Pallas kernels for 0%

profile of v10, /device:TPU:0, one launch (start us, length us, event | category | flops | bytes accessed | tf_op | source)
XLA Modules:
  0.0 50.0 jit_solution(2823828798614136338)
XLA Ops:
  0.6 0.0 copy-start.2
  0.6 0.0 copy-start.1
  0.7 0.7 %copy-done.2 = s32[1,1,1,256]{3,2,1,0:T(1,128)S(1)} copy-done((s32[1,1,1,256]{3,2,1,0:T(1,128)S(1)}, s32[1,1,1,256]{3,2,1,0:T(1,128)}, u32[]{:S(2)}) %copy-start.2) | copy-done | bytes 1048
  1.3 0.0 copy-done.1
  1.4 2.1 %fusion.1 = (bf16[256,4,2,128]{3,2,1,0:T(2,128)(2,1)S(1)}, bf16[256,4,2,128]{3,2,1,0:T(2,128)(2,1)S(1)}) fusion(bf16[1,1,1,256,4,2,128]{6,5,4,3,2,1,0:T(2,128)(2,1)} %param.5, bf16[1,1,1,256,4,2,128]{6,5,4,3,2,1,0:T(2,128)(2,1)} %param.6, pred[]{:T(512)S(6)} %eq.64), kind=kLoop, calls=%fused_computation.5 | loop fusion | flops 524288 | bytes 2097153 | tf_op jit(solution)/shard_map/jit(_where)/select_n | solution.py:40
  3.5 0.3 fusion.3
  3.8 0.5 %collective-permute-start = (f32[192,4,2,128]{3,0,2,1:T(8,128)S(1)}, f32[192,4,2,128]{3,0,2,1:T(8,128)S(1)}, u32[]{:S(2)}, u32[]{:S(2)}) collective-permute-start(f32[192,4,2,128]{3,0,2,1:T(8,128)S(1)} %fusion.3), channel_id=1, source_target_pairs={{0,16},{16,0},{1,17},{17,1},{2,18},{18,2},{3,19},{19,3},{4,20},{20... | collective-permute-start | bytes 2359304 | tf_op jit(solution)/shard_map/ppermute | solution.py:16
  4.3 1.9 %collective-permute-done = f32[192,4,2,128]{3,0,2,1:T(8,128)S(1)} collective-permute-done((f32[192,4,2,128]{3,0,2,1:T(8,128)S(1)}, f32[192,4,2,128]{3,0,2,1:T(8,128)S(1)}, u32[]{:S(2)}, u32[]{:S(2)}) %collective-permute-start) | collective-permute-done | bytes 786464 | tf_op jit(solution)/shard_map/ppermute | solution.py:16
  6.2 0.3 convolution_add_fusion
  6.5 2.9 %collective-permute-start.1 = (f32[48,4,2,128]{3,0,2,1:T(8,128)S(1)}, f32[48,4,2,128]{3,0,2,1:T(8,128)S(1)}, u32[]{:S(2)}, u32[]{:S(2)}) collective-permute-start(f32[48,4,2,128]{3,0,2,1:T(8,128)S(1)} %get-tuple-element.21), channel_id=1, source_target_pairs={{0,4},{4,8},{8,12},{12,0},{1,5},{5,9},{9,13},{13,1},{2,6},{6,10},{... | collective-permute-start | bytes 589832 | tf_op jit(solution)/shard_map/ppermute | solution.py:16
  9.5 1.5 %collective-permute-start.2 = (f32[48,4,2,128]{3,0,2,1:T(8,128)S(1)}, f32[48,4,2,128]{3,0,2,1:T(8,128)S(1)}, u32[]{:S(2)}, u32[]{:S(2)}) collective-permute-start(f32[48,4,2,128]{3,0,2,1:T(8,128)S(1)} %get-tuple-element.23), channel_id=1, source_target_pairs={{0,8},{4,12},{8,0},{12,4},{1,9},{5,13},{9,1},{13,5},{2,10},{6,14},... | collective-permute-start | bytes 589832 | tf_op jit(solution)/shard_map/ppermute | solution.py:16
  11.0 1.4 %collective-permute-start.3 = (f32[48,4,2,128]{3,0,2,1:T(8,128)S(1)}, f32[48,4,2,128]{3,0,2,1:T(8,128)S(1)}, u32[]{:S(2)}, u32[]{:S(2)}) collective-permute-start(f32[48,4,2,128]{3,0,2,1:T(8,128)S(1)} %get-tuple-element.22), channel_id=1, source_target_pairs={{0,12},{4,0},{8,4},{12,8},{1,13},{5,1},{9,5},{13,9},{2,14},{6,2},{... | collective-permute-start | bytes 589832 | tf_op jit(solution)/shard_map/ppermute | solution.py:16
  12.4 3.7 %collective-permute-done.1 = f32[48,4,2,128]{3,0,2,1:T(8,128)S(1)} collective-permute-done((f32[48,4,2,128]{3,0,2,1:T(8,128)S(1)}, f32[48,4,2,128]{3,0,2,1:T(8,128)S(1)}, u32[]{:S(2)}, u32[]{:S(2)}) %collective-permute-start.1) | collective-permute-done | bytes 196640 | tf_op jit(solution)/shard_map/ppermute | solution.py:16
  16.1 3.7 %collective-permute-done.2 = f32[48,4,2,128]{3,0,2,1:T(8,128)S(1)} collective-permute-done((f32[48,4,2,128]{3,0,2,1:T(8,128)S(1)}, f32[48,4,2,128]{3,0,2,1:T(8,128)S(1)}, u32[]{:S(2)}, u32[]{:S(2)}) %collective-permute-start.2) | collective-permute-done | bytes 196640 | tf_op jit(solution)/shard_map/ppermute | solution.py:16
  19.8 0.3 collective-permute-done.3
  20.2 0.1 copy.36
  20.3 0.1 copy.37
  20.4 0.1 copy.39
  20.6 0.5 fusion.6
  21.0 0.3 reshape.326
  21.3 0.2 reshape_reshape.3
  21.6 0.6 %slice_reduce_fusion.3 = (f32[13056]{0:T(1024)S(1)}, f32[13056]{0:T(1024)S(1)}, f32[13056]{0:T(1024)S(1)}, f32[13056]{0:T(1024)S(1)}) fusion(f32[4,13056]{1,0:T(4,128)S(1)} %constant_dynamic-update-slice_fusion), kind=kLoop, calls=%fused_computation.98 | loop fusion | bytes 417792 | tf_op jit(solution)/shard_map/slice | solution.py:85
  22.1 1.6 %collective-permute-start.4 = (f32[102,128]{1,0:T(8,128)S(1)}, f32[102,128]{1,0:T(8,128)S(1)}, u32[]{:S(2)}, u32[]{:S(2)}) collective-permute-start(f32[102,128]{1,0:T(8,128)S(1)} %bitcast.84), channel_id=1, source_target_pairs={{0,1},{1,2},{2,3},{3,0},{4,5},{5,6},{6,7},{7,4},{8,9},{9,10},{10,1... | collective-permute-start | bytes 156680 | tf_op jit(solution)/shard_map/ppermute | solution.py:16
  23.8 2.6 %collective-permute-start.5 = (f32[102,128]{1,0:T(8,128)S(1)}, f32[102,128]{1,0:T(8,128)S(1)}, u32[]{:S(2)}, u32[]{:S(2)}) collective-permute-start(f32[102,128]{1,0:T(8,128)S(1)} %bitcast.83), channel_id=1, source_target_pairs={{0,2},{1,3},{2,0},{3,1},{4,6},{5,7},{6,4},{7,5},{8,10},{9,11},{10,... | collective-permute-start | bytes 156680 | tf_op jit(solution)/shard_map/ppermute | solution.py:16
  26.3 1.3 %collective-permute-start.6 = (f32[102,128]{1,0:T(8,128)S(1)}, f32[102,128]{1,0:T(8,128)S(1)}, u32[]{:S(2)}, u32[]{:S(2)}) collective-permute-start(f32[102,128]{1,0:T(8,128)S(1)} %bitcast.82), channel_id=1, source_target_pairs={{0,3},{1,0},{2,1},{3,2},{4,7},{5,4},{6,5},{7,6},{8,11},{9,8},{10,9... | collective-permute-start | bytes 156680 | tf_op jit(solution)/shard_map/ppermute | solution.py:16
  27.7 0.7 %collective-permute-done.4 = f32[102,128]{1,0:T(8,128)S(1)} collective-permute-done((f32[102,128]{1,0:T(8,128)S(1)}, f32[102,128]{1,0:T(8,128)S(1)}, u32[]{:S(2)}, u32[]{:S(2)}) %collective-permute-start.4) | collective-permute-done | bytes 52256 | tf_op jit(solution)/shard_map/ppermute | solution.py:16
  28.4 2.0 %collective-permute-done.5 = f32[102,128]{1,0:T(8,128)S(1)} collective-permute-done((f32[102,128]{1,0:T(8,128)S(1)}, f32[102,128]{1,0:T(8,128)S(1)}, u32[]{:S(2)}, u32[]{:S(2)}) %collective-permute-start.5) | collective-permute-done | bytes 52256 | tf_op jit(solution)/shard_map/ppermute | solution.py:16
  30.4 0.3 collective-permute-done.6
  30.8 0.1 collective-permute-start.7
  30.8 0.1 broadcast_and_fusion
  30.9 0.1 slice.245
  31.0 1.1 %collective-permute-done.7 = f32[102,128]{1,0:T(8,128)S(1)} collective-permute-done((f32[102,128]{1,0:T(8,128)S(1)}, f32[102,128]{1,0:T(8,128)S(1)}, u32[]{:S(2)}, u32[]{:S(2)}) %collective-permute-start.7) | collective-permute-done | bytes 52256 | tf_op jit(solution)/shard_map/ppermute | solution.py:16
  32.1 0.1 reshape.327
  32.2 0.1 reshape.329
  32.4 0.2 fusion.79
  32.6 0.4 fusion.51
  33.0 0.2 fusion.22
  33.2 0.2 fusion.31
  33.4 0.2 fusion.40
  33.6 0.0 copy-start
  33.6 0.2 fusion.43
  33.8 0.6 %copy-done = f32[4,16,128]{2,1,0:T(8,128)S(1)} copy-done((f32[4,16,128]{2,1,0:T(8,128)S(1)}, f32[4,16,128]{2,1,0:T(8,128)}, u32[]{:S(2)}) %copy-start) | copy-done | bytes 32792
  34.4 0.2 fusion.75
  34.5 1.0 %collective-permute-start.8 = (bf16[8,4,2,128]{3,0,2,1:T(8,128)(2,1)S(1)}, bf16[8,4,2,128]{3,0,2,1:T(8,128)(2,1)S(1)}, u32[]{:S(2)}, u32[]{:S(2)}) collective-permute-start(bf16[8,4,2,128]{3,0,2,1:T(8,128)(2,1)S(1)} %bitcast.74), channel_id=1, source_target_pairs={{0,1},{1,2},{2,3},{3,0},{4,5},{5,6},{6,7},{7,4},{8,9},{9,10},{10,1... | collective-permute-start | bytes 49160 | tf_op jit(solution)/shard_map/ppermute | solution.py:16
  35.5 2.5 %collective-permute-start.9 = (bf16[8,4,2,128]{3,0,2,1:T(8,128)(2,1)S(1)}, bf16[8,4,2,128]{3,0,2,1:T(8,128)(2,1)S(1)}, u32[]{:S(2)}, u32[]{:S(2)}) collective-permute-start(bf16[8,4,2,128]{3,0,2,1:T(8,128)(2,1)S(1)} %bitcast.75), channel_id=1, source_target_pairs={{0,2},{1,3},{2,0},{3,1},{4,6},{5,7},{6,4},{7,5},{8,10},{9,11},{10,... | collective-permute-start | bytes 49160 | tf_op jit(solution)/shard_map/ppermute | solution.py:16
  38.0 0.5 %collective-permute-start.10 = (bf16[8,4,2,128]{3,0,2,1:T(8,128)(2,1)S(1)}, bf16[8,4,2,128]{3,0,2,1:T(8,128)(2,1)S(1)}, u32[]{:S(2)}, u32[]{:S(2)}) collective-permute-start(bf16[8,4,2,128]{3,0,2,1:T(8,128)(2,1)S(1)} %bitcast.76), channel_id=1, source_target_pairs={{0,3},{1,0},{2,1},{3,2},{4,7},{5,4},{6,5},{7,6},{8,11},{9,8},{10,9... | collective-permute-start | bytes 49160 | tf_op jit(solution)/shard_map/ppermute | solution.py:16
  38.5 1.6 %collective-permute-done.8 = bf16[8,4,2,128]{3,0,2,1:T(8,128)(2,1)S(1)} collective-permute-done((bf16[8,4,2,128]{3,0,2,1:T(8,128)(2,1)S(1)}, bf16[8,4,2,128]{3,0,2,1:T(8,128)(2,1)S(1)}, u32[]{:S(2)}, u32[]{:S(2)}) %collective-permute-start.8) | collective-permute-done | bytes 16416 | tf_op jit(solution)/shard_map/ppermute | solution.py:16
  40.2 0.3 collective-permute-done.9
  40.4 1.3 %collective-permute-done.10 = bf16[8,4,2,128]{3,0,2,1:T(8,128)(2,1)S(1)} collective-permute-done((bf16[8,4,2,128]{3,0,2,1:T(8,128)(2,1)S(1)}, bf16[8,4,2,128]{3,0,2,1:T(8,128)(2,1)S(1)}, u32[]{:S(2)}, u32[]{:S(2)}) %collective-permute-start.10) | collective-permute-done | bytes 16416 | tf_op jit(solution)/shard_map/ppermute | solution.py:16
  41.8 1.8 %collective-permute-start.11 = (bf16[4,8,4,2,128]{4,1,0,3,2:T(8,128)(2,1)S(1)}, bf16[4,8,4,2,128]{4,1,0,3,2:T(8,128)(2,1)S(1)}, u32[]{:S(2)}, u32[]{:S(2)}) collective-permute-start(bf16[4,8,4,2,128]{4,1,0,3,2:T(8,128)(2,1)S(1)} %get-tuple-element.35), channel_id=1, source_target_pairs={{0,4},{4,8},{8,12},{12,0},{1,5},{5,9},{9,13},{13,1},{2,6},{6,10},{... | collective-permute-start | bytes 196616 | tf_op jit(solution)/shard_map/ppermute | solution.py:16
  43.6 0.5 %collective-permute-start.12 = (bf16[4,8,4,2,128]{4,1,0,3,2:T(8,128)(2,1)S(1)}, bf16[4,8,4,2,128]{4,1,0,3,2:T(8,128)(2,1)S(1)}, u32[]{:S(2)}, u32[]{:S(2)}) collective-permute-start(bf16[4,8,4,2,128]{4,1,0,3,2:T(8,128)(2,1)S(1)} %get-tuple-element.35), channel_id=1, source_target_pairs={{0,8},{4,12},{8,0},{12,4},{1,9},{5,13},{9,1},{13,5},{2,10},{6,14},... | collective-permute-start | bytes 196616 | tf_op jit(solution)/shard_map/ppermute | solution.py:16
  44.1 2.1 %collective-permute-start.13 = (bf16[4,8,4,2,128]{4,1,0,3,2:T(8,128)(2,1)S(1)}, bf16[4,8,4,2,128]{4,1,0,3,2:T(8,128)(2,1)S(1)}, u32[]{:S(2)}, u32[]{:S(2)}) collective-permute-start(bf16[4,8,4,2,128]{4,1,0,3,2:T(8,128)(2,1)S(1)} %get-tuple-element.35), channel_id=1, source_target_pairs={{0,12},{4,0},{8,4},{12,8},{1,13},{5,1},{9,5},{13,9},{2,14},{6,2},{... | collective-permute-start | bytes 196616 | tf_op jit(solution)/shard_map/ppermute | solution.py:16
  46.2 0.6 %copy.50 = f32[4,16,128]{2,1,0:T(8,128)} copy(f32[4,16,128]{2,0,1:T(4,128)S(1)} %get-tuple-element.15) | data formatting | bytes 65536
  46.8 0.2 collective-permute-done.11
  47.0 0.8 %collective-permute-done.12 = bf16[4,8,4,2,128]{4,1,0,3,2:T(8,128)(2,1)S(1)} collective-permute-done((bf16[4,8,4,2,128]{4,1,0,3,2:T(8,128)(2,1)S(1)}, bf16[4,8,4,2,128]{4,1,0,3,2:T(8,128)(2,1)S(1)}, u32[]{:S(2)}, u32[]{:S(2)}) %collective-permute-start.12) | collective-permute-done | bytes 65568 | tf_op jit(solution)/shard_map/ppermute | solution.py:16
  47.8 0.5 %collective-permute-done.13 = bf16[4,8,4,2,128]{4,1,0,3,2:T(8,128)(2,1)S(1)} collective-permute-done((bf16[4,8,4,2,128]{4,1,0,3,2:T(8,128)(2,1)S(1)}, bf16[4,8,4,2,128]{4,1,0,3,2:T(8,128)(2,1)S(1)}, u32[]{:S(2)}, u32[]{:S(2)}) %collective-permute-start.13) | collective-permute-done | bytes 65568 | tf_op jit(solution)/shard_map/ppermute | solution.py:16
  48.4 0.3 fusion
  48.7 1.3 %copy.51 = bf16[1,1,1,256,4,2,128]{6,5,4,3,2,1,0:T(2,128)(2,1)} copy(bf16[1,1,1,256,4,2,128]{6,3,5,4,2,1,0:T(8,128)(2,1)S(1)} %fusion) | data formatting | bytes 1048576
  (24 shorter events, 0.4 us)
Async XLA Ops:
  0.6 0.7 %copy-start.2 = (s32[1,1,1,256]{3,2,1,0:T(1,128)S(1)}, s32[1,1,1,256]{3,2,1,0:T(1,128)}, u32[]{:S(2)}) copy-start(s32[1,1,1,256]{3,2,1,0:T(1,128)} %param.7) | copy-start | bytes 3076
  0.6 0.7 %copy-start.1 = (s32[1,1,1,256]{3,2,1,0:T(1,128)S(1)}, s32[1,1,1,256]{3,2,1,0:T(1,128)}, u32[]{:S(2)}) copy-start(s32[1,1,1,256]{3,2,1,0:T(1,128)} %param.8) | copy-start | bytes 3076
  3.8 2.4 %collective-permute-start = (f32[192,4,2,128]{3,0,2,1:T(8,128)S(1)}, f32[192,4,2,128]{3,0,2,1:T(8,128)S(1)}, u32[]{:S(2)}, u32[]{:S(2)}) collective-permute-start(f32[192,4,2,128]{3,0,2,1:T(8,128)S(1)} %fusion.3), channel_id=1, source_target_pairs={{0,16},{16,0},{1,17},{17,1},{2,18},{18,2},{3,19},{19,3},{4,20},{20... | collective-permute-start | bytes 2359304 | tf_op jit(solution)/shard_map/ppermute | solution.py:16
  6.5 9.6 %collective-permute-start.1 = (f32[48,4,2,128]{3,0,2,1:T(8,128)S(1)}, f32[48,4,2,128]{3,0,2,1:T(8,128)S(1)}, u32[]{:S(2)}, u32[]{:S(2)}) collective-permute-start(f32[48,4,2,128]{3,0,2,1:T(8,128)S(1)} %get-tuple-element.21), channel_id=1, source_target_pairs={{0,4},{4,8},{8,12},{12,0},{1,5},{5,9},{9,13},{13,1},{2,6},{6,10},{... | collective-permute-start | bytes 589832 | tf_op jit(solution)/shard_map/ppermute | solution.py:16
  9.5 10.4 %collective-permute-start.2 = (f32[48,4,2,128]{3,0,2,1:T(8,128)S(1)}, f32[48,4,2,128]{3,0,2,1:T(8,128)S(1)}, u32[]{:S(2)}, u32[]{:S(2)}) collective-permute-start(f32[48,4,2,128]{3,0,2,1:T(8,128)S(1)} %get-tuple-element.23), channel_id=1, source_target_pairs={{0,8},{4,12},{8,0},{12,4},{1,9},{5,13},{9,1},{13,5},{2,10},{6,14},... | collective-permute-start | bytes 589832 | tf_op jit(solution)/shard_map/ppermute | solution.py:16
  11.0 9.1 %collective-permute-start.3 = (f32[48,4,2,128]{3,0,2,1:T(8,128)S(1)}, f32[48,4,2,128]{3,0,2,1:T(8,128)S(1)}, u32[]{:S(2)}, u32[]{:S(2)}) collective-permute-start(f32[48,4,2,128]{3,0,2,1:T(8,128)S(1)} %get-tuple-element.22), channel_id=1, source_target_pairs={{0,12},{4,0},{8,4},{12,8},{1,13},{5,1},{9,5},{13,9},{2,14},{6,2},{... | collective-permute-start | bytes 589832 | tf_op jit(solution)/shard_map/ppermute | solution.py:16
  22.1 6.3 %collective-permute-start.4 = (f32[102,128]{1,0:T(8,128)S(1)}, f32[102,128]{1,0:T(8,128)S(1)}, u32[]{:S(2)}, u32[]{:S(2)}) collective-permute-start(f32[102,128]{1,0:T(8,128)S(1)} %bitcast.84), channel_id=1, source_target_pairs={{0,1},{1,2},{2,3},{3,0},{4,5},{5,6},{6,7},{7,4},{8,9},{9,10},{10,1... | collective-permute-start | bytes 156680 | tf_op jit(solution)/shard_map/ppermute | solution.py:16
  23.8 6.7 %collective-permute-start.5 = (f32[102,128]{1,0:T(8,128)S(1)}, f32[102,128]{1,0:T(8,128)S(1)}, u32[]{:S(2)}, u32[]{:S(2)}) collective-permute-start(f32[102,128]{1,0:T(8,128)S(1)} %bitcast.83), channel_id=1, source_target_pairs={{0,2},{1,3},{2,0},{3,1},{4,6},{5,7},{6,4},{7,5},{8,10},{9,11},{10,... | collective-permute-start | bytes 156680 | tf_op jit(solution)/shard_map/ppermute | solution.py:16
  26.3 4.4 %collective-permute-start.6 = (f32[102,128]{1,0:T(8,128)S(1)}, f32[102,128]{1,0:T(8,128)S(1)}, u32[]{:S(2)}, u32[]{:S(2)}) collective-permute-start(f32[102,128]{1,0:T(8,128)S(1)} %bitcast.82), channel_id=1, source_target_pairs={{0,3},{1,0},{2,1},{3,2},{4,7},{5,4},{6,5},{7,6},{8,11},{9,8},{10,9... | collective-permute-start | bytes 156680 | tf_op jit(solution)/shard_map/ppermute | solution.py:16
  30.8 1.3 %collective-permute-start.7 = (f32[102,128]{1,0:T(8,128)S(1)}, f32[102,128]{1,0:T(8,128)S(1)}, u32[]{:S(2)}, u32[]{:S(2)}) collective-permute-start(f32[102,128]{1,0:T(8,128)S(1)} %fusion.54), channel_id=1, source_target_pairs={{0,16},{16,0},{1,17},{17,1},{2,18},{18,2},{3,19},{19,3},{4,20},{20... | collective-permute-start | bytes 156680 | tf_op jit(solution)/shard_map/ppermute | solution.py:16
  33.6 0.8 %copy-start = (f32[4,16,128]{2,1,0:T(8,128)S(1)}, f32[4,16,128]{2,1,0:T(8,128)}, u32[]{:S(2)}) copy-start(f32[4,16,128]{2,1,0:T(8,128)} %param.9) | copy-start | bytes 98308
  34.5 5.6 %collective-permute-start.8 = (bf16[8,4,2,128]{3,0,2,1:T(8,128)(2,1)S(1)}, bf16[8,4,2,128]{3,0,2,1:T(8,128)(2,1)S(1)}, u32[]{:S(2)}, u32[]{:S(2)}) collective-permute-start(bf16[8,4,2,128]{3,0,2,1:T(8,128)(2,1)S(1)} %bitcast.74), channel_id=1, source_target_pairs={{0,1},{1,2},{2,3},{3,0},{4,5},{5,6},{6,7},{7,4},{8,9},{9,10},{10,1... | collective-permute-start | bytes 49160 | tf_op jit(solution)/shard_map/ppermute | solution.py:16
  35.5 4.9 %collective-permute-start.9 = (bf16[8,4,2,128]{3,0,2,1:T(8,128)(2,1)S(1)}, bf16[8,4,2,128]{3,0,2,1:T(8,128)(2,1)S(1)}, u32[]{:S(2)}, u32[]{:S(2)}) collective-permute-start(bf16[8,4,2,128]{3,0,2,1:T(8,128)(2,1)S(1)} %bitcast.75), channel_id=1, source_target_pairs={{0,2},{1,3},{2,0},{3,1},{4,6},{5,7},{6,4},{7,5},{8,10},{9,11},{10,... | collective-permute-start | bytes 49160 | tf_op jit(solution)/shard_map/ppermute | solution.py:16
  38.0 3.7 %collective-permute-start.10 = (bf16[8,4,2,128]{3,0,2,1:T(8,128)(2,1)S(1)}, bf16[8,4,2,128]{3,0,2,1:T(8,128)(2,1)S(1)}, u32[]{:S(2)}, u32[]{:S(2)}) collective-permute-start(bf16[8,4,2,128]{3,0,2,1:T(8,128)(2,1)S(1)} %bitcast.76), channel_id=1, source_target_pairs={{0,3},{1,0},{2,1},{3,2},{4,7},{5,4},{6,5},{7,6},{8,11},{9,8},{10,9... | collective-permute-start | bytes 49160 | tf_op jit(solution)/shard_map/ppermute | solution.py:16
  41.8 5.2 %collective-permute-start.11 = (bf16[4,8,4,2,128]{4,1,0,3,2:T(8,128)(2,1)S(1)}, bf16[4,8,4,2,128]{4,1,0,3,2:T(8,128)(2,1)S(1)}, u32[]{:S(2)}, u32[]{:S(2)}) collective-permute-start(bf16[4,8,4,2,128]{4,1,0,3,2:T(8,128)(2,1)S(1)} %get-tuple-element.35), channel_id=1, source_target_pairs={{0,4},{4,8},{8,12},{12,0},{1,5},{5,9},{9,13},{13,1},{2,6},{6,10},{... | collective-permute-start | bytes 196616 | tf_op jit(solution)/shard_map/ppermute | solution.py:16
  43.6 4.3 %collective-permute-start.12 = (bf16[4,8,4,2,128]{4,1,0,3,2:T(8,128)(2,1)S(1)}, bf16[4,8,4,2,128]{4,1,0,3,2:T(8,128)(2,1)S(1)}, u32[]{:S(2)}, u32[]{:S(2)}) collective-permute-start(bf16[4,8,4,2,128]{4,1,0,3,2:T(8,128)(2,1)S(1)} %get-tuple-element.35), channel_id=1, source_target_pairs={{0,8},{4,12},{8,0},{12,4},{1,9},{5,13},{9,1},{13,5},{2,10},{6,14},... | collective-permute-start | bytes 196616 | tf_op jit(solution)/shard_map/ppermute | solution.py:16
  44.1 4.3 %collective-permute-start.13 = (bf16[4,8,4,2,128]{4,1,0,3,2:T(8,128)(2,1)S(1)}, bf16[4,8,4,2,128]{4,1,0,3,2:T(8,128)(2,1)S(1)}, u32[]{:S(2)}, u32[]{:S(2)}) collective-permute-start(bf16[4,8,4,2,128]{4,1,0,3,2:T(8,128)(2,1)S(1)} %get-tuple-element.35), channel_id=1, source_target_pairs={{0,12},{4,0},{8,4},{12,8},{1,13},{5,1},{9,5},{13,9},{2,14},{6,2},{... | collective-permute-start | bytes 196616 | tf_op jit(solution)/shard_map/ppermute | solution.py:16

commit v11 on v4

--- a/solution.py
+++ b/solution.py
@@ -97,14 +97,13 @@
         whole_rows = jnp.concatenate([sides[..., :h], main, sides[..., h:]], axis=-1)
         return whole_rows.transpose(1, 0, 2, 3).reshape(levels, ext_rows, ext_cols)
 
-    grad_ext = unpack(grad_flat)
-    illum_ext = unpack(illum_flat)
+    precondition = unpack(grad_flat / (illum_flat + damping))
     pos_x = me_x * tile_rows - h + jnp.arange(ext_rows)
     pos_y = me_y * tile_cols - h + jnp.arange(ext_cols)
     inside = ((pos_x >= 0) & (pos_x < size_x * tile_rows))[:, None] & (
         (pos_y >= 0) & (pos_y < size_y * tile_cols)
     )[None, :]
-    field_now = jnp.where(inside, grad_ext / (illum_ext + damping), 0.0)
+    field_now = jnp.where(inside, precondition, 0.0)
     for sweep_index in range(SWEEPS):
         padded = jnp.pad(field_now, 1)
         beside = (

time: 48.7 us -> 49.5 us (1.016)
  local copies, waits for them, and re-layouts: 3.97 us -> 4.9 us
    div x1, local copies, waits for them, and re-layouts: 0.03 us -> 1.26 us  [local(): precondition = unpack(grad_flat / (illum_flat + damping))]
where the time goes in v11:
time: 49.5 us; the launch traced here: 49.3 us
  starting transfers between devices  20.3 us (41%)
  waiting for transfers between devices  18.5 us (37%)
  local copies, waits for them, and re-layouts  4.9 us (10%)
  other arithmetic  4 us (8%)
  between operations  0.9 us (2%)
  matrix products  0.71 us (1%)
    ppermute x15, starting transfers between devices, shifted(): lax.ppermute(value, axis, [(s, (s + step) % count) for s in range(count)])  20.3 us
    ppermute x15, waiting for transfers between devices, shifted(): lax.ppermute(value, axis, [(s, (s + step) % count) for s in range(count)])  18.5 us
    unnamed x9, local copies, waits for them, and re-layouts  1.98 us
    select_n x1, other arithmetic, local(): kept = jnp.where(is_grad, slot_grad, slot_illum)  1.39 us
    div x1, local copies, waits for them, and re-layouts, local(): precondition = unpack(grad_flat / (illum_flat + damping))  1.26 us
  transfers between devices with their start and end apart: 15, of which 14 were waited for; matrix products, arithmetic and copies ran while one was open for 5% of the time, Pallas kernels for 0%

profile of v11, /device:TPU:0, one launch (start us, length us, event | category | flops | bytes accessed | tf_op | source)
XLA Modules:
  0.0 49.3 jit_solution(14517267337676990118)
XLA Ops:
  0.6 0.7 %pad_add_fusion = s32[2,256]{1,0:T(2,128)S(1)} fusion(s32[1,256]{1,0:T(1,128)} %bitcast.89, s32[1,256]{1,0:T(1,128)} %bitcast.95), kind=kLoop, calls=%fused_computation.146 | loop fusion | flops 512 | bytes 4096 | tf_op jit(solution)/shard_map/stack | solution.py:42
  1.3 0.5 collective-permute-start
  1.8 0.0 copy-start.1
  1.8 0.0 copy-start.2
  1.8 1.4 %select_bitcast_fusion.1 = (bf16[256,4,2,128]{3,0,2,1:T(8,128)(2,1)S(1)}, bf16[256,4,2,128]{3,0,2,1:T(8,128)(2,1)S(1)}) fusion(pred[]{:T(512)S(6)} %eq.65, bf16[1,1,1,256,4,2,128]{6,5,4,3,2,1,0:T(2,128)(2,1)} %param.6, bf16[1,1,1,256,4,2,128]{6,5,4,3,2,1,0:T(2,128)(2,1)} %param.5), kind=kLoop, calls=%fused_computation.7 | loop fusion | flops 524288 | bytes 2097153 | tf_op jit(solution)/shard_map/jit(_where)/select_n | solution.py:40
  3.2 0.1 collective-permute-start.1
  3.3 0.0 collective-permute-done
  3.3 0.0 copy-done.1
  3.3 0.0 copy-done.2
  3.4 1.8 %collective-permute-done.1 = bf16[256,4,2,128]{3,0,2,1:T(8,128)(2,1)S(1)} collective-permute-done((bf16[256,4,2,128]{3,0,2,1:T(8,128)(2,1)S(1)}, bf16[256,4,2,128]{3,0,2,1:T(8,128)(2,1)S(1)}, u32[]{:S(2)}, u32[]{:S(2)}) %collective-permute-start.1) | collective-permute-done | bytes 524320 | tf_op jit(solution)/shard_map/ppermute | solution.py:16
  5.2 0.4 fusion.1
  5.6 2.7 %collective-permute-start.2 = (f32[48,4,2,128]{3,0,2,1:T(8,128)S(1)}, f32[48,4,2,128]{3,0,2,1:T(8,128)S(1)}, u32[]{:S(2)}, u32[]{:S(2)}) collective-permute-start(f32[48,4,2,128]{3,0,2,1:T(8,128)S(1)} %get-tuple-element.21), channel_id=1, source_target_pairs={{0,4},{4,8},{8,12},{12,0},{1,5},{5,9},{9,13},{13,1},{2,6},{6,10},{... | collective-permute-start | bytes 589832 | tf_op jit(solution)/shard_map/ppermute | solution.py:16
  8.3 1.5 %collective-permute-start.3 = (f32[48,4,2,128]{3,0,2,1:T(8,128)S(1)}, f32[48,4,2,128]{3,0,2,1:T(8,128)S(1)}, u32[]{:S(2)}, u32[]{:S(2)}) collective-permute-start(f32[48,4,2,128]{3,0,2,1:T(8,128)S(1)} %get-tuple-element.23), channel_id=1, source_target_pairs={{0,8},{4,12},{8,0},{12,4},{1,9},{5,13},{9,1},{13,5},{2,10},{6,14},... | collective-permute-start | bytes 589832 | tf_op jit(solution)/shard_map/ppermute | solution.py:16
  9.8 1.4 %collective-permute-start.4 = (f32[48,4,2,128]{3,0,2,1:T(8,128)S(1)}, f32[48,4,2,128]{3,0,2,1:T(8,128)S(1)}, u32[]{:S(2)}, u32[]{:S(2)}) collective-permute-start(f32[48,4,2,128]{3,0,2,1:T(8,128)S(1)} %get-tuple-element.22), channel_id=1, source_target_pairs={{0,12},{4,0},{8,4},{12,8},{1,13},{5,1},{9,5},{13,9},{2,14},{6,2},{... | collective-permute-start | bytes 589832 | tf_op jit(solution)/shard_map/ppermute | solution.py:16
  11.2 3.8 %collective-permute-done.2 = f32[48,4,2,128]{3,0,2,1:T(8,128)S(1)} collective-permute-done((f32[48,4,2,128]{3,0,2,1:T(8,128)S(1)}, f32[48,4,2,128]{3,0,2,1:T(8,128)S(1)}, u32[]{:S(2)}, u32[]{:S(2)}) %collective-permute-start.2) | collective-permute-done | bytes 196640 | tf_op jit(solution)/shard_map/ppermute | solution.py:16
  15.0 3.9 %collective-permute-done.3 = f32[48,4,2,128]{3,0,2,1:T(8,128)S(1)} collective-permute-done((f32[48,4,2,128]{3,0,2,1:T(8,128)S(1)}, f32[48,4,2,128]{3,0,2,1:T(8,128)S(1)}, u32[]{:S(2)}, u32[]{:S(2)}) %collective-permute-start.3) | collective-permute-done | bytes 196640 | tf_op jit(solution)/shard_map/ppermute | solution.py:16
  18.9 0.3 collective-permute-done.4
  19.3 0.1 copy.42
  19.4 0.1 copy.43
  19.5 0.1 copy.45
  19.6 0.5 fusion.9
  20.1 0.3 reshape.517
  20.4 0.2 reshape_reshape.3
  20.6 0.6 %slice_reduce_fusion.3 = (f32[13056]{0:T(1024)S(1)}, f32[13056]{0:T(1024)S(1)}, f32[13056]{0:T(1024)S(1)}, f32[13056]{0:T(1024)S(1)}) fusion(f32[4,13056]{1,0:T(4,128)S(1)} %constant_dynamic-update-slice_fusion), kind=kLoop, calls=%fused_computation.92 | loop fusion | bytes 417792 | tf_op jit(solution)/shard_map/slice | solution.py:86
  21.2 1.6 %collective-permute-start.5 = (f32[102,128]{1,0:T(8,128)S(1)}, f32[102,128]{1,0:T(8,128)S(1)}, u32[]{:S(2)}, u32[]{:S(2)}) collective-permute-start(f32[102,128]{1,0:T(8,128)S(1)} %bitcast.85), channel_id=1, source_target_pairs={{0,1},{1,2},{2,3},{3,0},{4,5},{5,6},{6,7},{7,4},{8,9},{9,10},{10,1... | collective-permute-start | bytes 156680 | tf_op jit(solution)/shard_map/ppermute | solution.py:16
  22.8 2.6 %collective-permute-start.6 = (f32[102,128]{1,0:T(8,128)S(1)}, f32[102,128]{1,0:T(8,128)S(1)}, u32[]{:S(2)}, u32[]{:S(2)}) collective-permute-start(f32[102,128]{1,0:T(8,128)S(1)} %bitcast.84), channel_id=1, source_target_pairs={{0,2},{1,3},{2,0},{3,1},{4,6},{5,7},{6,4},{7,5},{8,10},{9,11},{10,... | collective-permute-start | bytes 156680 | tf_op jit(solution)/shard_map/ppermute | solution.py:16
  25.4 1.3 %collective-permute-start.7 = (f32[102,128]{1,0:T(8,128)S(1)}, f32[102,128]{1,0:T(8,128)S(1)}, u32[]{:S(2)}, u32[]{:S(2)}) collective-permute-start(f32[102,128]{1,0:T(8,128)S(1)} %bitcast.83), channel_id=1, source_target_pairs={{0,3},{1,0},{2,1},{3,2},{4,7},{5,4},{6,5},{7,6},{8,11},{9,8},{10,9... | collective-permute-start | bytes 156680 | tf_op jit(solution)/shard_map/ppermute | solution.py:16
  26.8 0.7 %collective-permute-done.5 = f32[102,128]{1,0:T(8,128)S(1)} collective-permute-done((f32[102,128]{1,0:T(8,128)S(1)}, f32[102,128]{1,0:T(8,128)S(1)}, u32[]{:S(2)}, u32[]{:S(2)}) %collective-permute-start.5) | collective-permute-done | bytes 52256 | tf_op jit(solution)/shard_map/ppermute | solution.py:16
  27.4 2.1 %collective-permute-done.6 = f32[102,128]{1,0:T(8,128)S(1)} collective-permute-done((f32[102,128]{1,0:T(8,128)S(1)}, f32[102,128]{1,0:T(8,128)S(1)}, u32[]{:S(2)}, u32[]{:S(2)}) %collective-permute-start.6) | collective-permute-done | bytes 52256 | tf_op jit(solution)/shard_map/ppermute | solution.py:16
  29.5 0.3 collective-permute-done.7
  29.8 0.1 collective-permute-start.8
  29.9 0.1 broadcast_and_fusion
  30.0 0.1 slice.231
  30.0 1.1 %collective-permute-done.8 = f32[102,128]{1,0:T(8,128)S(1)} collective-permute-done((f32[102,128]{1,0:T(8,128)S(1)}, f32[102,128]{1,0:T(8,128)S(1)}, u32[]{:S(2)}, u32[]{:S(2)}) %collective-permute-start.8) | collective-permute-done | bytes 52256 | tf_op jit(solution)/shard_map/ppermute | solution.py:16
  31.1 1.3 %div.37 = f32[204,4,2,8]{3,2,1,0:T(2,128)S(1)} reshape(f32[102,128]{1,0:T(8,128)S(1)} %add_divide_fusion) | data formatting | bytes 104448 | tf_op jit(solution)/shard_map/div | solution.py:100
  32.4 0.1 fusion.84
  32.5 0.0 copy-start
  32.5 0.2 maximum_bitcast_fusion
  32.9 0.2 fusion.23
  33.0 0.2 fusion.32
  33.2 0.2 fusion.41
  33.4 0.2 fusion.44
  33.6 0.0 copy-done
  33.6 0.2 fusion.82
  33.8 1.0 %collective-permute-start.9 = (bf16[8,4,2,128]{3,0,2,1:T(8,128)(2,1)S(1)}, bf16[8,4,2,128]{3,0,2,1:T(8,128)(2,1)S(1)}, u32[]{:S(2)}, u32[]{:S(2)}) collective-permute-start(bf16[8,4,2,128]{3,0,2,1:T(8,128)(2,1)S(1)} %bitcast.75), channel_id=1, source_target_pairs={{0,1},{1,2},{2,3},{3,0},{4,5},{5,6},{6,7},{7,4},{8,9},{9,10},{10,1... | collective-permute-start | bytes 49160 | tf_op jit(solution)/shard_map/ppermute | solution.py:16
  34.8 2.5 %collective-permute-start.10 = (bf16[8,4,2,128]{3,0,2,1:T(8,128)(2,1)S(1)}, bf16[8,4,2,128]{3,0,2,1:T(8,128)(2,1)S(1)}, u32[]{:S(2)}, u32[]{:S(2)}) collective-permute-start(bf16[8,4,2,128]{3,0,2,1:T(8,128)(2,1)S(1)} %bitcast.76), channel_id=1, source_target_pairs={{0,2},{1,3},{2,0},{3,1},{4,6},{5,7},{6,4},{7,5},{8,10},{9,11},{10,... | collective-permute-start | bytes 49160 | tf_op jit(solution)/shard_map/ppermute | solution.py:16
  37.3 0.5 %collective-permute-start.11 = (bf16[8,4,2,128]{3,0,2,1:T(8,128)(2,1)S(1)}, bf16[8,4,2,128]{3,0,2,1:T(8,128)(2,1)S(1)}, u32[]{:S(2)}, u32[]{:S(2)}) collective-permute-start(bf16[8,4,2,128]{3,0,2,1:T(8,128)(2,1)S(1)} %bitcast.77), channel_id=1, source_target_pairs={{0,3},{1,0},{2,1},{3,2},{4,7},{5,4},{6,5},{7,6},{8,11},{9,8},{10,9... | collective-permute-start | bytes 49160 | tf_op jit(solution)/shard_map/ppermute | solution.py:16
  37.8 1.6 %collective-permute-done.9 = bf16[8,4,2,128]{3,0,2,1:T(8,128)(2,1)S(1)} collective-permute-done((bf16[8,4,2,128]{3,0,2,1:T(8,128)(2,1)S(1)}, bf16[8,4,2,128]{3,0,2,1:T(8,128)(2,1)S(1)}, u32[]{:S(2)}, u32[]{:S(2)}) %collective-permute-start.9) | collective-permute-done | bytes 16416 | tf_op jit(solution)/shard_map/ppermute | solution.py:16
  39.4 0.3 collective-permute-done.10
  39.7 1.3 %collective-permute-done.11 = bf16[8,4,2,128]{3,0,2,1:T(8,128)(2,1)S(1)} collective-permute-done((bf16[8,4,2,128]{3,0,2,1:T(8,128)(2,1)S(1)}, bf16[8,4,2,128]{3,0,2,1:T(8,128)(2,1)S(1)}, u32[]{:S(2)}, u32[]{:S(2)}) %collective-permute-start.11) | collective-permute-done | bytes 16416 | tf_op jit(solution)/shard_map/ppermute | solution.py:16
  41.1 1.8 %collective-permute-start.12 = (bf16[4,8,4,2,128]{4,1,0,3,2:T(8,128)(2,1)S(1)}, bf16[4,8,4,2,128]{4,1,0,3,2:T(8,128)(2,1)S(1)}, u32[]{:S(2)}, u32[]{:S(2)}) collective-permute-start(bf16[4,8,4,2,128]{4,1,0,3,2:T(8,128)(2,1)S(1)} %get-tuple-element.33), channel_id=1, source_target_pairs={{0,4},{4,8},{8,12},{12,0},{1,5},{5,9},{9,13},{13,1},{2,6},{6,10},{... | collective-permute-start | bytes 196616 | tf_op jit(solution)/shard_map/ppermute | solution.py:16
  42.8 0.5 %collective-permute-start.13 = (bf16[4,8,4,2,128]{4,1,0,3,2:T(8,128)(2,1)S(1)}, bf16[4,8,4,2,128]{4,1,0,3,2:T(8,128)(2,1)S(1)}, u32[]{:S(2)}, u32[]{:S(2)}) collective-permute-start(bf16[4,8,4,2,128]{4,1,0,3,2:T(8,128)(2,1)S(1)} %get-tuple-element.33), channel_id=1, source_target_pairs={{0,8},{4,12},{8,0},{12,4},{1,9},{5,13},{9,1},{13,5},{2,10},{6,14},... | collective-permute-start | bytes 196616 | tf_op jit(solution)/shard_map/ppermute | solution.py:16
  43.3 2.1 %collective-permute-start.14 = (bf16[4,8,4,2,128]{4,1,0,3,2:T(8,128)(2,1)S(1)}, bf16[4,8,4,2,128]{4,1,0,3,2:T(8,128)(2,1)S(1)}, u32[]{:S(2)}, u32[]{:S(2)}) collective-permute-start(bf16[4,8,4,2,128]{4,1,0,3,2:T(8,128)(2,1)S(1)} %get-tuple-element.33), channel_id=1, source_target_pairs={{0,12},{4,0},{8,4},{12,8},{1,13},{5,1},{9,5},{13,9},{2,14},{6,2},{... | collective-permute-start | bytes 196616 | tf_op jit(solution)/shard_map/ppermute | solution.py:16
  45.5 0.6 %copy.56 = f32[4,16,128]{2,1,0:T(8,128)} copy(f32[4,16,128]{2,0,1:T(4,128)S(1)} %get-tuple-element.13) | data formatting | bytes 65536
  46.1 0.2 collective-permute-done.12
  46.3 0.8 %collective-permute-done.13 = bf16[4,8,4,2,128]{4,1,0,3,2:T(8,128)(2,1)S(1)} collective-permute-done((bf16[4,8,4,2,128]{4,1,0,3,2:T(8,128)(2,1)S(1)}, bf16[4,8,4,2,128]{4,1,0,3,2:T(8,128)(2,1)S(1)}, u32[]{:S(2)}, u32[]{:S(2)}) %collective-permute-start.13) | collective-permute-done | bytes 65568 | tf_op jit(solution)/shard_map/ppermute | solution.py:16
  47.1 0.5 %collective-permute-done.14 = bf16[4,8,4,2,128]{4,1,0,3,2:T(8,128)(2,1)S(1)} collective-permute-done((bf16[4,8,4,2,128]{4,1,0,3,2:T(8,128)(2,1)S(1)}, bf16[4,8,4,2,128]{4,1,0,3,2:T(8,128)(2,1)S(1)}, u32[]{:S(2)}, u32[]{:S(2)}) %collective-permute-start.14) | collective-permute-done | bytes 65568 | tf_op jit(solution)/shard_map/ppermute | solution.py:16
  47.6 0.3 fusion
  48.0 1.3 %copy.57 = bf16[1,1,1,256,4,2,128]{6,5,4,3,2,1,0:T(2,128)(2,1)} copy(bf16[1,1,1,256,4,2,128]{6,3,5,4,2,1,0:T(8,128)(2,1)S(1)} %fusion) | data formatting | bytes 1048576
  (22 shorter events, 0.5 us)
Async XLA Ops:
  1.3 2.0 %collective-permute-start = (s32[2,256]{1,0:T(2,128)S(1)}, s32[2,256]{1,0:T(2,128)S(1)}, u32[]{:S(2)}, u32[]{:S(2)}) collective-permute-start(s32[2,256]{1,0:T(2,128)S(1)} %pad_add_fusion), channel_id=1, source_target_pairs={{0,16},{16,0},{1,17},{17,1},{2,18},{18,2},{3,19},{19,3},{4,20},{20... | collective-permute-start | bytes 6152 | tf_op jit(solution)/shard_map/ppermute | solution.py:16
  1.8 1.5 %copy-start.1 = (s32[1,1,1,256]{3,2,1,0:T(1,128)S(1)}, s32[1,1,1,256]{3,2,1,0:T(1,128)}, u32[]{:S(2)}) copy-start(s32[1,1,1,256]{3,2,1,0:T(1,128)} %param.8) | copy-start | bytes 3076
  1.8 1.5 %copy-start.2 = (s32[1,1,1,256]{3,2,1,0:T(1,128)S(1)}, s32[1,1,1,256]{3,2,1,0:T(1,128)}, u32[]{:S(2)}) copy-start(s32[1,1,1,256]{3,2,1,0:T(1,128)} %param.7) | copy-start | bytes 3076
  3.2 2.0 %collective-permute-start.1 = (bf16[256,4,2,128]{3,0,2,1:T(8,128)(2,1)S(1)}, bf16[256,4,2,128]{3,0,2,1:T(8,128)(2,1)S(1)}, u32[]{:S(2)}, u32[]{:S(2)}) collective-permute-start(bf16[256,4,2,128]{3,0,2,1:T(8,128)(2,1)S(1)} %get-tuple-element.18), channel_id=1, source_target_pairs={{0,16},{16,0},{1,17},{17,1},{2,18},{18,2},{3,19},{19,3},{4,20},{20... | collective-permute-start | bytes 1572872 | tf_op jit(solution)/shard_map/ppermute | solution.py:16
  5.6 9.4 %collective-permute-start.2 = (f32[48,4,2,128]{3,0,2,1:T(8,128)S(1)}, f32[48,4,2,128]{3,0,2,1:T(8,128)S(1)}, u32[]{:S(2)}, u32[]{:S(2)}) collective-permute-start(f32[48,4,2,128]{3,0,2,1:T(8,128)S(1)} %get-tuple-element.21), channel_id=1, source_target_pairs={{0,4},{4,8},{8,12},{12,0},{1,5},{5,9},{9,13},{13,1},{2,6},{6,10},{... | collective-permute-start | bytes 589832 | tf_op jit(solution)/shard_map/ppermute | solution.py:16
  8.3 10.6 %collective-permute-start.3 = (f32[48,4,2,128]{3,0,2,1:T(8,128)S(1)}, f32[48,4,2,128]{3,0,2,1:T(8,128)S(1)}, u32[]{:S(2)}, u32[]{:S(2)}) collective-permute-start(f32[48,4,2,128]{3,0,2,1:T(8,128)S(1)} %get-tuple-element.23), channel_id=1, source_target_pairs={{0,8},{4,12},{8,0},{12,4},{1,9},{5,13},{9,1},{13,5},{2,10},{6,14},... | collective-permute-start | bytes 589832 | tf_op jit(solution)/shard_map/ppermute | solution.py:16
  9.8 9.4 %collective-permute-start.4 = (f32[48,4,2,128]{3,0,2,1:T(8,128)S(1)}, f32[48,4,2,128]{3,0,2,1:T(8,128)S(1)}, u32[]{:S(2)}, u32[]{:S(2)}) collective-permute-start(f32[48,4,2,128]{3,0,2,1:T(8,128)S(1)} %get-tuple-element.22), channel_id=1, source_target_pairs={{0,12},{4,0},{8,4},{12,8},{1,13},{5,1},{9,5},{13,9},{2,14},{6,2},{... | collective-permute-start | bytes 589832 | tf_op jit(solution)/shard_map/ppermute | solution.py:16
  21.2 6.3 %collective-permute-start.5 = (f32[102,128]{1,0:T(8,128)S(1)}, f32[102,128]{1,0:T(8,128)S(1)}, u32[]{:S(2)}, u32[]{:S(2)}) collective-permute-start(f32[102,128]{1,0:T(8,128)S(1)} %bitcast.85), channel_id=1, source_target_pairs={{0,1},{1,2},{2,3},{3,0},{4,5},{5,6},{6,7},{7,4},{8,9},{9,10},{10,1... | collective-permute-start | bytes 156680 | tf_op jit(solution)/shard_map/ppermute | solution.py:16
  22.8 6.7 %collective-permute-start.6 = (f32[102,128]{1,0:T(8,128)S(1)}, f32[102,128]{1,0:T(8,128)S(1)}, u32[]{:S(2)}, u32[]{:S(2)}) collective-permute-start(f32[102,128]{1,0:T(8,128)S(1)} %bitcast.84), channel_id=1, source_target_pairs={{0,2},{1,3},{2,0},{3,1},{4,6},{5,7},{6,4},{7,5},{8,10},{9,11},{10,... | collective-permute-start | bytes 156680 | tf_op jit(solution)/shard_map/ppermute | solution.py:16
  25.4 4.4 %collective-permute-start.7 = (f32[102,128]{1,0:T(8,128)S(1)}, f32[102,128]{1,0:T(8,128)S(1)}, u32[]{:S(2)}, u32[]{:S(2)}) collective-permute-start(f32[102,128]{1,0:T(8,128)S(1)} %bitcast.83), channel_id=1, source_target_pairs={{0,3},{1,0},{2,1},{3,2},{4,7},{5,4},{6,5},{7,6},{8,11},{9,8},{10,9... | collective-permute-start | bytes 156680 | tf_op jit(solution)/shard_map/ppermute | solution.py:16
  29.8 1.3 %collective-permute-start.8 = (f32[102,128]{1,0:T(8,128)S(1)}, f32[102,128]{1,0:T(8,128)S(1)}, u32[]{:S(2)}, u32[]{:S(2)}) collective-permute-start(f32[102,128]{1,0:T(8,128)S(1)} %fusion.48), channel_id=1, source_target_pairs={{0,16},{16,0},{1,17},{17,1},{2,18},{18,2},{3,19},{19,3},{4,20},{20... | collective-permute-start | bytes 156680 | tf_op jit(solution)/shard_map/ppermute | solution.py:16
  32.5 1.1 %copy-start = (f32[4,16,128]{2,1,0:T(8,128)S(1)}, f32[4,16,128]{2,1,0:T(8,128)}, u32[]{:S(2)}) copy-start(f32[4,16,128]{2,1,0:T(8,128)} %param.9) | copy-start | bytes 98308
  33.8 5.6 %collective-permute-start.9 = (bf16[8,4,2,128]{3,0,2,1:T(8,128)(2,1)S(1)}, bf16[8,4,2,128]{3,0,2,1:T(8,128)(2,1)S(1)}, u32[]{:S(2)}, u32[]{:S(2)}) collective-permute-start(bf16[8,4,2,128]{3,0,2,1:T(8,128)(2,1)S(1)} %bitcast.75), channel_id=1, source_target_pairs={{0,1},{1,2},{2,3},{3,0},{4,5},{5,6},{6,7},{7,4},{8,9},{9,10},{10,1... | collective-permute-start | bytes 49160 | tf_op jit(solution)/shard_map/ppermute | solution.py:16
  34.8 4.9 %collective-permute-start.10 = (bf16[8,4,2,128]{3,0,2,1:T(8,128)(2,1)S(1)}, bf16[8,4,2,128]{3,0,2,1:T(8,128)(2,1)S(1)}, u32[]{:S(2)}, u32[]{:S(2)}) collective-permute-start(bf16[8,4,2,128]{3,0,2,1:T(8,128)(2,1)S(1)} %bitcast.76), channel_id=1, source_target_pairs={{0,2},{1,3},{2,0},{3,1},{4,6},{5,7},{6,4},{7,5},{8,10},{9,11},{10,... | collective-permute-start | bytes 49160 | tf_op jit(solution)/shard_map/ppermute | solution.py:16
  37.3 3.7 %collective-permute-start.11 = (bf16[8,4,2,128]{3,0,2,1:T(8,128)(2,1)S(1)}, bf16[8,4,2,128]{3,0,2,1:T(8,128)(2,1)S(1)}, u32[]{:S(2)}, u32[]{:S(2)}) collective-permute-start(bf16[8,4,2,128]{3,0,2,1:T(8,128)(2,1)S(1)} %bitcast.77), channel_id=1, source_target_pairs={{0,3},{1,0},{2,1},{3,2},{4,7},{5,4},{6,5},{7,6},{8,11},{9,8},{10,9... | collective-permute-start | bytes 49160 | tf_op jit(solution)/shard_map/ppermute | solution.py:16
  41.1 5.2 %collective-permute-start.12 = (bf16[4,8,4,2,128]{4,1,0,3,2:T(8,128)(2,1)S(1)}, bf16[4,8,4,2,128]{4,1,0,3,2:T(8,128)(2,1)S(1)}, u32[]{:S(2)}, u32[]{:S(2)}) collective-permute-start(bf16[4,8,4,2,128]{4,1,0,3,2:T(8,128)(2,1)S(1)} %get-tuple-element.33), channel_id=1, source_target_pairs={{0,4},{4,8},{8,12},{12,0},{1,5},{5,9},{9,13},{13,1},{2,6},{6,10},{... | collective-permute-start | bytes 196616 | tf_op jit(solution)/shard_map/ppermute | solution.py:16
  42.8 4.3 %collective-permute-start.13 = (bf16[4,8,4,2,128]{4,1,0,3,2:T(8,128)(2,1)S(1)}, bf16[4,8,4,2,128]{4,1,0,3,2:T(8,128)(2,1)S(1)}, u32[]{:S(2)}, u32[]{:S(2)}) collective-permute-start(bf16[4,8,4,2,128]{4,1,0,3,2:T(8,128)(2,1)S(1)} %get-tuple-element.33), channel_id=1, source_target_pairs={{0,8},{4,12},{8,0},{12,4},{1,9},{5,13},{9,1},{13,5},{2,10},{6,14},... | collective-permute-start | bytes 196616 | tf_op jit(solution)/shard_map/ppermute | solution.py:16
  43.3 4.3 %collective-permute-start.14 = (bf16[4,8,4,2,128]{4,1,0,3,2:T(8,128)(2,1)S(1)}, bf16[4,8,4,2,128]{4,1,0,3,2:T(8,128)(2,1)S(1)}, u32[]{:S(2)}, u32[]{:S(2)}) collective-permute-start(bf16[4,8,4,2,128]{4,1,0,3,2:T(8,128)(2,1)S(1)} %get-tuple-element.33), channel_id=1, source_target_pairs={{0,12},{4,0},{8,4},{12,8},{1,13},{5,1},{9,5},{13,9},{2,14},{6,2},{... | collective-permute-start | bytes 196616 | tf_op jit(solution)/shard_map/ppermute | solution.py:16

commit v12 on v4

--- a/solution.py
+++ b/solution.py
@@ -2,6 +2,8 @@
 import jax.numpy as jnp
 from jax import lax
 from jax.sharding import PartitionSpec as P
+from jax.experimental import pallas as pl
+from jax.experimental.pallas import tpu as pltpu
 
 SWEEPS = 4
 HALO = SWEEPS
@@ -14,6 +16,25 @@
 
 def shifted(value, axis, count, step):
     return lax.ppermute(value, axis, [(s, (s + step) % count) for s in range(count)])
+
+
+def sweeps_kernel(field_ref, inside_ref, out_ref):
+    inside = inside_ref[...] > 0.5
+    field_now = field_ref[...]
+    rows = field_now.shape[1]
+    cols = field_now.shape[2]
+    no_level = jnp.zeros_like(field_now[:1])
+    for sweep_index in range(SWEEPS):
+        beside = (
+            (pltpu.roll(field_now, rows - 1, 1) + pltpu.roll(field_now, 1, 1))
+            + (pltpu.roll(field_now, cols - 1, 2) + pltpu.roll(field_now, 1, 2))
+            + (
+                jnp.concatenate([field_now[1:], no_level], axis=0)
+                + jnp.concatenate([no_level, field_now[:-1]], axis=0)
+            )
+        )
+        field_now = jnp.where(inside, field_now + smooth_rate * (beside - 6.0 * field_now), 0.0)
+    out_ref[...] = field_now
 
 
 def local(gradient_windows, illumination_windows, window_owners, window_patches, velocity):
@@ -104,15 +125,18 @@
     inside = ((pos_x >= 0) & (pos_x < size_x * tile_rows))[:, None] & (
         (pos_y >= 0) & (pos_y < size_y * tile_cols)
     )[None, :]
-    field_now = jnp.where(inside, grad_ext / (illum_ext + damping), 0.0)
-    for sweep_index in range(SWEEPS):
-        padded = jnp.pad(field_now, 1)
-        beside = (
-            (padded[1:-1, 2:, 1:-1] + padded[1:-1, :-2, 1:-1])
-            + (padded[1:-1, 1:-1, 2:] + padded[1:-1, 1:-1, :-2])
-            + (padded[2:, 1:-1, 1:-1] + padded[:-2, 1:-1, 1:-1])
-        )
-        field_now = jnp.where(inside, field_now + smooth_rate * (beside - 6.0 * field_now), 0.0)
+    lanes = -(-ext_cols // 128) * 128
+    inside_wide = jnp.pad(inside, ((0, 0), (0, lanes - ext_cols))).astype(jnp.float32)
+    start = jnp.pad(
+        jnp.where(inside, grad_ext / (illum_ext + damping), 0.0),
+        ((0, 0), (0, 0), (0, lanes - ext_cols)),
+    )
+    field_now = pl.pallas_call(
+        sweeps_kernel,
+        out_shape=jax.ShapeDtypeStruct(start.shape, jnp.float32),
+        in_specs=[pl.BlockSpec(memory_space=pltpu.VMEM)] * 2,
+        out_specs=pl.BlockSpec(memory_space=pltpu.VMEM),
+    )(start, inside_wide)
     updated_model = velocity - step_length * field_now[:, h : h + tile_rows, h : h + tile_cols]
 
     tile_table = (

time: 48.7 us -> 52.7 us (1.082)
  Pallas kernels: 0 us -> 2.05 us
  other arithmetic: 4.15 us -> 6.09 us
    pallas_call x0 -> x1, Pallas kernels: none -> 2.05 us  [local(): pl.pallas_call(sweeps_kernel, out_shape=jax.ShapeDtypeStruct(start.shape,...]
    convert_element_type x1, other arithmetic: 0.16 us -> 1.59 us  [local(): tile_table = updated_model.reshape(levels, per_tile, patch_rows, tile_col...]
    pad x0 -> x1, local copies, waits for them, and re-layouts: none -> 0.65 us  [local(): jnp.pad(jnp.where(inside, grad_ext / (illum_ext + damping), 0.0), ((0, 0)...]
    unnamed x9 -> x8, local copies, waits for them, and re-layouts: 1.98 us -> 1.36 us
    convert_element_type x0 -> x1, other arithmetic: none -> 0.61 us  [local(): jnp.pad(inside, ((0, 0), (0, lanes - ext_cols))).astype(jnp.float32)]
    select_n x4 -> x1, other arithmetic: 0.59 us -> 0.01 us  [local(): jnp.where(inside, grad_ext / (illum_ext + damping), 0.0)]
    another operation x2, other arithmetic: 0.05 us -> 0.58 us  [local(): jnp.stack([along_y] + [shifted(along_y, 'gx', size_x, step) for step in r...]
  transfers between devices with their start and end apart: 15 -> 15, of which waited for: 14 -> 14; matrix products, arithmetic and copies ran while one was open for 5% -> 4% of each run, Pallas kernels for 0% -> 0%
where the time goes in v12:
time: 52.7 us; the launch traced here: 52.5 us
  starting transfers between devices  20.2 us (38%)
  waiting for transfers between devices  18.5 us (35%)
  other arithmetic  6.09 us (12%)
  local copies, waits for them, and re-layouts  4.01 us (8%)
  Pallas kernels  2.05 us (4%)
  between operations  0.89 us (2%)
  matrix products  0.71 us (1%)
    ppermute x15, starting transfers between devices, shifted(): lax.ppermute(value, axis, [(s, (s + step) % count) for s in range(count)])  20.2 us
    ppermute x15, waiting for transfers between devices, shifted(): lax.ppermute(value, axis, [(s, (s + step) % count) for s in range(count)])  18.5 us
    pallas_call x1, Pallas kernels, local(): pl.pallas_call(sweeps_kernel, out_shape=jax.ShapeDtypeStruct(start.shape,...  2.05 us
    convert_element_type x1, other arithmetic, local(): tile_table = updated_model.reshape(levels, per_tile, patch_rows, tile_col...  1.59 us
    select_n x1, other arithmetic, local(): kept = jnp.where(is_grad, slot_grad, slot_illum)  1.39 us
    unnamed x8, local copies, waits for them, and re-layouts  1.36 us
  transfers between devices with their start and end apart: 15, of which 14 were waited for; matrix products, arithmetic and copies ran while one was open for 4% of the time, Pallas kernels for 0%

profile of v12, /device:TPU:0, one launch (start us, length us, event | category | flops | bytes accessed | tf_op | source)
XLA Modules:
  0.0 52.5 jit_solution(11554142203705849941)
XLA Ops:
  0.6 0.7 %pad_add_fusion = s32[2,256]{1,0:T(2,128)S(1)} fusion(s32[1,256]{1,0:T(1,128)} %bitcast.78, s32[1,256]{1,0:T(1,128)} %bitcast.84), kind=kLoop, calls=%fused_computation.88 | loop fusion | flops 512 | bytes 4096 | tf_op jit(solution)/shard_map/stack | solution.py:63
  1.3 0.5 collective-permute-start
  1.8 0.0 copy-start.1
  1.8 0.0 copy-start.2
  1.8 1.4 %select_bitcast_fusion.1 = (bf16[256,4,2,128]{3,0,2,1:T(8,128)(2,1)S(1)}, bf16[256,4,2,128]{3,0,2,1:T(8,128)(2,1)S(1)}) fusion(pred[]{:T(512)S(6)} %eq.65, bf16[1,1,1,256,4,2,128]{6,5,4,3,2,1,0:T(2,128)(2,1)} %param.6, bf16[1,1,1,256,4,2,128]{6,5,4,3,2,1,0:T(2,128)(2,1)} %param.5), kind=kLoop, calls=%fused_computation.7 | loop fusion | flops 524288 | bytes 2097153 | tf_op jit(solution)/shard_map/jit(_where)/select_n | solution.py:61
  3.2 0.1 collective-permute-start.1
  3.3 0.0 collective-permute-done
  3.3 0.0 copy-done.1
  3.3 0.0 copy-done.2
  3.4 1.8 %collective-permute-done.1 = bf16[256,4,2,128]{3,0,2,1:T(8,128)(2,1)S(1)} collective-permute-done((bf16[256,4,2,128]{3,0,2,1:T(8,128)(2,1)S(1)}, bf16[256,4,2,128]{3,0,2,1:T(8,128)(2,1)S(1)}, u32[]{:S(2)}, u32[]{:S(2)}) %collective-permute-start.1) | collective-permute-done | bytes 524320 | tf_op jit(solution)/shard_map/ppermute | solution.py:18
  5.2 0.4 fusion.1
  5.6 2.7 %collective-permute-start.2 = (f32[48,4,2,128]{3,0,2,1:T(8,128)S(1)}, f32[48,4,2,128]{3,0,2,1:T(8,128)S(1)}, u32[]{:S(2)}, u32[]{:S(2)}) collective-permute-start(f32[48,4,2,128]{3,0,2,1:T(8,128)S(1)} %get-tuple-element.17), channel_id=1, source_target_pairs={{0,4},{4,8},{8,12},{12,0},{1,5},{5,9},{9,13},{13,1},{2,6},{6,10},{... | collective-permute-start | bytes 589832 | tf_op jit(solution)/shard_map/ppermute | solution.py:18
  8.3 1.5 %collective-permute-start.3 = (f32[48,4,2,128]{3,0,2,1:T(8,128)S(1)}, f32[48,4,2,128]{3,0,2,1:T(8,128)S(1)}, u32[]{:S(2)}, u32[]{:S(2)}) collective-permute-start(f32[48,4,2,128]{3,0,2,1:T(8,128)S(1)} %get-tuple-element.19), channel_id=1, source_target_pairs={{0,8},{4,12},{8,0},{12,4},{1,9},{5,13},{9,1},{13,5},{2,10},{6,14},... | collective-permute-start | bytes 589832 | tf_op jit(solution)/shard_map/ppermute | solution.py:18
  9.8 1.4 %collective-permute-start.4 = (f32[48,4,2,128]{3,0,2,1:T(8,128)S(1)}, f32[48,4,2,128]{3,0,2,1:T(8,128)S(1)}, u32[]{:S(2)}, u32[]{:S(2)}) collective-permute-start(f32[48,4,2,128]{3,0,2,1:T(8,128)S(1)} %get-tuple-element.18), channel_id=1, source_target_pairs={{0,12},{4,0},{8,4},{12,8},{1,13},{5,1},{9,5},{13,9},{2,14},{6,2},{... | collective-permute-start | bytes 589832 | tf_op jit(solution)/shard_map/ppermute | solution.py:18
  11.3 3.8 %collective-permute-done.2 = f32[48,4,2,128]{3,0,2,1:T(8,128)S(1)} collective-permute-done((f32[48,4,2,128]{3,0,2,1:T(8,128)S(1)}, f32[48,4,2,128]{3,0,2,1:T(8,128)S(1)}, u32[]{:S(2)}, u32[]{:S(2)}) %collective-permute-start.2) | collective-permute-done | bytes 196640 | tf_op jit(solution)/shard_map/ppermute | solution.py:18
  15.0 3.9 %collective-permute-done.3 = f32[48,4,2,128]{3,0,2,1:T(8,128)S(1)} collective-permute-done((f32[48,4,2,128]{3,0,2,1:T(8,128)S(1)}, f32[48,4,2,128]{3,0,2,1:T(8,128)S(1)}, u32[]{:S(2)}, u32[]{:S(2)}) %collective-permute-start.3) | collective-permute-done | bytes 196640 | tf_op jit(solution)/shard_map/ppermute | solution.py:18
  18.9 0.3 collective-permute-done.4
  19.3 0.1 copy.19
  19.4 0.1 copy.20
  19.5 0.1 copy.22
  19.6 0.5 fusion.9
  20.1 0.3 reshape.524
  20.4 0.2 reshape_reshape.3
  20.6 0.6 %slice_reduce_fusion.3 = (f32[13056]{0:T(1024)S(1)}, f32[13056]{0:T(1024)S(1)}, f32[13056]{0:T(1024)S(1)}, f32[13056]{0:T(1024)S(1)}) fusion(f32[4,13056]{1,0:T(4,128)S(1)} %constant_dynamic-update-slice_fusion), kind=kLoop, calls=%fused_computation.39 | loop fusion | bytes 417792 | tf_op jit(solution)/shard_map/slice | solution.py:107
  21.2 1.6 %collective-permute-start.5 = (f32[102,128]{1,0:T(8,128)S(1)}, f32[102,128]{1,0:T(8,128)S(1)}, u32[]{:S(2)}, u32[]{:S(2)}) collective-permute-start(f32[102,128]{1,0:T(8,128)S(1)} %bitcast.77), channel_id=1, source_target_pairs={{0,1},{1,2},{2,3},{3,0},{4,5},{5,6},{6,7},{7,4},{8,9},{9,10},{10,1... | collective-permute-start | bytes 156680 | tf_op jit(solution)/shard_map/ppermute | solution.py:18
  22.8 2.6 %collective-permute-start.6 = (f32[102,128]{1,0:T(8,128)S(1)}, f32[102,128]{1,0:T(8,128)S(1)}, u32[]{:S(2)}, u32[]{:S(2)}) collective-permute-start(f32[102,128]{1,0:T(8,128)S(1)} %bitcast.76), channel_id=1, source_target_pairs={{0,2},{1,3},{2,0},{3,1},{4,6},{5,7},{6,4},{7,5},{8,10},{9,11},{10,... | collective-permute-start | bytes 156680 | tf_op jit(solution)/shard_map/ppermute | solution.py:18
  25.4 1.3 %collective-permute-start.7 = (f32[102,128]{1,0:T(8,128)S(1)}, f32[102,128]{1,0:T(8,128)S(1)}, u32[]{:S(2)}, u32[]{:S(2)}) collective-permute-start(f32[102,128]{1,0:T(8,128)S(1)} %bitcast.75), channel_id=1, source_target_pairs={{0,3},{1,0},{2,1},{3,2},{4,7},{5,4},{6,5},{7,6},{8,11},{9,8},{10,9... | collective-permute-start | bytes 156680 | tf_op jit(solution)/shard_map/ppermute | solution.py:18
  26.8 0.1 broadcast_and_fusion
  26.8 0.6 %collective-permute-done.5 = f32[102,128]{1,0:T(8,128)S(1)} collective-permute-done((f32[102,128]{1,0:T(8,128)S(1)}, f32[102,128]{1,0:T(8,128)S(1)}, u32[]{:S(2)}, u32[]{:S(2)}) %collective-permute-start.5) | collective-permute-done | bytes 52256 | tf_op jit(solution)/shard_map/ppermute | solution.py:18
  27.5 2.0 %collective-permute-done.6 = f32[102,128]{1,0:T(8,128)S(1)} collective-permute-done((f32[102,128]{1,0:T(8,128)S(1)}, f32[102,128]{1,0:T(8,128)S(1)}, u32[]{:S(2)}, u32[]{:S(2)}) %collective-permute-start.6) | collective-permute-done | bytes 52256 | tf_op jit(solution)/shard_map/ppermute | solution.py:18
  29.5 0.3 collective-permute-done.7
  29.8 0.1 collective-permute-start.8
  29.9 0.6 %pad_convert_fusion.inside_ref = f32[24,256]{1,0:T(8,128)} fusion(pred[24,136]{1,0:T(8,128)(4,1)S(1)} %broadcast_and_fusion), kind=kLoop, calls=%fused_computation.45 | loop fusion | flops 6144 | bytes 27840 | tf_op jit(solution)/shard_map/convert_element_type | solution.py:129
  30.5 0.6 %collective-permute-done.8 = f32[102,128]{1,0:T(8,128)S(1)} collective-permute-done((f32[102,128]{1,0:T(8,128)S(1)}, f32[102,128]{1,0:T(8,128)S(1)}, u32[]{:S(2)}, u32[]{:S(2)}) %collective-permute-start.8) | collective-permute-done | bytes 52256 | tf_op jit(solution)/shard_map/ppermute | solution.py:18
  31.2 0.1 reshape.525
  31.3 0.1 reshape.527
  31.4 0.2 fusion.51
  31.6 0.0 copy-start
  31.6 0.4 fusion.17
  32.0 0.1 div.39
  32.1 0.6 %pad.8.field_ref = f32[4,24,256]{2,1,0:T(8,128)} pad(f32[4,24,136]{2,1,0:T(8,128)S(1)} %broadcast_select_fusion, f32[]{:T(128)} %constant.126.clone.1), padding=0_0x0_0x0_120 | pad | bytes 150532 | tf_op jit(solution)/shard_map/jit(_pad)/pad | solution.py:130
  32.8 2.0 %shard_map.68 = f32[4,24,256]{2,1,0:T(8,128)} custom-call(f32[4,24,256]{2,1,0:T(8,128)} %pad.8.field_ref, f32[24,256]{1,0:T(8,128)} %pad_convert_fusion.inside_ref), custom_call_target="tpu_custom_call" | custom-call | tf_op jit(solution)/shard_map/pallas_call | solution.py:134
  34.8 0.0 copy-done
  34.8 1.6 %fusion.47 = (bf16[4,16,128]{2,1,0:T(8,128)(2,1)S(1)}, f32[4,16,128]{2,1,0:T(8,128)}) fusion(f32[4,16,128]{2,1,0:T(8,128)S(1)} %copy-done, f32[4,24,256]{2,1,0:T(8,128)} %shard_map.68), kind=kLoop, calls=%fused_computation.111 | loop fusion | flops 24576 | bytes 114688 | tf_op jit(solution)/shard_map/convert_element_type | solution.py:145
  36.4 1.0 %collective-permute-start.9 = (bf16[8,4,2,128]{3,2,0,1:T(2,128)(2,1)S(1)}, bf16[8,4,2,128]{3,2,0,1:T(2,128)(2,1)S(1)}, u32[]{:S(2)}, u32[]{:S(2)}) collective-permute-start(bf16[8,4,2,128]{3,2,0,1:T(2,128)(2,1)S(1)} %bitcast.61), channel_id=1, source_target_pairs={{0,1},{1,2},{2,3},{3,0},{4,5},{5,6},{6,7},{7,4},{8,9},{9,10},{10,1... | collective-permute-start | bytes 49160 | tf_op jit(solution)/shard_map/ppermute | solution.py:18
  37.4 2.5 %collective-permute-start.10 = (bf16[8,4,2,128]{3,2,0,1:T(2,128)(2,1)S(1)}, bf16[8,4,2,128]{3,2,0,1:T(2,128)(2,1)S(1)}, u32[]{:S(2)}, u32[]{:S(2)}) collective-permute-start(bf16[8,4,2,128]{3,2,0,1:T(2,128)(2,1)S(1)} %bitcast.62), channel_id=1, source_target_pairs={{0,2},{1,3},{2,0},{3,1},{4,6},{5,7},{6,4},{7,5},{8,10},{9,11},{10,... | collective-permute-start | bytes 49160 | tf_op jit(solution)/shard_map/ppermute | solution.py:18
  39.9 0.5 collective-permute-start.11
  40.4 1.6 %collective-permute-done.9 = bf16[8,4,2,128]{3,2,0,1:T(2,128)(2,1)S(1)} collective-permute-done((bf16[8,4,2,128]{3,2,0,1:T(2,128)(2,1)S(1)}, bf16[8,4,2,128]{3,2,0,1:T(2,128)(2,1)S(1)}, u32[]{:S(2)}, u32[]{:S(2)}) %collective-permute-start.9) | collective-permute-done | bytes 16416 | tf_op jit(solution)/shard_map/ppermute | solution.py:18
  42.0 0.3 collective-permute-done.10
  42.3 1.3 %collective-permute-done.11 = bf16[8,4,2,128]{3,2,0,1:T(2,128)(2,1)S(1)} collective-permute-done((bf16[8,4,2,128]{3,2,0,1:T(2,128)(2,1)S(1)}, bf16[8,4,2,128]{3,2,0,1:T(2,128)(2,1)S(1)}, u32[]{:S(2)}, u32[]{:S(2)}) %collective-permute-start.11) | collective-permute-done | bytes 16416 | tf_op jit(solution)/shard_map/ppermute | solution.py:18
  43.6 0.1 pad_maximum_fusion.3
  43.7 1.8 %collective-permute-start.12 = (bf16[4,8,4,2,128]{4,3,1,2,0:T(2,128)(2,1)S(1)}, bf16[4,8,4,2,128]{4,3,1,2,0:T(2,128)(2,1)S(1)}, u32[]{:S(2)}, u32[]{:S(2)}) collective-permute-start(bf16[4,8,4,2,128]{4,3,1,2,0:T(2,128)(2,1)S(1)} %pad_maximum_fusion.3), channel_id=1, source_target_pairs={{0,4},{4,8},{8,12},{12,0},{1,5},{5,9},{9,13},{13,1},{2,6},{6,10},{... | collective-permute-start | bytes 196616 | tf_op jit(solution)/shard_map/ppermute | solution.py:18
  45.5 0.5 collective-permute-start.13
  46.0 2.1 %collective-permute-start.14 = (bf16[4,8,4,2,128]{4,3,1,2,0:T(2,128)(2,1)S(1)}, bf16[4,8,4,2,128]{4,3,1,2,0:T(2,128)(2,1)S(1)}, u32[]{:S(2)}, u32[]{:S(2)}) collective-permute-start(bf16[4,8,4,2,128]{4,3,1,2,0:T(2,128)(2,1)S(1)} %pad_maximum_fusion.3), channel_id=1, source_target_pairs={{0,12},{4,0},{8,4},{12,8},{1,13},{5,1},{9,5},{13,9},{2,14},{6,2},{... | collective-permute-start | bytes 196616 | tf_op jit(solution)/shard_map/ppermute | solution.py:18
  48.1 0.1 fusion.55
  48.2 0.7 %collective-permute-done.12 = bf16[4,8,4,2,128]{4,3,1,2,0:T(2,128)(2,1)S(1)} collective-permute-done((bf16[4,8,4,2,128]{4,3,1,2,0:T(2,128)(2,1)S(1)}, bf16[4,8,4,2,128]{4,3,1,2,0:T(2,128)(2,1)S(1)}, u32[]{:S(2)}, u32[]{:S(2)}) %collective-permute-start.12) | collective-permute-done | bytes 65568 | tf_op jit(solution)/shard_map/ppermute | solution.py:18
  48.9 0.8 %collective-permute-done.13 = bf16[4,8,4,2,128]{4,3,1,2,0:T(2,128)(2,1)S(1)} collective-permute-done((bf16[4,8,4,2,128]{4,3,1,2,0:T(2,128)(2,1)S(1)}, bf16[4,8,4,2,128]{4,3,1,2,0:T(2,128)(2,1)S(1)}, u32[]{:S(2)}, u32[]{:S(2)}) %collective-permute-start.13) | collective-permute-done | bytes 65568 | tf_op jit(solution)/shard_map/ppermute | solution.py:18
  49.8 0.5 collective-permute-done.14
  50.3 0.5 pad_maximum_fusion
  50.8 0.3 fusion
  51.1 1.3 %copy.26 = bf16[1,1,1,256,4,2,128]{6,5,4,3,2,1,0:T(2,128)(2,1)} copy(bf16[1,1,1,256,4,2,128]{6,3,5,4,2,1,0:T(8,128)(2,1)S(1)} %fusion) | data formatting | bytes 1048576
  (23 shorter events, 0.4 us)
Async XLA Ops:
  1.3 2.0 %collective-permute-start = (s32[2,256]{1,0:T(2,128)S(1)}, s32[2,256]{1,0:T(2,128)S(1)}, u32[]{:S(2)}, u32[]{:S(2)}) collective-permute-start(s32[2,256]{1,0:T(2,128)S(1)} %pad_add_fusion), channel_id=1, source_target_pairs={{0,16},{16,0},{1,17},{17,1},{2,18},{18,2},{3,19},{19,3},{4,20},{20... | collective-permute-start | bytes 6152 | tf_op jit(solution)/shard_map/ppermute | solution.py:18
  1.8 1.5 %copy-start.1 = (s32[1,1,1,256]{3,2,1,0:T(1,128)S(1)}, s32[1,1,1,256]{3,2,1,0:T(1,128)}, u32[]{:S(2)}) copy-start(s32[1,1,1,256]{3,2,1,0:T(1,128)} %param.8) | copy-start | bytes 3076
  1.8 1.5 %copy-start.2 = (s32[1,1,1,256]{3,2,1,0:T(1,128)S(1)}, s32[1,1,1,256]{3,2,1,0:T(1,128)}, u32[]{:S(2)}) copy-start(s32[1,1,1,256]{3,2,1,0:T(1,128)} %param.7) | copy-start | bytes 3076
  3.2 2.0 %collective-permute-start.1 = (bf16[256,4,2,128]{3,0,2,1:T(8,128)(2,1)S(1)}, bf16[256,4,2,128]{3,0,2,1:T(8,128)(2,1)S(1)}, u32[]{:S(2)}, u32[]{:S(2)}) collective-permute-start(bf16[256,4,2,128]{3,0,2,1:T(8,128)(2,1)S(1)} %get-tuple-element.16), channel_id=1, source_target_pairs={{0,16},{16,0},{1,17},{17,1},{2,18},{18,2},{3,19},{19,3},{4,20},{20... | collective-permute-start | bytes 1572872 | tf_op jit(solution)/shard_map/ppermute | solution.py:18
  5.6 9.4 %collective-permute-start.2 = (f32[48,4,2,128]{3,0,2,1:T(8,128)S(1)}, f32[48,4,2,128]{3,0,2,1:T(8,128)S(1)}, u32[]{:S(2)}, u32[]{:S(2)}) collective-permute-start(f32[48,4,2,128]{3,0,2,1:T(8,128)S(1)} %get-tuple-element.17), channel_id=1, source_target_pairs={{0,4},{4,8},{8,12},{12,0},{1,5},{5,9},{9,13},{13,1},{2,6},{6,10},{... | collective-permute-start | bytes 589832 | tf_op jit(solution)/shard_map/ppermute | solution.py:18
  8.3 10.6 %collective-permute-start.3 = (f32[48,4,2,128]{3,0,2,1:T(8,128)S(1)}, f32[48,4,2,128]{3,0,2,1:T(8,128)S(1)}, u32[]{:S(2)}, u32[]{:S(2)}) collective-permute-start(f32[48,4,2,128]{3,0,2,1:T(8,128)S(1)} %get-tuple-element.19), channel_id=1, source_target_pairs={{0,8},{4,12},{8,0},{12,4},{1,9},{5,13},{9,1},{13,5},{2,10},{6,14},... | collective-permute-start | bytes 589832 | tf_op jit(solution)/shard_map/ppermute | solution.py:18
  9.8 9.4 %collective-permute-start.4 = (f32[48,4,2,128]{3,0,2,1:T(8,128)S(1)}, f32[48,4,2,128]{3,0,2,1:T(8,128)S(1)}, u32[]{:S(2)}, u32[]{:S(2)}) collective-permute-start(f32[48,4,2,128]{3,0,2,1:T(8,128)S(1)} %get-tuple-element.18), channel_id=1, source_target_pairs={{0,12},{4,0},{8,4},{12,8},{1,13},{5,1},{9,5},{13,9},{2,14},{6,2},{... | collective-permute-start | bytes 589832 | tf_op jit(solution)/shard_map/ppermute | solution.py:18
  21.2 6.3 %collective-permute-start.5 = (f32[102,128]{1,0:T(8,128)S(1)}, f32[102,128]{1,0:T(8,128)S(1)}, u32[]{:S(2)}, u32[]{:S(2)}) collective-permute-start(f32[102,128]{1,0:T(8,128)S(1)} %bitcast.77), channel_id=1, source_target_pairs={{0,1},{1,2},{2,3},{3,0},{4,5},{5,6},{6,7},{7,4},{8,9},{9,10},{10,1... | collective-permute-start | bytes 156680 | tf_op jit(solution)/shard_map/ppermute | solution.py:18
  22.8 6.7 %collective-permute-start.6 = (f32[102,128]{1,0:T(8,128)S(1)}, f32[102,128]{1,0:T(8,128)S(1)}, u32[]{:S(2)}, u32[]{:S(2)}) collective-permute-start(f32[102,128]{1,0:T(8,128)S(1)} %bitcast.76), channel_id=1, source_target_pairs={{0,2},{1,3},{2,0},{3,1},{4,6},{5,7},{6,4},{7,5},{8,10},{9,11},{10,... | collective-permute-start | bytes 156680 | tf_op jit(solution)/shard_map/ppermute | solution.py:18
  25.4 4.4 %collective-permute-start.7 = (f32[102,128]{1,0:T(8,128)S(1)}, f32[102,128]{1,0:T(8,128)S(1)}, u32[]{:S(2)}, u32[]{:S(2)}) collective-permute-start(f32[102,128]{1,0:T(8,128)S(1)} %bitcast.75), channel_id=1, source_target_pairs={{0,3},{1,0},{2,1},{3,2},{4,7},{5,4},{6,5},{7,6},{8,11},{9,8},{10,9... | collective-permute-start | bytes 156680 | tf_op jit(solution)/shard_map/ppermute | solution.py:18
  29.8 1.3 %collective-permute-start.8 = (f32[102,128]{1,0:T(8,128)S(1)}, f32[102,128]{1,0:T(8,128)S(1)}, u32[]{:S(2)}, u32[]{:S(2)}) collective-permute-start(f32[102,128]{1,0:T(8,128)S(1)} %fusion.20), channel_id=1, source_target_pairs={{0,16},{16,0},{1,17},{17,1},{2,18},{18,2},{3,19},{19,3},{4,20},{20... | collective-permute-start | bytes 156680 | tf_op jit(solution)/shard_map/ppermute | solution.py:18
  31.6 3.2 %copy-start = (f32[4,16,128]{2,1,0:T(8,128)S(1)}, f32[4,16,128]{2,1,0:T(8,128)}, u32[]{:S(2)}) copy-start(f32[4,16,128]{2,1,0:T(8,128)} %param.9) | copy-start | bytes 98308
  36.4 5.6 %collective-permute-start.9 = (bf16[8,4,2,128]{3,2,0,1:T(2,128)(2,1)S(1)}, bf16[8,4,2,128]{3,2,0,1:T(2,128)(2,1)S(1)}, u32[]{:S(2)}, u32[]{:S(2)}) collective-permute-start(bf16[8,4,2,128]{3,2,0,1:T(2,128)(2,1)S(1)} %bitcast.61), channel_id=1, source_target_pairs={{0,1},{1,2},{2,3},{3,0},{4,5},{5,6},{6,7},{7,4},{8,9},{9,10},{10,1... | collective-permute-start | bytes 49160 | tf_op jit(solution)/shard_map/ppermute | solution.py:18
  37.4 4.9 %collective-permute-start.10 = (bf16[8,4,2,128]{3,2,0,1:T(2,128)(2,1)S(1)}, bf16[8,4,2,128]{3,2,0,1:T(2,128)(2,1)S(1)}, u32[]{:S(2)}, u32[]{:S(2)}) collective-permute-start(bf16[8,4,2,128]{3,2,0,1:T(2,128)(2,1)S(1)} %bitcast.62), channel_id=1, source_target_pairs={{0,2},{1,3},{2,0},{3,1},{4,6},{5,7},{6,4},{7,5},{8,10},{9,11},{10,... | collective-permute-start | bytes 49160 | tf_op jit(solution)/shard_map/ppermute | solution.py:18
  39.9 3.7 %collective-permute-start.11 = (bf16[8,4,2,128]{3,2,0,1:T(2,128)(2,1)S(1)}, bf16[8,4,2,128]{3,2,0,1:T(2,128)(2,1)S(1)}, u32[]{:S(2)}, u32[]{:S(2)}) collective-permute-start(bf16[8,4,2,128]{3,2,0,1:T(2,128)(2,1)S(1)} %bitcast.63), channel_id=1, source_target_pairs={{0,3},{1,0},{2,1},{3,2},{4,7},{5,4},{6,5},{7,6},{8,11},{9,8},{10,9... | collective-permute-start | bytes 49160 | tf_op jit(solution)/shard_map/ppermute | solution.py:18
  43.7 5.2 %collective-permute-start.12 = (bf16[4,8,4,2,128]{4,3,1,2,0:T(2,128)(2,1)S(1)}, bf16[4,8,4,2,128]{4,3,1,2,0:T(2,128)(2,1)S(1)}, u32[]{:S(2)}, u32[]{:S(2)}) collective-permute-start(bf16[4,8,4,2,128]{4,3,1,2,0:T(2,128)(2,1)S(1)} %pad_maximum_fusion.3), channel_id=1, source_target_pairs={{0,4},{4,8},{8,12},{12,0},{1,5},{5,9},{9,13},{13,1},{2,6},{6,10},{... | collective-permute-start | bytes 196616 | tf_op jit(solution)/shard_map/ppermute | solution.py:18
  45.5 4.3 %collective-permute-start.13 = (bf16[4,8,4,2,128]{4,3,1,2,0:T(2,128)(2,1)S(1)}, bf16[4,8,4,2,128]{4,3,1,2,0:T(2,128)(2,1)S(1)}, u32[]{:S(2)}, u32[]{:S(2)}) collective-permute-start(bf16[4,8,4,2,128]{4,3,1,2,0:T(2,128)(2,1)S(1)} %pad_maximum_fusion.3), channel_id=1, source_target_pairs={{0,8},{4,12},{8,0},{12,4},{1,9},{5,13},{9,1},{13,5},{2,10},{6,14},... | collective-permute-start | bytes 196616 | tf_op jit(solution)/shard_map/ppermute | solution.py:18
  46.0 4.3 %collective-permute-start.14 = (bf16[4,8,4,2,128]{4,3,1,2,0:T(2,128)(2,1)S(1)}, bf16[4,8,4,2,128]{4,3,1,2,0:T(2,128)(2,1)S(1)}, u32[]{:S(2)}, u32[]{:S(2)}) collective-permute-start(bf16[4,8,4,2,128]{4,3,1,2,0:T(2,128)(2,1)S(1)} %pad_maximum_fusion.3), channel_id=1, source_target_pairs={{0,12},{4,0},{8,4},{12,8},{1,13},{5,1},{9,5},{13,9},{2,14},{6,2},{... | collective-permute-start | bytes 196616 | tf_op jit(solution)/shard_map/ppermute | solution.py:18

commit v13 on v4

--- a/solution.py
+++ b/solution.py
@@ -37,12 +37,10 @@
 
     me_g = lax.axis_index("group")
     is_grad = me_g == 0
-    kept = jnp.where(is_grad, slot_grad, slot_illum)
     given = jnp.where(is_grad, slot_illum, slot_grad)
     places = jnp.stack([owners, patches])
     taken = shifted(given, "group", size_g, 1)
     taken_places = shifted(places, "group", size_g, 1)
-    rows_in = jnp.concatenate([kept, taken], axis=0)
     all_owners = jnp.concatenate([owners, taken_places[0]])
     all_patches = jnp.concatenate([patches, taken_places[1]])
 
@@ -70,7 +68,16 @@
     onehot = (
         (own_row[None, :] == row_ids) | (next_row[None, :] == row_ids) | (prev_row[None, :] == row_ids)
     ).astype(jnp.bfloat16)
-    table = jnp.einsum("rw,wlpc->rlpc", onehot, rows_in, preferred_element_type=jnp.float32)
+    own, theirs = onehot[:, :slot_count], onehot[:, slot_count:]
+    zero = jnp.zeros_like(own)
+    table = (
+        jnp.einsum(
+            "rw,wlpc->rlpc", jnp.where(is_grad, own, zero), slot_grad, preferred_element_type=jnp.float32
+        )
+        + jnp.einsum(
+            "rw,wlpc->rlpc", jnp.where(is_grad, zero, own), slot_illum, preferred_element_type=jnp.float32
+        )
+    ) + jnp.einsum("rw,wlpc->rlpc", theirs, taken, preferred_element_type=jnp.float32)
     flat = table.reshape(size_x, size_y * ext_patches, levels, patch_rows, patch_cols)
 
     part = flat[0]

time: 48.7 us -> 52.9 us (1.086)
  waiting for transfers between devices: 18.5 us -> 21.6 us
  local copies, waits for them, and re-layouts: 3.97 us -> 5.98 us
  starting transfers between devices: 20.3 us -> 19.3 us
  other arithmetic: 4.15 us -> 3.59 us
    ppermute x15, waiting for transfers between devices: 18.5 us -> 21.6 us  [shifted(): lax.ppermute(value, axis, [(s, (s + step) % count) for s in range(count)])]
    unnamed x9 -> x13, local copies, waits for them, and re-layouts: 1.98 us -> 3.98 us
    ppermute x15, starting transfers between devices: 20.3 us -> 19.3 us  [shifted(): lax.ppermute(value, axis, [(s, (s + step) % count) for s in range(count)])]
    another operation x1, other arithmetic: 0.71 us -> 0.01 us  [local(): places = jnp.stack([owners, patches])]
  transfers between devices with their start and end apart: 15 -> 15, of which waited for: 14 -> 11; matrix products, arithmetic and copies ran while one was open for 5% -> 6% of each run, Pallas kernels for 0% -> 0%
where the time goes in v13:
time: 52.9 us; the launch traced here: 52.6 us
  waiting for transfers between devices  21.6 us (41%)
  starting transfers between devices  19.3 us (36%)
  local copies, waits for them, and re-layouts  5.98 us (11%)
  other arithmetic  3.59 us (7%)
  matrix products  1.14 us (2%)
  between operations  0.97 us (2%)
    ppermute x15, waiting for transfers between devices, shifted(): lax.ppermute(value, axis, [(s, (s + step) % count) for s in range(count)])  21.6 us
    ppermute x15, starting transfers between devices, shifted(): lax.ppermute(value, axis, [(s, (s + step) % count) for s in range(count)])  19.3 us
    unnamed x13, local copies, waits for them, and re-layouts  3.98 us
    select_n x1, other arithmetic, local(): given = jnp.where(is_grad, slot_illum, slot_grad)  1.42 us
  transfers between devices with their start and end apart: 15, of which 11 were waited for; matrix products, arithmetic and copies ran while one was open for 6% of the time, Pallas kernels for 0%

profile of v13, /device:TPU:0, one launch (start us, length us, event | category | flops | bytes accessed | tf_op | source)
XLA Modules:
  0.0 52.6 jit_solution(11719443193069706880)
XLA Ops:
  0.6 0.0 copy-start.4
  0.6 0.0 copy-start.3
  0.6 0.7 %copy-done.4 = s32[1,1,1,256]{3,2,1,0:T(1,128)S(1)} copy-done((s32[1,1,1,256]{3,2,1,0:T(1,128)S(1)}, s32[1,1,1,256]{3,2,1,0:T(1,128)}, u32[]{:S(2)}) %copy-start.4) | copy-done | bytes 1048
  1.3 0.0 copy-done.3
  1.3 0.5 collective-permute-start
  1.8 1.4 %bitcast_select_fusion = bf16[256,4,2,128]{3,0,2,1:T(8,128)(2,1)S(1)} fusion(pred[]{:T(512)S(6)} %eq.65, bf16[1,1,1,256,4,2,128]{6,5,4,3,2,1,0:T(2,128)(2,1)} %param.6, bf16[1,1,1,256,4,2,128]{6,5,4,3,2,1,0:T(2,128)(2,1)} %param.5), kind=kLoop, calls=%fused_computation.4 | loop fusion | flops 262144 | bytes 1572865 | tf_op jit(solution)/shard_map/jit(_where)/select_n | solution.py:40
  3.3 0.1 collective-permute-start.1
  3.4 0.0 collective-permute-done
  3.5 0.1 fusion.7
  3.6 0.0 copy-start.1
  3.6 0.3 fusion.2
  3.9 0.8 %copy-done.1 = bf16[1,1,1,256,4,2,128]{6,5,4,3,2,1,0:T(2,128)(2,1)S(1)} copy-done((bf16[1,1,1,256,4,2,128]{6,5,4,3,2,1,0:T(2,128)(2,1)S(1)}, bf16[1,1,1,256,4,2,128]{6,5,4,3,2,1,0:T(2,128)(2,1)}, u32[]{:S(2)}) %copy-start.1) | copy-done | bytes 524312
  4.6 0.3 convolution_add_fusion.1
  4.9 0.3 collective-permute-done.1
  5.2 0.3 convolution_add_fusion
  5.6 2.7 %collective-permute-start.2 = (f32[48,4,2,128]{3,0,2,1:T(8,128)S(1)}, f32[48,4,2,128]{3,0,2,1:T(8,128)S(1)}, u32[]{:S(2)}, u32[]{:S(2)}) collective-permute-start(f32[48,4,2,128]{3,0,2,1:T(8,128)S(1)} %get-tuple-element.17), channel_id=1, source_target_pairs={{0,4},{4,8},{8,12},{12,0},{1,5},{5,9},{9,13},{13,1},{2,6},{6,10},{... | collective-permute-start | bytes 589832 | tf_op jit(solution)/shard_map/ppermute | solution.py:16
  8.3 1.0 %collective-permute-start.4 = (f32[48,4,2,128]{3,0,2,1:T(8,128)S(1)}, f32[48,4,2,128]{3,0,2,1:T(8,128)S(1)}, u32[]{:S(2)}, u32[]{:S(2)}) collective-permute-start(f32[48,4,2,128]{3,0,2,1:T(8,128)S(1)} %get-tuple-element.18), channel_id=1, source_target_pairs={{0,12},{4,0},{8,4},{12,8},{1,13},{5,1},{9,5},{13,9},{2,14},{6,2},{... | collective-permute-start | bytes 589832 | tf_op jit(solution)/shard_map/ppermute | solution.py:16
  9.3 1.9 %collective-permute-start.3 = (f32[48,4,2,128]{3,0,2,1:T(8,128)S(1)}, f32[48,4,2,128]{3,0,2,1:T(8,128)S(1)}, u32[]{:S(2)}, u32[]{:S(2)}) collective-permute-start(f32[48,4,2,128]{3,0,2,1:T(8,128)S(1)} %get-tuple-element.19), channel_id=1, source_target_pairs={{0,8},{4,12},{8,0},{12,4},{1,9},{5,13},{9,1},{13,5},{2,10},{6,14},... | collective-permute-start | bytes 589832 | tf_op jit(solution)/shard_map/ppermute | solution.py:16
  11.2 3.8 %collective-permute-done.2 = f32[48,4,2,128]{3,0,2,1:T(8,128)S(1)} collective-permute-done((f32[48,4,2,128]{3,0,2,1:T(8,128)S(1)}, f32[48,4,2,128]{3,0,2,1:T(8,128)S(1)}, u32[]{:S(2)}, u32[]{:S(2)}) %collective-permute-start.2) | collective-permute-done | bytes 196640 | tf_op jit(solution)/shard_map/ppermute | solution.py:16
  15.0 4.1 %collective-permute-done.4 = f32[48,4,2,128]{3,0,2,1:T(8,128)S(1)} collective-permute-done((f32[48,4,2,128]{3,0,2,1:T(8,128)S(1)}, f32[48,4,2,128]{3,0,2,1:T(8,128)S(1)}, u32[]{:S(2)}, u32[]{:S(2)}) %collective-permute-start.4) | collective-permute-done | bytes 196640 | tf_op jit(solution)/shard_map/ppermute | solution.py:16
  19.2 0.0 collective-permute-done.3
  19.2 0.1 copy.36
  19.4 0.2 reshape_reshape.3
  19.7 0.1 copy.37
  19.7 0.1 copy.39
  19.8 0.5 fusion.8
  20.3 0.3 reshape.520
  20.6 0.6 %slice_reduce_fusion.3 = (f32[13056]{0:T(1024)S(1)}, f32[13056]{0:T(1024)S(1)}, f32[13056]{0:T(1024)S(1)}, f32[13056]{0:T(1024)S(1)}) fusion(f32[4,13056]{1,0:T(4,128)S(1)} %constant_dynamic-update-slice_fusion), kind=kLoop, calls=%fused_computation.99 | loop fusion | bytes 417792 | tf_op jit(solution)/shard_map/slice | solution.py:93
  21.2 3.7 %collective-permute-start.7 = (f32[102,128]{1,0:T(8,128)S(1)}, f32[102,128]{1,0:T(8,128)S(1)}, u32[]{:S(2)}, u32[]{:S(2)}) collective-permute-start(f32[102,128]{1,0:T(8,128)S(1)} %bitcast.102), channel_id=1, source_target_pairs={{0,3},{1,0},{2,1},{3,2},{4,7},{5,4},{6,5},{7,6},{8,11},{9,8},{10,9... | collective-permute-start | bytes 156680 | tf_op jit(solution)/shard_map/ppermute | solution.py:16
  24.8 0.0 collective-permute-start.6
  24.8 1.0 %collective-permute-start.5 = (f32[102,128]{1,0:T(8,128)S(1)}, f32[102,128]{1,0:T(8,128)S(1)}, u32[]{:S(2)}, u32[]{:S(2)}) collective-permute-start(f32[102,128]{1,0:T(8,128)S(1)} %bitcast.100), channel_id=1, source_target_pairs={{0,1},{1,2},{2,3},{3,0},{4,5},{5,6},{6,7},{7,4},{8,9},{9,10},{10,1... | collective-permute-start | bytes 156680 | tf_op jit(solution)/shard_map/ppermute | solution.py:16
  25.9 1.2 %collective-permute-done.7 = f32[102,128]{1,0:T(8,128)S(1)} collective-permute-done((f32[102,128]{1,0:T(8,128)S(1)}, f32[102,128]{1,0:T(8,128)S(1)}, u32[]{:S(2)}, u32[]{:S(2)}) %collective-permute-start.7) | collective-permute-done | bytes 52256 | tf_op jit(solution)/shard_map/ppermute | solution.py:16
  27.1 2.9 %collective-permute-done.6 = f32[102,128]{1,0:T(8,128)S(1)} collective-permute-done((f32[102,128]{1,0:T(8,128)S(1)}, f32[102,128]{1,0:T(8,128)S(1)}, u32[]{:S(2)}, u32[]{:S(2)}) %collective-permute-start.6) | collective-permute-done | bytes 52256 | tf_op jit(solution)/shard_map/ppermute | solution.py:16
  30.0 0.8 %collective-permute-done.5 = f32[102,128]{1,0:T(8,128)S(1)} collective-permute-done((f32[102,128]{1,0:T(8,128)S(1)}, f32[102,128]{1,0:T(8,128)S(1)}, u32[]{:S(2)}, u32[]{:S(2)}) %collective-permute-start.5) | collective-permute-done | bytes 52256 | tf_op jit(solution)/shard_map/ppermute | solution.py:16
  30.8 0.1 collective-permute-start.8
  30.9 0.1 broadcast_and_fusion
  30.9 0.1 slice.269
  31.0 1.1 %collective-permute-done.8 = f32[102,128]{1,0:T(8,128)S(1)} collective-permute-done((f32[102,128]{1,0:T(8,128)S(1)}, f32[102,128]{1,0:T(8,128)S(1)}, u32[]{:S(2)}, u32[]{:S(2)}) %collective-permute-start.8) | collective-permute-done | bytes 52256 | tf_op jit(solution)/shard_map/ppermute | solution.py:16
  32.1 0.1 reshape.523
  32.3 0.1 reshape.521
  32.4 0.2 fusion.94
  32.6 0.4 fusion.50
  33.1 0.2 fusion.25
  33.2 0.2 fusion.34
  33.4 0.2 fusion.43
  33.6 0.0 copy-start.2
  33.6 0.2 fusion.46
  33.8 0.6 %copy-done.2 = f32[4,16,128]{2,1,0:T(8,128)S(1)} copy-done((f32[4,16,128]{2,1,0:T(8,128)S(1)}, f32[4,16,128]{2,1,0:T(8,128)}, u32[]{:S(2)}) %copy-start.2) | copy-done | bytes 32792
  34.4 0.2 fusion.90
  34.6 0.1 collective-permute-start.9
  34.6 3.8 %collective-permute-start.11 = (bf16[8,4,2,128]{3,0,2,1:T(8,128)(2,1)S(1)}, bf16[8,4,2,128]{3,0,2,1:T(8,128)(2,1)S(1)}, u32[]{:S(2)}, u32[]{:S(2)}) collective-permute-start(bf16[8,4,2,128]{3,0,2,1:T(8,128)(2,1)S(1)} %bitcast.93), channel_id=1, source_target_pairs={{0,3},{1,0},{2,1},{3,2},{4,7},{5,4},{6,5},{7,6},{8,11},{9,8},{10,9... | collective-permute-start | bytes 49160 | tf_op jit(solution)/shard_map/ppermute | solution.py:16
  38.4 0.0 collective-permute-start.10
  38.4 1.7 %collective-permute-done.9 = bf16[8,4,2,128]{3,0,2,1:T(8,128)(2,1)S(1)} collective-permute-done((bf16[8,4,2,128]{3,0,2,1:T(8,128)(2,1)S(1)}, bf16[8,4,2,128]{3,0,2,1:T(8,128)(2,1)S(1)}, u32[]{:S(2)}, u32[]{:S(2)}) %collective-permute-start.9) | collective-permute-done | bytes 16416 | tf_op jit(solution)/shard_map/ppermute | solution.py:16
  40.1 0.0 collective-permute-done.11
  40.2 2.9 %collective-permute-done.10 = bf16[8,4,2,128]{3,0,2,1:T(8,128)(2,1)S(1)} collective-permute-done((bf16[8,4,2,128]{3,0,2,1:T(8,128)(2,1)S(1)}, bf16[8,4,2,128]{3,0,2,1:T(8,128)(2,1)S(1)}, u32[]{:S(2)}, u32[]{:S(2)}) %collective-permute-start.10) | collective-permute-done | bytes 16416 | tf_op jit(solution)/shard_map/ppermute | solution.py:16
  43.1 1.5 %collective-permute-start.13 = (bf16[4,8,4,2,128]{4,1,0,3,2:T(8,128)(2,1)S(1)}, bf16[4,8,4,2,128]{4,1,0,3,2:T(8,128)(2,1)S(1)}, u32[]{:S(2)}, u32[]{:S(2)}) collective-permute-start(bf16[4,8,4,2,128]{4,1,0,3,2:T(8,128)(2,1)S(1)} %get-tuple-element.31), channel_id=1, source_target_pairs={{0,8},{4,12},{8,0},{12,4},{1,9},{5,13},{9,1},{13,5},{2,10},{6,14},... | collective-permute-start | bytes 196616 | tf_op jit(solution)/shard_map/ppermute | solution.py:16
  44.6 2.1 %collective-permute-start.12 = (bf16[4,8,4,2,128]{4,1,0,3,2:T(8,128)(2,1)S(1)}, bf16[4,8,4,2,128]{4,1,0,3,2:T(8,128)(2,1)S(1)}, u32[]{:S(2)}, u32[]{:S(2)}) collective-permute-start(bf16[4,8,4,2,128]{4,1,0,3,2:T(8,128)(2,1)S(1)} %get-tuple-element.31), channel_id=1, source_target_pairs={{0,4},{4,8},{8,12},{12,0},{1,5},{5,9},{9,13},{13,1},{2,6},{6,10},{... | collective-permute-start | bytes 196616 | tf_op jit(solution)/shard_map/ppermute | solution.py:16
  46.6 0.9 %collective-permute-start.14 = (bf16[4,8,4,2,128]{4,1,0,3,2:T(8,128)(2,1)S(1)}, bf16[4,8,4,2,128]{4,1,0,3,2:T(8,128)(2,1)S(1)}, u32[]{:S(2)}, u32[]{:S(2)}) collective-permute-start(bf16[4,8,4,2,128]{4,1,0,3,2:T(8,128)(2,1)S(1)} %get-tuple-element.31), channel_id=1, source_target_pairs={{0,12},{4,0},{8,4},{12,8},{1,13},{5,1},{9,5},{13,9},{2,14},{6,2},{... | collective-permute-start | bytes 196616 | tf_op jit(solution)/shard_map/ppermute | solution.py:16
  47.5 0.6 %copy.50 = f32[4,16,128]{2,1,0:T(8,128)} copy(f32[4,16,128]{2,0,1:T(4,128)S(1)} %get-tuple-element.13) | data formatting | bytes 65536
  48.1 0.0 collective-permute-done.13
  48.1 1.6 %collective-permute-done.12 = bf16[4,8,4,2,128]{4,1,0,3,2:T(8,128)(2,1)S(1)} collective-permute-done((bf16[4,8,4,2,128]{4,1,0,3,2:T(8,128)(2,1)S(1)}, bf16[4,8,4,2,128]{4,1,0,3,2:T(8,128)(2,1)S(1)}, u32[]{:S(2)}, u32[]{:S(2)}) %collective-permute-start.12) | collective-permute-done | bytes 65568 | tf_op jit(solution)/shard_map/ppermute | solution.py:16
  49.7 1.2 %collective-permute-done.14 = bf16[4,8,4,2,128]{4,1,0,3,2:T(8,128)(2,1)S(1)} collective-permute-done((bf16[4,8,4,2,128]{4,1,0,3,2:T(8,128)(2,1)S(1)}, bf16[4,8,4,2,128]{4,1,0,3,2:T(8,128)(2,1)S(1)}, u32[]{:S(2)}, u32[]{:S(2)}) %collective-permute-start.14) | collective-permute-done | bytes 65568 | tf_op jit(solution)/shard_map/ppermute | solution.py:16
  50.9 0.3 fusion
  51.3 1.3 %copy.51 = bf16[1,1,1,256,4,2,128]{6,5,4,3,2,1,0:T(2,128)(2,1)} copy(bf16[1,1,1,256,4,2,128]{6,3,5,4,2,1,0:T(8,128)(2,1)S(1)} %fusion) | data formatting | bytes 1048576
  (28 shorter events, 0.5 us)
Async XLA Ops:
  0.6 0.7 %copy-start.4 = (s32[1,1,1,256]{3,2,1,0:T(1,128)S(1)}, s32[1,1,1,256]{3,2,1,0:T(1,128)}, u32[]{:S(2)}) copy-start(s32[1,1,1,256]{3,2,1,0:T(1,128)} %param.7) | copy-start | bytes 3076
  0.6 0.7 %copy-start.3 = (s32[1,1,1,256]{3,2,1,0:T(1,128)S(1)}, s32[1,1,1,256]{3,2,1,0:T(1,128)}, u32[]{:S(2)}) copy-start(s32[1,1,1,256]{3,2,1,0:T(1,128)} %param.8) | copy-start | bytes 3076
  1.3 2.1 %collective-permute-start = (s32[2,256]{1,0:T(2,128)S(1)}, s32[2,256]{1,0:T(2,128)S(1)}, u32[]{:S(2)}, u32[]{:S(2)}) collective-permute-start(s32[2,256]{1,0:T(2,128)S(1)} %pad_add_fusion), channel_id=1, source_target_pairs={{0,16},{16,0},{1,17},{17,1},{2,18},{18,2},{3,19},{19,3},{4,20},{20... | collective-permute-start | bytes 6152 | tf_op jit(solution)/shard_map/ppermute | solution.py:16
  1.8 1.7 %copy-start = (bf16[1,1,1,256,4,2,128]{6,5,4,3,2,1,0:T(2,128)(2,1)S(1)}, bf16[1,1,1,256,4,2,128]{6,5,4,3,2,1,0:T(2,128)(2,1)}, u32[]{:S(2)}) copy-start(bf16[1,1,1,256,4,2,128]{6,5,4,3,2,1,0:T(2,128)(2,1)} %param.5) | copy-start | bytes 1572868
  3.3 2.0 %collective-permute-start.1 = (bf16[256,4,2,128]{3,0,2,1:T(8,128)(2,1)S(1)}, bf16[256,4,2,128]{3,0,2,1:T(8,128)(2,1)S(1)}, u32[]{:S(2)}, u32[]{:S(2)}) collective-permute-start(bf16[256,4,2,128]{3,0,2,1:T(8,128)(2,1)S(1)} %bitcast_select_fusion), channel_id=1, source_target_pairs={{0,16},{16,0},{1,17},{17,1},{2,18},{18,2},{3,19},{19,3},{4,20},{20... | collective-permute-start | bytes 1572872 | tf_op jit(solution)/shard_map/ppermute | solution.py:16
  3.6 1.0 %copy-start.1 = (bf16[1,1,1,256,4,2,128]{6,5,4,3,2,1,0:T(2,128)(2,1)S(1)}, bf16[1,1,1,256,4,2,128]{6,5,4,3,2,1,0:T(2,128)(2,1)}, u32[]{:S(2)}) copy-start(bf16[1,1,1,256,4,2,128]{6,5,4,3,2,1,0:T(2,128)(2,1)} %param.6) | copy-start | bytes 1572868
  5.6 9.4 %collective-permute-start.2 = (f32[48,4,2,128]{3,0,2,1:T(8,128)S(1)}, f32[48,4,2,128]{3,0,2,1:T(8,128)S(1)}, u32[]{:S(2)}, u32[]{:S(2)}) collective-permute-start(f32[48,4,2,128]{3,0,2,1:T(8,128)S(1)} %get-tuple-element.17), channel_id=1, source_target_pairs={{0,4},{4,8},{8,12},{12,0},{1,5},{5,9},{9,13},{13,1},{2,6},{6,10},{... | collective-permute-start | bytes 589832 | tf_op jit(solution)/shard_map/ppermute | solution.py:16
  8.3 10.9 %collective-permute-start.4 = (f32[48,4,2,128]{3,0,2,1:T(8,128)S(1)}, f32[48,4,2,128]{3,0,2,1:T(8,128)S(1)}, u32[]{:S(2)}, u32[]{:S(2)}) collective-permute-start(f32[48,4,2,128]{3,0,2,1:T(8,128)S(1)} %get-tuple-element.18), channel_id=1, source_target_pairs={{0,12},{4,0},{8,4},{12,8},{1,13},{5,1},{9,5},{13,9},{2,14},{6,2},{... | collective-permute-start | bytes 589832 | tf_op jit(solution)/shard_map/ppermute | solution.py:16
  9.3 9.9 %collective-permute-start.3 = (f32[48,4,2,128]{3,0,2,1:T(8,128)S(1)}, f32[48,4,2,128]{3,0,2,1:T(8,128)S(1)}, u32[]{:S(2)}, u32[]{:S(2)}) collective-permute-start(f32[48,4,2,128]{3,0,2,1:T(8,128)S(1)} %get-tuple-element.19), channel_id=1, source_target_pairs={{0,8},{4,12},{8,0},{12,4},{1,9},{5,13},{9,1},{13,5},{2,10},{6,14},... | collective-permute-start | bytes 589832 | tf_op jit(solution)/shard_map/ppermute | solution.py:16
  21.2 5.9 %collective-permute-start.7 = (f32[102,128]{1,0:T(8,128)S(1)}, f32[102,128]{1,0:T(8,128)S(1)}, u32[]{:S(2)}, u32[]{:S(2)}) collective-permute-start(f32[102,128]{1,0:T(8,128)S(1)} %bitcast.102), channel_id=1, source_target_pairs={{0,3},{1,0},{2,1},{3,2},{4,7},{5,4},{6,5},{7,6},{8,11},{9,8},{10,9... | collective-permute-start | bytes 156680 | tf_op jit(solution)/shard_map/ppermute | solution.py:16
  24.8 5.2 %collective-permute-start.6 = (f32[102,128]{1,0:T(8,128)S(1)}, f32[102,128]{1,0:T(8,128)S(1)}, u32[]{:S(2)}, u32[]{:S(2)}) collective-permute-start(f32[102,128]{1,0:T(8,128)S(1)} %bitcast.101), channel_id=1, source_target_pairs={{0,2},{1,3},{2,0},{3,1},{4,6},{5,7},{6,4},{7,5},{8,10},{9,11},{10,... | collective-permute-start | bytes 156680 | tf_op jit(solution)/shard_map/ppermute | solution.py:16
  24.8 5.9 %collective-permute-start.5 = (f32[102,128]{1,0:T(8,128)S(1)}, f32[102,128]{1,0:T(8,128)S(1)}, u32[]{:S(2)}, u32[]{:S(2)}) collective-permute-start(f32[102,128]{1,0:T(8,128)S(1)} %bitcast.100), channel_id=1, source_target_pairs={{0,1},{1,2},{2,3},{3,0},{4,5},{5,6},{6,7},{7,4},{8,9},{9,10},{10,1... | collective-permute-start | bytes 156680 | tf_op jit(solution)/shard_map/ppermute | solution.py:16
  30.8 1.3 %collective-permute-start.8 = (f32[102,128]{1,0:T(8,128)S(1)}, f32[102,128]{1,0:T(8,128)S(1)}, u32[]{:S(2)}, u32[]{:S(2)}) collective-permute-start(f32[102,128]{1,0:T(8,128)S(1)} %fusion.53), channel_id=1, source_target_pairs={{0,16},{16,0},{1,17},{17,1},{2,18},{18,2},{3,19},{19,3},{4,20},{20... | collective-permute-start | bytes 156680 | tf_op jit(solution)/shard_map/ppermute | solution.py:16
  33.6 0.8 %copy-start.2 = (f32[4,16,128]{2,1,0:T(8,128)S(1)}, f32[4,16,128]{2,1,0:T(8,128)}, u32[]{:S(2)}) copy-start(f32[4,16,128]{2,1,0:T(8,128)} %param.9) | copy-start | bytes 98308
  34.6 5.6 %collective-permute-start.9 = (bf16[8,4,2,128]{3,0,2,1:T(8,128)(2,1)S(1)}, bf16[8,4,2,128]{3,0,2,1:T(8,128)(2,1)S(1)}, u32[]{:S(2)}, u32[]{:S(2)}) collective-permute-start(bf16[8,4,2,128]{3,0,2,1:T(8,128)(2,1)S(1)} %bitcast.92), channel_id=1, source_target_pairs={{0,1},{1,2},{2,3},{3,0},{4,5},{5,6},{6,7},{7,4},{8,9},{9,10},{10,1... | collective-permute-start | bytes 49160 | tf_op jit(solution)/shard_map/ppermute | solution.py:16
  34.6 5.5 %collective-permute-start.11 = (bf16[8,4,2,128]{3,0,2,1:T(8,128)(2,1)S(1)}, bf16[8,4,2,128]{3,0,2,1:T(8,128)(2,1)S(1)}, u32[]{:S(2)}, u32[]{:S(2)}) collective-permute-start(bf16[8,4,2,128]{3,0,2,1:T(8,128)(2,1)S(1)} %bitcast.93), channel_id=1, source_target_pairs={{0,3},{1,0},{2,1},{3,2},{4,7},{5,4},{6,5},{7,6},{8,11},{9,8},{10,9... | collective-permute-start | bytes 49160 | tf_op jit(solution)/shard_map/ppermute | solution.py:16
  38.4 4.6 %collective-permute-start.10 = (bf16[8,4,2,128]{3,0,2,1:T(8,128)(2,1)S(1)}, bf16[8,4,2,128]{3,0,2,1:T(8,128)(2,1)S(1)}, u32[]{:S(2)}, u32[]{:S(2)}) collective-permute-start(bf16[8,4,2,128]{3,0,2,1:T(8,128)(2,1)S(1)} %bitcast.94), channel_id=1, source_target_pairs={{0,2},{1,3},{2,0},{3,1},{4,6},{5,7},{6,4},{7,5},{8,10},{9,11},{10,... | collective-permute-start | bytes 49160 | tf_op jit(solution)/shard_map/ppermute | solution.py:16
  43.1 5.0 %collective-permute-start.13 = (bf16[4,8,4,2,128]{4,1,0,3,2:T(8,128)(2,1)S(1)}, bf16[4,8,4,2,128]{4,1,0,3,2:T(8,128)(2,1)S(1)}, u32[]{:S(2)}, u32[]{:S(2)}) collective-permute-start(bf16[4,8,4,2,128]{4,1,0,3,2:T(8,128)(2,1)S(1)} %get-tuple-element.31), channel_id=1, source_target_pairs={{0,8},{4,12},{8,0},{12,4},{1,9},{5,13},{9,1},{13,5},{2,10},{6,14},... | collective-permute-start | bytes 196616 | tf_op jit(solution)/shard_map/ppermute | solution.py:16
  44.6 5.2 %collective-permute-start.12 = (bf16[4,8,4,2,128]{4,1,0,3,2:T(8,128)(2,1)S(1)}, bf16[4,8,4,2,128]{4,1,0,3,2:T(8,128)(2,1)S(1)}, u32[]{:S(2)}, u32[]{:S(2)}) collective-permute-start(bf16[4,8,4,2,128]{4,1,0,3,2:T(8,128)(2,1)S(1)} %get-tuple-element.31), channel_id=1, source_target_pairs={{0,4},{4,8},{8,12},{12,0},{1,5},{5,9},{9,13},{13,1},{2,6},{6,10},{... | collective-permute-start | bytes 196616 | tf_op jit(solution)/shard_map/ppermute | solution.py:16
  46.6 4.3 %collective-permute-start.14 = (bf16[4,8,4,2,128]{4,1,0,3,2:T(8,128)(2,1)S(1)}, bf16[4,8,4,2,128]{4,1,0,3,2:T(8,128)(2,1)S(1)}, u32[]{:S(2)}, u32[]{:S(2)}) collective-permute-start(bf16[4,8,4,2,128]{4,1,0,3,2:T(8,128)(2,1)S(1)} %get-tuple-element.31), channel_id=1, source_target_pairs={{0,12},{4,0},{8,4},{12,8},{1,13},{5,1},{9,5},{13,9},{2,14},{6,2},{... | collective-permute-start | bytes 196616 | tf_op jit(solution)/shard_map/ppermute | solution.py:16

commit v14 on v4

--- a/solution.py
+++ b/solution.py
@@ -14,6 +14,10 @@
 
 def shifted(value, axis, count, step):
     return lax.ppermute(value, axis, [(s, (s + step) % count) for s in range(count)])
+
+
+def swapped(value, axis, count, mask):
+    return lax.ppermute(value, axis, [(s, s ^ mask) for s in range(count)])
 
 
 def local(gradient_windows, illumination_windows, window_owners, window_patches, velocity):
@@ -48,19 +52,20 @@
 
     halo_patches = h // patch_rows
     ext_patches = per_tile + 2 * halo_patches
-    rel_x = (all_owners // size_y - me_x) % size_x
-    rel_y = (all_owners % size_y - me_y) % size_y
+    all_x = all_owners // size_y
+    rel_x = all_x ^ me_x
+    rel_y = (all_owners % size_y) ^ me_y
     own_row = (rel_x * size_y + rel_y) * ext_patches + all_patches + halo_patches
     next_row = jnp.where(
         all_patches >= per_tile - halo_patches,
-        (((rel_x + 1) % size_x) * size_y + rel_y) * ext_patches
+        ((((all_x + 1) % size_x) ^ me_x) * size_y + rel_y) * ext_patches
         + all_patches
         - (per_tile - halo_patches),
         -1,
     )
     prev_row = jnp.where(
         all_patches < halo_patches,
-        (((rel_x - 1) % size_x) * size_y + rel_y) * ext_patches
+        ((((all_x - 1) % size_x) ^ me_x) * size_y + rel_y) * ext_patches
         + all_patches
         + per_tile
         + halo_patches,
@@ -75,17 +80,18 @@
 
     part = flat[0]
     for step in range(1, size_x):
-        part = part + shifted(flat[step], "gx", size_x, step)
+        part = part + swapped(flat[step], "gx", size_x, step)
     part = part.reshape(size_y, ext_patches, levels, patch_rows, patch_cols)
-    left = jnp.roll(part, 1, axis=0)[..., patch_cols - h :]
-    right = jnp.roll(part, -1, axis=0)[..., :h]
+    slot_y = jnp.arange(size_y, dtype=jnp.int32) ^ me_y
+    left = jnp.take(part, ((slot_y - 1) % size_y) ^ me_y, axis=0)[..., patch_cols - h :]
+    right = jnp.take(part, ((slot_y + 1) % size_y) ^ me_y, axis=0)[..., :h]
     strips = jnp.concatenate([left, right], axis=-1)
     packed = jnp.concatenate(
         [part.reshape(size_y, -1), strips.reshape(size_y, -1)], axis=1
     ).reshape(size_y, -1, 128)
     total = packed[0]
     for step in range(1, size_y):
-        total = total + shifted(packed[step], "gy", size_y, step)
+        total = total + swapped(packed[step], "gy", size_y, step)
     other = shifted(total, "group", size_g, 1)
     grad_flat = jnp.where(is_grad, total, other).reshape(-1)
     illum_flat = jnp.where(is_grad, other, total).reshape(-1)
@@ -121,16 +127,16 @@
         .astype(jnp.bfloat16)
     )
     along_y = jnp.stack(
-        [tile_table] + [shifted(tile_table, "gy", size_y, step) for step in range(1, size_y)]
+        [tile_table] + [swapped(tile_table, "gy", size_y, step) for step in range(1, size_y)]
     )
     along_x = jnp.stack(
-        [along_y] + [shifted(along_y, "gx", size_x, step) for step in range(1, size_x)]
+        [along_y] + [swapped(along_y, "gx", size_x, step) for step in range(1, size_x)]
     )
     whole = along_x.reshape(tiles * per_tile, levels, patch_rows, patch_cols)
     owner_x = owners // size_y
     owner_y = owners % size_y
     back_row = (
-        ((me_x - owner_x) % size_x) * size_y + (me_y - owner_y) % size_y
+        (owner_x ^ me_x) * size_y + (owner_y ^ me_y)
     ) * per_tile + patches
     pick = (back_row[:, None] == jnp.arange(tiles * per_tile, dtype=jnp.int32)[None, :]).astype(
         jnp.bfloat16

time: 48.7 us -> 52.4 us (1.076)
  waiting for transfers between devices: 18.5 us -> 23.5 us
  starting transfers between devices: 20.3 us -> 17.3 us
  local copies, waits for them, and re-layouts: 3.97 us -> 5.28 us
    ppermute x0 -> x12, waiting for transfers between devices: none -> 20.7 us  [swapped(): return lax.ppermute(value, axis, [(s, s ^ mask) for s in range(count)])]
    ppermute x15 -> x3, starting transfers between devices: 20.3 us -> 0.65 us  [shifted(): lax.ppermute(value, axis, [(s, (s + step) % count) for s in range(count)])]
    ppermute x0 -> x12, starting transfers between devices: none -> 16.7 us  [swapped(): return lax.ppermute(value, axis, [(s, s ^ mask) for s in range(count)])]
    ppermute x15 -> x3, waiting for transfers between devices: 18.5 us -> 2.78 us  [shifted(): lax.ppermute(value, axis, [(s, (s + step) % count) for s in range(count)])]
    gather x0 -> x2, local copies, waits for them, and re-layouts: none -> 1.51 us  [the longest x1 0.76 us: local(): jnp.take(part, (slot_y - 1) % size_y ^ me_y, axis=0)[..., patch_cols - h:]]
  transfers between devices with their start and end apart: 15 -> 15, of which waited for: 14 -> 11; matrix products, arithmetic and copies ran while one was open for 5% -> 4% of each run, Pallas kernels for 0% -> 0%
where the time goes in v14:
time: 52.4 us; the launch traced here: 52.2 us
  waiting for transfers between devices  23.5 us (45%)
  starting transfers between devices  17.3 us (33%)
  local copies, waits for them, and re-layouts  5.28 us (10%)
  other arithmetic  4.4 us (8%)
  between operations  0.97 us (2%)
  matrix products  0.71 us (1%)
    ppermute x12, waiting for transfers between devices, swapped(): return lax.ppermute(value, axis, [(s, s ^ mask) for s in range(count)])  20.7 us
    ppermute x12, starting transfers between devices, swapped(): return lax.ppermute(value, axis, [(s, s ^ mask) for s in range(count)])  16.7 us
    ppermute x3, waiting for transfers between devices, shifted(): lax.ppermute(value, axis, [(s, (s + step) % count) for s in range(count)])  2.78 us
    unnamed x9, local copies, waits for them, and re-layouts  1.98 us
    select_n x1, other arithmetic, local(): kept = jnp.where(is_grad, slot_grad, slot_illum)  1.39 us
  transfers between devices with their start and end apart: 15, of which 11 were waited for; matrix products, arithmetic and copies ran while one was open for 4% of the time, Pallas kernels for 0%

profile of v14, /device:TPU:0, one launch (start us, length us, event | category | flops | bytes accessed | tf_op | source)
XLA Modules:
  0.0 52.2 jit_solution(4522591030130591355)
XLA Ops:
  0.6 0.7 %pad_add_fusion = s32[2,256]{1,0:T(2,128)S(1)} fusion(s32[1,256]{1,0:T(1,128)} %bitcast.86, s32[1,256]{1,0:T(1,128)} %bitcast.89), kind=kLoop, calls=%fused_computation.146 | loop fusion | flops 512 | bytes 4096 | tf_op jit(solution)/shard_map/stack | solution.py:46
  1.3 0.5 collective-permute-start
  1.8 0.0 copy-start.1
  1.8 0.0 copy-start.2
  1.8 1.4 %select_bitcast_fusion.1 = (bf16[256,4,2,128]{3,0,2,1:T(8,128)(2,1)S(1)}, bf16[256,4,2,128]{3,0,2,1:T(8,128)(2,1)S(1)}) fusion(pred[]{:T(512)S(6)} %eq.64, bf16[1,1,1,256,4,2,128]{6,5,4,3,2,1,0:T(2,128)(2,1)} %param.8, bf16[1,1,1,256,4,2,128]{6,5,4,3,2,1,0:T(2,128)(2,1)} %param.7), kind=kLoop, calls=%fused_computation.9 | loop fusion | flops 524288 | bytes 2097153 | tf_op jit(solution)/shard_map/jit(_where)/select_n | solution.py:44
  3.2 0.1 collective-permute-start.1
  3.4 0.0 collective-permute-done
  3.4 0.0 copy-done.1
  3.4 0.0 copy-done.2
  3.5 1.7 %collective-permute-done.1 = bf16[256,4,2,128]{3,0,2,1:T(8,128)(2,1)S(1)} collective-permute-done((bf16[256,4,2,128]{3,0,2,1:T(8,128)(2,1)S(1)}, bf16[256,4,2,128]{3,0,2,1:T(8,128)(2,1)S(1)}, u32[]{:S(2)}, u32[]{:S(2)}) %collective-permute-start.1) | collective-permute-done | bytes 524320 | tf_op jit(solution)/shard_map/ppermute | solution.py:16
  5.2 0.4 fusion.1
  5.6 2.7 %collective-permute-start.2 = (f32[48,4,2,128]{3,0,2,1:T(8,128)S(1)}, f32[48,4,2,128]{3,0,2,1:T(8,128)S(1)}, u32[]{:S(2)}, u32[]{:S(2)}) collective-permute-start(f32[48,4,2,128]{3,0,2,1:T(8,128)S(1)} %get-tuple-element.17), channel_id=1, source_target_pairs={{0,4},{4,0},{8,12},{12,8},{1,5},{5,1},{9,13},{13,9},{2,6},{6,2},{1... | collective-permute-start | bytes 589832 | tf_op jit(solution)/shard_map/ppermute | solution.py:20
  8.3 1.5 %collective-permute-start.3 = (f32[48,4,2,128]{3,0,2,1:T(8,128)S(1)}, f32[48,4,2,128]{3,0,2,1:T(8,128)S(1)}, u32[]{:S(2)}, u32[]{:S(2)}) collective-permute-start(f32[48,4,2,128]{3,0,2,1:T(8,128)S(1)} %get-tuple-element.19), channel_id=1, source_target_pairs={{0,8},{4,12},{8,0},{12,4},{1,9},{5,13},{9,1},{13,5},{2,10},{6,14},... | collective-permute-start | bytes 589832 | tf_op jit(solution)/shard_map/ppermute | solution.py:20
  9.8 0.0 collective-permute-start.4
  9.9 4.2 %collective-permute-done.2 = f32[48,4,2,128]{3,0,2,1:T(8,128)S(1)} collective-permute-done((f32[48,4,2,128]{3,0,2,1:T(8,128)S(1)}, f32[48,4,2,128]{3,0,2,1:T(8,128)S(1)}, u32[]{:S(2)}, u32[]{:S(2)}) %collective-permute-start.2) | collective-permute-done | bytes 196640 | tf_op jit(solution)/shard_map/ppermute | solution.py:20
  14.0 5.4 %collective-permute-done.3 = f32[48,4,2,128]{3,0,2,1:T(8,128)S(1)} collective-permute-done((f32[48,4,2,128]{3,0,2,1:T(8,128)S(1)}, f32[48,4,2,128]{3,0,2,1:T(8,128)S(1)}, u32[]{:S(2)}, u32[]{:S(2)}) %collective-permute-start.3) | collective-permute-done | bytes 196640 | tf_op jit(solution)/shard_map/ppermute | solution.py:20
  19.4 0.0 collective-permute-done.4
  19.5 0.1 copy.37
  19.6 0.2 reshape_reshape.3
  19.8 0.8 %gather_fusion.1 = f32[4,12,4,2,128]{4,3,2,1,0:T(2,128)S(1)} fusion(f32[4,12,4,2,128]{4,3,2,1,0:T(2,128)S(1)} %bitcast.67, s32[1024]{0:T(1024)S(1)} %pad_clamp_fusion), kind=kCustom, calls=%fused_computation.1.clone | custom fusion | bytes 393232 | tf_op jit(solution)/shard_map/jit(_take)/gather | solution.py:87
  20.5 0.8 %gather_fusion = f32[4,12,4,2,128]{4,3,2,1,0:T(2,128)S(1)} fusion(f32[4,12,4,2,128]{4,3,2,1,0:T(2,128)S(1)} %bitcast.68, s32[1024]{0:T(1024)S(1)} %pad_clamp_fusion.1), kind=kCustom, calls=%fused_computation.clone | custom fusion | bytes 393232 | tf_op jit(solution)/shard_map/jit(_take)/gather | solution.py:86
  21.3 0.1 slice_select_fusion
  21.5 0.3 slice_select_fusion.1
  21.7 0.3 pad_maximum_fusion.1
  22.0 0.3 reshape.486
  22.3 0.6 %slice_reduce_fusion.3 = (f32[13056]{0:T(1024)S(1)}, f32[13056]{0:T(1024)S(1)}, f32[13056]{0:T(1024)S(1)}, f32[13056]{0:T(1024)S(1)}) fusion(f32[4,13056]{1,0:T(4,128)S(1)} %constant_dynamic-update-slice_fusion), kind=kLoop, calls=%fused_computation.93 | loop fusion | bytes 417792 | tf_op jit(solution)/shard_map/slice | solution.py:92
  22.9 1.6 %collective-permute-start.5 = (f32[102,128]{1,0:T(8,128)S(1)}, f32[102,128]{1,0:T(8,128)S(1)}, u32[]{:S(2)}, u32[]{:S(2)}) collective-permute-start(f32[102,128]{1,0:T(8,128)S(1)} %bitcast.82), channel_id=1, source_target_pairs={{0,1},{1,0},{2,3},{3,2},{4,5},{5,4},{6,7},{7,6},{8,9},{9,8},{10,11... | collective-permute-start | bytes 156680 | tf_op jit(solution)/shard_map/ppermute | solution.py:20
  24.5 2.6 %collective-permute-start.6 = (f32[102,128]{1,0:T(8,128)S(1)}, f32[102,128]{1,0:T(8,128)S(1)}, u32[]{:S(2)}, u32[]{:S(2)}) collective-permute-start(f32[102,128]{1,0:T(8,128)S(1)} %bitcast.81), channel_id=1, source_target_pairs={{0,2},{1,3},{2,0},{3,1},{4,6},{5,7},{6,4},{7,5},{8,10},{9,11},{10,... | collective-permute-start | bytes 156680 | tf_op jit(solution)/shard_map/ppermute | solution.py:20
  27.1 0.2 collective-permute-start.7
  27.3 0.0 collective-permute-done.5
  27.4 2.8 %collective-permute-done.6 = f32[102,128]{1,0:T(8,128)S(1)} collective-permute-done((f32[102,128]{1,0:T(8,128)S(1)}, f32[102,128]{1,0:T(8,128)S(1)}, u32[]{:S(2)}, u32[]{:S(2)}) %collective-permute-start.6) | collective-permute-done | bytes 52256 | tf_op jit(solution)/shard_map/ppermute | solution.py:20
  30.1 2.9 %collective-permute-done.7 = f32[102,128]{1,0:T(8,128)S(1)} collective-permute-done((f32[102,128]{1,0:T(8,128)S(1)}, f32[102,128]{1,0:T(8,128)S(1)}, u32[]{:S(2)}, u32[]{:S(2)}) %collective-permute-start.7) | collective-permute-done | bytes 52256 | tf_op jit(solution)/shard_map/ppermute | solution.py:20
  33.1 0.1 collective-permute-start.8
  33.1 0.1 broadcast_and_fusion
  33.2 0.1 slice.221
  33.3 1.1 %collective-permute-done.8 = f32[102,128]{1,0:T(8,128)S(1)} collective-permute-done((f32[102,128]{1,0:T(8,128)S(1)}, f32[102,128]{1,0:T(8,128)S(1)}, u32[]{:S(2)}, u32[]{:S(2)}) %collective-permute-start.8) | collective-permute-done | bytes 52256 | tf_op jit(solution)/shard_map/ppermute | solution.py:16
  34.4 0.1 reshape.487
  34.6 0.1 fusion.85
  34.7 0.1 reshape.489
  34.8 0.1 fusion.86
  34.9 0.4 fusion.45
  35.3 0.0 copy-start
  35.4 0.2 fusion.22
  35.6 0.2 fusion.31
  35.8 0.2 fusion.40
  36.0 0.2 fusion.43
  36.2 0.0 copy-done
  36.2 0.2 fusion.82
  36.3 0.1 collective-permute-start.9
  36.4 1.2 %collective-permute-start.10 = (bf16[8,4,2,128]{3,0,2,1:T(8,128)(2,1)S(1)}, bf16[8,4,2,128]{3,0,2,1:T(8,128)(2,1)S(1)}, u32[]{:S(2)}, u32[]{:S(2)}) collective-permute-start(bf16[8,4,2,128]{3,0,2,1:T(8,128)(2,1)S(1)} %bitcast.73), channel_id=1, source_target_pairs={{0,2},{1,3},{2,0},{3,1},{4,6},{5,7},{6,4},{7,5},{8,10},{9,11},{10,... | collective-permute-start | bytes 49160 | tf_op jit(solution)/shard_map/ppermute | solution.py:20
  37.7 3.1 %collective-permute-start.11 = (bf16[8,4,2,128]{3,0,2,1:T(8,128)(2,1)S(1)}, bf16[8,4,2,128]{3,0,2,1:T(8,128)(2,1)S(1)}, u32[]{:S(2)}, u32[]{:S(2)}) collective-permute-start(bf16[8,4,2,128]{3,0,2,1:T(8,128)(2,1)S(1)} %bitcast.74), channel_id=1, source_target_pairs={{0,3},{1,2},{2,1},{3,0},{4,7},{5,6},{6,5},{7,4},{8,11},{9,10},{10,... | collective-permute-start | bytes 49160 | tf_op jit(solution)/shard_map/ppermute | solution.py:20
  40.8 0.0 collective-permute-done.9
  40.8 0.3 collective-permute-done.10
  41.1 2.1 %collective-permute-done.11 = bf16[8,4,2,128]{3,0,2,1:T(8,128)(2,1)S(1)} collective-permute-done((bf16[8,4,2,128]{3,0,2,1:T(8,128)(2,1)S(1)}, bf16[8,4,2,128]{3,0,2,1:T(8,128)(2,1)S(1)}, u32[]{:S(2)}, u32[]{:S(2)}) %collective-permute-start.11) | collective-permute-done | bytes 16416 | tf_op jit(solution)/shard_map/ppermute | solution.py:20
  43.2 1.3 %collective-permute-start.12 = (bf16[4,8,4,2,128]{4,1,0,3,2:T(8,128)(2,1)S(1)}, bf16[4,8,4,2,128]{4,1,0,3,2:T(8,128)(2,1)S(1)}, u32[]{:S(2)}, u32[]{:S(2)}) collective-permute-start(bf16[4,8,4,2,128]{4,1,0,3,2:T(8,128)(2,1)S(1)} %get-tuple-element.27), channel_id=1, source_target_pairs={{0,4},{4,0},{8,12},{12,8},{1,5},{5,1},{9,13},{13,9},{2,6},{6,2},{1... | collective-permute-start | bytes 196616 | tf_op jit(solution)/shard_map/ppermute | solution.py:20
  44.6 0.8 %collective-permute-start.13 = (bf16[4,8,4,2,128]{4,1,0,3,2:T(8,128)(2,1)S(1)}, bf16[4,8,4,2,128]{4,1,0,3,2:T(8,128)(2,1)S(1)}, u32[]{:S(2)}, u32[]{:S(2)}) collective-permute-start(bf16[4,8,4,2,128]{4,1,0,3,2:T(8,128)(2,1)S(1)} %get-tuple-element.27), channel_id=1, source_target_pairs={{0,8},{4,12},{8,0},{12,4},{1,9},{5,13},{9,1},{13,5},{2,10},{6,14},... | collective-permute-start | bytes 196616 | tf_op jit(solution)/shard_map/ppermute | solution.py:20
  45.3 1.4 %collective-permute-start.14 = (bf16[4,8,4,2,128]{4,1,0,3,2:T(8,128)(2,1)S(1)}, bf16[4,8,4,2,128]{4,1,0,3,2:T(8,128)(2,1)S(1)}, u32[]{:S(2)}, u32[]{:S(2)}) collective-permute-start(bf16[4,8,4,2,128]{4,1,0,3,2:T(8,128)(2,1)S(1)} %get-tuple-element.27), channel_id=1, source_target_pairs={{0,12},{4,8},{8,4},{12,0},{1,13},{5,9},{9,5},{13,1},{2,14},{6,10},... | collective-permute-start | bytes 196616 | tf_op jit(solution)/shard_map/ppermute | solution.py:20
  46.8 0.6 %copy.48 = f32[4,16,128]{2,1,0:T(8,128)} copy(f32[4,16,128]{2,0,1:T(4,128)S(1)} %get-tuple-element.14) | data formatting | bytes 65536
  47.4 0.5 collective-permute-done.12
  47.9 0.9 %collective-permute-done.13 = bf16[4,8,4,2,128]{4,1,0,3,2:T(8,128)(2,1)S(1)} collective-permute-done((bf16[4,8,4,2,128]{4,1,0,3,2:T(8,128)(2,1)S(1)}, bf16[4,8,4,2,128]{4,1,0,3,2:T(8,128)(2,1)S(1)}, u32[]{:S(2)}, u32[]{:S(2)}) %collective-permute-start.13) | collective-permute-done | bytes 65568 | tf_op jit(solution)/shard_map/ppermute | solution.py:20
  48.8 1.7 %collective-permute-done.14 = bf16[4,8,4,2,128]{4,1,0,3,2:T(8,128)(2,1)S(1)} collective-permute-done((bf16[4,8,4,2,128]{4,1,0,3,2:T(8,128)(2,1)S(1)}, bf16[4,8,4,2,128]{4,1,0,3,2:T(8,128)(2,1)S(1)}, u32[]{:S(2)}, u32[]{:S(2)}) %collective-permute-start.14) | collective-permute-done | bytes 65568 | tf_op jit(solution)/shard_map/ppermute | solution.py:20
  50.5 0.3 fusion
  50.9 1.3 %copy.49 = bf16[1,1,1,256,4,2,128]{6,5,4,3,2,1,0:T(2,128)(2,1)} copy(bf16[1,1,1,256,4,2,128]{6,3,5,4,2,1,0:T(8,128)(2,1)S(1)} %fusion) | data formatting | bytes 1048576
  (24 shorter events, 0.4 us)
Async XLA Ops:
  1.3 2.0 %collective-permute-start = (s32[2,256]{1,0:T(2,128)S(1)}, s32[2,256]{1,0:T(2,128)S(1)}, u32[]{:S(2)}, u32[]{:S(2)}) collective-permute-start(s32[2,256]{1,0:T(2,128)S(1)} %pad_add_fusion), channel_id=1, source_target_pairs={{0,16},{16,0},{1,17},{17,1},{2,18},{18,2},{3,19},{19,3},{4,20},{20... | collective-permute-start | bytes 6152 | tf_op jit(solution)/shard_map/ppermute | solution.py:16
  1.8 1.6 %copy-start.1 = (s32[1,1,1,256]{3,2,1,0:T(1,128)S(1)}, s32[1,1,1,256]{3,2,1,0:T(1,128)}, u32[]{:S(2)}) copy-start(s32[1,1,1,256]{3,2,1,0:T(1,128)} %param.10) | copy-start | bytes 3076
  1.8 1.6 %copy-start.2 = (s32[1,1,1,256]{3,2,1,0:T(1,128)S(1)}, s32[1,1,1,256]{3,2,1,0:T(1,128)}, u32[]{:S(2)}) copy-start(s32[1,1,1,256]{3,2,1,0:T(1,128)} %param.9) | copy-start | bytes 3076
  3.2 2.0 %collective-permute-start.1 = (bf16[256,4,2,128]{3,0,2,1:T(8,128)(2,1)S(1)}, bf16[256,4,2,128]{3,0,2,1:T(8,128)(2,1)S(1)}, u32[]{:S(2)}, u32[]{:S(2)}) collective-permute-start(bf16[256,4,2,128]{3,0,2,1:T(8,128)(2,1)S(1)} %get-tuple-element.16), channel_id=1, source_target_pairs={{0,16},{16,0},{1,17},{17,1},{2,18},{18,2},{3,19},{19,3},{4,20},{20... | collective-permute-start | bytes 1572872 | tf_op jit(solution)/shard_map/ppermute | solution.py:16
  5.6 8.4 %collective-permute-start.2 = (f32[48,4,2,128]{3,0,2,1:T(8,128)S(1)}, f32[48,4,2,128]{3,0,2,1:T(8,128)S(1)}, u32[]{:S(2)}, u32[]{:S(2)}) collective-permute-start(f32[48,4,2,128]{3,0,2,1:T(8,128)S(1)} %get-tuple-element.17), channel_id=1, source_target_pairs={{0,4},{4,0},{8,12},{12,8},{1,5},{5,1},{9,13},{13,9},{2,6},{6,2},{1... | collective-permute-start | bytes 589832 | tf_op jit(solution)/shard_map/ppermute | solution.py:20
  8.3 11.1 %collective-permute-start.3 = (f32[48,4,2,128]{3,0,2,1:T(8,128)S(1)}, f32[48,4,2,128]{3,0,2,1:T(8,128)S(1)}, u32[]{:S(2)}, u32[]{:S(2)}) collective-permute-start(f32[48,4,2,128]{3,0,2,1:T(8,128)S(1)} %get-tuple-element.19), channel_id=1, source_target_pairs={{0,8},{4,12},{8,0},{12,4},{1,9},{5,13},{9,1},{13,5},{2,10},{6,14},... | collective-permute-start | bytes 589832 | tf_op jit(solution)/shard_map/ppermute | solution.py:20
  9.8 9.6 %collective-permute-start.4 = (f32[48,4,2,128]{3,0,2,1:T(8,128)S(1)}, f32[48,4,2,128]{3,0,2,1:T(8,128)S(1)}, u32[]{:S(2)}, u32[]{:S(2)}) collective-permute-start(f32[48,4,2,128]{3,0,2,1:T(8,128)S(1)} %get-tuple-element.18), channel_id=1, source_target_pairs={{0,12},{4,8},{8,4},{12,0},{1,13},{5,9},{9,5},{13,1},{2,14},{6,10},... | collective-permute-start | bytes 589832 | tf_op jit(solution)/shard_map/ppermute | solution.py:20
  22.9 4.5 %collective-permute-start.5 = (f32[102,128]{1,0:T(8,128)S(1)}, f32[102,128]{1,0:T(8,128)S(1)}, u32[]{:S(2)}, u32[]{:S(2)}) collective-permute-start(f32[102,128]{1,0:T(8,128)S(1)} %bitcast.82), channel_id=1, source_target_pairs={{0,1},{1,0},{2,3},{3,2},{4,5},{5,4},{6,7},{7,6},{8,9},{9,8},{10,11... | collective-permute-start | bytes 156680 | tf_op jit(solution)/shard_map/ppermute | solution.py:20
  24.5 5.6 %collective-permute-start.6 = (f32[102,128]{1,0:T(8,128)S(1)}, f32[102,128]{1,0:T(8,128)S(1)}, u32[]{:S(2)}, u32[]{:S(2)}) collective-permute-start(f32[102,128]{1,0:T(8,128)S(1)} %bitcast.81), channel_id=1, source_target_pairs={{0,2},{1,3},{2,0},{3,1},{4,6},{5,7},{6,4},{7,5},{8,10},{9,11},{10,... | collective-permute-start | bytes 156680 | tf_op jit(solution)/shard_map/ppermute | solution.py:20
  27.1 5.9 %collective-permute-start.7 = (f32[102,128]{1,0:T(8,128)S(1)}, f32[102,128]{1,0:T(8,128)S(1)}, u32[]{:S(2)}, u32[]{:S(2)}) collective-permute-start(f32[102,128]{1,0:T(8,128)S(1)} %bitcast.80), channel_id=1, source_target_pairs={{0,3},{1,2},{2,1},{3,0},{4,7},{5,6},{6,5},{7,4},{8,11},{9,10},{10,... | collective-permute-start | bytes 156680 | tf_op jit(solution)/shard_map/ppermute | solution.py:20
  33.1 1.3 %collective-permute-start.8 = (f32[102,128]{1,0:T(8,128)S(1)}, f32[102,128]{1,0:T(8,128)S(1)}, u32[]{:S(2)}, u32[]{:S(2)}) collective-permute-start(f32[102,128]{1,0:T(8,128)S(1)} %fusion.48), channel_id=1, source_target_pairs={{0,16},{16,0},{1,17},{17,1},{2,18},{18,2},{3,19},{19,3},{4,20},{20... | collective-permute-start | bytes 156680 | tf_op jit(solution)/shard_map/ppermute | solution.py:16
  35.3 0.8 %copy-start = (f32[4,16,128]{2,1,0:T(8,128)S(1)}, f32[4,16,128]{2,1,0:T(8,128)}, u32[]{:S(2)}) copy-start(f32[4,16,128]{2,1,0:T(8,128)} %param.11) | copy-start | bytes 98308
  36.3 4.5 %collective-permute-start.9 = (bf16[8,4,2,128]{3,0,2,1:T(8,128)(2,1)S(1)}, bf16[8,4,2,128]{3,0,2,1:T(8,128)(2,1)S(1)}, u32[]{:S(2)}, u32[]{:S(2)}) collective-permute-start(bf16[8,4,2,128]{3,0,2,1:T(8,128)(2,1)S(1)} %bitcast.72), channel_id=1, source_target_pairs={{0,1},{1,0},{2,3},{3,2},{4,5},{5,4},{6,7},{7,6},{8,9},{9,8},{10,11... | collective-permute-start | bytes 49160 | tf_op jit(solution)/shard_map/ppermute | solution.py:20
  36.4 4.7 %collective-permute-start.10 = (bf16[8,4,2,128]{3,0,2,1:T(8,128)(2,1)S(1)}, bf16[8,4,2,128]{3,0,2,1:T(8,128)(2,1)S(1)}, u32[]{:S(2)}, u32[]{:S(2)}) collective-permute-start(bf16[8,4,2,128]{3,0,2,1:T(8,128)(2,1)S(1)} %bitcast.73), channel_id=1, source_target_pairs={{0,2},{1,3},{2,0},{3,1},{4,6},{5,7},{6,4},{7,5},{8,10},{9,11},{10,... | collective-permute-start | bytes 49160 | tf_op jit(solution)/shard_map/ppermute | solution.py:20
  37.7 5.5 %collective-permute-start.11 = (bf16[8,4,2,128]{3,0,2,1:T(8,128)(2,1)S(1)}, bf16[8,4,2,128]{3,0,2,1:T(8,128)(2,1)S(1)}, u32[]{:S(2)}, u32[]{:S(2)}) collective-permute-start(bf16[8,4,2,128]{3,0,2,1:T(8,128)(2,1)S(1)} %bitcast.74), channel_id=1, source_target_pairs={{0,3},{1,2},{2,1},{3,0},{4,7},{5,6},{6,5},{7,4},{8,11},{9,10},{10,... | collective-permute-start | bytes 49160 | tf_op jit(solution)/shard_map/ppermute | solution.py:20
  43.2 4.7 %collective-permute-start.12 = (bf16[4,8,4,2,128]{4,1,0,3,2:T(8,128)(2,1)S(1)}, bf16[4,8,4,2,128]{4,1,0,3,2:T(8,128)(2,1)S(1)}, u32[]{:S(2)}, u32[]{:S(2)}) collective-permute-start(bf16[4,8,4,2,128]{4,1,0,3,2:T(8,128)(2,1)S(1)} %get-tuple-element.27), channel_id=1, source_target_pairs={{0,4},{4,0},{8,12},{12,8},{1,5},{5,1},{9,13},{13,9},{2,6},{6,2},{1... | collective-permute-start | bytes 196616 | tf_op jit(solution)/shard_map/ppermute | solution.py:20
  44.6 4.3 %collective-permute-start.13 = (bf16[4,8,4,2,128]{4,1,0,3,2:T(8,128)(2,1)S(1)}, bf16[4,8,4,2,128]{4,1,0,3,2:T(8,128)(2,1)S(1)}, u32[]{:S(2)}, u32[]{:S(2)}) collective-permute-start(bf16[4,8,4,2,128]{4,1,0,3,2:T(8,128)(2,1)S(1)} %get-tuple-element.27), channel_id=1, source_target_pairs={{0,8},{4,12},{8,0},{12,4},{1,9},{5,13},{9,1},{13,5},{2,10},{6,14},... | collective-permute-start | bytes 196616 | tf_op jit(solution)/shard_map/ppermute | solution.py:20
  45.3 5.2 %collective-permute-start.14 = (bf16[4,8,4,2,128]{4,1,0,3,2:T(8,128)(2,1)S(1)}, bf16[4,8,4,2,128]{4,1,0,3,2:T(8,128)(2,1)S(1)}, u32[]{:S(2)}, u32[]{:S(2)}) collective-permute-start(bf16[4,8,4,2,128]{4,1,0,3,2:T(8,128)(2,1)S(1)} %get-tuple-element.27), channel_id=1, source_target_pairs={{0,12},{4,8},{8,4},{12,0},{1,13},{5,9},{9,5},{13,1},{2,14},{6,10},... | collective-permute-start | bytes 196616 | tf_op jit(solution)/shard_map/ppermute | solution.py:20

commit v15 on v4

--- a/solution.py
+++ b/solution.py
@@ -120,17 +120,17 @@
         .transpose(1, 0, 2, 3)
         .astype(jnp.bfloat16)
     )
+    along_x = jnp.stack(
+        [tile_table] + [shifted(tile_table, "gx", size_x, step) for step in range(1, size_x)]
+    )
     along_y = jnp.stack(
-        [tile_table] + [shifted(tile_table, "gy", size_y, step) for step in range(1, size_y)]
+        [along_x] + [shifted(along_x, "gy", size_y, step) for step in range(1, size_y)]
     )
-    along_x = jnp.stack(
-        [along_y] + [shifted(along_y, "gx", size_x, step) for step in range(1, size_x)]
-    )
-    whole = along_x.reshape(tiles * per_tile, levels, patch_rows, patch_cols)
+    whole = along_y.reshape(tiles * per_tile, levels, patch_rows, patch_cols)
     owner_x = owners // size_y
     owner_y = owners % size_y
     back_row = (
-        ((me_x - owner_x) % size_x) * size_y + (me_y - owner_y) % size_y
+        ((me_y - owner_y) % size_y) * size_x + (me_x - owner_x) % size_x
     ) * per_tile + patches
     pick = (back_row[:, None] == jnp.arange(tiles * per_tile, dtype=jnp.int32)[None, :]).astype(
         jnp.bfloat16

time: 48.7 us -> 49.3 us (1.012)
  waiting for transfers between devices: 18.5 us -> 19.2 us
    ppermute x15, waiting for transfers between devices: 18.5 us -> 19.2 us  [shifted(): lax.ppermute(value, axis, [(s, (s + step) % count) for s in range(count)])]
where the time goes in v15:
time: 49.3 us; the launch traced here: 49.2 us
  starting transfers between devices  20.2 us (41%)
  waiting for transfers between devices  19.2 us (39%)
  other arithmetic  4.15 us (8%)
  local copies, waits for them, and re-layouts  3.97 us (8%)
  between operations  0.92 us (2%)
  matrix products  0.71 us (1%)
    ppermute x15, starting transfers between devices, shifted(): lax.ppermute(value, axis, [(s, (s + step) % count) for s in range(count)])  20.2 us
    ppermute x15, waiting for transfers between devices, shifted(): lax.ppermute(value, axis, [(s, (s + step) % count) for s in range(count)])  19.2 us
    unnamed x9, local copies, waits for them, and re-layouts  1.98 us
    select_n x1, other arithmetic, local(): kept = jnp.where(is_grad, slot_grad, slot_illum)  1.39 us
  transfers between devices with their start and end apart: 15, of which 14 were waited for; matrix products, arithmetic and copies ran while one was open for 5% of the time, Pallas kernels for 0%

profile of v15, /device:TPU:0, one launch (start us, length us, event | category | flops | bytes accessed | tf_op | source)
XLA Modules:
  0.0 49.2 jit_solution(4623897928840858655)
XLA Ops:
  0.6 0.7 %pad_add_fusion = s32[2,256]{1,0:T(2,128)S(1)} fusion(s32[1,256]{1,0:T(1,128)} %bitcast.91, s32[1,256]{1,0:T(1,128)} %bitcast.97), kind=kLoop, calls=%fused_computation.149 | loop fusion | flops 512 | bytes 4096 | tf_op jit(solution)/shard_map/stack | solution.py:42
  1.3 0.5 collective-permute-start
  1.8 0.0 copy-start.1
  1.8 0.0 copy-start.2
  1.8 1.4 %select_bitcast_fusion.1 = (bf16[256,4,2,128]{3,0,2,1:T(8,128)(2,1)S(1)}, bf16[256,4,2,128]{3,0,2,1:T(8,128)(2,1)S(1)}) fusion(pred[]{:T(512)S(6)} %eq.65, bf16[1,1,1,256,4,2,128]{6,5,4,3,2,1,0:T(2,128)(2,1)} %param.6, bf16[1,1,1,256,4,2,128]{6,5,4,3,2,1,0:T(2,128)(2,1)} %param.5), kind=kLoop, calls=%fused_computation.7 | loop fusion | flops 524288 | bytes 2097153 | tf_op jit(solution)/shard_map/jit(_where)/select_n | solution.py:40
  3.2 0.1 collective-permute-start.1
  3.3 0.0 collective-permute-done
  3.3 0.0 copy-done.1
  3.3 0.0 copy-done.2
  3.4 1.8 %collective-permute-done.1 = bf16[256,4,2,128]{3,0,2,1:T(8,128)(2,1)S(1)} collective-permute-done((bf16[256,4,2,128]{3,0,2,1:T(8,128)(2,1)S(1)}, bf16[256,4,2,128]{3,0,2,1:T(8,128)(2,1)S(1)}, u32[]{:S(2)}, u32[]{:S(2)}) %collective-permute-start.1) | collective-permute-done | bytes 524320 | tf_op jit(solution)/shard_map/ppermute | solution.py:16
  5.2 0.4 fusion.1
  5.6 2.7 %collective-permute-start.2 = (f32[48,4,2,128]{3,0,2,1:T(8,128)S(1)}, f32[48,4,2,128]{3,0,2,1:T(8,128)S(1)}, u32[]{:S(2)}, u32[]{:S(2)}) collective-permute-start(f32[48,4,2,128]{3,0,2,1:T(8,128)S(1)} %get-tuple-element.19), channel_id=1, source_target_pairs={{0,4},{4,8},{8,12},{12,0},{1,5},{5,9},{9,13},{13,1},{2,6},{6,10},{... | collective-permute-start | bytes 589832 | tf_op jit(solution)/shard_map/ppermute | solution.py:16
  8.3 1.5 %collective-permute-start.3 = (f32[48,4,2,128]{3,0,2,1:T(8,128)S(1)}, f32[48,4,2,128]{3,0,2,1:T(8,128)S(1)}, u32[]{:S(2)}, u32[]{:S(2)}) collective-permute-start(f32[48,4,2,128]{3,0,2,1:T(8,128)S(1)} %get-tuple-element.21), channel_id=1, source_target_pairs={{0,8},{4,12},{8,0},{12,4},{1,9},{5,13},{9,1},{13,5},{2,10},{6,14},... | collective-permute-start | bytes 589832 | tf_op jit(solution)/shard_map/ppermute | solution.py:16
  9.8 1.4 %collective-permute-start.4 = (f32[48,4,2,128]{3,0,2,1:T(8,128)S(1)}, f32[48,4,2,128]{3,0,2,1:T(8,128)S(1)}, u32[]{:S(2)}, u32[]{:S(2)}) collective-permute-start(f32[48,4,2,128]{3,0,2,1:T(8,128)S(1)} %get-tuple-element.20), channel_id=1, source_target_pairs={{0,12},{4,0},{8,4},{12,8},{1,13},{5,1},{9,5},{13,9},{2,14},{6,2},{... | collective-permute-start | bytes 589832 | tf_op jit(solution)/shard_map/ppermute | solution.py:16
  11.2 3.8 %collective-permute-done.2 = f32[48,4,2,128]{3,0,2,1:T(8,128)S(1)} collective-permute-done((f32[48,4,2,128]{3,0,2,1:T(8,128)S(1)}, f32[48,4,2,128]{3,0,2,1:T(8,128)S(1)}, u32[]{:S(2)}, u32[]{:S(2)}) %collective-permute-start.2) | collective-permute-done | bytes 196640 | tf_op jit(solution)/shard_map/ppermute | solution.py:16
  15.0 3.9 %collective-permute-done.3 = f32[48,4,2,128]{3,0,2,1:T(8,128)S(1)} collective-permute-done((f32[48,4,2,128]{3,0,2,1:T(8,128)S(1)}, f32[48,4,2,128]{3,0,2,1:T(8,128)S(1)}, u32[]{:S(2)}, u32[]{:S(2)}) %collective-permute-start.3) | collective-permute-done | bytes 196640 | tf_op jit(solution)/shard_map/ppermute | solution.py:16
  18.9 0.3 collective-permute-done.4
  19.3 0.1 copy.42
  19.4 0.1 copy.43
  19.5 0.1 copy.45
  19.6 0.5 fusion.9
  20.1 0.3 reshape.524
  20.4 0.2 reshape_reshape.3
  20.6 0.6 %slice_reduce_fusion.3 = (f32[13056]{0:T(1024)S(1)}, f32[13056]{0:T(1024)S(1)}, f32[13056]{0:T(1024)S(1)}, f32[13056]{0:T(1024)S(1)}) fusion(f32[4,13056]{1,0:T(4,128)S(1)} %constant_dynamic-update-slice_fusion), kind=kLoop, calls=%fused_computation.93 | loop fusion | bytes 417792 | tf_op jit(solution)/shard_map/slice | solution.py:86
  21.2 1.6 %collective-permute-start.5 = (f32[102,128]{1,0:T(8,128)S(1)}, f32[102,128]{1,0:T(8,128)S(1)}, u32[]{:S(2)}, u32[]{:S(2)}) collective-permute-start(f32[102,128]{1,0:T(8,128)S(1)} %bitcast.87), channel_id=1, source_target_pairs={{0,1},{1,2},{2,3},{3,0},{4,5},{5,6},{6,7},{7,4},{8,9},{9,10},{10,1... | collective-permute-start | bytes 156680 | tf_op jit(solution)/shard_map/ppermute | solution.py:16
  22.8 2.6 %collective-permute-start.6 = (f32[102,128]{1,0:T(8,128)S(1)}, f32[102,128]{1,0:T(8,128)S(1)}, u32[]{:S(2)}, u32[]{:S(2)}) collective-permute-start(f32[102,128]{1,0:T(8,128)S(1)} %bitcast.86), channel_id=1, source_target_pairs={{0,2},{1,3},{2,0},{3,1},{4,6},{5,7},{6,4},{7,5},{8,10},{9,11},{10,... | collective-permute-start | bytes 156680 | tf_op jit(solution)/shard_map/ppermute | solution.py:16
  25.4 1.3 %collective-permute-start.7 = (f32[102,128]{1,0:T(8,128)S(1)}, f32[102,128]{1,0:T(8,128)S(1)}, u32[]{:S(2)}, u32[]{:S(2)}) collective-permute-start(f32[102,128]{1,0:T(8,128)S(1)} %bitcast.85), channel_id=1, source_target_pairs={{0,3},{1,0},{2,1},{3,2},{4,7},{5,4},{6,5},{7,6},{8,11},{9,8},{10,9... | collective-permute-start | bytes 156680 | tf_op jit(solution)/shard_map/ppermute | solution.py:16
  26.8 0.7 %collective-permute-done.5 = f32[102,128]{1,0:T(8,128)S(1)} collective-permute-done((f32[102,128]{1,0:T(8,128)S(1)}, f32[102,128]{1,0:T(8,128)S(1)}, u32[]{:S(2)}, u32[]{:S(2)}) %collective-permute-start.5) | collective-permute-done | bytes 52256 | tf_op jit(solution)/shard_map/ppermute | solution.py:16
  27.4 2.1 %collective-permute-done.6 = f32[102,128]{1,0:T(8,128)S(1)} collective-permute-done((f32[102,128]{1,0:T(8,128)S(1)}, f32[102,128]{1,0:T(8,128)S(1)}, u32[]{:S(2)}, u32[]{:S(2)}) %collective-permute-start.6) | collective-permute-done | bytes 52256 | tf_op jit(solution)/shard_map/ppermute | solution.py:16
  29.5 0.3 collective-permute-done.7
  29.8 0.1 collective-permute-start.8
  29.9 0.1 broadcast_and_fusion
  30.0 0.1 slice.255
  30.0 1.1 %collective-permute-done.8 = f32[102,128]{1,0:T(8,128)S(1)} collective-permute-done((f32[102,128]{1,0:T(8,128)S(1)}, f32[102,128]{1,0:T(8,128)S(1)}, u32[]{:S(2)}, u32[]{:S(2)}) %collective-permute-start.8) | collective-permute-done | bytes 52256 | tf_op jit(solution)/shard_map/ppermute | solution.py:16
  31.2 0.1 reshape.525
  31.3 0.1 reshape.527
  31.4 0.2 fusion.87
  31.6 0.4 fusion.46
  32.0 0.0 copy-start
  32.1 0.2 fusion.23
  32.3 0.2 fusion.32
  32.5 0.2 fusion.41
  32.7 0.2 fusion.44
  32.8 0.0 copy-done
  32.9 0.2 fusion.83
  33.0 1.7 %collective-permute-start.9 = (bf16[8,4,2,128]{3,0,2,1:T(8,128)(2,1)S(1)}, bf16[8,4,2,128]{3,0,2,1:T(8,128)(2,1)S(1)}, u32[]{:S(2)}, u32[]{:S(2)}) collective-permute-start(bf16[8,4,2,128]{3,0,2,1:T(8,128)(2,1)S(1)} %bitcast.77), channel_id=1, source_target_pairs={{0,4},{4,8},{8,12},{12,0},{1,5},{5,9},{9,13},{13,1},{2,6},{6,10},{... | collective-permute-start | bytes 49160 | tf_op jit(solution)/shard_map/ppermute | solution.py:16
  34.7 0.5 %collective-permute-start.10 = (bf16[8,4,2,128]{3,0,2,1:T(8,128)(2,1)S(1)}, bf16[8,4,2,128]{3,0,2,1:T(8,128)(2,1)S(1)}, u32[]{:S(2)}, u32[]{:S(2)}) collective-permute-start(bf16[8,4,2,128]{3,0,2,1:T(8,128)(2,1)S(1)} %bitcast.78), channel_id=1, source_target_pairs={{0,8},{4,12},{8,0},{12,4},{1,9},{5,13},{9,1},{13,5},{2,10},{6,14},... | collective-permute-start | bytes 49160 | tf_op jit(solution)/shard_map/ppermute | solution.py:16
  35.2 2.2 %collective-permute-start.11 = (bf16[8,4,2,128]{3,0,2,1:T(8,128)(2,1)S(1)}, bf16[8,4,2,128]{3,0,2,1:T(8,128)(2,1)S(1)}, u32[]{:S(2)}, u32[]{:S(2)}) collective-permute-start(bf16[8,4,2,128]{3,0,2,1:T(8,128)(2,1)S(1)} %bitcast.79), channel_id=1, source_target_pairs={{0,12},{4,0},{8,4},{12,8},{1,13},{5,1},{9,5},{13,9},{2,14},{6,2},{... | collective-permute-start | bytes 49160 | tf_op jit(solution)/shard_map/ppermute | solution.py:16
  37.4 0.3 collective-permute-done.9
  37.7 0.7 %collective-permute-done.10 = bf16[8,4,2,128]{3,0,2,1:T(8,128)(2,1)S(1)} collective-permute-done((bf16[8,4,2,128]{3,0,2,1:T(8,128)(2,1)S(1)}, bf16[8,4,2,128]{3,0,2,1:T(8,128)(2,1)S(1)}, u32[]{:S(2)}, u32[]{:S(2)}) %collective-permute-start.10) | collective-permute-done | bytes 16416 | tf_op jit(solution)/shard_map/ppermute | solution.py:16
  38.4 0.5 %collective-permute-done.11 = bf16[8,4,2,128]{3,0,2,1:T(8,128)(2,1)S(1)} collective-permute-done((bf16[8,4,2,128]{3,0,2,1:T(8,128)(2,1)S(1)}, bf16[8,4,2,128]{3,0,2,1:T(8,128)(2,1)S(1)}, u32[]{:S(2)}, u32[]{:S(2)}) %collective-permute-start.11) | collective-permute-done | bytes 16416 | tf_op jit(solution)/shard_map/ppermute | solution.py:16
  39.0 1.0 %collective-permute-start.12 = (bf16[4,8,4,2,128]{4,1,0,3,2:T(8,128)(2,1)S(1)}, bf16[4,8,4,2,128]{4,1,0,3,2:T(8,128)(2,1)S(1)}, u32[]{:S(2)}, u32[]{:S(2)}) collective-permute-start(bf16[4,8,4,2,128]{4,1,0,3,2:T(8,128)(2,1)S(1)} %get-tuple-element.33), channel_id=1, source_target_pairs={{0,1},{1,2},{2,3},{3,0},{4,5},{5,6},{6,7},{7,4},{8,9},{9,10},{10,1... | collective-permute-start | bytes 196616 | tf_op jit(solution)/shard_map/ppermute | solution.py:16
  40.0 2.6 %collective-permute-start.13 = (bf16[4,8,4,2,128]{4,1,0,3,2:T(8,128)(2,1)S(1)}, bf16[4,8,4,2,128]{4,1,0,3,2:T(8,128)(2,1)S(1)}, u32[]{:S(2)}, u32[]{:S(2)}) collective-permute-start(bf16[4,8,4,2,128]{4,1,0,3,2:T(8,128)(2,1)S(1)} %get-tuple-element.33), channel_id=1, source_target_pairs={{0,2},{1,3},{2,0},{3,1},{4,6},{5,7},{6,4},{7,5},{8,10},{9,11},{10,... | collective-permute-start | bytes 196616 | tf_op jit(solution)/shard_map/ppermute | solution.py:16
  42.6 0.4 collective-permute-start.14
  43.0 0.6 %copy.56 = f32[4,16,128]{2,1,0:T(8,128)} copy(f32[4,16,128]{2,0,1:T(4,128)S(1)} %get-tuple-element.13) | data formatting | bytes 65536
  43.6 1.6 %collective-permute-done.12 = bf16[4,8,4,2,128]{4,1,0,3,2:T(8,128)(2,1)S(1)} collective-permute-done((bf16[4,8,4,2,128]{4,1,0,3,2:T(8,128)(2,1)S(1)}, bf16[4,8,4,2,128]{4,1,0,3,2:T(8,128)(2,1)S(1)}, u32[]{:S(2)}, u32[]{:S(2)}) %collective-permute-start.12) | collective-permute-done | bytes 65568 | tf_op jit(solution)/shard_map/ppermute | solution.py:16
  45.2 1.8 %collective-permute-done.13 = bf16[4,8,4,2,128]{4,1,0,3,2:T(8,128)(2,1)S(1)} collective-permute-done((bf16[4,8,4,2,128]{4,1,0,3,2:T(8,128)(2,1)S(1)}, bf16[4,8,4,2,128]{4,1,0,3,2:T(8,128)(2,1)S(1)}, u32[]{:S(2)}, u32[]{:S(2)}) %collective-permute-start.13) | collective-permute-done | bytes 65568 | tf_op jit(solution)/shard_map/ppermute | solution.py:16
  47.0 0.4 collective-permute-done.14
  47.5 0.3 fusion
  47.8 1.3 %copy.57 = bf16[1,1,1,256,4,2,128]{6,5,4,3,2,1,0:T(2,128)(2,1)} copy(bf16[1,1,1,256,4,2,128]{6,3,5,4,2,1,0:T(8,128)(2,1)S(1)} %fusion) | data formatting | bytes 1048576
  (25 shorter events, 0.5 us)
Async XLA Ops:
  1.3 2.0 %collective-permute-start = (s32[2,256]{1,0:T(2,128)S(1)}, s32[2,256]{1,0:T(2,128)S(1)}, u32[]{:S(2)}, u32[]{:S(2)}) collective-permute-start(s32[2,256]{1,0:T(2,128)S(1)} %pad_add_fusion), channel_id=1, source_target_pairs={{0,16},{16,0},{1,17},{17,1},{2,18},{18,2},{3,19},{19,3},{4,20},{20... | collective-permute-start | bytes 6152 | tf_op jit(solution)/shard_map/ppermute | solution.py:16
  1.8 1.5 %copy-start.1 = (s32[1,1,1,256]{3,2,1,0:T(1,128)S(1)}, s32[1,1,1,256]{3,2,1,0:T(1,128)}, u32[]{:S(2)}) copy-start(s32[1,1,1,256]{3,2,1,0:T(1,128)} %param.8) | copy-start | bytes 3076
  1.8 1.5 %copy-start.2 = (s32[1,1,1,256]{3,2,1,0:T(1,128)S(1)}, s32[1,1,1,256]{3,2,1,0:T(1,128)}, u32[]{:S(2)}) copy-start(s32[1,1,1,256]{3,2,1,0:T(1,128)} %param.7) | copy-start | bytes 3076
  3.2 2.0 %collective-permute-start.1 = (bf16[256,4,2,128]{3,0,2,1:T(8,128)(2,1)S(1)}, bf16[256,4,2,128]{3,0,2,1:T(8,128)(2,1)S(1)}, u32[]{:S(2)}, u32[]{:S(2)}) collective-permute-start(bf16[256,4,2,128]{3,0,2,1:T(8,128)(2,1)S(1)} %get-tuple-element.18), channel_id=1, source_target_pairs={{0,16},{16,0},{1,17},{17,1},{2,18},{18,2},{3,19},{19,3},{4,20},{20... | collective-permute-start | bytes 1572872 | tf_op jit(solution)/shard_map/ppermute | solution.py:16
  5.6 9.4 %collective-permute-start.2 = (f32[48,4,2,128]{3,0,2,1:T(8,128)S(1)}, f32[48,4,2,128]{3,0,2,1:T(8,128)S(1)}, u32[]{:S(2)}, u32[]{:S(2)}) collective-permute-start(f32[48,4,2,128]{3,0,2,1:T(8,128)S(1)} %get-tuple-element.19), channel_id=1, source_target_pairs={{0,4},{4,8},{8,12},{12,0},{1,5},{5,9},{9,13},{13,1},{2,6},{6,10},{... | collective-permute-start | bytes 589832 | tf_op jit(solution)/shard_map/ppermute | solution.py:16
  8.3 10.6 %collective-permute-start.3 = (f32[48,4,2,128]{3,0,2,1:T(8,128)S(1)}, f32[48,4,2,128]{3,0,2,1:T(8,128)S(1)}, u32[]{:S(2)}, u32[]{:S(2)}) collective-permute-start(f32[48,4,2,128]{3,0,2,1:T(8,128)S(1)} %get-tuple-element.21), channel_id=1, source_target_pairs={{0,8},{4,12},{8,0},{12,4},{1,9},{5,13},{9,1},{13,5},{2,10},{6,14},... | collective-permute-start | bytes 589832 | tf_op jit(solution)/shard_map/ppermute | solution.py:16
  9.8 9.4 %collective-permute-start.4 = (f32[48,4,2,128]{3,0,2,1:T(8,128)S(1)}, f32[48,4,2,128]{3,0,2,1:T(8,128)S(1)}, u32[]{:S(2)}, u32[]{:S(2)}) collective-permute-start(f32[48,4,2,128]{3,0,2,1:T(8,128)S(1)} %get-tuple-element.20), channel_id=1, source_target_pairs={{0,12},{4,0},{8,4},{12,8},{1,13},{5,1},{9,5},{13,9},{2,14},{6,2},{... | collective-permute-start | bytes 589832 | tf_op jit(solution)/shard_map/ppermute | solution.py:16
  21.2 6.3 %collective-permute-start.5 = (f32[102,128]{1,0:T(8,128)S(1)}, f32[102,128]{1,0:T(8,128)S(1)}, u32[]{:S(2)}, u32[]{:S(2)}) collective-permute-start(f32[102,128]{1,0:T(8,128)S(1)} %bitcast.87), channel_id=1, source_target_pairs={{0,1},{1,2},{2,3},{3,0},{4,5},{5,6},{6,7},{7,4},{8,9},{9,10},{10,1... | collective-permute-start | bytes 156680 | tf_op jit(solution)/shard_map/ppermute | solution.py:16
  22.8 6.7 %collective-permute-start.6 = (f32[102,128]{1,0:T(8,128)S(1)}, f32[102,128]{1,0:T(8,128)S(1)}, u32[]{:S(2)}, u32[]{:S(2)}) collective-permute-start(f32[102,128]{1,0:T(8,128)S(1)} %bitcast.86), channel_id=1, source_target_pairs={{0,2},{1,3},{2,0},{3,1},{4,6},{5,7},{6,4},{7,5},{8,10},{9,11},{10,... | collective-permute-start | bytes 156680 | tf_op jit(solution)/shard_map/ppermute | solution.py:16
  25.4 4.4 %collective-permute-start.7 = (f32[102,128]{1,0:T(8,128)S(1)}, f32[102,128]{1,0:T(8,128)S(1)}, u32[]{:S(2)}, u32[]{:S(2)}) collective-permute-start(f32[102,128]{1,0:T(8,128)S(1)} %bitcast.85), channel_id=1, source_target_pairs={{0,3},{1,0},{2,1},{3,2},{4,7},{5,4},{6,5},{7,6},{8,11},{9,8},{10,9... | collective-permute-start | bytes 156680 | tf_op jit(solution)/shard_map/ppermute | solution.py:16
  29.8 1.3 %collective-permute-start.8 = (f32[102,128]{1,0:T(8,128)S(1)}, f32[102,128]{1,0:T(8,128)S(1)}, u32[]{:S(2)}, u32[]{:S(2)}) collective-permute-start(f32[102,128]{1,0:T(8,128)S(1)} %fusion.49), channel_id=1, source_target_pairs={{0,16},{16,0},{1,17},{17,1},{2,18},{18,2},{3,19},{19,3},{4,20},{20... | collective-permute-start | bytes 156680 | tf_op jit(solution)/shard_map/ppermute | solution.py:16
  32.0 0.8 %copy-start = (f32[4,16,128]{2,1,0:T(8,128)S(1)}, f32[4,16,128]{2,1,0:T(8,128)}, u32[]{:S(2)}) copy-start(f32[4,16,128]{2,1,0:T(8,128)} %param.9) | copy-start | bytes 98308
  33.0 4.7 %collective-permute-start.9 = (bf16[8,4,2,128]{3,0,2,1:T(8,128)(2,1)S(1)}, bf16[8,4,2,128]{3,0,2,1:T(8,128)(2,1)S(1)}, u32[]{:S(2)}, u32[]{:S(2)}) collective-permute-start(bf16[8,4,2,128]{3,0,2,1:T(8,128)(2,1)S(1)} %bitcast.77), channel_id=1, source_target_pairs={{0,4},{4,8},{8,12},{12,0},{1,5},{5,9},{9,13},{13,1},{2,6},{6,10},{... | collective-permute-start | bytes 49160 | tf_op jit(solution)/shard_map/ppermute | solution.py:16
  34.7 3.7 %collective-permute-start.10 = (bf16[8,4,2,128]{3,0,2,1:T(8,128)(2,1)S(1)}, bf16[8,4,2,128]{3,0,2,1:T(8,128)(2,1)S(1)}, u32[]{:S(2)}, u32[]{:S(2)}) collective-permute-start(bf16[8,4,2,128]{3,0,2,1:T(8,128)(2,1)S(1)} %bitcast.78), channel_id=1, source_target_pairs={{0,8},{4,12},{8,0},{12,4},{1,9},{5,13},{9,1},{13,5},{2,10},{6,14},... | collective-permute-start | bytes 49160 | tf_op jit(solution)/shard_map/ppermute | solution.py:16
  35.2 3.7 %collective-permute-start.11 = (bf16[8,4,2,128]{3,0,2,1:T(8,128)(2,1)S(1)}, bf16[8,4,2,128]{3,0,2,1:T(8,128)(2,1)S(1)}, u32[]{:S(2)}, u32[]{:S(2)}) collective-permute-start(bf16[8,4,2,128]{3,0,2,1:T(8,128)(2,1)S(1)} %bitcast.79), channel_id=1, source_target_pairs={{0,12},{4,0},{8,4},{12,8},{1,13},{5,1},{9,5},{13,9},{2,14},{6,2},{... | collective-permute-start | bytes 49160 | tf_op jit(solution)/shard_map/ppermute | solution.py:16
  39.0 6.2 %collective-permute-start.12 = (bf16[4,8,4,2,128]{4,1,0,3,2:T(8,128)(2,1)S(1)}, bf16[4,8,4,2,128]{4,1,0,3,2:T(8,128)(2,1)S(1)}, u32[]{:S(2)}, u32[]{:S(2)}) collective-permute-start(bf16[4,8,4,2,128]{4,1,0,3,2:T(8,128)(2,1)S(1)} %get-tuple-element.33), channel_id=1, source_target_pairs={{0,1},{1,2},{2,3},{3,0},{4,5},{5,6},{6,7},{7,4},{8,9},{9,10},{10,1... | collective-permute-start | bytes 196616 | tf_op jit(solution)/shard_map/ppermute | solution.py:16
  40.0 7.0 %collective-permute-start.13 = (bf16[4,8,4,2,128]{4,1,0,3,2:T(8,128)(2,1)S(1)}, bf16[4,8,4,2,128]{4,1,0,3,2:T(8,128)(2,1)S(1)}, u32[]{:S(2)}, u32[]{:S(2)}) collective-permute-start(bf16[4,8,4,2,128]{4,1,0,3,2:T(8,128)(2,1)S(1)} %get-tuple-element.33), channel_id=1, source_target_pairs={{0,2},{1,3},{2,0},{3,1},{4,6},{5,7},{6,4},{7,5},{8,10},{9,11},{10,... | collective-permute-start | bytes 196616 | tf_op jit(solution)/shard_map/ppermute | solution.py:16
  42.6 4.9 %collective-permute-start.14 = (bf16[4,8,4,2,128]{4,1,0,3,2:T(8,128)(2,1)S(1)}, bf16[4,8,4,2,128]{4,1,0,3,2:T(8,128)(2,1)S(1)}, u32[]{:S(2)}, u32[]{:S(2)}) collective-permute-start(bf16[4,8,4,2,128]{4,1,0,3,2:T(8,128)(2,1)S(1)} %get-tuple-element.33), channel_id=1, source_target_pairs={{0,3},{1,0},{2,1},{3,2},{4,7},{5,4},{6,5},{7,6},{8,11},{9,8},{10,9... | collective-permute-start | bytes 196616 | tf_op jit(solution)/shard_map/ppermute | solution.py:16
